TPU v7x, 32 devices: a whole 2x2x4 slice. The times are simulated.
32 devices in a mesh: lat: 8 (over z, y), grp: 4 (over x, core).
Axes of the slice: x: 2, y: 2, z: 4, core: 2. Of those that a mesh axis runs over, the one named last changes fastest.
Arguments:
- fine_source: float32 [8, 24, 4, 4, 512], P('lat', None, None, None, 'grp'), may hold values from -6 to 6
- links: bfloat16 [8, 4, 18, 4, 4, 512], P('lat', None, None, None, None, 'grp'), may hold values from -2.5 to 2.5
- test_vectors: bfloat16 [8, 24, 24, 4, 4, 512], P('lat', None, None, None, None, 'grp'), may hold values from -0.15625 to 0.15625
- aggregate_map: int32 [8, 4, 4, 8, 64], P('lat', None, None, 'grp'), may hold values from 0 to 15, never falling along the last dimension, each value on 1 to 8 neighbouring positions
- colouring: int32 [8, 4, 16], P('lat', 'grp'), may hold values 0 or 1
- coarse_operator: bfloat16 [8, 4, 9, 2, 48, 768], P('lat', 'grp'), may hold values from -1 to 3
- block_inverse: bfloat16 [8, 4, 2, 48, 768], P('lat', 'grp'), may hold values from -1 to 1
Outputs:
- solution: float32 [8, 24, 4, 4, 512], P('lat', None, None, None, 'grp')
- coarse_correction: float32 [8, 4, 2, 48, 16], P('lat', 'grp')
Inputs may be any that keep to these rules, and one draw needn't show every extreme that they name: `aggregate_map`: along each line of 64 sites in x the numbers never fall, and each of 0 to 15 covers 1 to 8 consecutive sites.
All inputs are finite; a program needn't handle non-finite values. No bound on the sum of `colouring` on one device may be relied on, other than what follows from the above.
Results may differ from a plain program's by a relative error of at most 0.0029.
Values may be sent and summed in bfloat16 or wider, within the bound.
No kernel may reach another device: no remote copies, remote signals or barrier semaphores. Data moves between devices by JAX's collectives and lax.ppermute only.
A program may use at most 128 MiB of HBM per device.

v0:
```python
import functools

import jax
import jax.numpy as jnp
from jax import lax
from jax.experimental import pallas as pl
from jax.experimental.pallas import tpu as pltpu
from jax.sharding import PartitionSpec as P

CX = 64
PZ = 8
NVEC = 24
AGG = 16
MR_STEPS = 2
CDOF = 48


def passed_along(shard, axis, by):
    size = lax.axis_size(axis)
    return lax.ppermute(shard, axis, [(i, (i + by) % size) for i in range(size)])


def padded_2(shard, sides, width):
    for axis, dim in sides:
        size, length = (lax.axis_size(axis), shard.shape[dim])
        up = [(i, (i + 1) % size) for i in range(size)]
        down = [(j, i) for i, j in up]
        last = lax.slice_in_dim(shard, length - width, length, axis=dim)
        first = lax.slice_in_dim(shard, 0, width, axis=dim)
        before = lax.ppermute(last, axis, up)
        after = lax.ppermute(first, axis, down)
        shard = jnp.concatenate([before, shard, after], axis=dim)
    return shard


def times_minus_i(values):
    return jnp.stack([values[1], -values[0]])


def times_plus_i(values):
    return jnp.stack([-values[1], values[0]])


def spin_factor(direction, spin_pair):
    if direction == 0:
        return jnp.stack([times_minus_i(spin_pair[:, 1]), times_minus_i(spin_pair[:, 0])], axis=1)
    if direction == 1:
        return jnp.stack([-spin_pair[:, 1], spin_pair[:, 0]], axis=1)
    if direction == 2:
        return jnp.stack([times_minus_i(spin_pair[:, 0]), times_plus_i(spin_pair[:, 1])], axis=1)
    return spin_pair


def project_minus(direction, spinor):
    return spinor[:, :2] - spin_factor(direction, spinor[:, 2:])


def project_plus(direction, spinor):
    return spinor[:, :2] + spin_factor(direction, spinor[:, 2:])


def rebuild_minus(direction, half_spinor):
    lower_part = spin_factor(direction, half_spinor) if direction < 3 else -half_spinor
    return jnp.concatenate([half_spinor, lower_part], axis=1)


def rebuild_plus(direction, half_spinor):
    lower_part = -spin_factor(direction, half_spinor) if direction < 3 else half_spinor
    return jnp.concatenate([half_spinor, lower_part], axis=1)


def colour_product(gauge_link, half_spinor, adjoint):
    link_real = gauge_link[0]
    link_imag = gauge_link[1]
    if adjoint:
        link_real = jnp.swapaxes(link_real, 0, 1)
        link_imag = -jnp.swapaxes(link_imag, 0, 1)
    spin_real = half_spinor[0][:, None]
    spin_imag = half_spinor[1][:, None]
    real_part = jnp.sum(link_real[None] * spin_real - link_imag[None] * spin_imag, axis=2)
    imag_part = jnp.sum(link_real[None] * spin_imag + link_imag[None] * spin_real, axis=2)
    return jnp.stack([real_part, imag_part])


def complex_scale(factor_real, factor_imag, lattice):
    return jnp.stack(
        [
            factor_real * lattice[0] - factor_imag * lattice[1],
            factor_real * lattice[1] + factor_imag * lattice[0],
        ]
    )


def apply_blocks(blocks, nearby):
    matrices = blocks.reshape(blocks.shape[0], 2, CDOF, CDOF, AGG)
    vector_real = nearby[:, 0][:, None]
    vector_imag = nearby[:, 1][:, None]
    real_part = jnp.sum(matrices[:, 0] * vector_real - matrices[:, 1] * vector_imag, axis=(0, 2))
    imag_part = jnp.sum(matrices[:, 0] * vector_imag + matrices[:, 1] * vector_real, axis=(0, 2))
    return jnp.stack([real_part, imag_part])


def keep_if(allowed, values):
    return jnp.where(allowed, values, jnp.zeros_like(values))


def permute_from(value, axis, offset, allowed):
    size = lax.axis_size(axis)
    pairs = [((i + offset) % size, i) for i in range(size) if allowed(i)]
    if not pairs:
        return None
    return lax.ppermute(value, axis, pairs)


class Shifts:
    def __init__(self, rows, lanes):
        self.rows = rows
        self.lanes = lanes
        self.lane = lax.broadcasted_iota(jnp.int32, (rows, lanes), 1)
        self.row = lax.broadcasted_iota(jnp.int32, (rows, lanes), 0)
        self.xpos = self.lane % CX
        self.zpos = self.row % 4

    def roll(self, a, shift, axis):
        n = a.shape[axis]
        return pltpu.roll(a, shift % n, a.ndim + axis)

    def ahead(self, direction, a, nbr):
        if direction == 0:
            return jnp.where(self.xpos == CX - 1, self.roll(a, CX - 1, -1), self.roll(a, -1, -1))
        if direction == 1:
            half = self.lanes // 2
            filled = jnp.where(self.lane < half, 0.0 if nbr is None else nbr, a)
            return self.roll(filled, half, -1)
        if direction == 2:
            inner = self.roll(a, -1, -2)
            outer = 0.0 if nbr is None else self.roll(nbr, 3, -2)
            return jnp.where(self.zpos == 3, outer, inner)
        filled = jnp.where(self.row < 4, 0.0 if nbr is None else nbr, a)
        return self.roll(filled, -4, -2)

    def behind(self, direction, a, nbr):
        if direction == 0:
            return jnp.where(self.xpos == 0, self.roll(a, 1 - CX, -1), self.roll(a, 1, -1))
        if direction == 1:
            half = self.lanes // 2
            filled = jnp.where(self.lane >= half, 0.0 if nbr is None else nbr, a)
            return self.roll(filled, half, -1)
        if direction == 2:
            inner = self.roll(a, 1, -2)
            outer = 0.0 if nbr is None else self.roll(nbr, -3, -2)
            return jnp.where(self.zpos == 0, outer, inner)
        filled = jnp.where(self.row >= self.rows - 4, 0.0 if nbr is None else nbr, a)
        return self.roll(filled, 4, -2)


def hopping(spinor, links, back_links, ahead_list, behind_list):
    hop_total = None
    for direction in range(4):
        ahead_half = colour_product(links[direction], project_minus(direction, ahead_list[direction]), False)
        behind_half = colour_product(back_links[direction], project_plus(direction, behind_list[direction]), True)
        term = rebuild_minus(direction, ahead_half) + rebuild_plus(direction, behind_half)
        hop_total = term if hop_total is None else hop_total + term
    return 4.5 * spinor - 0.5 * hop_total


def pass_kernel(*refs, first, residual_only, present):
    refs = list(refs)
    out_ref = refs.pop()

    def take():
        return refs.pop(0)

    src_ref = take()
    links_ref = take()
    ghost_refs = [None, None, None, None]
    for direction in (1, 2, 3):
        if present["ghost"][direction]:
            ghost_refs[direction] = take()
    labels_ref = take()
    member_ref = take()
    cmask_ref = None if residual_only else take()
    spinor_ref = None
    halo_refs = {}
    if not first:
        spinor_ref = take()
        for direction in (1, 2, 3):
            for side in ("ahead", "behind"):
                if present[side][direction]:
                    halo_refs[(side, direction)] = take()

    rows, lanes = src_ref.shape[-2], src_ref.shape[-1]
    sh = Shifts(rows, lanes)
    shape = (2, 4, 3, rows, lanes)
    source = src_ref[...].reshape(shape)
    link_all = links_ref[...].astype(jnp.float32)
    links = [link_all[d].reshape(2, 3, 3, rows, lanes) for d in range(4)]
    back_links = []
    for direction in range(4):
        ghost = None
        if ghost_refs[direction] is not None:
            ghost = ghost_refs[direction][...].astype(jnp.float32).reshape(2, 3, 3, rows, lanes)
        back_links.append(sh.behind(direction, links[direction], ghost))

    def load_halo(side, direction):
        ref = halo_refs.get((side, direction))
        return None if ref is None else ref[...].reshape(shape)

    def wilson_global(spinor):
        ahead_list = [sh.ahead(d, spinor, load_halo("ahead", d)) for d in range(4)]
        behind_list = [sh.behind(d, spinor, load_halo("behind", d)) for d in range(4)]
        return hopping(spinor, links, back_links, ahead_list, behind_list)

    if first:
        residue = source
        current = None
    else:
        current = spinor_ref[...].reshape(shape)
        residue = source - wilson_global(current)
    if residual_only:
        out_ref[...] = residue.reshape(out_ref.shape)
        return

    labels = labels_ref[...]
    ahead_masks = [(sh.ahead(d, labels, None) == labels).astype(jnp.float32) for d in range(4)]
    behind_masks = [(sh.behind(d, labels, None) == labels).astype(jnp.float32) for d in range(4)]
    member = member_ref[...]

    def wilson_block(spinor):
        ahead_list = [sh.ahead(d, spinor, None) * ahead_masks[d] for d in range(4)]
        behind_list = [sh.behind(d, spinor, None) * behind_masks[d] for d in range(4)]
        return hopping(spinor, links, back_links, ahead_list, behind_list)

    def block_total(values):
        return jnp.sum(jnp.sum(member * values[None], axis=2, keepdims=True), axis=1, keepdims=True)

    update = None
    remainder = residue
    for repeat in range(MR_STEPS):
        image = wilson_block(remainder)
        image_flat = image.reshape(2, 12, rows, lanes)
        rest_flat = remainder.reshape(2, 12, rows, lanes)
        dot_real = jnp.sum(image_flat[0] * rest_flat[0] + image_flat[1] * rest_flat[1], axis=0)
        dot_imag = jnp.sum(image_flat[0] * rest_flat[1] - image_flat[1] * rest_flat[0], axis=0)
        norm = jnp.sum(image_flat[0] * image_flat[0] + image_flat[1] * image_flat[1], axis=0)
        denominator = block_total(norm) + 1e-06
        factor_real = jnp.sum(member * (block_total(dot_real) / denominator), axis=0)
        factor_imag = jnp.sum(member * (block_total(dot_imag) / denominator), axis=0)
        step = complex_scale(factor_real, factor_imag, remainder)
        update = step if update is None else update + step
        remainder = remainder - complex_scale(factor_real, factor_imag, image)
    update = update * cmask_ref[...]
    result = update if current is None else current + update
    out_ref[...] = result.reshape(out_ref.shape)


def run_pass(source, links, ghosts, labels, member, cmask, spinor, halos, residual_only=False):
    first = spinor is None
    present = {
        "ghost": [g is not None for g in ghosts],
        "ahead": [h is not None for h in halos["ahead"]] if not first else [False] * 4,
        "behind": [h is not None for h in halos["behind"]] if not first else [False] * 4,
    }
    operands = [source, links] + [g for g in ghosts[1:] if g is not None] + [labels, member]
    if not residual_only:
        operands.append(cmask)
    if not first:
        operands.append(spinor)
        for direction in (1, 2, 3):
            for side in ("ahead", "behind"):
                if present[side][direction]:
                    operands.append(halos[side][direction])
    kernel = functools.partial(pass_kernel, first=first, residual_only=residual_only, present=present)
    return pl.pallas_call(kernel, out_shape=jax.ShapeDtypeStruct(source.shape, jnp.float32))(*operands)


def body(
    fine_source, links, test_vectors, aggregate_map, colouring, coarse_operator, block_inverse
):
    time_extent = fine_source.shape[2]
    plane_extent = fine_source.shape[3]
    line_extent = fine_source.shape[4]
    rows = time_extent * plane_extent
    site_count = rows * line_extent
    domain_index = lax.axis_index("lat")
    domain_count = lax.axis_size("lat")
    plane_position = (domain_index + 2) % PZ
    upper_valid = plane_position < PZ - 1
    lower_valid = plane_position > 0
    later_valid = domain_index < domain_count - PZ
    earlier_valid = domain_index >= PZ

    source = fine_source.reshape(24, rows, line_extent)
    link_rows = links.reshape(4, 18, rows, line_extent)
    label_rows = aggregate_map.reshape(rows, line_extent)
    member = (label_rows[None] == jnp.arange(AGG, dtype=jnp.int32)[:, None, None]).astype(jnp.float32)
    colour_list = colouring.reshape(AGG)
    colour_masks = [
        jnp.sum(member * (colour_list == k).astype(jnp.float32)[:, None, None], axis=0) for k in range(2)
    ]
    labels = (label_rows + 1).astype(jnp.float32)

    def z_up_ok(i):
        return (i + 2) % PZ != PZ - 1

    def z_down_ok(i):
        return (i + 2) % PZ != 0

    def t_up_ok(i):
        return i + PZ < domain_count

    def t_down_ok(i):
        return i - PZ >= 0

    ghosts = [
        None,
        permute_from(link_rows[1], "grp", -1, lambda i: True),
        permute_from(link_rows[2], "lat", -1, z_down_ok),
        permute_from(link_rows[3], "lat", -PZ, t_down_ok),
    ]

    def halos_of(spinor):
        return {
            "ahead": [
                None,
                permute_from(spinor, "grp", 1, lambda i: True),
                permute_from(spinor, "lat", 1, z_up_ok),
                permute_from(spinor, "lat", PZ, t_up_ok),
            ],
            "behind": [
                None,
                permute_from(spinor, "grp", -1, lambda i: True),
                permute_from(spinor, "lat", -1, z_down_ok),
                permute_from(spinor, "lat", -PZ, t_down_ok),
            ],
        }

    def smoother_pass(spinor, colour_pass):
        halos = None if spinor is None else halos_of(spinor)
        return run_pass(source, link_rows, ghosts, labels, member, colour_masks[colour_pass], spinor, halos)

    def sweep(start):
        current = smoother_pass(start, 0)
        return smoother_pass(current, 1)

    smoothed = sweep(None)
    residue = run_pass(
        source, link_rows, ghosts, labels, member, None, smoothed, halos_of(smoothed), residual_only=True
    )
    residual = residue.astype(jnp.bfloat16)
    membership = member.reshape(AGG, site_count).T
    member_weights = membership.astype(jnp.bfloat16)
    weighted = residual.reshape(2, 2, 6, site_count)[..., None] * member_weights
    vectors = test_vectors.reshape(NVEC, 2, 2, 6, site_count)

    def contract(left, right):
        return jnp.einsum("kxqn,xqnj->xkj", left, right, preferred_element_type=jnp.float32)

    real_part = contract(vectors[:, 0], weighted[0]) + contract(vectors[:, 1], weighted[1])
    imag_part = contract(vectors[:, 0], weighted[1]) - contract(vectors[:, 1], weighted[0])
    coarse_source = jnp.stack([real_part, imag_part]).reshape(2, CDOF, AGG)
    operator_blocks = coarse_operator.reshape(9, 2, CDOF, CDOF * AGG)
    inverse_blocks = block_inverse.reshape(1, 2, CDOF, CDOF * AGG)

    def precondition(vector):
        return apply_blocks(inverse_blocks, vector[None])

    correction = precondition(coarse_source)
    for repeat in range(2):
        loop_values = padded_2(correction[None], (("grp", 0),), 1)
        nearby_arrived = []
        for nearby_offset in (-1, 1, -PZ, PZ):
            nearby_arrived.append(passed_along(correction, "lat", nearby_offset))
        correction = correction + precondition(
            coarse_source
            - apply_blocks(
                operator_blocks,
                jnp.stack(
                    [
                        correction,
                        jnp.roll(correction, -1, axis=2),
                        jnp.roll(correction, 1, axis=2),
                        loop_values[2],
                        loop_values[0],
                        keep_if(upper_valid, nearby_arrived[0]),
                        keep_if(lower_valid, nearby_arrived[1]),
                        keep_if(later_valid, nearby_arrived[2]),
                        keep_if(earlier_valid, nearby_arrived[3]),
                    ]
                ),
            )
        )
    expanded = jnp.dot(
        correction.reshape(2 * CDOF, AGG), membership.T, precision=lax.Precision.HIGHEST
    ).reshape(2, 2, NVEC, site_count)
    spread_real = jnp.swapaxes(expanded[0], 0, 1)[:, :, None]
    spread_imag = jnp.swapaxes(expanded[1], 0, 1)[:, :, None]
    real_part = jnp.sum(vectors[:, 0] * spread_real - vectors[:, 1] * spread_imag, axis=0)
    imag_part = jnp.sum(vectors[:, 0] * spread_imag + vectors[:, 1] * spread_real, axis=0)
    corrected = smoothed + jnp.stack([real_part, imag_part]).reshape(24, rows, line_extent)
    solution = sweep(corrected)
    return (
        solution.reshape(1, 24, time_extent, plane_extent, line_extent),
        correction.reshape(1, 1, 2, CDOF, AGG),
    )


def solution(mesh):
    return jax.shard_map(
        body,
        mesh=mesh,
        in_specs=(
            P("lat", None, None, None, "grp"),
            P("lat", None, None, None, None, "grp"),
            P("lat", None, None, None, None, "grp"),
            P("lat", None, None, "grp", None),
            P("lat", "grp", None),
            P("lat", "grp", None, None, None, None),
            P("lat", "grp", None, None, None),
        ),
        out_specs=(P("lat", None, None, None, "grp"), P("lat", "grp", None, None, None)),
        check_vma=False,
    )
```

profile of v0, /device:TPU:0, one launch (start us, length us, event | category | flops | bytes accessed | tf_op | source)
XLA Modules:
  0.0 191.8 jit_solution(2652293766024304769)
XLA Ops:
  2.1 4.4 %collective-permute-start.1 = (bf16[18,16,128]{2,1,0:T(8,128)(2,1)S(1)}, bf16[18,16,128]{2,1,0:T(8,128)(2,1)S(1)}, u32[]{:S(2)}, u32[]{:S(2)}) collective-permute-start(bf16[18,16,128]{2,1,0:T(8,128)(2,1)S(1)} %bitcast.254), channel_id=1, source_target_pairs={{28,0},{0,4},{4,8},{8,12},{12,16},{16,20},{24,28},{29,1},{1,5},{5,... | collective-permute-start | bytes 221192 | tf_op jit(solution)/shard_map/ppermute | solution.py:112
  10.0 1.9 %collective-permute-done.1.refs_3_ = bf16[18,16,128]{2,1,0:T(8,128)(2,1)S(1)} collective-permute-done((bf16[18,16,128]{2,1,0:T(8,128)(2,1)S(1)}, bf16[18,16,128]{2,1,0:T(8,128)(2,1)S(1)}, u32[]{:S(2)}, u32[]{:S(2)}) %collective-permute-start.1) | collective-permute-done | bytes 73760 | tf_op jit(solution)/shard_map/ppermute | solution.py:112
  12.5 4.1 %shard_map.86.refs_7_ = f32[24,16,128]{2,1,0:T(8,128)} custom-call(f32[24,16,128]{2,1,0:T(8,128)} %bitcast.214, bf16[4,18,16,128]{3,2,1,0:T(8,128)(2,1)} %bitcast.206, bf16[18,16,128]{2,1,0:T(8,128)(2,1)} %copy-done.3, bf16[18,16,128]{2,1,0:T(8,128)(2,1)} %copy-done.4, f32[16,128]{1,0:T(8,128)} %add_convert_fusion.refs_4_, f32[16,16,128]{2,1,0:T(8,128)} %fusion.28.refs_5_, ...), custom_call_target="tpu_custom_call" | custom-call | tf_op jit(solution)/shard_map/pallas_call | solution.py:274
  18.6 6.6 %collective-permute-start.4 = (f32[24,16,128]{2,1,0:T(8,128)}, f32[24,16,128]{2,1,0:T(8,128)S(1)}, u32[]{:S(2)}, u32[]{:S(2)}) collective-permute-start(f32[24,16,128]{2,1,0:T(8,128)} %shard_map.86.refs_7_), channel_id=1, source_target_pairs={{4,0},{8,4},{12,8},{16,12},{20,16},{28,24},{0,28},{5,1},{9,5},{13,... | collective-permute-start | bytes 589832 | tf_op jit(solution)/shard_map/ppermute | solution.py:112
  29.1 3.3 %collective-permute-done.4.refs_10_ = f32[24,16,128]{2,1,0:T(8,128)S(1)} collective-permute-done((f32[24,16,128]{2,1,0:T(8,128)}, f32[24,16,128]{2,1,0:T(8,128)S(1)}, u32[]{:S(2)}, u32[]{:S(2)}) %collective-permute-start.4) | collective-permute-done | bytes 196640 | tf_op jit(solution)/shard_map/ppermute | solution.py:112
  33.2 5.3 %shard_map.87.refs_6_ = f32[24,16,128]{2,1,0:T(8,128)} custom-call(f32[24,16,128]{2,1,0:T(8,128)} %bitcast.215, bf16[4,18,16,128]{3,2,1,0:T(8,128)(2,1)} %bitcast.207, bf16[18,16,128]{2,1,0:T(8,128)(2,1)} %copy-done.3, bf16[18,16,128]{2,1,0:T(8,128)(2,1)} %copy-done.4, f32[16,128]{1,0:T(8,128)} %add_convert_fusion.refs_4_, f32[16,16,128]{2,1,0:T(8,128)} %fusion.28.refs_5_, ...), custom_call_target="tpu_custom_call" | custom-call | tf_op jit(solution)/shard_map/pallas_call | solution.py:274
  40.4 6.6 %collective-permute-start.8 = (f32[24,16,128]{2,1,0:T(8,128)}, f32[24,16,128]{2,1,0:T(8,128)}, u32[]{:S(2)}, u32[]{:S(2)}) collective-permute-start(f32[24,16,128]{2,1,0:T(8,128)} %shard_map.87.refs_6_), channel_id=1, source_target_pairs={{4,0},{8,4},{12,8},{16,12},{20,16},{28,24},{0,28},{5,1},{9,5},{13,... | collective-permute-start | bytes 589832 | tf_op jit(solution)/shard_map/ppermute | solution.py:112
  49.5 3.3 %copy.40 = bf16[1,1,9,2,48,768]{4,5,2,3,0,1:T(8,128)(2,1)S(1)} copy(bf16[1,1,9,2,48,768]{5,4,3,2,1,0:T(8,128)(2,1)} %param.12) | data formatting | bytes 2654208 | tf_op jit(solution)/shard_map/reshape;reshape | solution.py:95
  52.8 4.5 %copy.23 = bf16[1,1,9,2,48,768]{4,5,3,2,1,0:T(8,128)(2,1)} copy(bf16[1,1,9,2,48,768]{5,4,3,2,1,0:T(8,128)(2,1)} %param.12) | data formatting | bytes 2654208 | tf_op args[5]
  59.1 4.3 %copy.15 = bf16[1,24,24,4,4,128]{5,4,3,1,2,0:T(4,128)(2,1)} copy(bf16[1,24,24,4,4,128]{5,4,3,2,1,0:T(4,128)(2,1)} %param.9) | data formatting | bytes 4718592 | tf_op args[2]
  63.5 5.1 %reshape.506 = bf16[24,2,2,6,2048]{4,0,3,2,1:T(8,128)(2,1)} reshape(bf16[1,24,24,4,4,128]{5,4,3,1,2,0:T(4,128)(2,1)} %copy.15) | data formatting | bytes 4718592 | tf_op jit(solution)/shard_map/reshape | solution.py:354
  68.6 3.2 %shard_map.88 = f32[24,16,128]{2,1,0:T(8,128)} custom-call(f32[24,16,128]{2,1,0:T(8,128)} %bitcast.216, bf16[4,18,16,128]{3,2,1,0:T(8,128)(2,1)} %bitcast.208, bf16[18,16,128]{2,1,0:T(8,128)(2,1)} %copy-done.3, bf16[18,16,128]{2,1,0:T(8,128)(2,1)} %copy-done.4, f32[16,128]{1,0:T(8,128)} %add_convert_fusion.refs_4_, f32[16,16,128]{2,1,0:T(8,128)} %fusion.28.refs_5_, ...), custom_call_target="tpu_custom_call" | custom-call | tf_op jit(solution)/shard_map/pallas_call | solution.py:274
  76.2 2.3 %convolution_bitcast_fusion = f32[2,16,24]{2,1,0:T(8,128)S(1)} fusion(bf16[24,2,2,6,2048]{4,0,3,2,1:T(8,128)(2,1)} %reshape.506, bf16[2,2,6,2048,16]{3,4,2,1,0:T(8,128)(2,1)S(1)} %broadcast_multiply_fusion), kind=kOutput, calls=%fused_computation.28 | convolution fusion | flops 18874368 | bytes 1969152 | tf_op jit(solution)/shard_map/kxqn,xqnj->xkj/dot_general | solution.py:357
  80.3 2.1 %convolution_bitcast_fusion.2 = f32[2,16,24]{2,1,0:T(8,128)S(1)} fusion(bf16[24,2,2,6,2048]{4,0,3,2,1:T(8,128)(2,1)} %reshape.506, bf16[2,2,6,2048,16]{3,4,2,1,0:T(8,128)(2,1)} %copy-done.6), kind=kOutput, calls=%fused_computation.30 | convolution fusion | flops 18874368 | bytes 1969152 | tf_op jit(solution)/shard_map/kxqn,xqnj->xkj/dot_general | solution.py:357
  113.9 4.7 %fusion.1 = (f32[48,16]{0,1:T(8,128)S(1)}, f32[48,16]{0,1:T(8,128)S(1)}) fusion(f32[9,48,16]{2,1,0:T(8,128)} %copy.26, f32[9,48,16]{2,1,0:T(8,128)} %copy.25, bf16[9,2,48,48,16]{2,4,3,0,1:T(8,128)(2,1)S(1)} %bitcast.202, bf16[9,2,48,48,16]{2,4,3,1,0:T(8,128)(2,1)} %bitcast.204), kind=kLoop, calls=%fused_computation.9 | loop fusion | flops 3316224 | bytes 1388544 | tf_op jit(solution)/shard_map/reduce_sum | solution.py:98
  124.0 3.6 %collective-permute-start.17 = (f32[2,48,16]{1,2,0:T(8,128)S(1)}, f32[2,48,16]{1,2,0:T(8,128)S(1)}, u32[]{:S(2)}, u32[]{:S(2)}) collective-permute-start(f32[2,48,16]{1,2,0:T(8,128)S(1)} %maximum_add_fusion), channel_id=1, source_target_pairs={{0,28},{4,0},{8,4},{12,8},{16,12},{20,16},{24,20},{28,24},{1,29},{... | collective-permute-start | bytes 18440 | tf_op jit(solution)/shard_map/ppermute | solution.py:20
  130.9 3.1 %collective-permute-done.18 = f32[2,48,16]{1,2,0:T(8,128)S(1)} collective-permute-done((f32[2,48,16]{1,2,0:T(8,128)S(1)}, f32[2,48,16]{1,2,0:T(8,128)S(1)}, u32[]{:S(2)}, u32[]{:S(2)}) %collective-permute-start.18) | collective-permute-done | bytes 6176 | tf_op jit(solution)/shard_map/ppermute | solution.py:20
  138.1 4.7 %fusion.5 = (f32[48,16]{0,1:T(8,128)S(1)}, f32[48,16]{0,1:T(8,128)S(1)}) fusion(f32[9,48,16]{2,1,0:T(8,128)} %copy.30, f32[9,48,16]{2,1,0:T(8,128)} %copy.29, bf16[9,2,48,48,16]{2,4,3,0,1:T(8,128)(2,1)S(1)} %bitcast.203, bf16[9,2,48,48,16]{2,4,3,1,0:T(8,128)(2,1)} %bitcast.205), kind=kLoop, calls=%fused_computation.13 | loop fusion | flops 3316224 | bytes 1388544 | tf_op jit(solution)/shard_map/reduce_sum | solution.py:98
  150.5 6.6 %collective-permute-start.22 = (f32[24,16,128]{2,1,0:T(8,128)S(1)}, f32[24,16,128]{2,1,0:T(8,128)S(1)}, u32[]{:S(2)}, u32[]{:S(2)}) collective-permute-start(f32[24,16,128]{2,1,0:T(8,128)S(1)} %add.119.refs_7_), channel_id=1, source_target_pairs={{4,0},{8,4},{12,8},{16,12},{20,16},{28,24},{0,28},{5,1},{9,5},{13,... | collective-permute-start | bytes 589832 | tf_op jit(solution)/shard_map/ppermute | solution.py:112
  158.9 2.9 %collective-permute-done.22.refs_10_ = f32[24,16,128]{2,1,0:T(8,128)S(1)} collective-permute-done((f32[24,16,128]{2,1,0:T(8,128)S(1)}, f32[24,16,128]{2,1,0:T(8,128)S(1)}, u32[]{:S(2)}, u32[]{:S(2)}) %collective-permute-start.22) | collective-permute-done | bytes 196640 | tf_op jit(solution)/shard_map/ppermute | solution.py:112
  163.9 5.3 %shard_map.89.refs_7_ = f32[24,16,128]{2,1,0:T(8,128)} custom-call(f32[24,16,128]{2,1,0:T(8,128)} %bitcast.217, bf16[4,18,16,128]{3,2,1,0:T(8,128)(2,1)} %bitcast.209, bf16[18,16,128]{2,1,0:T(8,128)(2,1)} %copy-done.3, bf16[18,16,128]{2,1,0:T(8,128)(2,1)} %copy-done.4, f32[16,128]{1,0:T(8,128)} %add_convert_fusion.refs_4_, f32[16,16,128]{2,1,0:T(8,128)} %fusion.28.refs_5_, ...), custom_call_target="tpu_custom_call" | custom-call | tf_op jit(solution)/shard_map/pallas_call | solution.py:274
  171.1 6.6 %collective-permute-start.26 = (f32[24,16,128]{2,1,0:T(8,128)}, f32[24,16,128]{2,1,0:T(8,128)S(1)}, u32[]{:S(2)}, u32[]{:S(2)}) collective-permute-start(f32[24,16,128]{2,1,0:T(8,128)} %shard_map.89.refs_7_), channel_id=1, source_target_pairs={{4,0},{8,4},{12,8},{16,12},{20,16},{28,24},{0,28},{5,1},{9,5},{13,... | collective-permute-start | bytes 589832 | tf_op jit(solution)/shard_map/ppermute | solution.py:112
  181.8 3.3 %collective-permute-done.26.refs_10_ = f32[24,16,128]{2,1,0:T(8,128)S(1)} collective-permute-done((f32[24,16,128]{2,1,0:T(8,128)}, f32[24,16,128]{2,1,0:T(8,128)S(1)}, u32[]{:S(2)}, u32[]{:S(2)}) %collective-permute-start.26) | collective-permute-done | bytes 196640 | tf_op jit(solution)/shard_map/ppermute | solution.py:112
  186.6 5.3 %shard_map.90 = f32[24,16,128]{2,1,0:T(8,128)} custom-call(f32[24,16,128]{2,1,0:T(8,128)} %bitcast.218, bf16[4,18,16,128]{3,2,1,0:T(8,128)(2,1)} %bitcast.210, bf16[18,16,128]{2,1,0:T(8,128)(2,1)} %copy-done.3, bf16[18,16,128]{2,1,0:T(8,128)(2,1)} %copy-done.4, f32[16,128]{1,0:T(8,128)} %add_convert_fusion.refs_4_, f32[16,16,128]{2,1,0:T(8,128)} %fusion.28.refs_5_, ...), custom_call_target="tpu_custom_call" | custom-call | tf_op jit(solution)/shard_map/pallas_call | solution.py:274
  (168 shorter events, 87.6 us)
Async XLA Ops:
  1.6 8.4 %collective-permute-start = (bf16[18,16,128]{2,1,0:T(8,128)(2,1)S(1)}, bf16[18,16,128]{2,1,0:T(8,128)(2,1)S(1)}, u32[]{:S(2)}, u32[]{:S(2)}) collective-permute-start(bf16[18,16,128]{2,1,0:T(8,128)(2,1)S(1)} %bitcast.255), channel_id=1, source_target_pairs={{3,0},{0,1},{1,2},{2,3},{7,4},{4,5},{5,6},{6,7},{11,8},{8,9},{9,10... | collective-permute-start | bytes 221192 | tf_op jit(solution)/shard_map/ppermute | solution.py:112
  2.1 9.8 %collective-permute-start.1 = (bf16[18,16,128]{2,1,0:T(8,128)(2,1)S(1)}, bf16[18,16,128]{2,1,0:T(8,128)(2,1)S(1)}, u32[]{:S(2)}, u32[]{:S(2)}) collective-permute-start(bf16[18,16,128]{2,1,0:T(8,128)(2,1)S(1)} %bitcast.254), channel_id=1, source_target_pairs={{28,0},{0,4},{4,8},{8,12},{12,16},{16,20},{24,28},{29,1},{1,5},{5,... | collective-permute-start | bytes 221192 | tf_op jit(solution)/shard_map/ppermute | solution.py:112
  16.6 12.4 %collective-permute-start.5 = (f32[24,16,128]{2,1,0:T(8,128)}, f32[24,16,128]{2,1,0:T(8,128)S(1)}, u32[]{:S(2)}, u32[]{:S(2)}) collective-permute-start(f32[24,16,128]{2,1,0:T(8,128)} %shard_map.86.refs_7_), channel_id=1, source_target_pairs={{28,0},{0,4},{4,8},{8,12},{12,16},{16,20},{24,28},{29,1},{1,5},{5,... | collective-permute-start | bytes 589832 | tf_op jit(solution)/shard_map/ppermute | solution.py:112
  18.6 13.8 %collective-permute-start.4 = (f32[24,16,128]{2,1,0:T(8,128)}, f32[24,16,128]{2,1,0:T(8,128)S(1)}, u32[]{:S(2)}, u32[]{:S(2)}) collective-permute-start(f32[24,16,128]{2,1,0:T(8,128)} %shard_map.86.refs_7_), channel_id=1, source_target_pairs={{4,0},{8,4},{12,8},{16,12},{20,16},{28,24},{0,28},{5,1},{9,5},{13,... | collective-permute-start | bytes 589832 | tf_op jit(solution)/shard_map/ppermute | solution.py:112
  25.2 7.2 %collective-permute-start.3 = (f32[24,16,128]{2,1,0:T(8,128)}, f32[24,16,128]{2,1,0:T(8,128)S(1)}, u32[]{:S(2)}, u32[]{:S(2)}) collective-permute-start(f32[24,16,128]{2,1,0:T(8,128)} %shard_map.86.refs_7_), channel_id=1, source_target_pairs={{3,0},{0,1},{1,2},{2,3},{7,4},{4,5},{5,6},{6,7},{11,8},{8,9},{9,10... | collective-permute-start | bytes 589832 | tf_op jit(solution)/shard_map/ppermute | solution.py:112
  25.4 7.1 %collective-permute-start.2 = (f32[24,16,128]{2,1,0:T(8,128)}, f32[24,16,128]{2,1,0:T(8,128)S(1)}, u32[]{:S(2)}, u32[]{:S(2)}) collective-permute-start(f32[24,16,128]{2,1,0:T(8,128)} %shard_map.86.refs_7_), channel_id=1, source_target_pairs={{1,0},{2,1},{3,2},{0,3},{5,4},{6,5},{7,6},{4,7},{9,8},{10,9},{11,1... | collective-permute-start | bytes 589832 | tf_op jit(solution)/shard_map/ppermute | solution.py:112
  38.5 30.1 %collective-permute-start.9 = (f32[24,16,128]{2,1,0:T(8,128)}, f32[24,16,128]{2,1,0:T(8,128)}, u32[]{:S(2)}, u32[]{:S(2)}) collective-permute-start(f32[24,16,128]{2,1,0:T(8,128)} %shard_map.87.refs_6_), channel_id=1, source_target_pairs={{28,0},{0,4},{4,8},{8,12},{12,16},{16,20},{24,28},{29,1},{1,5},{5,... | collective-permute-start | bytes 589832 | tf_op jit(solution)/shard_map/ppermute | solution.py:112
  40.4 28.2 %collective-permute-start.8 = (f32[24,16,128]{2,1,0:T(8,128)}, f32[24,16,128]{2,1,0:T(8,128)}, u32[]{:S(2)}, u32[]{:S(2)}) collective-permute-start(f32[24,16,128]{2,1,0:T(8,128)} %shard_map.87.refs_6_), channel_id=1, source_target_pairs={{4,0},{8,4},{12,8},{16,12},{20,16},{28,24},{0,28},{5,1},{9,5},{13,... | collective-permute-start | bytes 589832 | tf_op jit(solution)/shard_map/ppermute | solution.py:112
  47.1 21.6 %collective-permute-start.7 = (f32[24,16,128]{2,1,0:T(8,128)}, f32[24,16,128]{2,1,0:T(8,128)}, u32[]{:S(2)}, u32[]{:S(2)}) collective-permute-start(f32[24,16,128]{2,1,0:T(8,128)} %shard_map.87.refs_6_), channel_id=1, source_target_pairs={{3,0},{0,1},{1,2},{2,3},{7,4},{4,5},{5,6},{6,7},{11,8},{8,9},{9,10... | collective-permute-start | bytes 589832 | tf_op jit(solution)/shard_map/ppermute | solution.py:112
  47.1 21.5 %collective-permute-start.6 = (f32[24,16,128]{2,1,0:T(8,128)}, f32[24,16,128]{2,1,0:T(8,128)}, u32[]{:S(2)}, u32[]{:S(2)}) collective-permute-start(f32[24,16,128]{2,1,0:T(8,128)} %shard_map.87.refs_6_), channel_id=1, source_target_pairs={{1,0},{2,1},{3,2},{0,3},{5,4},{6,5},{7,6},{4,7},{9,8},{10,9},{11,1... | collective-permute-start | bytes 589832 | tf_op jit(solution)/shard_map/ppermute | solution.py:112
  88.6 15.1 %collective-permute-start.11 = (f32[1,2,48,16]{2,3,1,0:T(8,128)}, f32[1,2,48,16]{2,3,1,0:T(8,128)}, u32[]{:S(2)}, u32[]{:S(2)}) collective-permute-start(f32[1,2,48,16]{2,3,1,0:T(8,128)} %get-tuple-element.35), channel_id=1, source_target_pairs={{0,1},{1,2},{2,3},{3,0},{4,5},{5,6},{6,7},{7,4},{8,9},{9,10},{10,1... | collective-permute-start | bytes 18440 | tf_op jit(solution)/shard_map/ppermute | solution.py:30
  89.3 13.1 %collective-permute-start.10 = (f32[1,2,48,16]{2,3,1,0:T(8,128)}, f32[1,2,48,16]{2,3,1,0:T(8,128)}, u32[]{:S(2)}, u32[]{:S(2)}) collective-permute-start(f32[1,2,48,16]{2,3,1,0:T(8,128)} %get-tuple-element.35), channel_id=1, source_target_pairs={{1,0},{2,1},{3,2},{0,3},{5,4},{6,5},{7,6},{4,7},{9,8},{10,9},{11,1... | collective-permute-start | bytes 18440 | tf_op jit(solution)/shard_map/ppermute | solution.py:31
  90.4 17.3 %collective-permute-start.14 = (f32[2,48,16]{1,2,0:T(8,128)}, f32[2,48,16]{1,2,0:T(8,128)}, u32[]{:S(2)}, u32[]{:S(2)}) collective-permute-start(f32[2,48,16]{1,2,0:T(8,128)} %get-tuple-element.34), channel_id=1, source_target_pairs={{0,0},{4,4},{8,8},{12,12},{16,16},{20,20},{24,24},{28,28},{1,1},{5... | collective-permute-start | bytes 18440 | tf_op jit(solution)/shard_map/ppermute | solution.py:20
  91.7 13.3 %collective-permute-start.12 = (f32[2,48,16]{1,2,0:T(8,128)}, f32[2,48,16]{1,2,0:T(8,128)}, u32[]{:S(2)}, u32[]{:S(2)}) collective-permute-start(f32[2,48,16]{1,2,0:T(8,128)} %get-tuple-element.34), channel_id=1, source_target_pairs={{0,28},{4,0},{8,4},{12,8},{16,12},{20,16},{24,20},{28,24},{1,29},{... | collective-permute-start | bytes 18440 | tf_op jit(solution)/shard_map/ppermute | solution.py:20
  92.6 13.8 %collective-permute-start.13 = (f32[2,48,16]{1,2,0:T(8,128)}, f32[2,48,16]{1,2,0:T(8,128)}, u32[]{:S(2)}, u32[]{:S(2)}) collective-permute-start(f32[2,48,16]{1,2,0:T(8,128)} %get-tuple-element.34), channel_id=1, source_target_pairs={{0,4},{4,8},{8,12},{12,16},{16,20},{20,24},{24,28},{28,0},{1,5},{5... | collective-permute-start | bytes 18440 | tf_op jit(solution)/shard_map/ppermute | solution.py:20
  124.0 6.9 %collective-permute-start.17 = (f32[2,48,16]{1,2,0:T(8,128)S(1)}, f32[2,48,16]{1,2,0:T(8,128)S(1)}, u32[]{:S(2)}, u32[]{:S(2)}) collective-permute-start(f32[2,48,16]{1,2,0:T(8,128)S(1)} %maximum_add_fusion), channel_id=1, source_target_pairs={{0,28},{4,0},{8,4},{12,8},{16,12},{20,16},{24,20},{28,24},{1,29},{... | collective-permute-start | bytes 18440 | tf_op jit(solution)/shard_map/ppermute | solution.py:20
  127.6 6.4 %collective-permute-start.18 = (f32[2,48,16]{1,2,0:T(8,128)S(1)}, f32[2,48,16]{1,2,0:T(8,128)S(1)}, u32[]{:S(2)}, u32[]{:S(2)}) collective-permute-start(f32[2,48,16]{1,2,0:T(8,128)S(1)} %maximum_add_fusion), channel_id=1, source_target_pairs={{0,4},{4,8},{8,12},{12,16},{16,20},{20,24},{24,28},{28,0},{1,5},{5... | collective-permute-start | bytes 18440 | tf_op jit(solution)/shard_map/ppermute | solution.py:20
  127.6 6.4 %collective-permute-start.19 = (f32[2,48,16]{1,2,0:T(8,128)S(1)}, f32[2,48,16]{1,2,0:T(8,128)S(1)}, u32[]{:S(2)}, u32[]{:S(2)}) collective-permute-start(f32[2,48,16]{1,2,0:T(8,128)S(1)} %maximum_add_fusion), channel_id=1, source_target_pairs={{0,0},{4,4},{8,8},{12,12},{16,16},{20,20},{24,24},{28,28},{1,1},{5... | collective-permute-start | bytes 18440 | tf_op jit(solution)/shard_map/ppermute | solution.py:20
  148.5 10.4 %collective-permute-start.23 = (f32[24,16,128]{2,1,0:T(8,128)S(1)}, f32[24,16,128]{2,1,0:T(8,128)S(1)}, u32[]{:S(2)}, u32[]{:S(2)}) collective-permute-start(f32[24,16,128]{2,1,0:T(8,128)S(1)} %add.119.refs_7_), channel_id=1, source_target_pairs={{28,0},{0,4},{4,8},{8,12},{12,16},{16,20},{24,28},{29,1},{1,5},{5,... | collective-permute-start | bytes 589832 | tf_op jit(solution)/shard_map/ppermute | solution.py:112
  150.5 11.3 %collective-permute-start.22 = (f32[24,16,128]{2,1,0:T(8,128)S(1)}, f32[24,16,128]{2,1,0:T(8,128)S(1)}, u32[]{:S(2)}, u32[]{:S(2)}) collective-permute-start(f32[24,16,128]{2,1,0:T(8,128)S(1)} %add.119.refs_7_), channel_id=1, source_target_pairs={{4,0},{8,4},{12,8},{16,12},{20,16},{28,24},{0,28},{5,1},{9,5},{13,... | collective-permute-start | bytes 589832 | tf_op jit(solution)/shard_map/ppermute | solution.py:112
  169.2 12.6 %collective-permute-start.27 = (f32[24,16,128]{2,1,0:T(8,128)}, f32[24,16,128]{2,1,0:T(8,128)S(1)}, u32[]{:S(2)}, u32[]{:S(2)}) collective-permute-start(f32[24,16,128]{2,1,0:T(8,128)} %shard_map.89.refs_7_), channel_id=1, source_target_pairs={{28,0},{0,4},{4,8},{8,12},{12,16},{16,20},{24,28},{29,1},{1,5},{5,... | collective-permute-start | bytes 589832 | tf_op jit(solution)/shard_map/ppermute | solution.py:112
  171.1 14.0 %collective-permute-start.26 = (f32[24,16,128]{2,1,0:T(8,128)}, f32[24,16,128]{2,1,0:T(8,128)S(1)}, u32[]{:S(2)}, u32[]{:S(2)}) collective-permute-start(f32[24,16,128]{2,1,0:T(8,128)} %shard_map.89.refs_7_), channel_id=1, source_target_pairs={{4,0},{8,4},{12,8},{16,12},{20,16},{28,24},{0,28},{5,1},{9,5},{13,... | collective-permute-start | bytes 589832 | tf_op jit(solution)/shard_map/ppermute | solution.py:112
  177.7 7.4 %collective-permute-start.25 = (f32[24,16,128]{2,1,0:T(8,128)}, f32[24,16,128]{2,1,0:T(8,128)S(1)}, u32[]{:S(2)}, u32[]{:S(2)}) collective-permute-start(f32[24,16,128]{2,1,0:T(8,128)} %shard_map.89.refs_7_), channel_id=1, source_target_pairs={{3,0},{0,1},{1,2},{2,3},{7,4},{4,5},{5,6},{6,7},{11,8},{8,9},{9,10... | collective-permute-start | bytes 589832 | tf_op jit(solution)/shard_map/ppermute | solution.py:112
  178.1 7.0 %collective-permute-start.24 = (f32[24,16,128]{2,1,0:T(8,128)}, f32[24,16,128]{2,1,0:T(8,128)S(1)}, u32[]{:S(2)}, u32[]{:S(2)}) collective-permute-start(f32[24,16,128]{2,1,0:T(8,128)} %shard_map.89.refs_7_), channel_id=1, source_target_pairs={{1,0},{2,1},{3,2},{0,3},{5,4},{6,5},{7,6},{4,7},{9,8},{10,9},{11,1... | collective-permute-start | bytes 589832 | tf_op jit(solution)/shard_map/ppermute | solution.py:112
  (29 other events, 159.5 us)
where the time goes:
time: 194 us; the launch traced here: 192 us
  starting transfers between devices  56.8 us (29%)
  local copies, waits for them, and re-layouts  50.3 us (26%)
  other arithmetic  32.4 us (17%)
  Pallas kernels  23 us (12%)
  waiting for transfers between devices  20.6 us (11%)
  matrix products  7.65 us (4%)
    ppermute x18, starting transfers between devices, permute_from(): return lax.ppermute(value, axis, pairs)  46.2 us
    pallas_call x5, Pallas kernels, run_pass(): pl.pallas_call(kernel, out_shape=jax.ShapeDtypeStruct(source.shape, jnp.f...  23 us
    unnamed x58, local copies, waits for them, and re-layouts  18.3 us
    ppermute x18, waiting for transfers between devices, permute_from(): return lax.ppermute(value, axis, pairs)  16 us
    reduce_sum x5, other arithmetic, apply_blocks(): jnp.sum(matrices[:, 0] * vector_real - matrices[:, 1] * vector_imag, axis...  13.3 us
    mul x9, local copies, waits for them, and re-layouts, apply_blocks(): matrices[:, 0] * vector_real - matrices[:, 1] * vector_imag  8.35 us
    ppermute x6, starting transfers between devices, passed_along(): lax.ppermute(shard, axis, [(i, (i + by) % size) for i in range(size)])  6.99 us
    unnamed x12, other arithmetic  6.58 us
  transfers between devices with their start and end apart: 28, of which 11 were waited for; matrix products, arithmetic and copies ran while one was open for 20% of the time, Pallas kernels for 0%

commit v1 on v0

--- a/solution.py
+++ b/solution.py
@@ -359,37 +359,48 @@
     real_part = contract(vectors[:, 0], weighted[0]) + contract(vectors[:, 1], weighted[1])
     imag_part = contract(vectors[:, 0], weighted[1]) - contract(vectors[:, 1], weighted[0])
     coarse_source = jnp.stack([real_part, imag_part]).reshape(2, CDOF, AGG)
-    operator_blocks = coarse_operator.reshape(9, 2, CDOF, CDOF * AGG)
-    inverse_blocks = block_inverse.reshape(1, 2, CDOF, CDOF * AGG)
+    operator_blocks = coarse_operator.reshape(9, 2 * CDOF, CDOF * AGG)
+    inverse_blocks = block_inverse.reshape(2 * CDOF, CDOF * AGG)
+    eye = jnp.eye(AGG, dtype=jnp.float32)
+
+    def block_product(blocks, vector):
+        expanded_vector = jnp.transpose(vector, (1, 2, 0))[:, :, :, None] * eye[None, :, None, :]
+        product = jnp.dot(
+            blocks,
+            expanded_vector.reshape(CDOF * AGG, 2 * AGG),
+            precision=lax.Precision.HIGHEST,
+            preferred_element_type=jnp.float32,
+        )
+        return product.reshape(2, CDOF, 2, AGG)
+
+    def combine(product):
+        return jnp.stack(
+            [product[0, :, 0] - product[1, :, 1], product[0, :, 1] + product[1, :, 0]]
+        )
 
     def precondition(vector):
-        return apply_blocks(inverse_blocks, vector[None])
+        return combine(block_product(inverse_blocks, vector))
 
     correction = precondition(coarse_source)
     for repeat in range(2):
-        loop_values = padded_2(correction[None], (("grp", 0),), 1)
-        nearby_arrived = []
-        for nearby_offset in (-1, 1, -PZ, PZ):
-            nearby_arrived.append(passed_along(correction, "lat", nearby_offset))
-        correction = correction + precondition(
-            coarse_source
-            - apply_blocks(
-                operator_blocks,
-                jnp.stack(
-                    [
-                        correction,
-                        jnp.roll(correction, -1, axis=2),
-                        jnp.roll(correction, 1, axis=2),
-                        loop_values[2],
-                        loop_values[0],
-                        keep_if(upper_valid, nearby_arrived[0]),
-                        keep_if(lower_valid, nearby_arrived[1]),
-                        keep_if(later_valid, nearby_arrived[2]),
-                        keep_if(earlier_valid, nearby_arrived[3]),
-                    ]
-                ),
-            )
-        )
+        nearby = [
+            correction,
+            jnp.roll(correction, -1, axis=2),
+            jnp.roll(correction, 1, axis=2),
+            permute_from(correction, "grp", 1, lambda i: True),
+            permute_from(correction, "grp", -1, lambda i: True),
+            permute_from(correction, "lat", 1, z_up_ok),
+            permute_from(correction, "lat", -1, z_down_ok),
+            permute_from(correction, "lat", PZ, t_up_ok),
+            permute_from(correction, "lat", -PZ, t_down_ok),
+        ]
+        total = None
+        for direction, vector in enumerate(nearby):
+            if vector is None:
+                continue
+            product = block_product(operator_blocks[direction], vector)
+            total = product if total is None else total + product
+        correction = correction + precondition(coarse_source - combine(total))
     expanded = jnp.dot(
         correction.reshape(2 * CDOF, AGG), membership.T, precision=lax.Precision.HIGHEST
     ).reshape(2, 2, NVEC, site_count)

time: 194 us -> 200 us (1.031)
  other arithmetic: 32.4 us -> 16 us
  matrix products: 7.65 us -> 20.5 us
  local copies, waits for them, and re-layouts: 50.3 us -> 55.1 us
  starting transfers between devices: 56.8 us -> 60.9 us
    dot_general x0 -> x17, matrix products: none -> 16.3 us  [block_product(): jnp.dot(blocks, expanded_vector.reshape(CDOF * AGG, 2 * AGG), precision=l...]
    ppermute x18 -> x26, starting transfers between devices: 46.2 us -> 60.9 us  [permute_from(): return lax.ppermute(value, axis, pairs)]
    reduce_sum x5 -> x0, other arithmetic: 13.3 us -> none  [apply_blocks(): jnp.sum(matrices[:, 0] * vector_real - matrices[:, 1] * vector_imag, axis...]
    mul x14 -> x17, local copies, waits for them, and re-layouts: 13.9 us -> 26.4 us  [block_product(): jnp.transpose(vector, (1, 2, 0))[:, :, :, None] * eye[None, :, None, :]]
    ppermute x10 -> x0, starting transfers between devices: 10.5 us -> none  [the longest x6 6.99 us: passed_along(): lax.ppermute(shard, axis, [(i, (i + by) % size) for i in range(size)])]
    transpose x0 -> x17, local copies, waits for them, and re-layouts: none -> 8.14 us  [block_product(): jnp.transpose(vector, (1, 2, 0))[:, :, :, None] * eye[None, :, None, :]]
    mul x0 -> x5, other arithmetic: none -> 7.9 us  [block_product(): jnp.transpose(vector, (1, 2, 0))[:, :, :, None] * eye[None, :, None, :]]
    unnamed x58 -> x68, local copies, waits for them, and re-layouts: 18.3 us -> 10.5 us
  transfers between devices with their start and end apart: 28 -> 26, of which waited for: 11 -> 13; matrix products, arithmetic and copies ran while one was open for 20% -> 11% of each run, Pallas kernels for 0% -> 0%
where the time goes in v1:
time: 200 us; the launch traced here: 198 us
  starting transfers between devices  60.9 us (30%)
  local copies, waits for them, and re-layouts  55.1 us (28%)
  Pallas kernels  23 us (12%)
  waiting for transfers between devices  20.9 us (10%)
  matrix products  20.5 us (10%)
  other arithmetic  16 us (8%)
    ppermute x26, starting transfers between devices, permute_from(): return lax.ppermute(value, axis, pairs)  60.9 us
    mul x17, local copies, waits for them, and re-layouts, block_product(): jnp.transpose(vector, (1, 2, 0))[:, :, :, None] * eye[None, :, None, :]  26.4 us
    pallas_call x5, Pallas kernels, run_pass(): pl.pallas_call(kernel, out_shape=jax.ShapeDtypeStruct(source.shape, jnp.f...  23 us
    ppermute x26, waiting for transfers between devices, permute_from(): return lax.ppermute(value, axis, pairs)  20.9 us
    dot_general x17, matrix products, block_product(): jnp.dot(blocks, expanded_vector.reshape(CDOF * AGG, 2 * AGG), precision=l...  16.3 us
    unnamed x68, local copies, waits for them, and re-layouts  10.5 us
    transpose x17, local copies, waits for them, and re-layouts, block_product(): jnp.transpose(vector, (1, 2, 0))[:, :, :, None] * eye[None, :, None, :]  8.14 us
    mul x5, other arithmetic, block_product(): jnp.transpose(vector, (1, 2, 0))[:, :, :, None] * eye[None, :, None, :]  7.9 us
  transfers between devices with their start and end apart: 26, of which 13 were waited for; matrix products, arithmetic and copies ran while one was open for 11% of the time, Pallas kernels for 0%

profile of v1, /device:TPU:0, one launch (start us, length us, event | category | flops | bytes accessed | tf_op | source)
XLA Modules:
  0.0 197.9 jit_solution(1546195710004649268)
XLA Ops:
  2.2 4.4 %collective-permute-start.1 = (bf16[18,16,128]{2,1,0:T(8,128)(2,1)S(1)}, bf16[18,16,128]{2,1,0:T(8,128)(2,1)S(1)}, u32[]{:S(2)}, u32[]{:S(2)}) collective-permute-start(bf16[18,16,128]{2,1,0:T(8,128)(2,1)S(1)} %bitcast.314), channel_id=1, source_target_pairs={{28,0},{0,4},{4,8},{8,12},{12,16},{16,20},{24,28},{29,1},{1,5},{5,... | collective-permute-start | bytes 221192 | tf_op jit(solution)/shard_map/ppermute | solution.py:112
  12.6 4.1 %shard_map.86.refs_7_ = f32[24,16,128]{2,1,0:T(8,128)} custom-call(f32[24,16,128]{2,1,0:T(8,128)} %bitcast.289, bf16[4,18,16,128]{3,2,1,0:T(8,128)(2,1)} %bitcast.284, bf16[18,16,128]{2,1,0:T(8,128)(2,1)} %copy-done.1, bf16[18,16,128]{2,1,0:T(8,128)(2,1)} %copy-done.2, f32[16,128]{1,0:T(8,128)} %add_convert_fusion.refs_4_, f32[16,16,128]{2,1,0:T(8,128)} %fusion.10.refs_5_, ...), custom_call_target="tpu_custom_call" | custom-call | tf_op jit(solution)/shard_map/pallas_call | solution.py:274
  16.7 2.3 %collective-permute-start.5 = (f32[24,16,128]{2,1,0:T(8,128)}, f32[24,16,128]{2,1,0:T(8,128)S(1)}, u32[]{:S(2)}, u32[]{:S(2)}) collective-permute-start(f32[24,16,128]{2,1,0:T(8,128)} %shard_map.86.refs_7_), channel_id=1, source_target_pairs={{28,0},{0,4},{4,8},{8,12},{12,16},{16,20},{24,28},{29,1},{1,5},{5,... | collective-permute-start | bytes 589832 | tf_op jit(solution)/shard_map/ppermute | solution.py:112
  19.0 6.2 %collective-permute-start.4 = (f32[24,16,128]{2,1,0:T(8,128)}, f32[24,16,128]{2,1,0:T(8,128)S(1)}, u32[]{:S(2)}, u32[]{:S(2)}) collective-permute-start(f32[24,16,128]{2,1,0:T(8,128)} %shard_map.86.refs_7_), channel_id=1, source_target_pairs={{4,0},{8,4},{12,8},{16,12},{20,16},{28,24},{0,28},{5,1},{9,5},{13,... | collective-permute-start | bytes 589832 | tf_op jit(solution)/shard_map/ppermute | solution.py:112
  27.1 4.3 %copy.45 = bf16[1,24,24,4,4,128]{5,4,3,1,2,0:T(4,128)(2,1)} copy(bf16[1,24,24,4,4,128]{5,4,3,2,1,0:T(4,128)(2,1)} %param.9) | data formatting | bytes 4718592 | tf_op args[2]
  31.3 4.0 %reshape.686 = bf16[24,2,2,6,2048]{4,0,3,2,1:T(8,128)(2,1)S(1)} reshape(bf16[1,24,24,4,4,128]{5,4,3,1,2,0:T(4,128)(2,1)} %copy.45) | data formatting | bytes 4718592 | tf_op jit(solution)/shard_map/reshape | solution.py:354
  36.3 5.3 %shard_map.87.refs_6_ = f32[24,16,128]{2,1,0:T(8,128)} custom-call(f32[24,16,128]{2,1,0:T(8,128)} %bitcast.290, bf16[4,18,16,128]{3,2,1,0:T(8,128)(2,1)} %bitcast.285, bf16[18,16,128]{2,1,0:T(8,128)(2,1)} %copy-done.1, bf16[18,16,128]{2,1,0:T(8,128)(2,1)} %copy-done.2, f32[16,128]{1,0:T(8,128)} %add_convert_fusion.refs_4_, f32[16,16,128]{2,1,0:T(8,128)} %fusion.10.refs_5_, ...), custom_call_target="tpu_custom_call" | custom-call | tf_op jit(solution)/shard_map/pallas_call | solution.py:274
  43.5 6.6 %collective-permute-start.8 = (f32[24,16,128]{2,1,0:T(8,128)}, f32[24,16,128]{2,1,0:T(8,128)S(1)}, u32[]{:S(2)}, u32[]{:S(2)}) collective-permute-start(f32[24,16,128]{2,1,0:T(8,128)} %shard_map.87.refs_6_), channel_id=1, source_target_pairs={{4,0},{8,4},{12,8},{16,12},{20,16},{28,24},{0,28},{5,1},{9,5},{13,... | collective-permute-start | bytes 589832 | tf_op jit(solution)/shard_map/ppermute | solution.py:112
  51.9 2.2 %fusion.24 = (bf16[1,1,1,2,48,768]{5,4,3,2,1,0:T(8,128)(2,1)S(1)}, bf16[1,1,1,2,48,768]{5,4,3,2,1,0:T(8,128)(2,1)}, bf16[1,1,1,2,48,768]{5,4,3,2,1,0:T(8,128)(2,...) fusion(bf16[1,1,9,2,48,768]{5,4,3,2,1,0:T(8,128)(2,1)} %param.12), kind=kLoop, calls=%fused_computation.116 | loop fusion | bytes 2064384 | tf_op jit(solution)/shard_map/slice | solution.py:401
  54.2 3.0 %collective-permute-done.8.refs_9_ = f32[24,16,128]{2,1,0:T(8,128)S(1)} collective-permute-done((f32[24,16,128]{2,1,0:T(8,128)}, f32[24,16,128]{2,1,0:T(8,128)S(1)}, u32[]{:S(2)}, u32[]{:S(2)}) %collective-permute-start.8) | collective-permute-done | bytes 196640 | tf_op jit(solution)/shard_map/ppermute | solution.py:112
  58.7 3.1 %shard_map.88 = f32[24,16,128]{2,1,0:T(8,128)} custom-call(f32[24,16,128]{2,1,0:T(8,128)} %bitcast.291, bf16[4,18,16,128]{3,2,1,0:T(8,128)(2,1)} %bitcast.286, bf16[18,16,128]{2,1,0:T(8,128)(2,1)} %copy-done.1, bf16[18,16,128]{2,1,0:T(8,128)(2,1)} %copy-done.2, f32[16,128]{1,0:T(8,128)} %add_convert_fusion.refs_4_, f32[16,16,128]{2,1,0:T(8,128)} %fusion.10.refs_5_, ...), custom_call_target="tpu_custom_call" | custom-call | tf_op jit(solution)/shard_map/pallas_call | solution.py:274
  68.5 4.8 %collective-permute-start.12 = (f32[2,48,16]{1,2,0:T(8,128)S(1)}, f32[2,48,16]{1,2,0:T(8,128)S(1)}, u32[]{:S(2)}, u32[]{:S(2)}) collective-permute-start(f32[2,48,16]{1,2,0:T(8,128)S(1)} %get-tuple-element.53), channel_id=1, source_target_pairs={{4,0},{8,4},{12,8},{16,12},{20,16},{28,24},{0,28},{5,1},{9,5},{13,... | collective-permute-start | bytes 18440 | tf_op jit(solution)/shard_map/ppermute | solution.py:112
  83.1 3.2 %broadcast_multiply_fusion.10 = (f32[48,16,2,16]{1,0,3,2:T(8,128)}, f32[48,16,2,16]{1,0,3,2:T(8,128)}, f32[48,16,2,16]{1,0,3,2:T(8,128)}, f32[48,16,2,16]{1,0,3,...) fusion(f32[48,16,2]{1,0,2:T(8,128)} %copy.59, ...), kind=kLoop, calls=%fused_computation.47 | loop fusion | flops 172032 | bytes 732160 | tf_op jit(solution)/shard_map/mul | solution.py:367
  109.5 5.1 %collective-permute-start.16 = (f32[2,48,16]{1,2,0:T(8,128)S(1)}, f32[2,48,16]{1,2,0:T(8,128)S(1)}, u32[]{:S(2)}, u32[]{:S(2)}) collective-permute-start(f32[2,48,16]{1,2,0:T(8,128)S(1)} %maximum_add_fusion), channel_id=1, source_target_pairs={{4,0},{8,4},{12,8},{16,12},{20,16},{28,24},{0,28},{5,1},{9,5},{13,... | collective-permute-start | bytes 18440 | tf_op jit(solution)/shard_map/ppermute | solution.py:112
  117.7 2.1 %collective-permute-done.15 = f32[2,48,16]{1,2,0:T(8,128)S(1)} collective-permute-done((f32[2,48,16]{1,2,0:T(8,128)S(1)}, f32[2,48,16]{1,2,0:T(8,128)S(1)}, u32[]{:S(2)}, u32[]{:S(2)}) %collective-permute-start.15) | collective-permute-done | bytes 6176 | tf_op jit(solution)/shard_map/ppermute | solution.py:112
  120.5 2.5 %collective-permute-done.17 = f32[2,48,16]{1,2,0:T(8,128)S(1)} collective-permute-done((f32[2,48,16]{1,2,0:T(8,128)S(1)}, f32[2,48,16]{1,2,0:T(8,128)S(1)}, u32[]{:S(2)}, u32[]{:S(2)}) %collective-permute-start.17) | collective-permute-done | bytes 6176 | tf_op jit(solution)/shard_map/ppermute | solution.py:112
  125.1 3.2 %broadcast_multiply_fusion.2 = (f32[48,16,2,16]{1,0,3,2:T(8,128)}, f32[48,16,2,16]{1,0,3,2:T(8,128)}, f32[48,16,2,16]{1,0,3,2:T(8,128)}, f32[48,16,2,16]{1,0,3,2...) fusion(f32[48,16,2]{1,0,2:T(8,128)} %copy.75, ...), kind=kLoop, calls=%fused_computation.39 | loop fusion | flops 172032 | bytes 732160 | tf_op jit(solution)/shard_map/mul | solution.py:367
  139.8 2.1 %mul.500 = f32[768,32]{0,1:T(8,128)} reshape(f32[48,16,2,16]{1,0,3,2:T(8,128)} %get-tuple-element.64) | data formatting | bytes 196608 | tf_op jit(solution)/shard_map/mul | solution.py:367
  156.3 6.6 %collective-permute-start.20 = (f32[24,16,128]{2,1,0:T(8,128)S(1)}, f32[24,16,128]{2,1,0:T(8,128)S(1)}, u32[]{:S(2)}, u32[]{:S(2)}) collective-permute-start(f32[24,16,128]{2,1,0:T(8,128)S(1)} %add.223.refs_7_), channel_id=1, source_target_pairs={{4,0},{8,4},{12,8},{16,12},{20,16},{28,24},{0,28},{5,1},{9,5},{13,... | collective-permute-start | bytes 589832 | tf_op jit(solution)/shard_map/ppermute | solution.py:112
  164.9 3.3 %collective-permute-done.20.refs_10_ = f32[24,16,128]{2,1,0:T(8,128)S(1)} collective-permute-done((f32[24,16,128]{2,1,0:T(8,128)S(1)}, f32[24,16,128]{2,1,0:T(8,128)S(1)}, u32[]{:S(2)}, u32[]{:S(2)}) %collective-permute-start.20) | collective-permute-done | bytes 196640 | tf_op jit(solution)/shard_map/ppermute | solution.py:112
  170.4 5.3 %shard_map.89.refs_7_ = f32[24,16,128]{2,1,0:T(8,128)} custom-call(f32[24,16,128]{2,1,0:T(8,128)} %bitcast.292, bf16[4,18,16,128]{3,2,1,0:T(8,128)(2,1)} %bitcast.287, bf16[18,16,128]{2,1,0:T(8,128)(2,1)} %copy-done.1, bf16[18,16,128]{2,1,0:T(8,128)(2,1)} %copy-done.2, f32[16,128]{1,0:T(8,128)} %add_convert_fusion.refs_4_, f32[16,16,128]{2,1,0:T(8,128)} %fusion.10.refs_5_, ...), custom_call_target="tpu_custom_call" | custom-call | tf_op jit(solution)/shard_map/pallas_call | solution.py:274
  177.6 6.6 %collective-permute-start.24 = (f32[24,16,128]{2,1,0:T(8,128)}, f32[24,16,128]{2,1,0:T(8,128)S(1)}, u32[]{:S(2)}, u32[]{:S(2)}) collective-permute-start(f32[24,16,128]{2,1,0:T(8,128)} %shard_map.89.refs_7_), channel_id=1, source_target_pairs={{4,0},{8,4},{12,8},{16,12},{20,16},{28,24},{0,28},{5,1},{9,5},{13,... | collective-permute-start | bytes 589832 | tf_op jit(solution)/shard_map/ppermute | solution.py:112
  187.7 3.3 %collective-permute-done.24.refs_10_ = f32[24,16,128]{2,1,0:T(8,128)S(1)} collective-permute-done((f32[24,16,128]{2,1,0:T(8,128)}, f32[24,16,128]{2,1,0:T(8,128)S(1)}, u32[]{:S(2)}, u32[]{:S(2)}) %collective-permute-start.24) | collective-permute-done | bytes 196640 | tf_op jit(solution)/shard_map/ppermute | solution.py:112
  192.6 5.3 %shard_map.90 = f32[24,16,128]{2,1,0:T(8,128)} custom-call(f32[24,16,128]{2,1,0:T(8,128)} %bitcast.293, bf16[4,18,16,128]{3,2,1,0:T(8,128)(2,1)} %bitcast.288, bf16[18,16,128]{2,1,0:T(8,128)(2,1)} %copy-done.1, bf16[18,16,128]{2,1,0:T(8,128)(2,1)} %copy-done.2, f32[16,128]{1,0:T(8,128)} %add_convert_fusion.refs_4_, f32[16,16,128]{2,1,0:T(8,128)} %fusion.10.refs_5_, ...), custom_call_target="tpu_custom_call" | custom-call | tf_op jit(solution)/shard_map/pallas_call | solution.py:274
  (222 shorter events, 97.3 us)
Async XLA Ops:
  1.7 9.2 %collective-permute-start = (bf16[18,16,128]{2,1,0:T(8,128)(2,1)S(1)}, bf16[18,16,128]{2,1,0:T(8,128)(2,1)S(1)}, u32[]{:S(2)}, u32[]{:S(2)}) collective-permute-start(bf16[18,16,128]{2,1,0:T(8,128)(2,1)S(1)} %bitcast.315), channel_id=1, source_target_pairs={{3,0},{0,1},{1,2},{2,3},{7,4},{4,5},{5,6},{6,7},{11,8},{8,9},{9,10... | collective-permute-start | bytes 221192 | tf_op jit(solution)/shard_map/ppermute | solution.py:112
  2.2 9.8 %collective-permute-start.1 = (bf16[18,16,128]{2,1,0:T(8,128)(2,1)S(1)}, bf16[18,16,128]{2,1,0:T(8,128)(2,1)S(1)}, u32[]{:S(2)}, u32[]{:S(2)}) collective-permute-start(bf16[18,16,128]{2,1,0:T(8,128)(2,1)S(1)} %bitcast.314), channel_id=1, source_target_pairs={{28,0},{0,4},{4,8},{8,12},{12,16},{16,20},{24,28},{29,1},{1,5},{5,... | collective-permute-start | bytes 221192 | tf_op jit(solution)/shard_map/ppermute | solution.py:112
  16.7 18.7 %collective-permute-start.5 = (f32[24,16,128]{2,1,0:T(8,128)}, f32[24,16,128]{2,1,0:T(8,128)S(1)}, u32[]{:S(2)}, u32[]{:S(2)}) collective-permute-start(f32[24,16,128]{2,1,0:T(8,128)} %shard_map.86.refs_7_), channel_id=1, source_target_pairs={{28,0},{0,4},{4,8},{8,12},{12,16},{16,20},{24,28},{29,1},{1,5},{5,... | collective-permute-start | bytes 589832 | tf_op jit(solution)/shard_map/ppermute | solution.py:112
  19.0 16.4 %collective-permute-start.4 = (f32[24,16,128]{2,1,0:T(8,128)}, f32[24,16,128]{2,1,0:T(8,128)S(1)}, u32[]{:S(2)}, u32[]{:S(2)}) collective-permute-start(f32[24,16,128]{2,1,0:T(8,128)} %shard_map.86.refs_7_), channel_id=1, source_target_pairs={{4,0},{8,4},{12,8},{16,12},{20,16},{28,24},{0,28},{5,1},{9,5},{13,... | collective-permute-start | bytes 589832 | tf_op jit(solution)/shard_map/ppermute | solution.py:112
  25.2 10.2 %collective-permute-start.3 = (f32[24,16,128]{2,1,0:T(8,128)}, f32[24,16,128]{2,1,0:T(8,128)S(1)}, u32[]{:S(2)}, u32[]{:S(2)}) collective-permute-start(f32[24,16,128]{2,1,0:T(8,128)} %shard_map.86.refs_7_), channel_id=1, source_target_pairs={{3,0},{0,1},{1,2},{2,3},{7,4},{4,5},{5,6},{6,7},{11,8},{8,9},{9,10... | collective-permute-start | bytes 589832 | tf_op jit(solution)/shard_map/ppermute | solution.py:112
  25.4 10.0 %collective-permute-start.2 = (f32[24,16,128]{2,1,0:T(8,128)}, f32[24,16,128]{2,1,0:T(8,128)S(1)}, u32[]{:S(2)}, u32[]{:S(2)}) collective-permute-start(f32[24,16,128]{2,1,0:T(8,128)} %shard_map.86.refs_7_), channel_id=1, source_target_pairs={{1,0},{2,1},{3,2},{0,3},{5,4},{6,5},{7,6},{4,7},{9,8},{10,9},{11,1... | collective-permute-start | bytes 589832 | tf_op jit(solution)/shard_map/ppermute | solution.py:112
  41.6 12.6 %collective-permute-start.9 = (f32[24,16,128]{2,1,0:T(8,128)}, f32[24,16,128]{2,1,0:T(8,128)S(1)}, u32[]{:S(2)}, u32[]{:S(2)}) collective-permute-start(f32[24,16,128]{2,1,0:T(8,128)} %shard_map.87.refs_6_), channel_id=1, source_target_pairs={{28,0},{0,4},{4,8},{8,12},{12,16},{16,20},{24,28},{29,1},{1,5},{5,... | collective-permute-start | bytes 589832 | tf_op jit(solution)/shard_map/ppermute | solution.py:112
  43.5 13.7 %collective-permute-start.8 = (f32[24,16,128]{2,1,0:T(8,128)}, f32[24,16,128]{2,1,0:T(8,128)S(1)}, u32[]{:S(2)}, u32[]{:S(2)}) collective-permute-start(f32[24,16,128]{2,1,0:T(8,128)} %shard_map.87.refs_6_), channel_id=1, source_target_pairs={{4,0},{8,4},{12,8},{16,12},{20,16},{28,24},{0,28},{5,1},{9,5},{13,... | collective-permute-start | bytes 589832 | tf_op jit(solution)/shard_map/ppermute | solution.py:112
  50.1 7.1 %collective-permute-start.7 = (f32[24,16,128]{2,1,0:T(8,128)}, f32[24,16,128]{2,1,0:T(8,128)S(1)}, u32[]{:S(2)}, u32[]{:S(2)}) collective-permute-start(f32[24,16,128]{2,1,0:T(8,128)} %shard_map.87.refs_6_), channel_id=1, source_target_pairs={{3,0},{0,1},{1,2},{2,3},{7,4},{4,5},{5,6},{6,7},{11,8},{8,9},{9,10... | collective-permute-start | bytes 589832 | tf_op jit(solution)/shard_map/ppermute | solution.py:112
  50.2 7.2 %collective-permute-start.6 = (f32[24,16,128]{2,1,0:T(8,128)}, f32[24,16,128]{2,1,0:T(8,128)S(1)}, u32[]{:S(2)}, u32[]{:S(2)}) collective-permute-start(f32[24,16,128]{2,1,0:T(8,128)} %shard_map.87.refs_6_), channel_id=1, source_target_pairs={{1,0},{2,1},{3,2},{0,3},{5,4},{6,5},{7,6},{4,7},{9,8},{10,9},{11,1... | collective-permute-start | bytes 589832 | tf_op jit(solution)/shard_map/ppermute | solution.py:112
  68.5 13.9 %collective-permute-start.12 = (f32[2,48,16]{1,2,0:T(8,128)S(1)}, f32[2,48,16]{1,2,0:T(8,128)S(1)}, u32[]{:S(2)}, u32[]{:S(2)}) collective-permute-start(f32[2,48,16]{1,2,0:T(8,128)S(1)} %get-tuple-element.53), channel_id=1, source_target_pairs={{4,0},{8,4},{12,8},{16,12},{20,16},{28,24},{0,28},{5,1},{9,5},{13,... | collective-permute-start | bytes 18440 | tf_op jit(solution)/shard_map/ppermute | solution.py:112
  73.4 8.3 %collective-permute-start.13 = (f32[2,48,16]{1,2,0:T(8,128)S(1)}, f32[2,48,16]{1,2,0:T(8,128)S(1)}, u32[]{:S(2)}, u32[]{:S(2)}) collective-permute-start(f32[2,48,16]{1,2,0:T(8,128)S(1)} %get-tuple-element.53), channel_id=1, source_target_pairs={{28,0},{0,4},{4,8},{8,12},{12,16},{16,20},{24,28},{29,1},{1,5},{5,... | collective-permute-start | bytes 18440 | tf_op jit(solution)/shard_map/ppermute | solution.py:112
  75.3 4.2 %collective-permute-start.10 = (f32[2,48,16]{1,2,0:T(8,128)S(1)}, f32[2,48,16]{1,2,0:T(8,128)S(1)}, u32[]{:S(2)}, u32[]{:S(2)}) collective-permute-start(f32[2,48,16]{1,2,0:T(8,128)S(1)} %get-tuple-element.53), channel_id=1, source_target_pairs={{1,0},{2,1},{3,2},{0,3},{5,4},{6,5},{7,6},{4,7},{9,8},{10,9},{11,1... | collective-permute-start | bytes 18440 | tf_op jit(solution)/shard_map/ppermute | solution.py:112
  109.5 14.9 %collective-permute-start.14 = (f32[2,48,16]{1,2,0:T(8,128)S(1)}, f32[2,48,16]{1,2,0:T(8,128)S(1)}, u32[]{:S(2)}, u32[]{:S(2)}) collective-permute-start(f32[2,48,16]{1,2,0:T(8,128)S(1)} %maximum_add_fusion), channel_id=1, source_target_pairs={{1,0},{2,1},{3,2},{0,3},{5,4},{6,5},{7,6},{4,7},{9,8},{10,9},{11,1... | collective-permute-start | bytes 18440 | tf_op jit(solution)/shard_map/ppermute | solution.py:112
  109.5 14.2 %collective-permute-start.16 = (f32[2,48,16]{1,2,0:T(8,128)S(1)}, f32[2,48,16]{1,2,0:T(8,128)S(1)}, u32[]{:S(2)}, u32[]{:S(2)}) collective-permute-start(f32[2,48,16]{1,2,0:T(8,128)S(1)} %maximum_add_fusion), channel_id=1, source_target_pairs={{4,0},{8,4},{12,8},{16,12},{20,16},{28,24},{0,28},{5,1},{9,5},{13,... | collective-permute-start | bytes 18440 | tf_op jit(solution)/shard_map/ppermute | solution.py:112
  114.7 8.3 %collective-permute-start.17 = (f32[2,48,16]{1,2,0:T(8,128)S(1)}, f32[2,48,16]{1,2,0:T(8,128)S(1)}, u32[]{:S(2)}, u32[]{:S(2)}) collective-permute-start(f32[2,48,16]{1,2,0:T(8,128)S(1)} %maximum_add_fusion), channel_id=1, source_target_pairs={{28,0},{0,4},{4,8},{8,12},{12,16},{16,20},{24,28},{29,1},{1,5},{5,... | collective-permute-start | bytes 18440 | tf_op jit(solution)/shard_map/ppermute | solution.py:112
  154.3 10.5 %collective-permute-start.21 = (f32[24,16,128]{2,1,0:T(8,128)S(1)}, f32[24,16,128]{2,1,0:T(8,128)S(1)}, u32[]{:S(2)}, u32[]{:S(2)}) collective-permute-start(f32[24,16,128]{2,1,0:T(8,128)S(1)} %add.223.refs_7_), channel_id=1, source_target_pairs={{28,0},{0,4},{4,8},{8,12},{12,16},{16,20},{24,28},{29,1},{1,5},{5,... | collective-permute-start | bytes 589832 | tf_op jit(solution)/shard_map/ppermute | solution.py:112
  156.3 11.9 %collective-permute-start.20 = (f32[24,16,128]{2,1,0:T(8,128)S(1)}, f32[24,16,128]{2,1,0:T(8,128)S(1)}, u32[]{:S(2)}, u32[]{:S(2)}) collective-permute-start(f32[24,16,128]{2,1,0:T(8,128)S(1)} %add.223.refs_7_), channel_id=1, source_target_pairs={{4,0},{8,4},{12,8},{16,12},{20,16},{28,24},{0,28},{5,1},{9,5},{13,... | collective-permute-start | bytes 589832 | tf_op jit(solution)/shard_map/ppermute | solution.py:112
  162.9 6.2 %collective-permute-start.19 = (f32[24,16,128]{2,1,0:T(8,128)S(1)}, f32[24,16,128]{2,1,0:T(8,128)S(1)}, u32[]{:S(2)}, u32[]{:S(2)}) collective-permute-start(f32[24,16,128]{2,1,0:T(8,128)S(1)} %add.223.refs_7_), channel_id=1, source_target_pairs={{3,0},{0,1},{1,2},{2,3},{7,4},{4,5},{5,6},{6,7},{11,8},{8,9},{9,10... | collective-permute-start | bytes 589832 | tf_op jit(solution)/shard_map/ppermute | solution.py:112
  163.0 6.1 %collective-permute-start.18 = (f32[24,16,128]{2,1,0:T(8,128)S(1)}, f32[24,16,128]{2,1,0:T(8,128)S(1)}, u32[]{:S(2)}, u32[]{:S(2)}) collective-permute-start(f32[24,16,128]{2,1,0:T(8,128)S(1)} %add.223.refs_7_), channel_id=1, source_target_pairs={{1,0},{2,1},{3,2},{0,3},{5,4},{6,5},{7,6},{4,7},{9,8},{10,9},{11,1... | collective-permute-start | bytes 589832 | tf_op jit(solution)/shard_map/ppermute | solution.py:112
  175.7 11.9 %collective-permute-start.25 = (f32[24,16,128]{2,1,0:T(8,128)}, f32[24,16,128]{2,1,0:T(8,128)S(1)}, u32[]{:S(2)}, u32[]{:S(2)}) collective-permute-start(f32[24,16,128]{2,1,0:T(8,128)} %shard_map.89.refs_7_), channel_id=1, source_target_pairs={{28,0},{0,4},{4,8},{8,12},{12,16},{16,20},{24,28},{29,1},{1,5},{5,... | collective-permute-start | bytes 589832 | tf_op jit(solution)/shard_map/ppermute | solution.py:112
  177.6 13.4 %collective-permute-start.24 = (f32[24,16,128]{2,1,0:T(8,128)}, f32[24,16,128]{2,1,0:T(8,128)S(1)}, u32[]{:S(2)}, u32[]{:S(2)}) collective-permute-start(f32[24,16,128]{2,1,0:T(8,128)} %shard_map.89.refs_7_), channel_id=1, source_target_pairs={{4,0},{8,4},{12,8},{16,12},{20,16},{28,24},{0,28},{5,1},{9,5},{13,... | collective-permute-start | bytes 589832 | tf_op jit(solution)/shard_map/ppermute | solution.py:112
  184.2 7.0 %collective-permute-start.23 = (f32[24,16,128]{2,1,0:T(8,128)}, f32[24,16,128]{2,1,0:T(8,128)S(1)}, u32[]{:S(2)}, u32[]{:S(2)}) collective-permute-start(f32[24,16,128]{2,1,0:T(8,128)} %shard_map.89.refs_7_), channel_id=1, source_target_pairs={{3,0},{0,1},{1,2},{2,3},{7,4},{4,5},{5,6},{6,7},{11,8},{8,9},{9,10... | collective-permute-start | bytes 589832 | tf_op jit(solution)/shard_map/ppermute | solution.py:112
  184.3 6.9 %collective-permute-start.22 = (f32[24,16,128]{2,1,0:T(8,128)}, f32[24,16,128]{2,1,0:T(8,128)S(1)}, u32[]{:S(2)}, u32[]{:S(2)}) collective-permute-start(f32[24,16,128]{2,1,0:T(8,128)} %shard_map.89.refs_7_), channel_id=1, source_target_pairs={{1,0},{2,1},{3,2},{0,3},{5,4},{6,5},{7,6},{4,7},{9,8},{10,9},{11,1... | collective-permute-start | bytes 589832 | tf_op jit(solution)/shard_map/ppermute | solution.py:112
  (35 other events, 352.4 us)

commit v2 on v1

--- a/solution.py
+++ b/solution.py
@@ -274,6 +274,87 @@
     return pl.pallas_call(kernel, out_shape=jax.ShapeDtypeStruct(source.shape, jnp.float32))(*operands)
 
 
+def coarse_kernel(*refs, present):
+    refs = list(refs)
+    out_ref = refs.pop()
+    source_ref, inverse_ref = refs[0], refs[1]
+    first = len(refs) == 2
+    width = source_ref.shape[-1]
+    chunks = width // 128
+    lane = lax.broadcasted_iota(jnp.int32, (1, width), 1)
+    position = lane % AGG
+    selector = (
+        lax.broadcasted_iota(jnp.int32, (8, 128), 1) // AGG == lax.broadcasted_iota(jnp.int32, (8, 128), 0)
+    ).astype(jnp.float32)
+
+    def reduce_flat(product):
+        partial = product[:, 0:128]
+        for q in range(1, chunks):
+            partial = partial + product[:, q * 128:(q + 1) * 128]
+        for shift in (64, 32, 16):
+            partial = partial + pltpu.roll(partial, shift, 1)
+        pieces = [
+            jnp.sum(partial[8 * q:8 * q + 8] * selector, axis=0, keepdims=True) for q in range(chunks)
+        ]
+        return jnp.concatenate(pieces, axis=1)
+
+    def roll_within(vector, shift):
+        pieces = [pltpu.roll(vector[:, q * 128:(q + 1) * 128], shift % 128, 1) for q in range(chunks)]
+        return jnp.concatenate(pieces, axis=1)
+
+    def accumulate(acc, blocks_ref, index, vector):
+        block_real = blocks_ref[index + (0,)].astype(jnp.float32)
+        block_imag = blocks_ref[index + (1,)].astype(jnp.float32)
+        real_part = block_real * vector[0] - block_imag * vector[1]
+        imag_part = block_real * vector[1] + block_imag * vector[0]
+        if acc is None:
+            return [real_part, imag_part]
+        return [acc[0] + real_part, acc[1] + imag_part]
+
+    def precondition(vector):
+        acc = accumulate(None, inverse_ref, (), vector)
+        return [reduce_flat(acc[0]), reduce_flat(acc[1])]
+
+    source = [source_ref[0], source_ref[1]]
+    if first:
+        result = precondition(source)
+    else:
+        operator_ref, current_ref = refs[2], refs[3]
+        nearby_refs = refs[4:]
+        current = [current_ref[0], current_ref[1]]
+        ahead = [
+            jnp.where(position == AGG - 1, roll_within(c, AGG - 1), roll_within(c, -1)) for c in current
+        ]
+        behind = [jnp.where(position == 0, roll_within(c, 1 - AGG), roll_within(c, 1)) for c in current]
+        vectors = [current, ahead, behind]
+        taken = 0
+        for flag in present:
+            if flag:
+                vectors.append([nearby_refs[taken][0], nearby_refs[taken][1]])
+                taken += 1
+            else:
+                vectors.append(None)
+        acc = None
+        for direction, vector in enumerate(vectors):
+            if vector is not None:
+                acc = accumulate(acc, operator_ref, (direction,), vector)
+        residue = [source[0] - reduce_flat(acc[0]), source[1] - reduce_flat(acc[1])]
+        step = precondition(residue)
+        result = [current[0] + step[0], current[1] + step[1]]
+    out_ref[0] = result[0]
+    out_ref[1] = result[1]
+
+
+def run_coarse(source, inverse_blocks, operator_blocks, current, nearby):
+    operands = [source, inverse_blocks]
+    present = ()
+    if current is not None:
+        present = tuple(v is not None for v in nearby)
+        operands += [operator_blocks, current] + [v for v in nearby if v is not None]
+    kernel = functools.partial(coarse_kernel, present=present)
+    return pl.pallas_call(kernel, out_shape=jax.ShapeDtypeStruct(source.shape, jnp.float32))(*operands)
+
+
 def body(
     fine_source, links, test_vectors, aggregate_map, colouring, coarse_operator, block_inverse
 ):
@@ -359,34 +440,12 @@
     real_part = contract(vectors[:, 0], weighted[0]) + contract(vectors[:, 1], weighted[1])
     imag_part = contract(vectors[:, 0], weighted[1]) - contract(vectors[:, 1], weighted[0])
     coarse_source = jnp.stack([real_part, imag_part]).reshape(2, CDOF, AGG)
-    operator_blocks = coarse_operator.reshape(9, 2 * CDOF, CDOF * AGG)
-    inverse_blocks = block_inverse.reshape(2 * CDOF, CDOF * AGG)
-    eye = jnp.eye(AGG, dtype=jnp.float32)
-
-    def block_product(blocks, vector):
-        expanded_vector = jnp.transpose(vector, (1, 2, 0))[:, :, :, None] * eye[None, :, None, :]
-        product = jnp.dot(
-            blocks,
-            expanded_vector.reshape(CDOF * AGG, 2 * AGG),
-            precision=lax.Precision.HIGHEST,
-            preferred_element_type=jnp.float32,
-        )
-        return product.reshape(2, CDOF, 2, AGG)
-
-    def combine(product):
-        return jnp.stack(
-            [product[0, :, 0] - product[1, :, 1], product[0, :, 1] + product[1, :, 0]]
-        )
-
-    def precondition(vector):
-        return combine(block_product(inverse_blocks, vector))
-
-    correction = precondition(coarse_source)
+    flat_source = coarse_source.reshape(2, 1, CDOF * AGG)
+    operator_blocks = coarse_operator.reshape(9, 2, CDOF, CDOF * AGG)
+    inverse_blocks = block_inverse.reshape(2, CDOF, CDOF * AGG)
+    correction = run_coarse(flat_source, inverse_blocks, operator_blocks, None, None)
     for repeat in range(2):
         nearby = [
-            correction,
-            jnp.roll(correction, -1, axis=2),
-            jnp.roll(correction, 1, axis=2),
             permute_from(correction, "grp", 1, lambda i: True),
             permute_from(correction, "grp", -1, lambda i: True),
             permute_from(correction, "lat", 1, z_up_ok),
@@ -394,13 +453,8 @@
             permute_from(correction, "lat", PZ, t_up_ok),
             permute_from(correction, "lat", -PZ, t_down_ok),
         ]
-        total = None
-        for direction, vector in enumerate(nearby):
-            if vector is None:
-                continue
-            product = block_product(operator_blocks[direction], vector)
-            total = product if total is None else total + product
-        correction = correction + precondition(coarse_source - combine(total))
+        correction = run_coarse(flat_source, inverse_blocks, operator_blocks, correction, nearby)
+    correction = correction.reshape(2, CDOF, AGG)
     expanded = jnp.dot(
         correction.reshape(2 * CDOF, AGG), membership.T, precision=lax.Precision.HIGHEST
     ).reshape(2, 2, NVEC, site_count)

time: 200 us -> 147 us (0.73)
  local copies, waits for them, and re-layouts: 55.1 us -> 16 us
  waiting for transfers between devices: 20.9 us -> 42.9 us
  matrix products: 20.5 us -> 3.45 us
  starting transfers between devices: 60.9 us -> 45.6 us
  other arithmetic: 16 us -> 5.73 us
  Pallas kernels: 23 us -> 30.8 us
    mul x17 -> x0, local copies, waits for them, and re-layouts: 26.4 us -> none  [block_product(): jnp.transpose(vector, (1, 2, 0))[:, :, :, None] * eye[None, :, None, :]]
    ppermute x26, waiting for transfers between devices: 20.9 us -> 42.9 us  [permute_from(): return lax.ppermute(value, axis, pairs)]
    dot_general x17 -> x0, matrix products: 16.3 us -> none  [block_product(): jnp.dot(blocks, expanded_vector.reshape(CDOF * AGG, 2 * AGG), precision=l...]
    ppermute x26, starting transfers between devices: 60.9 us -> 45.6 us  [permute_from(): return lax.ppermute(value, axis, pairs)]
    transpose x17 -> x0, local copies, waits for them, and re-layouts: 8.14 us -> none  [block_product(): jnp.transpose(vector, (1, 2, 0))[:, :, :, None] * eye[None, :, None, :]]
    mul x5 -> x0, other arithmetic: 7.9 us -> none  [block_product(): jnp.transpose(vector, (1, 2, 0))[:, :, :, None] * eye[None, :, None, :]]
    pallas_call x0 -> x3, Pallas kernels: none -> 7.77 us  [run_coarse(): pl.pallas_call(kernel, out_shape=jax.ShapeDtypeStruct(source.shape, jnp.f...]
    slice x8 -> x0, local copies, waits for them, and re-layouts: 2.39 us -> none  [the longest x1 2.24 us: body(): product = block_product(operator_blocks[direction], vector)]
  transfers between devices with their start and end apart: 26 -> 26, of which waited for: 13 -> 12; matrix products, arithmetic and copies ran while one was open for 11% -> 8% of each run, Pallas kernels for 0% -> 0%
where the time goes in v2:
time: 147 us; the launch traced here: 146 us
  starting transfers between devices  45.6 us (31%)
  waiting for transfers between devices  42.9 us (29%)
  Pallas kernels  30.8 us (21%)
  local copies, waits for them, and re-layouts  16 us (11%)
  other arithmetic  5.73 us (4%)
  matrix products  3.45 us (2%)
    ppermute x26, starting transfers between devices, permute_from(): return lax.ppermute(value, axis, pairs)  45.6 us
    ppermute x26, waiting for transfers between devices, permute_from(): return lax.ppermute(value, axis, pairs)  42.9 us
    pallas_call x5, Pallas kernels, run_pass(): pl.pallas_call(kernel, out_shape=jax.ShapeDtypeStruct(source.shape, jnp.f...  23 us
    unnamed x65, local copies, waits for them, and re-layouts  8.66 us
    pallas_call x3, Pallas kernels, run_coarse(): pl.pallas_call(kernel, out_shape=jax.ShapeDtypeStruct(source.shape, jnp.f...  7.77 us
    reshape x1, local copies, waits for them, and re-layouts, body(): vectors = test_vectors.reshape(NVEC, 2, 2, 6, site_count)  4.03 us
    dot_general x4, matrix products, contract(): jnp.einsum('kxqn,xqnj->xkj', left, right, preferred_element_type=jnp.floa...  3 us
  transfers between devices with their start and end apart: 26, of which 12 were waited for; matrix products, arithmetic and copies ran while one was open for 8% of the time, Pallas kernels for 0%

profile of v2, /device:TPU:0, one launch (start us, length us, event | category | flops | bytes accessed | tf_op | source)
XLA Modules:
  0.0 145.8 jit_solution(12100408203309656060)
XLA Ops:
  2.1 4.4 %collective-permute-start.1 = (bf16[18,16,128]{2,1,0:T(8,128)(2,1)S(1)}, bf16[18,16,128]{2,1,0:T(8,128)(2,1)S(1)}, u32[]{:S(2)}, u32[]{:S(2)}) collective-permute-start(bf16[18,16,128]{2,1,0:T(8,128)(2,1)S(1)} %bitcast.90), channel_id=1, source_target_pairs={{28,0},{0,4},{4,8},{8,12},{12,16},{16,20},{24,28},{29,1},{1,5},{5,... | collective-permute-start | bytes 221192 | tf_op jit(solution)/shard_map/ppermute | solution.py:112
  12.5 4.1 %shard_map.86.refs_7_ = f32[24,16,128]{2,1,0:T(8,128)} custom-call(f32[24,16,128]{2,1,0:T(8,128)} %bitcast.77, bf16[4,18,16,128]{3,2,1,0:T(8,128)(2,1)} %bitcast.70, bf16[18,16,128]{2,1,0:T(8,128)(2,1)} %copy-done.1, bf16[18,16,128]{2,1,0:T(8,128)(2,1)} %copy-done.2, f32[16,128]{1,0:T(8,128)} %add_convert_fusion.refs_4_, f32[16,16,128]{2,1,0:T(8,128)} %fusion.8.refs_5_, ...), custom_call_target="tpu_custom_call" | custom-call | tf_op jit(solution)/shard_map/pallas_call | solution.py:274
  18.4 3.5 %collective-permute-start.4 = (f32[24,16,128]{2,1,0:T(8,128)}, f32[24,16,128]{2,1,0:T(8,128)S(1)}, u32[]{:S(2)}, u32[]{:S(2)}) collective-permute-start(f32[24,16,128]{2,1,0:T(8,128)} %shard_map.86.refs_7_), channel_id=1, source_target_pairs={{4,0},{8,4},{12,8},{16,12},{20,16},{28,24},{0,28},{5,1},{9,5},{13,... | collective-permute-start | bytes 589832 | tf_op jit(solution)/shard_map/ppermute | solution.py:112
  25.0 3.0 %collective-permute-done.4.refs_10_ = f32[24,16,128]{2,1,0:T(8,128)S(1)} collective-permute-done((f32[24,16,128]{2,1,0:T(8,128)}, f32[24,16,128]{2,1,0:T(8,128)S(1)}, u32[]{:S(2)}, u32[]{:S(2)}) %collective-permute-start.4) | collective-permute-done | bytes 196640 | tf_op jit(solution)/shard_map/ppermute | solution.py:112
  28.0 6.4 %collective-permute-done.5.refs_11_ = f32[24,16,128]{2,1,0:T(8,128)S(1)} collective-permute-done((f32[24,16,128]{2,1,0:T(8,128)}, f32[24,16,128]{2,1,0:T(8,128)S(1)}, u32[]{:S(2)}, u32[]{:S(2)}) %collective-permute-start.5) | collective-permute-done | bytes 196640 | tf_op jit(solution)/shard_map/ppermute | solution.py:112
  35.1 5.3 %shard_map.87.refs_6_ = f32[24,16,128]{2,1,0:T(8,128)} custom-call(f32[24,16,128]{2,1,0:T(8,128)} %bitcast.78, bf16[4,18,16,128]{3,2,1,0:T(8,128)(2,1)} %bitcast.71, bf16[18,16,128]{2,1,0:T(8,128)(2,1)} %copy-done.1, bf16[18,16,128]{2,1,0:T(8,128)(2,1)} %copy-done.2, f32[16,128]{1,0:T(8,128)} %add_convert_fusion.refs_4_, f32[16,16,128]{2,1,0:T(8,128)} %fusion.8.refs_5_, ...), custom_call_target="tpu_custom_call" | custom-call | tf_op jit(solution)/shard_map/pallas_call | solution.py:274
  40.9 4.5 %collective-permute-start.8 = (f32[24,16,128]{2,1,0:T(8,128)}, f32[24,16,128]{2,1,0:T(8,128)S(1)}, u32[]{:S(2)}, u32[]{:S(2)}) collective-permute-start(f32[24,16,128]{2,1,0:T(8,128)} %shard_map.87.refs_6_), channel_id=1, source_target_pairs={{4,0},{8,4},{12,8},{16,12},{20,16},{28,24},{0,28},{5,1},{9,5},{13,... | collective-permute-start | bytes 589832 | tf_op jit(solution)/shard_map/ppermute | solution.py:112
  50.1 4.0 %reshape.75 = bf16[24,2,2,6,2048]{4,0,3,2,1:T(8,128)(2,1)S(1)} reshape(bf16[1,24,24,4,4,128]{5,4,3,1,2,0:T(4,128)(2,1)} %copy.13) | data formatting | bytes 4718592 | tf_op jit(solution)/shard_map/reshape | solution.py:435
  54.2 3.6 %collective-permute-done.9.refs_10_ = f32[24,16,128]{2,1,0:T(8,128)S(1)} collective-permute-done((f32[24,16,128]{2,1,0:T(8,128)}, f32[24,16,128]{2,1,0:T(8,128)S(1)}, u32[]{:S(2)}, u32[]{:S(2)}) %collective-permute-start.9) | collective-permute-done | bytes 196640 | tf_op jit(solution)/shard_map/ppermute | solution.py:112
  58.5 3.2 %shard_map.88 = f32[24,16,128]{2,1,0:T(8,128)} custom-call(f32[24,16,128]{2,1,0:T(8,128)} %bitcast.79, bf16[4,18,16,128]{3,2,1,0:T(8,128)(2,1)} %bitcast.72, bf16[18,16,128]{2,1,0:T(8,128)(2,1)} %copy-done.1, bf16[18,16,128]{2,1,0:T(8,128)(2,1)} %copy-done.2, f32[16,128]{1,0:T(8,128)} %add_convert_fusion.refs_4_, f32[16,16,128]{2,1,0:T(8,128)} %fusion.8.refs_5_, ...), custom_call_target="tpu_custom_call" | custom-call | tf_op jit(solution)/shard_map/pallas_call | solution.py:274
  69.6 4.1 %collective-permute-start.12 = (f32[2,1,768]{2,1,0:T(1,128)}, f32[2,1,768]{2,1,0:T(1,128)S(1)}, u32[]{:S(2)}, u32[]{:S(2)}) collective-permute-start(f32[2,1,768]{2,1,0:T(1,128)} %shard_map.89.refs_3_), channel_id=1, source_target_pairs={{4,0},{8,4},{12,8},{16,12},{20,16},{28,24},{0,28},{5,1},{9,5},{13,... | collective-permute-start | bytes 18440 | tf_op jit(solution)/shard_map/ppermute | solution.py:112
  75.7 6.4 %collective-permute-done.13.refs_7_ = f32[2,1,768]{2,1,0:T(1,128)S(1)} collective-permute-done((f32[2,1,768]{2,1,0:T(1,128)}, f32[2,1,768]{2,1,0:T(1,128)S(1)}, u32[]{:S(2)}, u32[]{:S(2)}) %collective-permute-start.13) | collective-permute-done | bytes 6176 | tf_op jit(solution)/shard_map/ppermute | solution.py:112
  82.7 3.0 %shard_map.90.refs_3_ = f32[2,1,768]{2,1,0:T(1,128)} custom-call(f32[2,1,768]{2,1,0:T(1,128)} %copy-done.22, bf16[2,48,768]{2,1,0:T(8,128)(2,1)} %bitcast.85, bf16[9,2,48,768]{3,2,1,0:T(8,128)(2,1)} %bitcast.75, f32[2,1,768]{2,1,0:T(1,128)} %shard_map.89.refs_3_, f32[2,1,768]{2,1,0:T(1,128)} %copy-done.24, f32[2,1,768]{2,1,0:T(1,128)} %copy-done.26, ...), custom_call_target="tpu_custom_call" | custom-call | tf_op jit(solution)/shard_map/pallas_call | solution.py:355
  88.3 3.9 %collective-permute-start.17 = (f32[2,1,768]{2,1,0:T(1,128)}, f32[2,1,768]{2,1,0:T(1,128)S(1)}, u32[]{:S(2)}, u32[]{:S(2)}) collective-permute-start(f32[2,1,768]{2,1,0:T(1,128)} %shard_map.90.refs_3_), channel_id=1, source_target_pairs={{28,0},{0,4},{4,8},{8,12},{12,16},{16,20},{24,28},{29,1},{1,5},{5,... | collective-permute-start | bytes 18440 | tf_op jit(solution)/shard_map/ppermute | solution.py:112
  92.3 4.4 %collective-permute-done.17.refs_7_ = f32[2,1,768]{2,1,0:T(1,128)S(1)} collective-permute-done((f32[2,1,768]{2,1,0:T(1,128)}, f32[2,1,768]{2,1,0:T(1,128)S(1)}, u32[]{:S(2)}, u32[]{:S(2)}) %collective-permute-start.17) | collective-permute-done | bytes 6176 | tf_op jit(solution)/shard_map/ppermute | solution.py:112
  97.3 3.0 %shard_map.91 = f32[2,1,768]{2,1,0:T(1,128)} custom-call(f32[2,1,768]{2,1,0:T(1,128)} %copy-done.22, bf16[2,48,768]{2,1,0:T(8,128)(2,1)} %bitcast.86, bf16[9,2,48,768]{3,2,1,0:T(8,128)(2,1)} %bitcast.76, f32[2,1,768]{2,1,0:T(1,128)} %shard_map.90.refs_3_, f32[2,1,768]{2,1,0:T(1,128)} %copy-done.23, f32[2,1,768]{2,1,0:T(1,128)} %copy-done.25, ...), custom_call_target="tpu_custom_call" | custom-call | tf_op jit(solution)/shard_map/pallas_call | solution.py:355
  105.5 3.9 %collective-permute-start.21 = (f32[24,16,128]{2,1,0:T(8,128)S(1)}, f32[24,16,128]{2,1,0:T(8,128)S(1)}, u32[]{:S(2)}, u32[]{:S(2)}) collective-permute-start(f32[24,16,128]{2,1,0:T(8,128)S(1)} %add.23.refs_7_), channel_id=1, source_target_pairs={{28,0},{0,4},{4,8},{8,12},{12,16},{16,20},{24,28},{29,1},{1,5},{5,... | collective-permute-start | bytes 589832 | tf_op jit(solution)/shard_map/ppermute | solution.py:112
  109.9 3.1 %collective-permute-done.20.refs_10_ = f32[24,16,128]{2,1,0:T(8,128)S(1)} collective-permute-done((f32[24,16,128]{2,1,0:T(8,128)S(1)}, f32[24,16,128]{2,1,0:T(8,128)S(1)}, u32[]{:S(2)}, u32[]{:S(2)}) %collective-permute-start.20) | collective-permute-done | bytes 196640 | tf_op jit(solution)/shard_map/ppermute | solution.py:112
  112.9 4.6 %collective-permute-done.21.refs_11_ = f32[24,16,128]{2,1,0:T(8,128)S(1)} collective-permute-done((f32[24,16,128]{2,1,0:T(8,128)S(1)}, f32[24,16,128]{2,1,0:T(8,128)S(1)}, u32[]{:S(2)}, u32[]{:S(2)}) %collective-permute-start.21) | collective-permute-done | bytes 196640 | tf_op jit(solution)/shard_map/ppermute | solution.py:112
  118.2 5.3 %shard_map.92.refs_7_ = f32[24,16,128]{2,1,0:T(8,128)} custom-call(f32[24,16,128]{2,1,0:T(8,128)} %bitcast.80, bf16[4,18,16,128]{3,2,1,0:T(8,128)(2,1)} %bitcast.73, bf16[18,16,128]{2,1,0:T(8,128)(2,1)} %copy-done.1, bf16[18,16,128]{2,1,0:T(8,128)(2,1)} %copy-done.2, f32[16,128]{1,0:T(8,128)} %add_convert_fusion.refs_4_, f32[16,16,128]{2,1,0:T(8,128)} %fusion.8.refs_5_, ...), custom_call_target="tpu_custom_call" | custom-call | tf_op jit(solution)/shard_map/pallas_call | solution.py:274
  124.0 3.5 %collective-permute-start.24 = (f32[24,16,128]{2,1,0:T(8,128)}, f32[24,16,128]{2,1,0:T(8,128)S(1)}, u32[]{:S(2)}, u32[]{:S(2)}) collective-permute-start(f32[24,16,128]{2,1,0:T(8,128)} %shard_map.92.refs_7_), channel_id=1, source_target_pairs={{4,0},{8,4},{12,8},{16,12},{20,16},{28,24},{0,28},{5,1},{9,5},{13,... | collective-permute-start | bytes 589832 | tf_op jit(solution)/shard_map/ppermute | solution.py:112
  130.9 2.8 %collective-permute-done.24.refs_10_ = f32[24,16,128]{2,1,0:T(8,128)S(1)} collective-permute-done((f32[24,16,128]{2,1,0:T(8,128)}, f32[24,16,128]{2,1,0:T(8,128)S(1)}, u32[]{:S(2)}, u32[]{:S(2)}) %collective-permute-start.24) | collective-permute-done | bytes 196640 | tf_op jit(solution)/shard_map/ppermute | solution.py:112
  133.8 6.1 %collective-permute-done.25.refs_11_ = f32[24,16,128]{2,1,0:T(8,128)S(1)} collective-permute-done((f32[24,16,128]{2,1,0:T(8,128)}, f32[24,16,128]{2,1,0:T(8,128)S(1)}, u32[]{:S(2)}, u32[]{:S(2)}) %collective-permute-start.25) | collective-permute-done | bytes 196640 | tf_op jit(solution)/shard_map/ppermute | solution.py:112
  140.5 5.3 %shard_map.93 = f32[24,16,128]{2,1,0:T(8,128)} custom-call(f32[24,16,128]{2,1,0:T(8,128)} %bitcast.81, bf16[4,18,16,128]{3,2,1,0:T(8,128)(2,1)} %bitcast.74, bf16[18,16,128]{2,1,0:T(8,128)(2,1)} %copy-done.1, bf16[18,16,128]{2,1,0:T(8,128)(2,1)} %copy-done.2, f32[16,128]{1,0:T(8,128)} %add_convert_fusion.refs_4_, f32[16,16,128]{2,1,0:T(8,128)} %fusion.8.refs_5_, ...), custom_call_target="tpu_custom_call" | custom-call | tf_op jit(solution)/shard_map/pallas_call | solution.py:274
  (131 shorter events, 43.3 us)
Async XLA Ops:
  1.6 8.5 %collective-permute-start = (bf16[18,16,128]{2,1,0:T(8,128)(2,1)S(1)}, bf16[18,16,128]{2,1,0:T(8,128)(2,1)S(1)}, u32[]{:S(2)}, u32[]{:S(2)}) collective-permute-start(bf16[18,16,128]{2,1,0:T(8,128)(2,1)S(1)} %bitcast.91), channel_id=1, source_target_pairs={{3,0},{0,1},{1,2},{2,3},{7,4},{4,5},{5,6},{6,7},{11,8},{8,9},{9,10... | collective-permute-start | bytes 221192 | tf_op jit(solution)/shard_map/ppermute | solution.py:112
  2.1 9.8 %collective-permute-start.1 = (bf16[18,16,128]{2,1,0:T(8,128)(2,1)S(1)}, bf16[18,16,128]{2,1,0:T(8,128)(2,1)S(1)}, u32[]{:S(2)}, u32[]{:S(2)}) collective-permute-start(bf16[18,16,128]{2,1,0:T(8,128)(2,1)S(1)} %bitcast.90), channel_id=1, source_target_pairs={{28,0},{0,4},{4,8},{8,12},{12,16},{16,20},{24,28},{29,1},{1,5},{5,... | collective-permute-start | bytes 221192 | tf_op jit(solution)/shard_map/ppermute | solution.py:112
  16.7 8.4 %collective-permute-start.2 = (f32[24,16,128]{2,1,0:T(8,128)}, f32[24,16,128]{2,1,0:T(8,128)S(1)}, u32[]{:S(2)}, u32[]{:S(2)}) collective-permute-start(f32[24,16,128]{2,1,0:T(8,128)} %shard_map.86.refs_7_), channel_id=1, source_target_pairs={{1,0},{2,1},{3,2},{0,3},{5,4},{6,5},{7,6},{4,7},{9,8},{10,9},{11,1... | collective-permute-start | bytes 589832 | tf_op jit(solution)/shard_map/ppermute | solution.py:112
  18.4 6.7 %collective-permute-start.3 = (f32[24,16,128]{2,1,0:T(8,128)}, f32[24,16,128]{2,1,0:T(8,128)S(1)}, u32[]{:S(2)}, u32[]{:S(2)}) collective-permute-start(f32[24,16,128]{2,1,0:T(8,128)} %shard_map.86.refs_7_), channel_id=1, source_target_pairs={{3,0},{0,1},{1,2},{2,3},{7,4},{4,5},{5,6},{6,7},{11,8},{8,9},{9,10... | collective-permute-start | bytes 589832 | tf_op jit(solution)/shard_map/ppermute | solution.py:112
  18.4 9.6 %collective-permute-start.4 = (f32[24,16,128]{2,1,0:T(8,128)}, f32[24,16,128]{2,1,0:T(8,128)S(1)}, u32[]{:S(2)}, u32[]{:S(2)}) collective-permute-start(f32[24,16,128]{2,1,0:T(8,128)} %shard_map.86.refs_7_), channel_id=1, source_target_pairs={{4,0},{8,4},{12,8},{16,12},{20,16},{28,24},{0,28},{5,1},{9,5},{13,... | collective-permute-start | bytes 589832 | tf_op jit(solution)/shard_map/ppermute | solution.py:112
  21.9 12.5 %collective-permute-start.5 = (f32[24,16,128]{2,1,0:T(8,128)}, f32[24,16,128]{2,1,0:T(8,128)S(1)}, u32[]{:S(2)}, u32[]{:S(2)}) collective-permute-start(f32[24,16,128]{2,1,0:T(8,128)} %shard_map.86.refs_7_), channel_id=1, source_target_pairs={{28,0},{0,4},{4,8},{8,12},{12,16},{16,20},{24,28},{29,1},{1,5},{5,... | collective-permute-start | bytes 589832 | tf_op jit(solution)/shard_map/ppermute | solution.py:112
  40.4 13.7 %collective-permute-start.6 = (f32[24,16,128]{2,1,0:T(8,128)}, f32[24,16,128]{2,1,0:T(8,128)S(1)}, u32[]{:S(2)}, u32[]{:S(2)}) collective-permute-start(f32[24,16,128]{2,1,0:T(8,128)} %shard_map.87.refs_6_), channel_id=1, source_target_pairs={{1,0},{2,1},{3,2},{0,3},{5,4},{6,5},{7,6},{4,7},{9,8},{10,9},{11,1... | collective-permute-start | bytes 589832 | tf_op jit(solution)/shard_map/ppermute | solution.py:112
  40.7 13.4 %collective-permute-start.7 = (f32[24,16,128]{2,1,0:T(8,128)}, f32[24,16,128]{2,1,0:T(8,128)S(1)}, u32[]{:S(2)}, u32[]{:S(2)}) collective-permute-start(f32[24,16,128]{2,1,0:T(8,128)} %shard_map.87.refs_6_), channel_id=1, source_target_pairs={{3,0},{0,1},{1,2},{2,3},{7,4},{4,5},{5,6},{6,7},{11,8},{8,9},{9,10... | collective-permute-start | bytes 589832 | tf_op jit(solution)/shard_map/ppermute | solution.py:112
  40.9 13.2 %collective-permute-start.8 = (f32[24,16,128]{2,1,0:T(8,128)}, f32[24,16,128]{2,1,0:T(8,128)S(1)}, u32[]{:S(2)}, u32[]{:S(2)}) collective-permute-start(f32[24,16,128]{2,1,0:T(8,128)} %shard_map.87.refs_6_), channel_id=1, source_target_pairs={{4,0},{8,4},{12,8},{16,12},{20,16},{28,24},{0,28},{5,1},{9,5},{13,... | collective-permute-start | bytes 589832 | tf_op jit(solution)/shard_map/ppermute | solution.py:112
  45.4 12.3 %collective-permute-start.9 = (f32[24,16,128]{2,1,0:T(8,128)}, f32[24,16,128]{2,1,0:T(8,128)S(1)}, u32[]{:S(2)}, u32[]{:S(2)}) collective-permute-start(f32[24,16,128]{2,1,0:T(8,128)} %shard_map.87.refs_6_), channel_id=1, source_target_pairs={{28,0},{0,4},{4,8},{8,12},{12,16},{16,20},{24,28},{29,1},{1,5},{5,... | collective-permute-start | bytes 589832 | tf_op jit(solution)/shard_map/ppermute | solution.py:112
  68.8 6.8 %collective-permute-start.10 = (f32[2,1,768]{2,1,0:T(1,128)}, f32[2,1,768]{2,1,0:T(1,128)S(1)}, u32[]{:S(2)}, u32[]{:S(2)}) collective-permute-start(f32[2,1,768]{2,1,0:T(1,128)} %shard_map.89.refs_3_), channel_id=1, source_target_pairs={{1,0},{2,1},{3,2},{0,3},{5,4},{6,5},{7,6},{4,7},{9,8},{10,9},{11,1... | collective-permute-start | bytes 18440 | tf_op jit(solution)/shard_map/ppermute | solution.py:112
  69.6 6.0 %collective-permute-start.11 = (f32[2,1,768]{2,1,0:T(1,128)}, f32[2,1,768]{2,1,0:T(1,128)S(1)}, u32[]{:S(2)}, u32[]{:S(2)}) collective-permute-start(f32[2,1,768]{2,1,0:T(1,128)} %shard_map.89.refs_3_), channel_id=1, source_target_pairs={{3,0},{0,1},{1,2},{2,3},{7,4},{4,5},{5,6},{6,7},{11,8},{8,9},{9,10... | collective-permute-start | bytes 18440 | tf_op jit(solution)/shard_map/ppermute | solution.py:112
  69.6 6.0 %collective-permute-start.12 = (f32[2,1,768]{2,1,0:T(1,128)}, f32[2,1,768]{2,1,0:T(1,128)S(1)}, u32[]{:S(2)}, u32[]{:S(2)}) collective-permute-start(f32[2,1,768]{2,1,0:T(1,128)} %shard_map.89.refs_3_), channel_id=1, source_target_pairs={{4,0},{8,4},{12,8},{16,12},{20,16},{28,24},{0,28},{5,1},{9,5},{13,... | collective-permute-start | bytes 18440 | tf_op jit(solution)/shard_map/ppermute | solution.py:112
  73.7 8.4 %collective-permute-start.13 = (f32[2,1,768]{2,1,0:T(1,128)}, f32[2,1,768]{2,1,0:T(1,128)S(1)}, u32[]{:S(2)}, u32[]{:S(2)}) collective-permute-start(f32[2,1,768]{2,1,0:T(1,128)} %shard_map.89.refs_3_), channel_id=1, source_target_pairs={{28,0},{0,4},{4,8},{8,12},{12,16},{16,20},{24,28},{29,1},{1,5},{5,... | collective-permute-start | bytes 18440 | tf_op jit(solution)/shard_map/ppermute | solution.py:112
  85.7 6.5 %collective-permute-start.14 = (f32[2,1,768]{2,1,0:T(1,128)}, f32[2,1,768]{2,1,0:T(1,128)S(1)}, u32[]{:S(2)}, u32[]{:S(2)}) collective-permute-start(f32[2,1,768]{2,1,0:T(1,128)} %shard_map.90.refs_3_), channel_id=1, source_target_pairs={{1,0},{2,1},{3,2},{0,3},{5,4},{6,5},{7,6},{4,7},{9,8},{10,9},{11,1... | collective-permute-start | bytes 18440 | tf_op jit(solution)/shard_map/ppermute | solution.py:112
  88.3 8.4 %collective-permute-start.17 = (f32[2,1,768]{2,1,0:T(1,128)}, f32[2,1,768]{2,1,0:T(1,128)S(1)}, u32[]{:S(2)}, u32[]{:S(2)}) collective-permute-start(f32[2,1,768]{2,1,0:T(1,128)} %shard_map.90.refs_3_), channel_id=1, source_target_pairs={{28,0},{0,4},{4,8},{8,12},{12,16},{16,20},{24,28},{29,1},{1,5},{5,... | collective-permute-start | bytes 18440 | tf_op jit(solution)/shard_map/ppermute | solution.py:112
  102.9 6.5 %collective-permute-start.18 = (f32[24,16,128]{2,1,0:T(8,128)S(1)}, f32[24,16,128]{2,1,0:T(8,128)S(1)}, u32[]{:S(2)}, u32[]{:S(2)}) collective-permute-start(f32[24,16,128]{2,1,0:T(8,128)S(1)} %add.23.refs_7_), channel_id=1, source_target_pairs={{1,0},{2,1},{3,2},{0,3},{5,4},{6,5},{7,6},{4,7},{9,8},{10,9},{11,1... | collective-permute-start | bytes 589832 | tf_op jit(solution)/shard_map/ppermute | solution.py:112
  103.6 6.3 %collective-permute-start.19 = (f32[24,16,128]{2,1,0:T(8,128)S(1)}, f32[24,16,128]{2,1,0:T(8,128)S(1)}, u32[]{:S(2)}, u32[]{:S(2)}) collective-permute-start(f32[24,16,128]{2,1,0:T(8,128)S(1)} %add.23.refs_7_), channel_id=1, source_target_pairs={{3,0},{0,1},{1,2},{2,3},{7,4},{4,5},{5,6},{6,7},{11,8},{8,9},{9,10... | collective-permute-start | bytes 589832 | tf_op jit(solution)/shard_map/ppermute | solution.py:112
  103.6 9.3 %collective-permute-start.20 = (f32[24,16,128]{2,1,0:T(8,128)S(1)}, f32[24,16,128]{2,1,0:T(8,128)S(1)}, u32[]{:S(2)}, u32[]{:S(2)}) collective-permute-start(f32[24,16,128]{2,1,0:T(8,128)S(1)} %add.23.refs_7_), channel_id=1, source_target_pairs={{4,0},{8,4},{12,8},{16,12},{20,16},{28,24},{0,28},{5,1},{9,5},{13,... | collective-permute-start | bytes 589832 | tf_op jit(solution)/shard_map/ppermute | solution.py:112
  105.5 12.0 %collective-permute-start.21 = (f32[24,16,128]{2,1,0:T(8,128)S(1)}, f32[24,16,128]{2,1,0:T(8,128)S(1)}, u32[]{:S(2)}, u32[]{:S(2)}) collective-permute-start(f32[24,16,128]{2,1,0:T(8,128)S(1)} %add.23.refs_7_), channel_id=1, source_target_pairs={{28,0},{0,4},{4,8},{8,12},{12,16},{16,20},{24,28},{29,1},{1,5},{5,... | collective-permute-start | bytes 589832 | tf_op jit(solution)/shard_map/ppermute | solution.py:112
  123.5 7.1 %collective-permute-start.22 = (f32[24,16,128]{2,1,0:T(8,128)}, f32[24,16,128]{2,1,0:T(8,128)S(1)}, u32[]{:S(2)}, u32[]{:S(2)}) collective-permute-start(f32[24,16,128]{2,1,0:T(8,128)} %shard_map.92.refs_7_), channel_id=1, source_target_pairs={{1,0},{2,1},{3,2},{0,3},{5,4},{6,5},{7,6},{4,7},{9,8},{10,9},{11,1... | collective-permute-start | bytes 589832 | tf_op jit(solution)/shard_map/ppermute | solution.py:112
  123.9 7.0 %collective-permute-start.23 = (f32[24,16,128]{2,1,0:T(8,128)}, f32[24,16,128]{2,1,0:T(8,128)S(1)}, u32[]{:S(2)}, u32[]{:S(2)}) collective-permute-start(f32[24,16,128]{2,1,0:T(8,128)} %shard_map.92.refs_7_), channel_id=1, source_target_pairs={{3,0},{0,1},{1,2},{2,3},{7,4},{4,5},{5,6},{6,7},{11,8},{8,9},{9,10... | collective-permute-start | bytes 589832 | tf_op jit(solution)/shard_map/ppermute | solution.py:112
  124.0 9.7 %collective-permute-start.24 = (f32[24,16,128]{2,1,0:T(8,128)}, f32[24,16,128]{2,1,0:T(8,128)S(1)}, u32[]{:S(2)}, u32[]{:S(2)}) collective-permute-start(f32[24,16,128]{2,1,0:T(8,128)} %shard_map.92.refs_7_), channel_id=1, source_target_pairs={{4,0},{8,4},{12,8},{16,12},{20,16},{28,24},{0,28},{5,1},{9,5},{13,... | collective-permute-start | bytes 589832 | tf_op jit(solution)/shard_map/ppermute | solution.py:112
  127.5 12.3 %collective-permute-start.25 = (f32[24,16,128]{2,1,0:T(8,128)}, f32[24,16,128]{2,1,0:T(8,128)S(1)}, u32[]{:S(2)}, u32[]{:S(2)}) collective-permute-start(f32[24,16,128]{2,1,0:T(8,128)} %shard_map.92.refs_7_), channel_id=1, source_target_pairs={{28,0},{0,4},{4,8},{8,12},{12,16},{16,20},{24,28},{29,1},{1,5},{5,... | collective-permute-start | bytes 589832 | tf_op jit(solution)/shard_map/ppermute | solution.py:112
  (33 other events, 188.1 us)

commit v3 on v2

--- a/solution.py
+++ b/solution.py
@@ -125,7 +125,7 @@
         n = a.shape[axis]
         return pltpu.roll(a, shift % n, a.ndim + axis)
 
-    def ahead(self, direction, a, nbr):
+    def ahead(self, direction, a, nbr, placed=False):
         if direction == 0:
             return jnp.where(self.xpos == CX - 1, self.roll(a, CX - 1, -1), self.roll(a, -1, -1))
         if direction == 1:
@@ -134,12 +134,12 @@
             return self.roll(filled, half, -1)
         if direction == 2:
             inner = self.roll(a, -1, -2)
-            outer = 0.0 if nbr is None else self.roll(nbr, 3, -2)
+            outer = 0.0 if nbr is None else (nbr if placed else self.roll(nbr, 3, -2))
             return jnp.where(self.zpos == 3, outer, inner)
         filled = jnp.where(self.row < 4, 0.0 if nbr is None else nbr, a)
         return self.roll(filled, -4, -2)
 
-    def behind(self, direction, a, nbr):
+    def behind(self, direction, a, nbr, placed=False):
         if direction == 0:
             return jnp.where(self.xpos == 0, self.roll(a, 1 - CX, -1), self.roll(a, 1, -1))
         if direction == 1:
@@ -148,7 +148,7 @@
             return self.roll(filled, half, -1)
         if direction == 2:
             inner = self.roll(a, 1, -2)
-            outer = 0.0 if nbr is None else self.roll(nbr, -3, -2)
+            outer = 0.0 if nbr is None else (nbr if placed else self.roll(nbr, -3, -2))
             return jnp.where(self.zpos == 0, outer, inner)
         filled = jnp.where(self.row >= self.rows - 4, 0.0 if nbr is None else nbr, a)
         return self.roll(filled, 4, -2)
@@ -164,8 +164,21 @@
     return 4.5 * spinor - 0.5 * hop_total
 
 
-def pass_kernel(*refs, first, residual_only, present):
+FACES = ("z_low", "z_high", "t_low", "t_high")
+
+
+def face_rows(name):
+    return {"z_low": (0, 4), "z_high": (3, 4), "t_low": (0, 1), "t_high": (12, 1)}[name]
+
+
+def pass_kernel(*refs, first, residual_only, present, faces):
     refs = list(refs)
+    scratch_refs = {}
+    for key in reversed([k for k in (("ahead", 2), ("behind", 2), ("ahead", 3), ("behind", 3)) if present[k[0]][k[1]]]):
+        scratch_refs[key] = refs.pop()
+    face_refs = {}
+    for name in reversed(faces):
+        face_refs[name] = refs.pop()
     out_ref = refs.pop()
 
     def take():
@@ -202,13 +215,18 @@
             ghost = ghost_refs[direction][...].astype(jnp.float32).reshape(2, 3, 3, rows, lanes)
         back_links.append(sh.behind(direction, links[direction], ghost))
 
+    placement = {("ahead", 2): (3, 4), ("behind", 2): (0, 4), ("ahead", 3): (0, 1), ("behind", 3): (12, 1)}
+    for key, scratch in scratch_refs.items():
+        start, stride = placement[key]
+        scratch[:, pl.ds(start, 4, stride=stride), :] = halo_refs[key][...]
+
     def load_halo(side, direction):
-        ref = halo_refs.get((side, direction))
+        ref = scratch_refs.get((side, direction), halo_refs.get((side, direction)))
         return None if ref is None else ref[...].reshape(shape)
 
     def wilson_global(spinor):
-        ahead_list = [sh.ahead(d, spinor, load_halo("ahead", d)) for d in range(4)]
-        behind_list = [sh.behind(d, spinor, load_halo("behind", d)) for d in range(4)]
+        ahead_list = [sh.ahead(d, spinor, load_halo("ahead", d), True) for d in range(4)]
+        behind_list = [sh.behind(d, spinor, load_halo("behind", d), True) for d in range(4)]
         return hopping(spinor, links, back_links, ahead_list, behind_list)
 
     if first:
@@ -252,10 +270,15 @@
     update = update * cmask_ref[...]
     result = update if current is None else current + update
     out_ref[...] = result.reshape(out_ref.shape)
-
-
-def run_pass(source, links, ghosts, labels, member, cmask, spinor, halos, residual_only=False):
+    for name, face_ref in face_refs.items():
+        start, stride = face_rows(name)
+        face_ref[...] = out_ref[:, pl.ds(start, 4, stride=stride), :]
+
+
+def run_pass(source, links, ghosts, labels, member, cmask, spinor, halos, residual_only=False, faces=()):
     first = spinor is None
+    if first:
+        ghosts = [None, None, None, None]
     present = {
         "ghost": [g is not None for g in ghosts],
         "ahead": [h is not None for h in halos["ahead"]] if not first else [False] * 4,
@@ -270,8 +293,19 @@
             for side in ("ahead", "behind"):
                 if present[side][direction]:
                     operands.append(halos[side][direction])
-    kernel = functools.partial(pass_kernel, first=first, residual_only=residual_only, present=present)
-    return pl.pallas_call(kernel, out_shape=jax.ShapeDtypeStruct(source.shape, jnp.float32))(*operands)
+    kernel = functools.partial(
+        pass_kernel, first=first, residual_only=residual_only, present=present, faces=faces
+    )
+    face_shape = (source.shape[0], 4, source.shape[2])
+    out_shape = [jax.ShapeDtypeStruct(source.shape, jnp.float32)]
+    out_shape += [jax.ShapeDtypeStruct(face_shape, jnp.float32) for name in faces]
+    scratch = [
+        pltpu.VMEM(source.shape, jnp.float32)
+        for k in (("ahead", 2), ("behind", 2), ("ahead", 3), ("behind", 3))
+        if present[k[0]][k[1]]
+    ]
+    results = pl.pallas_call(kernel, out_shape=out_shape, scratch_shapes=scratch)(*operands)
+    return results[0], dict(zip(faces, results[1:]))
 
 
 def coarse_kernel(*refs, present):
@@ -400,33 +434,50 @@
         permute_from(link_rows[3], "lat", -PZ, t_down_ok),
     ]
 
-    def halos_of(spinor):
+    needed = [name for name, ok in zip(FACES, (z_up_ok, z_down_ok, t_up_ok, t_down_ok))
+              if any(ok(i) for i in range(domain_count))]
+
+    def faces_of(spinor):
+        result = {}
+        for name in needed:
+            start, stride = face_rows(name)
+            result[name] = lax.slice_in_dim(spinor, start, start + 3 * stride + 1, stride, axis=1)
+        return result
+
+    def halos_of(spinor, faces):
+        def face(name):
+            return faces[name] if name in faces else None
+
         return {
             "ahead": [
                 None,
                 permute_from(spinor, "grp", 1, lambda i: True),
-                permute_from(spinor, "lat", 1, z_up_ok),
-                permute_from(spinor, "lat", PZ, t_up_ok),
+                permute_from(face("z_low"), "lat", 1, z_up_ok) if face("z_low") is not None else None,
+                permute_from(face("t_low"), "lat", PZ, t_up_ok) if face("t_low") is not None else None,
             ],
             "behind": [
                 None,
                 permute_from(spinor, "grp", -1, lambda i: True),
-                permute_from(spinor, "lat", -1, z_down_ok),
-                permute_from(spinor, "lat", -PZ, t_down_ok),
+                permute_from(face("z_high"), "lat", -1, z_down_ok) if face("z_high") is not None else None,
+                permute_from(face("t_high"), "lat", -PZ, t_down_ok) if face("t_high") is not None else None,
             ],
         }
 
-    def smoother_pass(spinor, colour_pass):
-        halos = None if spinor is None else halos_of(spinor)
-        return run_pass(source, link_rows, ghosts, labels, member, colour_masks[colour_pass], spinor, halos)
-
-    def sweep(start):
-        current = smoother_pass(start, 0)
-        return smoother_pass(current, 1)
-
-    smoothed = sweep(None)
-    residue = run_pass(
-        source, link_rows, ghosts, labels, member, None, smoothed, halos_of(smoothed), residual_only=True
+    def smoother_pass(spinor, faces, colour_pass, out_faces):
+        halos = None if spinor is None else halos_of(spinor, faces)
+        return run_pass(
+            source, link_rows, ghosts, labels, member, colour_masks[colour_pass], spinor, halos,
+            faces=out_faces,
+        )
+
+    def sweep(start, faces, last_faces):
+        current, current_faces = smoother_pass(start, faces, 0, tuple(needed))
+        return smoother_pass(current, current_faces, 1, last_faces)
+
+    smoothed, smoothed_faces = sweep(None, None, tuple(needed))
+    residue, _ = run_pass(
+        source, link_rows, ghosts, labels, member, None, smoothed, halos_of(smoothed, smoothed_faces),
+        residual_only=True,
     )
     residual = residue.astype(jnp.bfloat16)
     membership = member.reshape(AGG, site_count).T
@@ -463,7 +514,7 @@
     real_part = jnp.sum(vectors[:, 0] * spread_real - vectors[:, 1] * spread_imag, axis=0)
     imag_part = jnp.sum(vectors[:, 0] * spread_imag + vectors[:, 1] * spread_real, axis=0)
     corrected = smoothed + jnp.stack([real_part, imag_part]).reshape(24, rows, line_extent)
-    solution = sweep(corrected)
+    solution, _ = sweep(corrected, faces_of(corrected), ())
     return (
         solution.reshape(1, 24, time_extent, plane_extent, line_extent),
         correction.reshape(1, 1, 2, CDOF, AGG),

time: 147 us -> 134 us (0.912)
  waiting for transfers between devices: 42.9 us -> 27.2 us
  starting transfers between devices: 45.6 us -> 47.7 us
  local copies, waits for them, and re-layouts: 16 us -> 17.8 us
    ppermute x26, waiting for transfers between devices: 42.9 us -> 27.2 us  [permute_from(): return lax.ppermute(value, axis, pairs)]
    ppermute x26, starting transfers between devices: 45.6 us -> 47.7 us  [permute_from(): return lax.ppermute(value, axis, pairs)]
    unnamed x65, local copies, waits for them, and re-layouts: 8.66 us -> 10.2 us
  transfers between devices with their start and end apart: 26 -> 26, of which waited for: 12 -> 7; matrix products, arithmetic and copies ran while one was open for 8% -> 7% of each run, Pallas kernels for 0% -> 0%
where the time goes in v3:
time: 134 us; the launch traced here: 133 us
  starting transfers between devices  47.7 us (36%)
  Pallas kernels  30.2 us (23%)
  waiting for transfers between devices  27.2 us (20%)
  local copies, waits for them, and re-layouts  17.8 us (13%)
  other arithmetic  5.58 us (4%)
  matrix products  3.41 us (3%)
    ppermute x26, starting transfers between devices, permute_from(): return lax.ppermute(value, axis, pairs)  47.7 us
    ppermute x26, waiting for transfers between devices, permute_from(): return lax.ppermute(value, axis, pairs)  27.2 us
    pallas_call x5, Pallas kernels, run_pass(): pl.pallas_call(kernel, out_shape=out_shape, scratch_shapes=scratch)  22.4 us
    unnamed x65, local copies, waits for them, and re-layouts  10.2 us
    pallas_call x3, Pallas kernels, run_coarse(): pl.pallas_call(kernel, out_shape=jax.ShapeDtypeStruct(source.shape, jnp.f...  7.77 us
    reshape x1, local copies, waits for them, and re-layouts, body(): vectors = test_vectors.reshape(NVEC, 2, 2, 6, site_count)  4.03 us
    dot_general x4, matrix products, contract(): jnp.einsum('kxqn,xqnj->xkj', left, right, preferred_element_type=jnp.floa...  2.96 us
  transfers between devices with their start and end apart: 26, of which 7 were waited for; matrix products, arithmetic and copies ran while one was open for 7% of the time, Pallas kernels for 0%

profile of v3, /device:TPU:0, one launch (start us, length us, event | category | flops | bytes accessed | tf_op | source)
XLA Modules:
  0.0 133.0 jit_solution(17991675298701822950)
XLA Ops:
  4.2 4.0 %shard_map.86 = (f32[24,16,128]{2,1,0:T(8,128)}, f32[24,4,128]{2,1,0:T(4,128)}, f32[24,4,128]{2,1,0:T(4,128)}) custom-call(f32[24,16,128]{2,1,0:T(8,128)} %bitcast.77, bf16[4,18,16,128]{3,2,1,0:T(8,128)(2,1)} %bitcast.70, f32[16,128]{1,0:T(8,128)} %add_convert_fusion.refs_2_.refs_4_, f32[16,16,128]{2,1,0:T(8,128)} %fusion.8.refs_3_.refs_5_, ...), custom_call_target="tpu_custom_call" | custom-call | tf_op jit(solution)/shard_map/pallas_call | solution.py:307
  8.2 2.4 %collective-permute-start.2 = (f32[24,16,128]{2,1,0:T(8,128)}, f32[24,16,128]{2,1,0:T(8,128)S(1)}, u32[]{:S(2)}, u32[]{:S(2)}) collective-permute-start(f32[24,16,128]{2,1,0:T(8,128)} %get-tuple-element.11.refs_7_), channel_id=1, source_target_pairs={{1,0},{2,1},{3,2},{0,3},{5,4},{6,5},{7,6},{4,7},{9,8},{10,9},{11,1... | collective-permute-start | bytes 589832 | tf_op jit(solution)/shard_map/ppermute | solution.py:112
  10.6 6.5 %collective-permute-start.4 = (f32[24,4,128]{2,1,0:T(4,128)}, f32[24,4,128]{2,1,0:T(4,128)S(1)}, u32[]{:S(2)}, u32[]{:S(2)}) collective-permute-start(f32[24,4,128]{2,1,0:T(4,128)} %get-tuple-element.12), channel_id=1, source_target_pairs={{4,0},{8,4},{12,8},{16,12},{20,16},{28,24},{0,28},{5,1},{9,5},{13,... | collective-permute-start | bytes 147464 | tf_op jit(solution)/shard_map/ppermute | solution.py:112
  20.4 1.9 %collective-permute-start.5 = (f32[24,4,128]{2,1,0:T(4,128)}, f32[24,4,128]{2,1,0:T(4,128)S(1)}, u32[]{:S(2)}, u32[]{:S(2)}) collective-permute-start(f32[24,4,128]{2,1,0:T(4,128)} %get-tuple-element.13), channel_id=1, source_target_pairs={{28,0},{0,4},{4,8},{8,12},{12,16},{16,20},{24,28},{29,1},{1,5},{5,... | collective-permute-start | bytes 147464 | tf_op jit(solution)/shard_map/ppermute | solution.py:112
  23.2 6.5 %collective-permute-done.5.refs_11_ = f32[24,4,128]{2,1,0:T(4,128)S(1)} collective-permute-done((f32[24,4,128]{2,1,0:T(4,128)}, f32[24,4,128]{2,1,0:T(4,128)S(1)}, u32[]{:S(2)}, u32[]{:S(2)}) %collective-permute-start.5) | collective-permute-done | bytes 49184 | tf_op jit(solution)/shard_map/ppermute | solution.py:112
  30.5 5.1 %shard_map.87 = (f32[24,16,128]{2,1,0:T(8,128)}, f32[24,4,128]{2,1,0:T(4,128)}, f32[24,4,128]{2,1,0:T(4,128)}) custom-call(f32[24,16,128]{2,1,0:T(8,128)} %bitcast.78, bf16[4,18,16,128]{3,2,1,0:T(8,128)(2,1)} %bitcast.71, bf16[18,16,128]{2,1,0:T(8,128)(2,1)} %copy-done.3, bf16[18,16,128]{2,1,0:T(8,128)(2,1)} %copy-done.4, ...), custom_call_target="tpu_custom_call" | custom-call | tf_op jit(solution)/shard_map/pallas_call | solution.py:307
  36.1 3.6 %collective-permute-start.8 = (f32[24,4,128]{2,1,0:T(4,128)}, f32[24,4,128]{2,1,0:T(4,128)S(1)}, u32[]{:S(2)}, u32[]{:S(2)}) collective-permute-start(f32[24,4,128]{2,1,0:T(4,128)} %get-tuple-element.15), channel_id=1, source_target_pairs={{4,0},{8,4},{12,8},{16,12},{20,16},{28,24},{0,28},{5,1},{9,5},{13,... | collective-permute-start | bytes 147464 | tf_op jit(solution)/shard_map/ppermute | solution.py:112
  39.8 2.2 %collective-permute-start.9 = (f32[24,4,128]{2,1,0:T(4,128)}, f32[24,4,128]{2,1,0:T(4,128)S(1)}, u32[]{:S(2)}, u32[]{:S(2)}) collective-permute-start(f32[24,4,128]{2,1,0:T(4,128)} %get-tuple-element.16), channel_id=1, source_target_pairs={{28,0},{0,4},{4,8},{8,12},{12,16},{16,20},{24,28},{29,1},{1,5},{5,... | collective-permute-start | bytes 147464 | tf_op jit(solution)/shard_map/ppermute | solution.py:112
  42.0 2.6 %copy.13 = bf16[1,24,24,4,4,128]{5,4,3,1,2,0:T(4,128)(2,1)} copy(bf16[1,24,24,4,4,128]{5,4,3,2,1,0:T(4,128)(2,1)S(1)} %copy-done) | data formatting | bytes 4718592 | tf_op args[2]
  44.6 4.0 %reshape.75 = bf16[24,2,2,6,2048]{4,0,3,2,1:T(8,128)(2,1)S(1)} reshape(bf16[1,24,24,4,4,128]{5,4,3,1,2,0:T(4,128)(2,1)} %copy.13) | data formatting | bytes 4718592 | tf_op jit(solution)/shard_map/reshape | solution.py:486
  50.4 3.0 %shard_map.88 = f32[24,16,128]{2,1,0:T(8,128)} custom-call(f32[24,16,128]{2,1,0:T(8,128)} %bitcast.79, bf16[4,18,16,128]{3,2,1,0:T(8,128)(2,1)} %bitcast.72, bf16[18,16,128]{2,1,0:T(8,128)(2,1)} %copy-done.3, bf16[18,16,128]{2,1,0:T(8,128)(2,1)} %copy-done.4, f32[16,128]{1,0:T(8,128)} %add_convert_fusion.refs_2_.refs_4_, ...), custom_call_target="tpu_custom_call" | custom-call | tf_op jit(solution)/shard_map/pallas_call | solution.py:307
  61.1 6.3 %collective-permute-start.12 = (f32[2,1,768]{2,1,0:T(1,128)}, f32[2,1,768]{2,1,0:T(1,128)S(1)}, u32[]{:S(2)}, u32[]{:S(2)}) collective-permute-start(f32[2,1,768]{2,1,0:T(1,128)} %shard_map.89.refs_3_), channel_id=1, source_target_pairs={{4,0},{8,4},{12,8},{16,12},{20,16},{28,24},{0,28},{5,1},{9,5},{13,... | collective-permute-start | bytes 18440 | tf_op jit(solution)/shard_map/ppermute | solution.py:112
  69.4 6.4 %collective-permute-done.13.refs_7_ = f32[2,1,768]{2,1,0:T(1,128)S(1)} collective-permute-done((f32[2,1,768]{2,1,0:T(1,128)}, f32[2,1,768]{2,1,0:T(1,128)S(1)}, u32[]{:S(2)}, u32[]{:S(2)}) %collective-permute-start.13) | collective-permute-done | bytes 6176 | tf_op jit(solution)/shard_map/ppermute | solution.py:112
  76.4 3.0 %shard_map.90.refs_3_ = f32[2,1,768]{2,1,0:T(1,128)} custom-call(f32[2,1,768]{2,1,0:T(1,128)} %copy-done.14, bf16[2,48,768]{2,1,0:T(8,128)(2,1)} %bitcast.85, bf16[9,2,48,768]{3,2,1,0:T(8,128)(2,1)} %bitcast.75, f32[2,1,768]{2,1,0:T(1,128)} %shard_map.89.refs_3_, f32[2,1,768]{2,1,0:T(1,128)} %copy-done.24, f32[2,1,768]{2,1,0:T(1,128)} %copy-done.26, ...), custom_call_target="tpu_custom_call" | custom-call | tf_op jit(solution)/shard_map/pallas_call | solution.py:389
  81.8 4.1 %collective-permute-start.17 = (f32[2,1,768]{2,1,0:T(1,128)}, f32[2,1,768]{2,1,0:T(1,128)S(1)}, u32[]{:S(2)}, u32[]{:S(2)}) collective-permute-start(f32[2,1,768]{2,1,0:T(1,128)} %shard_map.90.refs_3_), channel_id=1, source_target_pairs={{28,0},{0,4},{4,8},{8,12},{12,16},{16,20},{24,28},{29,1},{1,5},{5,... | collective-permute-start | bytes 18440 | tf_op jit(solution)/shard_map/ppermute | solution.py:112
  86.0 4.4 %collective-permute-done.17.refs_7_ = f32[2,1,768]{2,1,0:T(1,128)S(1)} collective-permute-done((f32[2,1,768]{2,1,0:T(1,128)}, f32[2,1,768]{2,1,0:T(1,128)S(1)}, u32[]{:S(2)}, u32[]{:S(2)}) %collective-permute-start.17) | collective-permute-done | bytes 6176 | tf_op jit(solution)/shard_map/ppermute | solution.py:112
  91.0 3.0 %shard_map.91 = f32[2,1,768]{2,1,0:T(1,128)} custom-call(f32[2,1,768]{2,1,0:T(1,128)} %copy-done.14, bf16[2,48,768]{2,1,0:T(8,128)(2,1)} %bitcast.86, bf16[9,2,48,768]{3,2,1,0:T(8,128)(2,1)} %bitcast.76, f32[2,1,768]{2,1,0:T(1,128)} %shard_map.90.refs_3_, f32[2,1,768]{2,1,0:T(1,128)} %copy-done.23, f32[2,1,768]{2,1,0:T(1,128)} %copy-done.25, ...), custom_call_target="tpu_custom_call" | custom-call | tf_op jit(solution)/shard_map/pallas_call | solution.py:389
  97.2 1.9 %collective-permute-start.20 = (f32[24,4,128]{2,1,0:T(4,128)S(1)}, f32[24,4,128]{2,1,0:T(4,128)S(1)}, u32[]{:S(2)}, u32[]{:S(2)}) collective-permute-start(f32[24,4,128]{2,1,0:T(4,128)S(1)} %slice.50), channel_id=1, source_target_pairs={{4,0},{8,4},{12,8},{16,12},{20,16},{28,24},{0,28},{5,1},{9,5},{13,... | collective-permute-start | bytes 147464 | tf_op jit(solution)/shard_map/ppermute | solution.py:112
  99.2 3.9 %collective-permute-start.21 = (f32[24,4,128]{2,1,0:T(4,128)S(1)}, f32[24,4,128]{2,1,0:T(4,128)S(1)}, u32[]{:S(2)}, u32[]{:S(2)}) collective-permute-start(f32[24,4,128]{2,1,0:T(4,128)S(1)} %slice.51), channel_id=1, source_target_pairs={{28,0},{0,4},{4,8},{8,12},{12,16},{16,20},{24,28},{29,1},{1,5},{5,... | collective-permute-start | bytes 147464 | tf_op jit(solution)/shard_map/ppermute | solution.py:112
  103.4 4.6 %collective-permute-done.21.refs_11_ = f32[24,4,128]{2,1,0:T(4,128)S(1)} collective-permute-done((f32[24,4,128]{2,1,0:T(4,128)S(1)}, f32[24,4,128]{2,1,0:T(4,128)S(1)}, u32[]{:S(2)}, u32[]{:S(2)}) %collective-permute-start.21) | collective-permute-done | bytes 49184 | tf_op jit(solution)/shard_map/ppermute | solution.py:112
  109.4 5.2 %shard_map.92 = (f32[24,16,128]{2,1,0:T(8,128)}, f32[24,4,128]{2,1,0:T(4,128)}, f32[24,4,128]{2,1,0:T(4,128)}) custom-call(f32[24,16,128]{2,1,0:T(8,128)} %bitcast.80, bf16[4,18,16,128]{3,2,1,0:T(8,128)(2,1)} %bitcast.73, bf16[18,16,128]{2,1,0:T(8,128)(2,1)} %copy-done.3, bf16[18,16,128]{2,1,0:T(8,128)(2,1)} %copy-done.4, ...), custom_call_target="tpu_custom_call" | custom-call | tf_op jit(solution)/shard_map/pallas_call | solution.py:307
  117.3 3.9 %collective-permute-start.25 = (f32[24,4,128]{2,1,0:T(4,128)}, f32[24,4,128]{2,1,0:T(4,128)S(1)}, u32[]{:S(2)}, u32[]{:S(2)}) collective-permute-start(f32[24,4,128]{2,1,0:T(4,128)} %get-tuple-element.19), channel_id=1, source_target_pairs={{28,0},{0,4},{4,8},{8,12},{12,16},{16,20},{24,28},{29,1},{1,5},{5,... | collective-permute-start | bytes 147464 | tf_op jit(solution)/shard_map/ppermute | solution.py:112
  122.0 4.6 %collective-permute-done.25.refs_11_ = f32[24,4,128]{2,1,0:T(4,128)S(1)} collective-permute-done((f32[24,4,128]{2,1,0:T(4,128)}, f32[24,4,128]{2,1,0:T(4,128)S(1)}, u32[]{:S(2)}, u32[]{:S(2)}) %collective-permute-start.25) | collective-permute-done | bytes 49184 | tf_op jit(solution)/shard_map/ppermute | solution.py:112
  127.9 5.1 %shard_map.93 = f32[24,16,128]{2,1,0:T(8,128)} custom-call(f32[24,16,128]{2,1,0:T(8,128)} %bitcast.81, bf16[4,18,16,128]{3,2,1,0:T(8,128)(2,1)} %bitcast.74, bf16[18,16,128]{2,1,0:T(8,128)(2,1)} %copy-done.3, bf16[18,16,128]{2,1,0:T(8,128)(2,1)} %copy-done.4, f32[16,128]{1,0:T(8,128)} %add_convert_fusion.refs_2_.refs_4_, ...), custom_call_target="tpu_custom_call" | custom-call | tf_op jit(solution)/shard_map/pallas_call | solution.py:307
  (133 shorter events, 33.6 us)
Async XLA Ops:
  8.2 21.5 %collective-permute-start.2 = (f32[24,16,128]{2,1,0:T(8,128)}, f32[24,16,128]{2,1,0:T(8,128)S(1)}, u32[]{:S(2)}, u32[]{:S(2)}) collective-permute-start(f32[24,16,128]{2,1,0:T(8,128)} %get-tuple-element.11.refs_7_), channel_id=1, source_target_pairs={{1,0},{2,1},{3,2},{0,3},{5,4},{6,5},{7,6},{4,7},{9,8},{10,9},{11,1... | collective-permute-start | bytes 589832 | tf_op jit(solution)/shard_map/ppermute | solution.py:112
  10.6 19.1 %collective-permute-start.3 = (f32[24,16,128]{2,1,0:T(8,128)}, f32[24,16,128]{2,1,0:T(8,128)S(1)}, u32[]{:S(2)}, u32[]{:S(2)}) collective-permute-start(f32[24,16,128]{2,1,0:T(8,128)} %get-tuple-element.11.refs_7_), channel_id=1, source_target_pairs={{3,0},{0,1},{1,2},{2,3},{7,4},{4,5},{5,6},{6,7},{11,8},{8,9},{9,10... | collective-permute-start | bytes 589832 | tf_op jit(solution)/shard_map/ppermute | solution.py:112
  10.6 9.8 %collective-permute-start.4 = (f32[24,4,128]{2,1,0:T(4,128)}, f32[24,4,128]{2,1,0:T(4,128)S(1)}, u32[]{:S(2)}, u32[]{:S(2)}) collective-permute-start(f32[24,4,128]{2,1,0:T(4,128)} %get-tuple-element.12), channel_id=1, source_target_pairs={{4,0},{8,4},{12,8},{16,12},{20,16},{28,24},{0,28},{5,1},{9,5},{13,... | collective-permute-start | bytes 147464 | tf_op jit(solution)/shard_map/ppermute | solution.py:112
  18.1 11.6 %collective-permute-start = (bf16[18,16,128]{2,1,0:T(8,128)(2,1)S(1)}, bf16[18,16,128]{2,1,0:T(8,128)(2,1)S(1)}, u32[]{:S(2)}, u32[]{:S(2)}) collective-permute-start(bf16[18,16,128]{2,1,0:T(8,128)(2,1)S(1)} %bitcast.91), channel_id=1, source_target_pairs={{3,0},{0,1},{1,2},{2,3},{7,4},{4,5},{5,6},{6,7},{11,8},{8,9},{9,10... | collective-permute-start | bytes 221192 | tf_op jit(solution)/shard_map/ppermute | solution.py:112
  18.5 11.2 %collective-permute-start.1 = (bf16[18,16,128]{2,1,0:T(8,128)(2,1)S(1)}, bf16[18,16,128]{2,1,0:T(8,128)(2,1)S(1)}, u32[]{:S(2)}, u32[]{:S(2)}) collective-permute-start(bf16[18,16,128]{2,1,0:T(8,128)(2,1)S(1)} %bitcast.90), channel_id=1, source_target_pairs={{28,0},{0,4},{4,8},{8,12},{12,16},{16,20},{24,28},{29,1},{1,5},{5,... | collective-permute-start | bytes 221192 | tf_op jit(solution)/shard_map/ppermute | solution.py:112
  20.4 9.2 %collective-permute-start.5 = (f32[24,4,128]{2,1,0:T(4,128)}, f32[24,4,128]{2,1,0:T(4,128)S(1)}, u32[]{:S(2)}, u32[]{:S(2)}) collective-permute-start(f32[24,4,128]{2,1,0:T(4,128)} %get-tuple-element.13), channel_id=1, source_target_pairs={{28,0},{0,4},{4,8},{8,12},{12,16},{16,20},{24,28},{29,1},{1,5},{5,... | collective-permute-start | bytes 147464 | tf_op jit(solution)/shard_map/ppermute | solution.py:112
  35.6 13.4 %collective-permute-start.6 = (f32[24,16,128]{2,1,0:T(8,128)}, f32[24,16,128]{2,1,0:T(8,128)S(1)}, u32[]{:S(2)}, u32[]{:S(2)}) collective-permute-start(f32[24,16,128]{2,1,0:T(8,128)} %get-tuple-element.14.refs_6_), channel_id=1, source_target_pairs={{1,0},{2,1},{3,2},{0,3},{5,4},{6,5},{7,6},{4,7},{9,8},{10,9},{11,1... | collective-permute-start | bytes 589832 | tf_op jit(solution)/shard_map/ppermute | solution.py:112
  35.6 13.4 %collective-permute-start.7 = (f32[24,16,128]{2,1,0:T(8,128)}, f32[24,16,128]{2,1,0:T(8,128)S(1)}, u32[]{:S(2)}, u32[]{:S(2)}) collective-permute-start(f32[24,16,128]{2,1,0:T(8,128)} %get-tuple-element.14.refs_6_), channel_id=1, source_target_pairs={{3,0},{0,1},{1,2},{2,3},{7,4},{4,5},{5,6},{6,7},{11,8},{8,9},{9,10... | collective-permute-start | bytes 589832 | tf_op jit(solution)/shard_map/ppermute | solution.py:112
  36.1 12.5 %collective-permute-start.8 = (f32[24,4,128]{2,1,0:T(4,128)}, f32[24,4,128]{2,1,0:T(4,128)S(1)}, u32[]{:S(2)}, u32[]{:S(2)}) collective-permute-start(f32[24,4,128]{2,1,0:T(4,128)} %get-tuple-element.15), channel_id=1, source_target_pairs={{4,0},{8,4},{12,8},{16,12},{20,16},{28,24},{0,28},{5,1},{9,5},{13,... | collective-permute-start | bytes 147464 | tf_op jit(solution)/shard_map/ppermute | solution.py:112
  39.8 9.2 %collective-permute-start.9 = (f32[24,4,128]{2,1,0:T(4,128)}, f32[24,4,128]{2,1,0:T(4,128)S(1)}, u32[]{:S(2)}, u32[]{:S(2)}) collective-permute-start(f32[24,4,128]{2,1,0:T(4,128)} %get-tuple-element.16), channel_id=1, source_target_pairs={{28,0},{0,4},{4,8},{8,12},{12,16},{16,20},{24,28},{29,1},{1,5},{5,... | collective-permute-start | bytes 147464 | tf_op jit(solution)/shard_map/ppermute | solution.py:112
  60.6 8.7 %collective-permute-start.10 = (f32[2,1,768]{2,1,0:T(1,128)}, f32[2,1,768]{2,1,0:T(1,128)S(1)}, u32[]{:S(2)}, u32[]{:S(2)}) collective-permute-start(f32[2,1,768]{2,1,0:T(1,128)} %shard_map.89.refs_3_), channel_id=1, source_target_pairs={{1,0},{2,1},{3,2},{0,3},{5,4},{6,5},{7,6},{4,7},{9,8},{10,9},{11,1... | collective-permute-start | bytes 18440 | tf_op jit(solution)/shard_map/ppermute | solution.py:112
  61.0 8.3 %collective-permute-start.11 = (f32[2,1,768]{2,1,0:T(1,128)}, f32[2,1,768]{2,1,0:T(1,128)S(1)}, u32[]{:S(2)}, u32[]{:S(2)}) collective-permute-start(f32[2,1,768]{2,1,0:T(1,128)} %shard_map.89.refs_3_), channel_id=1, source_target_pairs={{3,0},{0,1},{1,2},{2,3},{7,4},{4,5},{5,6},{6,7},{11,8},{8,9},{9,10... | collective-permute-start | bytes 18440 | tf_op jit(solution)/shard_map/ppermute | solution.py:112
  61.1 8.2 %collective-permute-start.12 = (f32[2,1,768]{2,1,0:T(1,128)}, f32[2,1,768]{2,1,0:T(1,128)S(1)}, u32[]{:S(2)}, u32[]{:S(2)}) collective-permute-start(f32[2,1,768]{2,1,0:T(1,128)} %shard_map.89.refs_3_), channel_id=1, source_target_pairs={{4,0},{8,4},{12,8},{16,12},{20,16},{28,24},{0,28},{5,1},{9,5},{13,... | collective-permute-start | bytes 18440 | tf_op jit(solution)/shard_map/ppermute | solution.py:112
  67.4 8.4 %collective-permute-start.13 = (f32[2,1,768]{2,1,0:T(1,128)}, f32[2,1,768]{2,1,0:T(1,128)S(1)}, u32[]{:S(2)}, u32[]{:S(2)}) collective-permute-start(f32[2,1,768]{2,1,0:T(1,128)} %shard_map.89.refs_3_), channel_id=1, source_target_pairs={{28,0},{0,4},{4,8},{8,12},{12,16},{16,20},{24,28},{29,1},{1,5},{5,... | collective-permute-start | bytes 18440 | tf_op jit(solution)/shard_map/ppermute | solution.py:112
  79.4 6.5 %collective-permute-start.14 = (f32[2,1,768]{2,1,0:T(1,128)}, f32[2,1,768]{2,1,0:T(1,128)S(1)}, u32[]{:S(2)}, u32[]{:S(2)}) collective-permute-start(f32[2,1,768]{2,1,0:T(1,128)} %shard_map.90.refs_3_), channel_id=1, source_target_pairs={{1,0},{2,1},{3,2},{0,3},{5,4},{6,5},{7,6},{4,7},{9,8},{10,9},{11,1... | collective-permute-start | bytes 18440 | tf_op jit(solution)/shard_map/ppermute | solution.py:112
  79.7 6.2 %collective-permute-start.15 = (f32[2,1,768]{2,1,0:T(1,128)}, f32[2,1,768]{2,1,0:T(1,128)S(1)}, u32[]{:S(2)}, u32[]{:S(2)}) collective-permute-start(f32[2,1,768]{2,1,0:T(1,128)} %shard_map.90.refs_3_), channel_id=1, source_target_pairs={{3,0},{0,1},{1,2},{2,3},{7,4},{4,5},{5,6},{6,7},{11,8},{8,9},{9,10... | collective-permute-start | bytes 18440 | tf_op jit(solution)/shard_map/ppermute | solution.py:112
  81.8 8.6 %collective-permute-start.17 = (f32[2,1,768]{2,1,0:T(1,128)}, f32[2,1,768]{2,1,0:T(1,128)S(1)}, u32[]{:S(2)}, u32[]{:S(2)}) collective-permute-start(f32[2,1,768]{2,1,0:T(1,128)} %shard_map.90.refs_3_), channel_id=1, source_target_pairs={{28,0},{0,4},{4,8},{8,12},{12,16},{16,20},{24,28},{29,1},{1,5},{5,... | collective-permute-start | bytes 18440 | tf_op jit(solution)/shard_map/ppermute | solution.py:112
  96.6 11.4 %collective-permute-start.18 = (f32[24,16,128]{2,1,0:T(8,128)S(1)}, f32[24,16,128]{2,1,0:T(8,128)S(1)}, u32[]{:S(2)}, u32[]{:S(2)}) collective-permute-start(f32[24,16,128]{2,1,0:T(8,128)S(1)} %add.23.refs_7_), channel_id=1, source_target_pairs={{1,0},{2,1},{3,2},{0,3},{5,4},{6,5},{7,6},{4,7},{9,8},{10,9},{11,1... | collective-permute-start | bytes 589832 | tf_op jit(solution)/shard_map/ppermute | solution.py:112
  97.1 10.9 %collective-permute-start.19 = (f32[24,16,128]{2,1,0:T(8,128)S(1)}, f32[24,16,128]{2,1,0:T(8,128)S(1)}, u32[]{:S(2)}, u32[]{:S(2)}) collective-permute-start(f32[24,16,128]{2,1,0:T(8,128)S(1)} %add.23.refs_7_), channel_id=1, source_target_pairs={{3,0},{0,1},{1,2},{2,3},{7,4},{4,5},{5,6},{6,7},{11,8},{8,9},{9,10... | collective-permute-start | bytes 589832 | tf_op jit(solution)/shard_map/ppermute | solution.py:112
  99.2 8.8 %collective-permute-start.21 = (f32[24,4,128]{2,1,0:T(4,128)S(1)}, f32[24,4,128]{2,1,0:T(4,128)S(1)}, u32[]{:S(2)}, u32[]{:S(2)}) collective-permute-start(f32[24,4,128]{2,1,0:T(4,128)S(1)} %slice.51), channel_id=1, source_target_pairs={{28,0},{0,4},{4,8},{8,12},{12,16},{16,20},{24,28},{29,1},{1,5},{5,... | collective-permute-start | bytes 147464 | tf_op jit(solution)/shard_map/ppermute | solution.py:112
  114.5 12.0 %collective-permute-start.22 = (f32[24,16,128]{2,1,0:T(8,128)}, f32[24,16,128]{2,1,0:T(8,128)S(1)}, u32[]{:S(2)}, u32[]{:S(2)}) collective-permute-start(f32[24,16,128]{2,1,0:T(8,128)} %get-tuple-element.17.refs_7_), channel_id=1, source_target_pairs={{1,0},{2,1},{3,2},{0,3},{5,4},{6,5},{7,6},{4,7},{9,8},{10,9},{11,1... | collective-permute-start | bytes 589832 | tf_op jit(solution)/shard_map/ppermute | solution.py:112
  115.4 11.2 %collective-permute-start.23 = (f32[24,16,128]{2,1,0:T(8,128)}, f32[24,16,128]{2,1,0:T(8,128)S(1)}, u32[]{:S(2)}, u32[]{:S(2)}) collective-permute-start(f32[24,16,128]{2,1,0:T(8,128)} %get-tuple-element.17.refs_7_), channel_id=1, source_target_pairs={{3,0},{0,1},{1,2},{2,3},{7,4},{4,5},{5,6},{6,7},{11,8},{8,9},{9,10... | collective-permute-start | bytes 589832 | tf_op jit(solution)/shard_map/ppermute | solution.py:112
  115.4 6.6 %collective-permute-start.24 = (f32[24,4,128]{2,1,0:T(4,128)}, f32[24,4,128]{2,1,0:T(4,128)S(1)}, u32[]{:S(2)}, u32[]{:S(2)}) collective-permute-start(f32[24,4,128]{2,1,0:T(4,128)} %get-tuple-element.18), channel_id=1, source_target_pairs={{4,0},{8,4},{12,8},{16,12},{20,16},{28,24},{0,28},{5,1},{9,5},{13,... | collective-permute-start | bytes 147464 | tf_op jit(solution)/shard_map/ppermute | solution.py:112
  117.3 9.3 %collective-permute-start.25 = (f32[24,4,128]{2,1,0:T(4,128)}, f32[24,4,128]{2,1,0:T(4,128)S(1)}, u32[]{:S(2)}, u32[]{:S(2)}) collective-permute-start(f32[24,4,128]{2,1,0:T(4,128)} %get-tuple-element.19), channel_id=1, source_target_pairs={{28,0},{0,4},{4,8},{8,12},{12,16},{16,20},{24,28},{29,1},{1,5},{5,... | collective-permute-start | bytes 147464 | tf_op jit(solution)/shard_map/ppermute | solution.py:112
  (33 other events, 130.6 us)

commit v4 on v3

--- a/solution.py
+++ b/solution.py
@@ -130,6 +130,8 @@
             return jnp.where(self.xpos == CX - 1, self.roll(a, CX - 1, -1), self.roll(a, -1, -1))
         if direction == 1:
             half = self.lanes // 2
+            if placed and nbr is not None:
+                return jnp.where(self.lane >= half, self.roll(nbr, half, -1), self.roll(a, half, -1))
             filled = jnp.where(self.lane < half, 0.0 if nbr is None else nbr, a)
             return self.roll(filled, half, -1)
         if direction == 2:
@@ -144,6 +146,8 @@
             return jnp.where(self.xpos == 0, self.roll(a, 1 - CX, -1), self.roll(a, 1, -1))
         if direction == 1:
             half = self.lanes // 2
+            if placed and nbr is not None:
+                return jnp.where(self.lane < half, nbr, self.roll(a, half, -1))
             filled = jnp.where(self.lane >= half, 0.0 if nbr is None else nbr, a)
             return self.roll(filled, half, -1)
         if direction == 2:
@@ -164,17 +168,31 @@
     return 4.5 * spinor - 0.5 * hop_total
 
 
-FACES = ("z_low", "z_high", "t_low", "t_high")
+FACES = ("y_low", "y_high", "z_low", "z_high", "t_low", "t_high")
+HALO_KEYS = tuple((side, d) for d in (1, 2, 3) for side in ("ahead", "behind"))
 
 
 def face_rows(name):
     return {"z_low": (0, 4), "z_high": (3, 4), "t_low": (0, 1), "t_high": (12, 1)}[name]
 
 
+def place(scratch, value, side, direction):
+    if direction == 1:
+        scratch[..., pl.ds(0, value.shape[-1])] = value
+        return
+    start, stride = {("ahead", 2): (3, 4), ("behind", 2): (0, 4), ("ahead", 3): (0, 1), ("behind", 3): (12, 1)}[
+        (side, direction)
+    ]
+    scratch[:, pl.ds(start, 4, stride=stride), :] = value
+
+
 def pass_kernel(*refs, first, residual_only, present, faces):
     refs = list(refs)
+    ghost_scratch = {}
+    for direction in reversed([d for d in (1, 2, 3) if present["ghost"][d]]):
+        ghost_scratch[direction] = refs.pop()
     scratch_refs = {}
-    for key in reversed([k for k in (("ahead", 2), ("behind", 2), ("ahead", 3), ("behind", 3)) if present[k[0]][k[1]]]):
+    for key in reversed([k for k in HALO_KEYS if present[k[0]][k[1]]]):
         scratch_refs[key] = refs.pop()
     face_refs = {}
     for name in reversed(faces):
@@ -212,13 +230,12 @@
     for direction in range(4):
         ghost = None
         if ghost_refs[direction] is not None:
-            ghost = ghost_refs[direction][...].astype(jnp.float32).reshape(2, 3, 3, rows, lanes)
-        back_links.append(sh.behind(direction, links[direction], ghost))
-
-    placement = {("ahead", 2): (3, 4), ("behind", 2): (0, 4), ("ahead", 3): (0, 1), ("behind", 3): (12, 1)}
+            place(ghost_scratch[direction], ghost_refs[direction][...].astype(jnp.float32), "behind", direction)
+            ghost = ghost_scratch[direction][...].reshape(2, 3, 3, rows, lanes)
+        back_links.append(sh.behind(direction, links[direction], ghost, True))
+
     for key, scratch in scratch_refs.items():
-        start, stride = placement[key]
-        scratch[:, pl.ds(start, 4, stride=stride), :] = halo_refs[key][...]
+        place(scratch, halo_refs[key][...], key[0], key[1])
 
     def load_halo(side, direction):
         ref = scratch_refs.get((side, direction), halo_refs.get((side, direction)))
@@ -271,8 +288,13 @@
     result = update if current is None else current + update
     out_ref[...] = result.reshape(out_ref.shape)
     for name, face_ref in face_refs.items():
-        start, stride = face_rows(name)
-        face_ref[...] = out_ref[:, pl.ds(start, 4, stride=stride), :]
+        if name == "y_low":
+            face_ref[...] = out_ref[:, :, pl.ds(0, lanes // 2)]
+        elif name == "y_high":
+            face_ref[...] = pltpu.roll(out_ref[...], lanes // 2, 2)[:, :, : lanes // 2]
+        else:
+            start, stride = face_rows(name)
+            face_ref[...] = out_ref[:, pl.ds(start, 4, stride=stride), :]
 
 
 def run_pass(source, links, ghosts, labels, member, cmask, spinor, halos, residual_only=False, faces=()):
@@ -296,14 +318,15 @@
     kernel = functools.partial(
         pass_kernel, first=first, residual_only=residual_only, present=present, faces=faces
     )
-    face_shape = (source.shape[0], 4, source.shape[2])
+    def face_shape(name):
+        if name.startswith("y"):
+            return (source.shape[0], source.shape[1], source.shape[2] // 2)
+        return (source.shape[0], 4, source.shape[2])
+
     out_shape = [jax.ShapeDtypeStruct(source.shape, jnp.float32)]
-    out_shape += [jax.ShapeDtypeStruct(face_shape, jnp.float32) for name in faces]
-    scratch = [
-        pltpu.VMEM(source.shape, jnp.float32)
-        for k in (("ahead", 2), ("behind", 2), ("ahead", 3), ("behind", 3))
-        if present[k[0]][k[1]]
-    ]
+    out_shape += [jax.ShapeDtypeStruct(face_shape(name), jnp.float32) for name in faces]
+    scratch = [pltpu.VMEM(source.shape, jnp.float32) for k in HALO_KEYS if present[k[0]][k[1]]]
+    scratch += [pltpu.VMEM(links.shape[1:], jnp.float32) for d in (1, 2, 3) if present["ghost"][d]]
     results = pl.pallas_call(kernel, out_shape=out_shape, scratch_shapes=scratch)(*operands)
     return results[0], dict(zip(faces, results[1:]))
 
@@ -427,19 +450,22 @@
     def t_down_ok(i):
         return i - PZ >= 0
 
+    half = line_extent // 2
     ghosts = [
         None,
-        permute_from(link_rows[1], "grp", -1, lambda i: True),
-        permute_from(link_rows[2], "lat", -1, z_down_ok),
-        permute_from(link_rows[3], "lat", -PZ, t_down_ok),
+        permute_from(link_rows[1][..., half:], "grp", -1, lambda i: True),
+        permute_from(lax.slice_in_dim(link_rows[2], 3, 16, 4, axis=1), "lat", -1, z_down_ok),
+        permute_from(lax.slice_in_dim(link_rows[3], 12, 16, 1, axis=1), "lat", -PZ, t_down_ok),
     ]
 
-    needed = [name for name, ok in zip(FACES, (z_up_ok, z_down_ok, t_up_ok, t_down_ok))
-              if any(ok(i) for i in range(domain_count))]
+    needed = ["y_low", "y_high"] + [
+        name for name, ok in zip(FACES[2:], (z_up_ok, z_down_ok, t_up_ok, t_down_ok))
+        if any(ok(i) for i in range(domain_count))
+    ]
 
     def faces_of(spinor):
-        result = {}
-        for name in needed:
+        result = {"y_low": spinor[..., :half], "y_high": spinor[..., half:]}
+        for name in needed[2:]:
             start, stride = face_rows(name)
             result[name] = lax.slice_in_dim(spinor, start, start + 3 * stride + 1, stride, axis=1)
         return result
@@ -451,13 +477,13 @@
         return {
             "ahead": [
                 None,
-                permute_from(spinor, "grp", 1, lambda i: True),
+                permute_from(faces["y_low"], "grp", 1, lambda i: True),
                 permute_from(face("z_low"), "lat", 1, z_up_ok) if face("z_low") is not None else None,
                 permute_from(face("t_low"), "lat", PZ, t_up_ok) if face("t_low") is not None else None,
             ],
             "behind": [
                 None,
-                permute_from(spinor, "grp", -1, lambda i: True),
+                permute_from(faces["y_high"], "grp", -1, lambda i: True),
                 permute_from(face("z_high"), "lat", -1, z_down_ok) if face("z_high") is not None else None,
                 permute_from(face("t_high"), "lat", -PZ, t_down_ok) if face("t_high") is not None else None,
             ],

time: 134 us -> 132 us (0.985)
  no operation moved by 1% of the time
where the time goes in v4:
time: 132 us; the launch traced here: 131 us
  starting transfers between devices  47.8 us (36%)
  Pallas kernels  30.3 us (23%)
  waiting for transfers between devices  26.3 us (20%)
  local copies, waits for them, and re-layouts  16.7 us (13%)
  other arithmetic  5.57 us (4%)
  matrix products  3.41 us (3%)
    ppermute x26, starting transfers between devices, permute_from(): return lax.ppermute(value, axis, pairs)  47.8 us
    ppermute x26, waiting for transfers between devices, permute_from(): return lax.ppermute(value, axis, pairs)  26.3 us
    pallas_call x5, Pallas kernels, run_pass(): pl.pallas_call(kernel, out_shape=out_shape, scratch_shapes=scratch)  22.5 us
    unnamed x65, local copies, waits for them, and re-layouts  8.89 us
    pallas_call x3, Pallas kernels, run_coarse(): pl.pallas_call(kernel, out_shape=jax.ShapeDtypeStruct(source.shape, jnp.f...  7.77 us
    reshape x1, local copies, waits for them, and re-layouts, body(): vectors = test_vectors.reshape(NVEC, 2, 2, 6, site_count)  4.03 us
    dot_general x4, matrix products, contract(): jnp.einsum('kxqn,xqnj->xkj', left, right, preferred_element_type=jnp.floa...  2.97 us
  transfers between devices with their start and end apart: 26, of which 7 were waited for; matrix products, arithmetic and copies ran while one was open for 7% of the time, Pallas kernels for 0%

profile of v4, /device:TPU:0, one launch (start us, length us, event | category | flops | bytes accessed | tf_op | source)
XLA Modules:
  0.0 131.4 jit_solution(15141647329725422286)
XLA Ops:
  4.2 4.2 %shard_map.86 = (f32[24,16,128]{2,1,0:T(8,128)}, f32[24,16,64]{2,1,0:T(8,128)}, f32[24,16,64]{2,1,0:T(8,128)}, f32[24,4,128]{2,1,0:T(4,128)}, f32[24,4,128]{2,1,0:T(4,128)}) custom-call(f32[24,16,128]{2,1,0:T(8,128)} %bitcast.77, bf16[4,18,16,128]{3,2,1,0:T(8,128)(2,1)} %bitcast.70, f32[16,128]{1,0:T(8,128)} %add_convert_fusion.refs_2_.refs_4_, ...), custom_call_target="tpu_custom_call" | custom-call | tf_op jit(solution)/shard_map/pallas_call | solution.py:330
  8.4 2.4 %collective-permute-start.2 = (f32[24,16,64]{2,1,0:T(8,128)}, f32[24,16,64]{2,1,0:T(8,128)S(1)}, u32[]{:S(2)}, u32[]{:S(2)}) collective-permute-start(f32[24,16,64]{2,1,0:T(8,128)} %get-tuple-element.18), channel_id=1, source_target_pairs={{1,0},{2,1},{3,2},{0,3},{5,4},{6,5},{7,6},{4,7},{9,8},{10,9},{11,1... | collective-permute-start | bytes 294920 | tf_op jit(solution)/shard_map/ppermute | solution.py:112
  11.8 3.4 %collective-permute-start.1 = (bf16[18,4,128]{2,1,0:T(4,128)(2,1)S(1)}, bf16[18,4,128]{2,1,0:T(4,128)(2,1)S(1)}, u32[]{:S(2)}, u32[]{:S(2)}) collective-permute-start(bf16[18,4,128]{2,1,0:T(4,128)(2,1)S(1)} %slice.57), channel_id=1, source_target_pairs={{28,0},{0,4},{4,8},{8,12},{12,16},{16,20},{24,28},{29,1},{1,5},{5,... | collective-permute-start | bytes 55304 | tf_op jit(solution)/shard_map/ppermute | solution.py:112
  15.2 5.1 %collective-permute-start.4 = (f32[24,4,128]{2,1,0:T(4,128)}, f32[24,4,128]{2,1,0:T(4,128)S(1)}, u32[]{:S(2)}, u32[]{:S(2)}) collective-permute-start(f32[24,4,128]{2,1,0:T(4,128)} %get-tuple-element.20), channel_id=1, source_target_pairs={{4,0},{8,4},{12,8},{16,12},{20,16},{28,24},{0,28},{5,1},{9,5},{13,... | collective-permute-start | bytes 147464 | tf_op jit(solution)/shard_map/ppermute | solution.py:112
  23.5 2.7 %collective-permute-done.refs_2_ = bf16[18,16,64]{2,1,0:T(8,128)(2,1)S(1)} collective-permute-done((bf16[18,16,64]{2,1,0:T(8,128)(2,1)S(1)}, bf16[18,16,64]{2,1,0:T(8,128)(2,1)S(1)}, u32[]{:S(2)}, u32[]{:S(2)}) %collective-permute-start) | collective-permute-done | bytes 36896 | tf_op jit(solution)/shard_map/ppermute | solution.py:112
  26.2 3.0 %collective-permute-done.5.refs_11_ = f32[24,4,128]{2,1,0:T(4,128)S(1)} collective-permute-done((f32[24,4,128]{2,1,0:T(4,128)}, f32[24,4,128]{2,1,0:T(4,128)S(1)}, u32[]{:S(2)}, u32[]{:S(2)}) %collective-permute-start.5) | collective-permute-done | bytes 49184 | tf_op jit(solution)/shard_map/ppermute | solution.py:112
  30.0 5.2 %shard_map.87 = (f32[24,16,128]{2,1,0:T(8,128)}, f32[24,16,64]{2,1,0:T(8,128)}, f32[24,16,64]{2,1,0:T(8,128)}, f32[24,4,128]{2,1,0:T(4,128)}, f32[24,4,128]{2,1,0:T(4,128)}) custom-call(f32[24,16,128]{2,1,0:T(8,128)} %bitcast.78, bf16[4,18,16,128]{3,2,1,0:T(8,128)(2,1)} %bitcast.71, bf16[18,16,64]{2,1,0:T(8,128)(2,1)} %copy-done.3, ...), custom_call_target="tpu_custom_call" | custom-call | tf_op jit(solution)/shard_map/pallas_call | solution.py:330
  35.8 3.5 %collective-permute-start.8 = (f32[24,4,128]{2,1,0:T(4,128)}, f32[24,4,128]{2,1,0:T(4,128)S(1)}, u32[]{:S(2)}, u32[]{:S(2)}) collective-permute-start(f32[24,4,128]{2,1,0:T(4,128)} %get-tuple-element.25), channel_id=1, source_target_pairs={{4,0},{8,4},{12,8},{16,12},{20,16},{28,24},{0,28},{5,1},{9,5},{13,... | collective-permute-start | bytes 147464 | tf_op jit(solution)/shard_map/ppermute | solution.py:112
  39.4 2.3 %collective-permute-start.9 = (f32[24,4,128]{2,1,0:T(4,128)}, f32[24,4,128]{2,1,0:T(4,128)S(1)}, u32[]{:S(2)}, u32[]{:S(2)}) collective-permute-start(f32[24,4,128]{2,1,0:T(4,128)} %get-tuple-element.26), channel_id=1, source_target_pairs={{28,0},{0,4},{4,8},{8,12},{12,16},{16,20},{24,28},{29,1},{1,5},{5,... | collective-permute-start | bytes 147464 | tf_op jit(solution)/shard_map/ppermute | solution.py:112
  41.7 2.6 %copy.13 = bf16[1,24,24,4,4,128]{5,4,3,1,2,0:T(4,128)(2,1)} copy(bf16[1,24,24,4,4,128]{5,4,3,2,1,0:T(4,128)(2,1)S(1)} %copy-done.1) | data formatting | bytes 4718592 | tf_op args[2]
  44.4 4.0 %reshape.75 = bf16[24,2,2,6,2048]{4,0,3,2,1:T(8,128)(2,1)S(1)} reshape(bf16[1,24,24,4,4,128]{5,4,3,1,2,0:T(4,128)(2,1)} %copy.13) | data formatting | bytes 4718592 | tf_op jit(solution)/shard_map/reshape | solution.py:512
  49.2 2.9 %shard_map.88 = f32[24,16,128]{2,1,0:T(8,128)} custom-call(f32[24,16,128]{2,1,0:T(8,128)} %bitcast.79, bf16[4,18,16,128]{3,2,1,0:T(8,128)(2,1)} %bitcast.72, bf16[18,16,64]{2,1,0:T(8,128)(2,1)} %copy-done.3, bf16[18,4,128]{2,1,0:T(4,128)(2,1)} %copy-done.5, f32[16,128]{1,0:T(8,128)} %add_convert_fusion.refs_2_.refs_4_, ...), custom_call_target="tpu_custom_call" | custom-call | tf_op jit(solution)/shard_map/pallas_call | solution.py:330
  60.5 5.8 %collective-permute-start.12 = (f32[2,1,768]{2,1,0:T(1,128)}, f32[2,1,768]{2,1,0:T(1,128)S(1)}, u32[]{:S(2)}, u32[]{:S(2)}) collective-permute-start(f32[2,1,768]{2,1,0:T(1,128)} %shard_map.89.refs_3_), channel_id=1, source_target_pairs={{4,0},{8,4},{12,8},{16,12},{20,16},{28,24},{0,28},{5,1},{9,5},{13,... | collective-permute-start | bytes 18440 | tf_op jit(solution)/shard_map/ppermute | solution.py:112
  68.2 6.4 %collective-permute-done.13.refs_7_ = f32[2,1,768]{2,1,0:T(1,128)S(1)} collective-permute-done((f32[2,1,768]{2,1,0:T(1,128)}, f32[2,1,768]{2,1,0:T(1,128)S(1)}, u32[]{:S(2)}, u32[]{:S(2)}) %collective-permute-start.13) | collective-permute-done | bytes 6176 | tf_op jit(solution)/shard_map/ppermute | solution.py:112
  75.2 3.0 %shard_map.90.refs_3_ = f32[2,1,768]{2,1,0:T(1,128)} custom-call(f32[2,1,768]{2,1,0:T(1,128)} %copy-done.14, bf16[2,48,768]{2,1,0:T(8,128)(2,1)} %bitcast.85, bf16[9,2,48,768]{3,2,1,0:T(8,128)(2,1)} %bitcast.75, f32[2,1,768]{2,1,0:T(1,128)} %shard_map.89.refs_3_, f32[2,1,768]{2,1,0:T(1,128)} %copy-done.24, f32[2,1,768]{2,1,0:T(1,128)} %copy-done.26, ...), custom_call_target="tpu_custom_call" | custom-call | tf_op jit(solution)/shard_map/pallas_call | solution.py:412
  80.7 3.9 %collective-permute-start.17 = (f32[2,1,768]{2,1,0:T(1,128)}, f32[2,1,768]{2,1,0:T(1,128)S(1)}, u32[]{:S(2)}, u32[]{:S(2)}) collective-permute-start(f32[2,1,768]{2,1,0:T(1,128)} %shard_map.90.refs_3_), channel_id=1, source_target_pairs={{28,0},{0,4},{4,8},{8,12},{12,16},{16,20},{24,28},{29,1},{1,5},{5,... | collective-permute-start | bytes 18440 | tf_op jit(solution)/shard_map/ppermute | solution.py:112
  84.7 4.5 %collective-permute-done.17.refs_7_ = f32[2,1,768]{2,1,0:T(1,128)S(1)} collective-permute-done((f32[2,1,768]{2,1,0:T(1,128)}, f32[2,1,768]{2,1,0:T(1,128)S(1)}, u32[]{:S(2)}, u32[]{:S(2)}) %collective-permute-start.17) | collective-permute-done | bytes 6176 | tf_op jit(solution)/shard_map/ppermute | solution.py:112
  89.7 3.0 %shard_map.91 = f32[2,1,768]{2,1,0:T(1,128)} custom-call(f32[2,1,768]{2,1,0:T(1,128)} %copy-done.14, bf16[2,48,768]{2,1,0:T(8,128)(2,1)} %bitcast.86, bf16[9,2,48,768]{3,2,1,0:T(8,128)(2,1)} %bitcast.76, f32[2,1,768]{2,1,0:T(1,128)} %shard_map.90.refs_3_, f32[2,1,768]{2,1,0:T(1,128)} %copy-done.23, f32[2,1,768]{2,1,0:T(1,128)} %copy-done.25, ...), custom_call_target="tpu_custom_call" | custom-call | tf_op jit(solution)/shard_map/pallas_call | solution.py:412
  98.0 3.9 %collective-permute-start.21 = (f32[24,4,128]{2,1,0:T(4,128)S(1)}, f32[24,4,128]{2,1,0:T(4,128)S(1)}, u32[]{:S(2)}, u32[]{:S(2)}) collective-permute-start(f32[24,4,128]{2,1,0:T(4,128)S(1)} %slice.67), channel_id=1, source_target_pairs={{28,0},{0,4},{4,8},{8,12},{12,16},{16,20},{24,28},{29,1},{1,5},{5,... | collective-permute-start | bytes 147464 | tf_op jit(solution)/shard_map/ppermute | solution.py:112
  102.3 4.6 %collective-permute-done.21.refs_11_ = f32[24,4,128]{2,1,0:T(4,128)S(1)} collective-permute-done((f32[24,4,128]{2,1,0:T(4,128)S(1)}, f32[24,4,128]{2,1,0:T(4,128)S(1)}, u32[]{:S(2)}, u32[]{:S(2)}) %collective-permute-start.21) | collective-permute-done | bytes 49184 | tf_op jit(solution)/shard_map/ppermute | solution.py:112
  108.3 5.2 %shard_map.92 = (f32[24,16,128]{2,1,0:T(8,128)}, f32[24,16,64]{2,1,0:T(8,128)}, f32[24,16,64]{2,1,0:T(8,128)}, f32[24,4,128]{2,1,0:T(4,128)}, f32[24,4,128]{2,1,0:T(4,128)}) custom-call(f32[24,16,128]{2,1,0:T(8,128)} %bitcast.80, bf16[4,18,16,128]{3,2,1,0:T(8,128)(2,1)} %bitcast.73, bf16[18,16,64]{2,1,0:T(8,128)(2,1)} %copy-done.3, ...), custom_call_target="tpu_custom_call" | custom-call | tf_op jit(solution)/shard_map/pallas_call | solution.py:330
  116.2 3.9 %collective-permute-start.25 = (f32[24,4,128]{2,1,0:T(4,128)}, f32[24,4,128]{2,1,0:T(4,128)S(1)}, u32[]{:S(2)}, u32[]{:S(2)}) collective-permute-start(f32[24,4,128]{2,1,0:T(4,128)} %get-tuple-element.31), channel_id=1, source_target_pairs={{28,0},{0,4},{4,8},{8,12},{12,16},{16,20},{24,28},{29,1},{1,5},{5,... | collective-permute-start | bytes 147464 | tf_op jit(solution)/shard_map/ppermute | solution.py:112
  120.9 4.6 %collective-permute-done.25.refs_11_ = f32[24,4,128]{2,1,0:T(4,128)S(1)} collective-permute-done((f32[24,4,128]{2,1,0:T(4,128)}, f32[24,4,128]{2,1,0:T(4,128)S(1)}, u32[]{:S(2)}, u32[]{:S(2)}) %collective-permute-start.25) | collective-permute-done | bytes 49184 | tf_op jit(solution)/shard_map/ppermute | solution.py:112
  126.3 5.0 %shard_map.93 = f32[24,16,128]{2,1,0:T(8,128)} custom-call(f32[24,16,128]{2,1,0:T(8,128)} %bitcast.81, bf16[4,18,16,128]{3,2,1,0:T(8,128)(2,1)} %bitcast.74, bf16[18,16,64]{2,1,0:T(8,128)(2,1)} %copy-done.3, bf16[18,4,128]{2,1,0:T(4,128)(2,1)} %copy-done.5, f32[16,128]{1,0:T(8,128)} %add_convert_fusion.refs_2_.refs_4_, ...), custom_call_target="tpu_custom_call" | custom-call | tf_op jit(solution)/shard_map/pallas_call | solution.py:330
  (136 shorter events, 34.8 us)
Async XLA Ops:
  8.4 20.9 %collective-permute-start.2 = (f32[24,16,64]{2,1,0:T(8,128)}, f32[24,16,64]{2,1,0:T(8,128)S(1)}, u32[]{:S(2)}, u32[]{:S(2)}) collective-permute-start(f32[24,16,64]{2,1,0:T(8,128)} %get-tuple-element.18), channel_id=1, source_target_pairs={{1,0},{2,1},{3,2},{0,3},{5,4},{6,5},{7,6},{4,7},{9,8},{10,9},{11,1... | collective-permute-start | bytes 294920 | tf_op jit(solution)/shard_map/ppermute | solution.py:112
  10.8 18.5 %collective-permute-start.3 = (f32[24,16,64]{2,1,0:T(8,128)}, f32[24,16,64]{2,1,0:T(8,128)S(1)}, u32[]{:S(2)}, u32[]{:S(2)}) collective-permute-start(f32[24,16,64]{2,1,0:T(8,128)} %get-tuple-element.19), channel_id=1, source_target_pairs={{3,0},{0,1},{1,2},{2,3},{7,4},{4,5},{5,6},{6,7},{11,8},{8,9},{9,10... | collective-permute-start | bytes 294920 | tf_op jit(solution)/shard_map/ppermute | solution.py:112
  11.8 10.6 %collective-permute-start.1 = (bf16[18,4,128]{2,1,0:T(4,128)(2,1)S(1)}, bf16[18,4,128]{2,1,0:T(4,128)(2,1)S(1)}, u32[]{:S(2)}, u32[]{:S(2)}) collective-permute-start(bf16[18,4,128]{2,1,0:T(4,128)(2,1)S(1)} %slice.57), channel_id=1, source_target_pairs={{28,0},{0,4},{4,8},{8,12},{12,16},{16,20},{24,28},{29,1},{1,5},{5,... | collective-permute-start | bytes 55304 | tf_op jit(solution)/shard_map/ppermute | solution.py:112
  15.2 11.0 %collective-permute-start.4 = (f32[24,4,128]{2,1,0:T(4,128)}, f32[24,4,128]{2,1,0:T(4,128)S(1)}, u32[]{:S(2)}, u32[]{:S(2)}) collective-permute-start(f32[24,4,128]{2,1,0:T(4,128)} %get-tuple-element.20), channel_id=1, source_target_pairs={{4,0},{8,4},{12,8},{16,12},{20,16},{28,24},{0,28},{5,1},{9,5},{13,... | collective-permute-start | bytes 147464 | tf_op jit(solution)/shard_map/ppermute | solution.py:112
  20.3 8.9 %collective-permute-start.5 = (f32[24,4,128]{2,1,0:T(4,128)}, f32[24,4,128]{2,1,0:T(4,128)S(1)}, u32[]{:S(2)}, u32[]{:S(2)}) collective-permute-start(f32[24,4,128]{2,1,0:T(4,128)} %get-tuple-element.21), channel_id=1, source_target_pairs={{28,0},{0,4},{4,8},{8,12},{12,16},{16,20},{24,28},{29,1},{1,5},{5,... | collective-permute-start | bytes 147464 | tf_op jit(solution)/shard_map/ppermute | solution.py:112
  35.2 13.2 %collective-permute-start.6 = (f32[24,16,64]{2,1,0:T(8,128)}, f32[24,16,64]{2,1,0:T(8,128)S(1)}, u32[]{:S(2)}, u32[]{:S(2)}) collective-permute-start(f32[24,16,64]{2,1,0:T(8,128)} %get-tuple-element.23), channel_id=1, source_target_pairs={{1,0},{2,1},{3,2},{0,3},{5,4},{6,5},{7,6},{4,7},{9,8},{10,9},{11,1... | collective-permute-start | bytes 294920 | tf_op jit(solution)/shard_map/ppermute | solution.py:112
  35.8 12.6 %collective-permute-start.7 = (f32[24,16,64]{2,1,0:T(8,128)}, f32[24,16,64]{2,1,0:T(8,128)S(1)}, u32[]{:S(2)}, u32[]{:S(2)}) collective-permute-start(f32[24,16,64]{2,1,0:T(8,128)} %get-tuple-element.24), channel_id=1, source_target_pairs={{3,0},{0,1},{1,2},{2,3},{7,4},{4,5},{5,6},{6,7},{11,8},{8,9},{9,10... | collective-permute-start | bytes 294920 | tf_op jit(solution)/shard_map/ppermute | solution.py:112
  35.8 12.5 %collective-permute-start.8 = (f32[24,4,128]{2,1,0:T(4,128)}, f32[24,4,128]{2,1,0:T(4,128)S(1)}, u32[]{:S(2)}, u32[]{:S(2)}) collective-permute-start(f32[24,4,128]{2,1,0:T(4,128)} %get-tuple-element.25), channel_id=1, source_target_pairs={{4,0},{8,4},{12,8},{16,12},{20,16},{28,24},{0,28},{5,1},{9,5},{13,... | collective-permute-start | bytes 147464 | tf_op jit(solution)/shard_map/ppermute | solution.py:112
  39.4 9.0 %collective-permute-start.9 = (f32[24,4,128]{2,1,0:T(4,128)}, f32[24,4,128]{2,1,0:T(4,128)S(1)}, u32[]{:S(2)}, u32[]{:S(2)}) collective-permute-start(f32[24,4,128]{2,1,0:T(4,128)} %get-tuple-element.26), channel_id=1, source_target_pairs={{28,0},{0,4},{4,8},{8,12},{12,16},{16,20},{24,28},{29,1},{1,5},{5,... | collective-permute-start | bytes 147464 | tf_op jit(solution)/shard_map/ppermute | solution.py:112
  59.3 8.9 %collective-permute-start.10 = (f32[2,1,768]{2,1,0:T(1,128)}, f32[2,1,768]{2,1,0:T(1,128)S(1)}, u32[]{:S(2)}, u32[]{:S(2)}) collective-permute-start(f32[2,1,768]{2,1,0:T(1,128)} %shard_map.89.refs_3_), channel_id=1, source_target_pairs={{1,0},{2,1},{3,2},{0,3},{5,4},{6,5},{7,6},{4,7},{9,8},{10,9},{11,1... | collective-permute-start | bytes 18440 | tf_op jit(solution)/shard_map/ppermute | solution.py:112
  60.5 7.7 %collective-permute-start.11 = (f32[2,1,768]{2,1,0:T(1,128)}, f32[2,1,768]{2,1,0:T(1,128)S(1)}, u32[]{:S(2)}, u32[]{:S(2)}) collective-permute-start(f32[2,1,768]{2,1,0:T(1,128)} %shard_map.89.refs_3_), channel_id=1, source_target_pairs={{3,0},{0,1},{1,2},{2,3},{7,4},{4,5},{5,6},{6,7},{11,8},{8,9},{9,10... | collective-permute-start | bytes 18440 | tf_op jit(solution)/shard_map/ppermute | solution.py:112
  60.5 7.7 %collective-permute-start.12 = (f32[2,1,768]{2,1,0:T(1,128)}, f32[2,1,768]{2,1,0:T(1,128)S(1)}, u32[]{:S(2)}, u32[]{:S(2)}) collective-permute-start(f32[2,1,768]{2,1,0:T(1,128)} %shard_map.89.refs_3_), channel_id=1, source_target_pairs={{4,0},{8,4},{12,8},{16,12},{20,16},{28,24},{0,28},{5,1},{9,5},{13,... | collective-permute-start | bytes 18440 | tf_op jit(solution)/shard_map/ppermute | solution.py:112
  66.2 8.4 %collective-permute-start.13 = (f32[2,1,768]{2,1,0:T(1,128)}, f32[2,1,768]{2,1,0:T(1,128)S(1)}, u32[]{:S(2)}, u32[]{:S(2)}) collective-permute-start(f32[2,1,768]{2,1,0:T(1,128)} %shard_map.89.refs_3_), channel_id=1, source_target_pairs={{28,0},{0,4},{4,8},{8,12},{12,16},{16,20},{24,28},{29,1},{1,5},{5,... | collective-permute-start | bytes 18440 | tf_op jit(solution)/shard_map/ppermute | solution.py:112
  78.2 6.4 %collective-permute-start.14 = (f32[2,1,768]{2,1,0:T(1,128)}, f32[2,1,768]{2,1,0:T(1,128)S(1)}, u32[]{:S(2)}, u32[]{:S(2)}) collective-permute-start(f32[2,1,768]{2,1,0:T(1,128)} %shard_map.90.refs_3_), channel_id=1, source_target_pairs={{1,0},{2,1},{3,2},{0,3},{5,4},{6,5},{7,6},{4,7},{9,8},{10,9},{11,1... | collective-permute-start | bytes 18440 | tf_op jit(solution)/shard_map/ppermute | solution.py:112
  78.5 6.1 %collective-permute-start.15 = (f32[2,1,768]{2,1,0:T(1,128)}, f32[2,1,768]{2,1,0:T(1,128)S(1)}, u32[]{:S(2)}, u32[]{:S(2)}) collective-permute-start(f32[2,1,768]{2,1,0:T(1,128)} %shard_map.90.refs_3_), channel_id=1, source_target_pairs={{3,0},{0,1},{1,2},{2,3},{7,4},{4,5},{5,6},{6,7},{11,8},{8,9},{9,10... | collective-permute-start | bytes 18440 | tf_op jit(solution)/shard_map/ppermute | solution.py:112
  80.7 8.5 %collective-permute-start.17 = (f32[2,1,768]{2,1,0:T(1,128)}, f32[2,1,768]{2,1,0:T(1,128)S(1)}, u32[]{:S(2)}, u32[]{:S(2)}) collective-permute-start(f32[2,1,768]{2,1,0:T(1,128)} %shard_map.90.refs_3_), channel_id=1, source_target_pairs={{28,0},{0,4},{4,8},{8,12},{12,16},{16,20},{24,28},{29,1},{1,5},{5,... | collective-permute-start | bytes 18440 | tf_op jit(solution)/shard_map/ppermute | solution.py:112
  95.4 11.5 %collective-permute-start.18 = (f32[24,16,64]{2,1,0:T(8,128)S(1)}, f32[24,16,64]{2,1,0:T(8,128)S(1)}, u32[]{:S(2)}, u32[]{:S(2)}) collective-permute-start(f32[24,16,64]{2,1,0:T(8,128)S(1)} %get-tuple-element.45), channel_id=1, source_target_pairs={{1,0},{2,1},{3,2},{0,3},{5,4},{6,5},{7,6},{4,7},{9,8},{10,9},{11,1... | collective-permute-start | bytes 294920 | tf_op jit(solution)/shard_map/ppermute | solution.py:112
  95.8 11.1 %collective-permute-start.19 = (f32[24,16,64]{2,1,0:T(8,128)S(1)}, f32[24,16,64]{2,1,0:T(8,128)S(1)}, u32[]{:S(2)}, u32[]{:S(2)}) collective-permute-start(f32[24,16,64]{2,1,0:T(8,128)S(1)} %get-tuple-element.44), channel_id=1, source_target_pairs={{3,0},{0,1},{1,2},{2,3},{7,4},{4,5},{5,6},{6,7},{11,8},{8,9},{9,10... | collective-permute-start | bytes 294920 | tf_op jit(solution)/shard_map/ppermute | solution.py:112
  96.1 6.2 %collective-permute-start.20 = (f32[24,4,128]{2,1,0:T(4,128)S(1)}, f32[24,4,128]{2,1,0:T(4,128)S(1)}, u32[]{:S(2)}, u32[]{:S(2)}) collective-permute-start(f32[24,4,128]{2,1,0:T(4,128)S(1)} %slice.66), channel_id=1, source_target_pairs={{4,0},{8,4},{12,8},{16,12},{20,16},{28,24},{0,28},{5,1},{9,5},{13,... | collective-permute-start | bytes 147464 | tf_op jit(solution)/shard_map/ppermute | solution.py:112
  98.0 8.9 %collective-permute-start.21 = (f32[24,4,128]{2,1,0:T(4,128)S(1)}, f32[24,4,128]{2,1,0:T(4,128)S(1)}, u32[]{:S(2)}, u32[]{:S(2)}) collective-permute-start(f32[24,4,128]{2,1,0:T(4,128)S(1)} %slice.67), channel_id=1, source_target_pairs={{28,0},{0,4},{4,8},{8,12},{12,16},{16,20},{24,28},{29,1},{1,5},{5,... | collective-permute-start | bytes 147464 | tf_op jit(solution)/shard_map/ppermute | solution.py:112
  113.5 12.0 %collective-permute-start.22 = (f32[24,16,64]{2,1,0:T(8,128)}, f32[24,16,64]{2,1,0:T(8,128)S(1)}, u32[]{:S(2)}, u32[]{:S(2)}) collective-permute-start(f32[24,16,64]{2,1,0:T(8,128)} %get-tuple-element.28), channel_id=1, source_target_pairs={{1,0},{2,1},{3,2},{0,3},{5,4},{6,5},{7,6},{4,7},{9,8},{10,9},{11,1... | collective-permute-start | bytes 294920 | tf_op jit(solution)/shard_map/ppermute | solution.py:112
  114.3 11.3 %collective-permute-start.23 = (f32[24,16,64]{2,1,0:T(8,128)}, f32[24,16,64]{2,1,0:T(8,128)S(1)}, u32[]{:S(2)}, u32[]{:S(2)}) collective-permute-start(f32[24,16,64]{2,1,0:T(8,128)} %get-tuple-element.29), channel_id=1, source_target_pairs={{3,0},{0,1},{1,2},{2,3},{7,4},{4,5},{5,6},{6,7},{11,8},{8,9},{9,10... | collective-permute-start | bytes 294920 | tf_op jit(solution)/shard_map/ppermute | solution.py:112
  114.3 6.6 %collective-permute-start.24 = (f32[24,4,128]{2,1,0:T(4,128)}, f32[24,4,128]{2,1,0:T(4,128)S(1)}, u32[]{:S(2)}, u32[]{:S(2)}) collective-permute-start(f32[24,4,128]{2,1,0:T(4,128)} %get-tuple-element.30), channel_id=1, source_target_pairs={{4,0},{8,4},{12,8},{16,12},{20,16},{28,24},{0,28},{5,1},{9,5},{13,... | collective-permute-start | bytes 147464 | tf_op jit(solution)/shard_map/ppermute | solution.py:112
  116.2 9.3 %collective-permute-start.25 = (f32[24,4,128]{2,1,0:T(4,128)}, f32[24,4,128]{2,1,0:T(4,128)S(1)}, u32[]{:S(2)}, u32[]{:S(2)}) collective-permute-start(f32[24,4,128]{2,1,0:T(4,128)} %get-tuple-element.31), channel_id=1, source_target_pairs={{28,0},{0,4},{4,8},{8,12},{12,16},{16,20},{24,28},{29,1},{1,5},{5,... | collective-permute-start | bytes 147464 | tf_op jit(solution)/shard_map/ppermute | solution.py:112
  (33 other events, 130.6 us)

commit v5 on v4

--- a/solution.py
+++ b/solution.py
@@ -186,14 +186,18 @@
     scratch[:, pl.ds(start, 4, stride=stride), :] = value
 
 
-def pass_kernel(*refs, first, residual_only, present, faces):
+def pass_kernel(*refs, first, residual_only, present, faces, link_mode, append_links, emit_back):
     refs = list(refs)
+    width = 24
+    ghost_dirs = [d for d in (1, 2, 3) if link_mode == "combined" and present["behind"][d]]
+    link_face_scratch = refs.pop() if append_links and "z_high" in faces else None
     ghost_scratch = {}
-    for direction in reversed([d for d in (1, 2, 3) if present["ghost"][d]]):
+    for direction in reversed(ghost_dirs):
         ghost_scratch[direction] = refs.pop()
     scratch_refs = {}
     for key in reversed([k for k in HALO_KEYS if present[k[0]][k[1]]]):
         scratch_refs[key] = refs.pop()
+    back_out_ref = refs.pop() if emit_back else None
     face_refs = {}
     for name in reversed(faces):
         face_refs[name] = refs.pop()
@@ -204,10 +208,7 @@
 
     src_ref = take()
     links_ref = take()
-    ghost_refs = [None, None, None, None]
-    for direction in (1, 2, 3):
-        if present["ghost"][direction]:
-            ghost_refs[direction] = take()
+    back_ref = take() if link_mode == "given" else None
     labels_ref = take()
     member_ref = take()
     cmask_ref = None if residual_only else take()
@@ -215,10 +216,9 @@
     halo_refs = {}
     if not first:
         spinor_ref = take()
-        for direction in (1, 2, 3):
-            for side in ("ahead", "behind"):
-                if present[side][direction]:
-                    halo_refs[(side, direction)] = take()
+        for key in HALO_KEYS:
+            if present[key[0]][key[1]]:
+                halo_refs[key] = take()
 
     rows, lanes = src_ref.shape[-2], src_ref.shape[-1]
     sh = Shifts(rows, lanes)
@@ -226,16 +226,26 @@
     source = src_ref[...].reshape(shape)
     link_all = links_ref[...].astype(jnp.float32)
     links = [link_all[d].reshape(2, 3, 3, rows, lanes) for d in range(4)]
-    back_links = []
-    for direction in range(4):
-        ghost = None
-        if ghost_refs[direction] is not None:
-            place(ghost_scratch[direction], ghost_refs[direction][...].astype(jnp.float32), "behind", direction)
-            ghost = ghost_scratch[direction][...].reshape(2, 3, 3, rows, lanes)
-        back_links.append(sh.behind(direction, links[direction], ghost, True))
+    if back_ref is not None:
+        back_all = back_ref[...].astype(jnp.float32)
+        back_links = [back_all[d].reshape(2, 3, 3, rows, lanes) for d in range(4)]
+    else:
+        back_links = []
+        for direction in range(4):
+            ghost = None
+            if direction in ghost_scratch:
+                halo = halo_refs[("behind", direction)]
+                place(ghost_scratch[direction], halo[width:], "behind", direction)
+                ghost = ghost_scratch[direction][...].reshape(2, 3, 3, rows, lanes)
+            back_links.append(sh.behind(direction, links[direction], ghost, True))
+    if back_out_ref is not None:
+        for direction in range(4):
+            back_out_ref[direction] = back_links[direction].reshape(18, rows, lanes).astype(back_out_ref.dtype)
 
     for key, scratch in scratch_refs.items():
-        place(scratch, halo_refs[key][...], key[0], key[1])
+        halo = halo_refs[key]
+        value = halo[:width] if (key[0] == "behind" and key[1] in ghost_scratch) else halo[...]
+        place(scratch, value, key[0], key[1])
 
     def load_halo(side, direction):
         ref = scratch_refs.get((side, direction), halo_refs.get((side, direction)))
@@ -287,48 +297,63 @@
     update = update * cmask_ref[...]
     result = update if current is None else current + update
     out_ref[...] = result.reshape(out_ref.shape)
+    if link_face_scratch is not None:
+        link_face_scratch[...] = link_all[2]
     for name, face_ref in face_refs.items():
         if name == "y_low":
             face_ref[...] = out_ref[:, :, pl.ds(0, lanes // 2)]
         elif name == "y_high":
-            face_ref[...] = pltpu.roll(out_ref[...], lanes // 2, 2)[:, :, : lanes // 2]
+            face_ref[0:width] = pltpu.roll(out_ref[...], lanes // 2, 2)[:, :, : lanes // 2]
+            if append_links:
+                face_ref[width:] = pltpu.roll(link_all[1], lanes // 2, 2)[:, :, : lanes // 2]
         else:
             start, stride = face_rows(name)
-            face_ref[...] = out_ref[:, pl.ds(start, 4, stride=stride), :]
-
-
-def run_pass(source, links, ghosts, labels, member, cmask, spinor, halos, residual_only=False, faces=()):
+            face_ref[0:width] = out_ref[:, pl.ds(start, 4, stride=stride), :]
+            if append_links and name == "z_high":
+                face_ref[width:] = link_face_scratch[:, pl.ds(start, 4, stride=stride), :]
+            elif append_links and name == "t_high":
+                face_ref[width:] = link_all[3][:, start:start + 4, :]
+
+
+def run_pass(source, links, back, labels, member, cmask, spinor, halos, residual_only=False, faces=(),
+             link_mode="given", append_links=False, emit_back=False):
     first = spinor is None
-    if first:
-        ghosts = [None, None, None, None]
     present = {
-        "ghost": [g is not None for g in ghosts],
         "ahead": [h is not None for h in halos["ahead"]] if not first else [False] * 4,
         "behind": [h is not None for h in halos["behind"]] if not first else [False] * 4,
     }
-    operands = [source, links] + [g for g in ghosts[1:] if g is not None] + [labels, member]
+    operands = [source, links] + ([back] if link_mode == "given" else []) + [labels, member]
     if not residual_only:
         operands.append(cmask)
     if not first:
         operands.append(spinor)
-        for direction in (1, 2, 3):
-            for side in ("ahead", "behind"):
-                if present[side][direction]:
-                    operands.append(halos[side][direction])
+        for key in HALO_KEYS:
+            if present[key[0]][key[1]]:
+                operands.append(halos[key[0]][key[1]])
     kernel = functools.partial(
-        pass_kernel, first=first, residual_only=residual_only, present=present, faces=faces
-    )
+        pass_kernel, first=first, residual_only=residual_only, present=present, faces=faces,
+        link_mode=link_mode, append_links=append_links, emit_back=emit_back,
+    )
+    width = source.shape[0]
+
     def face_shape(name):
+        rows = width + (18 if append_links and name.endswith("high") else 0)
         if name.startswith("y"):
-            return (source.shape[0], source.shape[1], source.shape[2] // 2)
-        return (source.shape[0], 4, source.shape[2])
+            return (rows, source.shape[1], source.shape[2] // 2)
+        return (rows, 4, source.shape[2])
 
     out_shape = [jax.ShapeDtypeStruct(source.shape, jnp.float32)]
     out_shape += [jax.ShapeDtypeStruct(face_shape(name), jnp.float32) for name in faces]
+    if emit_back:
+        out_shape.append(jax.ShapeDtypeStruct(links.shape, links.dtype))
     scratch = [pltpu.VMEM(source.shape, jnp.float32) for k in HALO_KEYS if present[k[0]][k[1]]]
-    scratch += [pltpu.VMEM(links.shape[1:], jnp.float32) for d in (1, 2, 3) if present["ghost"][d]]
+    if link_mode == "combined":
+        scratch += [pltpu.VMEM(links.shape[1:], jnp.float32) for d in (1, 2, 3) if present["behind"][d]]
+    if append_links and "z_high" in faces:
+        scratch.append(pltpu.VMEM(links.shape[1:], jnp.float32))
     results = pl.pallas_call(kernel, out_shape=out_shape, scratch_shapes=scratch)(*operands)
-    return results[0], dict(zip(faces, results[1:]))
+    face_values = dict(zip(faces, results[1:1 + len(faces)]))
+    return results[0], face_values, (results[-1] if emit_back else None)
 
 
 def coarse_kernel(*refs, present):
@@ -451,12 +476,6 @@
         return i - PZ >= 0
 
     half = line_extent // 2
-    ghosts = [
-        None,
-        permute_from(link_rows[1][..., half:], "grp", -1, lambda i: True),
-        permute_from(lax.slice_in_dim(link_rows[2], 3, 16, 4, axis=1), "lat", -1, z_down_ok),
-        permute_from(lax.slice_in_dim(link_rows[3], 12, 16, 1, axis=1), "lat", -PZ, t_down_ok),
-    ]
 
     needed = ["y_low", "y_high"] + [
         name for name, ok in zip(FACES[2:], (z_up_ok, z_down_ok, t_up_ok, t_down_ok))
@@ -489,20 +508,28 @@
             ],
         }
 
-    def smoother_pass(spinor, faces, colour_pass, out_faces):
-        halos = None if spinor is None else halos_of(spinor, faces)
-        return run_pass(
-            source, link_rows, ghosts, labels, member, colour_masks[colour_pass], spinor, halos,
-            faces=out_faces,
+    smoothed_first, first_faces, _ = run_pass(
+        source, link_rows, None, labels, member, colour_masks[0], None, None,
+        faces=tuple(needed), link_mode="none", append_links=True,
+    )
+    smoothed, smoothed_faces, back_rows = run_pass(
+        source, link_rows, None, labels, member, colour_masks[1], smoothed_first,
+        halos_of(smoothed_first, first_faces), faces=tuple(needed), link_mode="combined", emit_back=True,
+    )
+
+    def sweep(start, faces):
+        current, current_faces, _ = run_pass(
+            source, link_rows, back_rows, labels, member, colour_masks[0], start, halos_of(start, faces),
+            faces=tuple(needed),
         )
-
-    def sweep(start, faces, last_faces):
-        current, current_faces = smoother_pass(start, faces, 0, tuple(needed))
-        return smoother_pass(current, current_faces, 1, last_faces)
-
-    smoothed, smoothed_faces = sweep(None, None, tuple(needed))
-    residue, _ = run_pass(
-        source, link_rows, ghosts, labels, member, None, smoothed, halos_of(smoothed, smoothed_faces),
+        result, _, _ = run_pass(
+            source, link_rows, back_rows, labels, member, colour_masks[1], current,
+            halos_of(current, current_faces),
+        )
+        return result
+
+    residue, _, _ = run_pass(
+        source, link_rows, back_rows, labels, member, None, smoothed, halos_of(smoothed, smoothed_faces),
         residual_only=True,
     )
     residual = residue.astype(jnp.bfloat16)
@@ -540,7 +567,7 @@
     real_part = jnp.sum(vectors[:, 0] * spread_real - vectors[:, 1] * spread_imag, axis=0)
     imag_part = jnp.sum(vectors[:, 0] * spread_imag + vectors[:, 1] * spread_real, axis=0)
     corrected = smoothed + jnp.stack([real_part, imag_part]).reshape(24, rows, line_extent)
-    solution, _ = sweep(corrected, faces_of(corrected), ())
+    solution = sweep(corrected, faces_of(corrected))
     return (
         solution.reshape(1, 24, time_extent, plane_extent, line_extent),
         correction.reshape(1, 1, 2, CDOF, AGG),

time: 132 us -> 128 us (0.970)
  waiting for transfers between devices: 26.3 us -> 21.6 us
    ppermute x26 -> x24, waiting for transfers between devices: 26.3 us -> 21.6 us  [permute_from(): return lax.ppermute(value, axis, pairs)]
    ppermute x26 -> x24, starting transfers between devices: 47.8 us -> 48.7 us  [permute_from(): return lax.ppermute(value, axis, pairs)]
    unnamed x65 -> x61, local copies, waits for them, and re-layouts: 8.89 us -> 9.03 us
  transfers between devices with their start and end apart: 26 -> 24, of which waited for: 7 -> 7; matrix products, arithmetic and copies ran while one was open for 7% -> 7% of each run, Pallas kernels for 0% -> 0%
where the time goes in v5:
time: 128 us; the launch traced here: 127 us
  starting transfers between devices  48.7 us (38%)
  Pallas kernels  30.4 us (24%)
  waiting for transfers between devices  21.6 us (17%)
  local copies, waits for them, and re-layouts  15.7 us (12%)
  other arithmetic  5.59 us (4%)
  matrix products  3.41 us (3%)
    ppermute x24, starting transfers between devices, permute_from(): return lax.ppermute(value, axis, pairs)  48.7 us
    pallas_call x5, Pallas kernels, run_pass(): pl.pallas_call(kernel, out_shape=out_shape, scratch_shapes=scratch)  22.7 us
    ppermute x24, waiting for transfers between devices, permute_from(): return lax.ppermute(value, axis, pairs)  21.6 us
    unnamed x61, local copies, waits for them, and re-layouts  9.03 us
    pallas_call x3, Pallas kernels, run_coarse(): pl.pallas_call(kernel, out_shape=jax.ShapeDtypeStruct(source.shape, jnp.f...  7.76 us
    reshape x1, local copies, waits for them, and re-layouts, body(): vectors = test_vectors.reshape(NVEC, 2, 2, 6, site_count)  4.03 us
    dot_general x4, matrix products, contract(): jnp.einsum('kxqn,xqnj->xkj', left, right, preferred_element_type=jnp.floa...  2.97 us
  transfers between devices with their start and end apart: 24, of which 7 were waited for; matrix products, arithmetic and copies ran while one was open for 7% of the time, Pallas kernels for 0%

profile of v5, /device:TPU:0, one launch (start us, length us, event | category | flops | bytes accessed | tf_op | source)
XLA Modules:
  0.0 126.7 jit_solution(5650545173983363362)
XLA Ops:
  4.2 4.2 %shard_map.86 = (f32[24,16,128]{2,1,0:T(8,128)}, f32[24,16,64]{2,1,0:T(8,128)}, f32[42,16,64]{2,1,0:T(8,128)}, f32[24,4,128]{2,1,0:T(4,128)}, f32[42,4,128]{2,1,0:T(4,128)}) custom-call(f32[24,16,128]{2,1,0:T(8,128)} %bitcast.75, bf16[4,18,16,128]{3,2,1,0:T(8,128)(2,1)} %bitcast.68, f32[16,128]{1,0:T(8,128)} %add_convert_fusion.refs_2_.refs_3_, ...), custom_call_target="tpu_custom_call" | custom-call | tf_op jit(solution)/shard_map/pallas_call | solution.py:354
  8.9 1.9 %collective-permute-start = (f32[24,16,64]{2,1,0:T(8,128)}, f32[24,16,64]{2,1,0:T(8,128)S(1)}, u32[]{:S(2)}, u32[]{:S(2)}) collective-permute-start(f32[24,16,64]{2,1,0:T(8,128)} %get-tuple-element.19), channel_id=1, source_target_pairs={{1,0},{2,1},{3,2},{0,3},{5,4},{6,5},{7,6},{4,7},{9,8},{10,9},{11,1... | collective-permute-start | bytes 294920 | tf_op jit(solution)/shard_map/ppermute | solution.py:112
  10.9 4.2 %collective-permute-start.3 = (f32[42,4,128]{2,1,0:T(4,128)}, f32[42,4,128]{2,1,0:T(4,128)S(1)}, u32[]{:S(2)}, u32[]{:S(2)}) collective-permute-start(f32[42,4,128]{2,1,0:T(4,128)} %get-tuple-element.22), channel_id=1, source_target_pairs={{28,0},{0,4},{4,8},{8,12},{12,16},{16,20},{24,28},{29,1},{1,5},{5,... | collective-permute-start | bytes 258056 | tf_op jit(solution)/shard_map/ppermute | solution.py:112
  15.1 5.0 %collective-permute-start.2 = (f32[24,4,128]{2,1,0:T(4,128)}, f32[24,4,128]{2,1,0:T(4,128)S(1)}, u32[]{:S(2)}, u32[]{:S(2)}) collective-permute-start(f32[24,4,128]{2,1,0:T(4,128)} %get-tuple-element.21), channel_id=1, source_target_pairs={{4,0},{8,4},{12,8},{16,12},{20,16},{28,24},{0,28},{5,1},{9,5},{13,... | collective-permute-start | bytes 147464 | tf_op jit(solution)/shard_map/ppermute | solution.py:112
  23.0 5.4 %shard_map.87 = (f32[24,16,128]{2,1,0:T(8,128)}, f32[24,16,64]{2,1,0:T(8,128)}, f32[24,16,64]{2,1,0:T(8,128)}, f32[24,4,128]{2,1,0:T(4,128)}, f32[24,4,128]{2,1,0:T(4,128)}, /*index=5*/bf16[4,18,16,128]{3,2,1,0:T(8,128)(2,1)}) custom-call(f32[24,16,128]{2,1,0:T(8,128)} %bitcast.76, bf16[4,18,16,128]{3,2,1,0:T(8,128)(2,1)} %bitcast.69, ...), custom_call_target="tpu_custom_call" | custom-call | tf_op jit(solution)/shard_map/pallas_call | solution.py:354
  28.9 6.8 %collective-permute-start.6 = (f32[24,4,128]{2,1,0:T(4,128)}, f32[24,4,128]{2,1,0:T(4,128)S(1)}, u32[]{:S(2)}, u32[]{:S(2)}) collective-permute-start(f32[24,4,128]{2,1,0:T(4,128)} %get-tuple-element.27), channel_id=1, source_target_pairs={{4,0},{8,4},{12,8},{16,12},{20,16},{28,24},{0,28},{5,1},{9,5},{13,... | collective-permute-start | bytes 147464 | tf_op jit(solution)/shard_map/ppermute | solution.py:112
  35.7 1.9 %collective-permute-start.7 = (f32[24,4,128]{2,1,0:T(4,128)}, f32[24,4,128]{2,1,0:T(4,128)S(1)}, u32[]{:S(2)}, u32[]{:S(2)}) collective-permute-start(f32[24,4,128]{2,1,0:T(4,128)} %get-tuple-element.28), channel_id=1, source_target_pairs={{28,0},{0,4},{4,8},{8,12},{12,16},{16,20},{24,28},{29,1},{1,5},{5,... | collective-permute-start | bytes 147464 | tf_op jit(solution)/shard_map/ppermute | solution.py:112
  37.6 2.7 %copy.13 = bf16[1,24,24,4,4,128]{5,4,3,1,2,0:T(4,128)(2,1)} copy(bf16[1,24,24,4,4,128]{5,4,3,2,1,0:T(4,128)(2,1)S(1)} %copy-done.1) | data formatting | bytes 4718592 | tf_op args[2]
  40.3 4.0 %reshape.71 = bf16[24,2,2,6,2048]{4,0,3,2,1:T(8,128)(2,1)S(1)} reshape(bf16[1,24,24,4,4,128]{5,4,3,1,2,0:T(4,128)(2,1)} %copy.13) | data formatting | bytes 4718592 | tf_op jit(solution)/shard_map/reshape | solution.py:539
  45.8 2.9 %shard_map.88 = f32[24,16,128]{2,1,0:T(8,128)} custom-call(f32[24,16,128]{2,1,0:T(8,128)} %bitcast.77, bf16[4,18,16,128]{3,2,1,0:T(8,128)(2,1)} %bitcast.70, bf16[4,18,16,128]{3,2,1,0:T(8,128)(2,1)} %get-tuple-element.23.refs_2_, f32[16,128]{1,0:T(8,128)} %add_convert_fusion.refs_2_.refs_3_, f32[16,16,128]{2,1,0:T(8,128)} %fusion.8.refs_3_.refs_4_, ...), custom_call_target="tpu_custom_call" | custom-call | tf_op jit(solution)/shard_map/pallas_call | solution.py:354
  56.4 6.2 %collective-permute-start.10 = (f32[2,1,768]{2,1,0:T(1,128)}, f32[2,1,768]{2,1,0:T(1,128)S(1)}, u32[]{:S(2)}, u32[]{:S(2)}) collective-permute-start(f32[2,1,768]{2,1,0:T(1,128)} %shard_map.89.refs_3_), channel_id=1, source_target_pairs={{4,0},{8,4},{12,8},{16,12},{20,16},{28,24},{0,28},{5,1},{9,5},{13,... | collective-permute-start | bytes 18440 | tf_op jit(solution)/shard_map/ppermute | solution.py:112
  62.5 1.9 %collective-permute-start.11 = (f32[2,1,768]{2,1,0:T(1,128)}, f32[2,1,768]{2,1,0:T(1,128)S(1)}, u32[]{:S(2)}, u32[]{:S(2)}) collective-permute-start(f32[2,1,768]{2,1,0:T(1,128)} %shard_map.89.refs_3_), channel_id=1, source_target_pairs={{28,0},{0,4},{4,8},{8,12},{12,16},{16,20},{24,28},{29,1},{1,5},{5,... | collective-permute-start | bytes 18440 | tf_op jit(solution)/shard_map/ppermute | solution.py:112
  64.5 6.4 %collective-permute-done.11.refs_7_ = f32[2,1,768]{2,1,0:T(1,128)S(1)} collective-permute-done((f32[2,1,768]{2,1,0:T(1,128)}, f32[2,1,768]{2,1,0:T(1,128)S(1)}, u32[]{:S(2)}, u32[]{:S(2)}) %collective-permute-start.11) | collective-permute-done | bytes 6176 | tf_op jit(solution)/shard_map/ppermute | solution.py:112
  71.6 3.0 %shard_map.90.refs_3_ = f32[2,1,768]{2,1,0:T(1,128)} custom-call(f32[2,1,768]{2,1,0:T(1,128)} %copy-done.13, bf16[2,48,768]{2,1,0:T(8,128)(2,1)} %bitcast.83, bf16[9,2,48,768]{3,2,1,0:T(8,128)(2,1)} %bitcast.73, f32[2,1,768]{2,1,0:T(1,128)} %shard_map.89.refs_3_, f32[2,1,768]{2,1,0:T(1,128)} %copy-done.22, f32[2,1,768]{2,1,0:T(1,128)} %copy-done.24, ...), custom_call_target="tpu_custom_call" | custom-call | tf_op jit(solution)/shard_map/pallas_call | solution.py:437
  77.0 4.1 %collective-permute-start.15 = (f32[2,1,768]{2,1,0:T(1,128)}, f32[2,1,768]{2,1,0:T(1,128)S(1)}, u32[]{:S(2)}, u32[]{:S(2)}) collective-permute-start(f32[2,1,768]{2,1,0:T(1,128)} %shard_map.90.refs_3_), channel_id=1, source_target_pairs={{28,0},{0,4},{4,8},{8,12},{12,16},{16,20},{24,28},{29,1},{1,5},{5,... | collective-permute-start | bytes 18440 | tf_op jit(solution)/shard_map/ppermute | solution.py:112
  81.1 4.3 %collective-permute-done.15.refs_7_ = f32[2,1,768]{2,1,0:T(1,128)S(1)} collective-permute-done((f32[2,1,768]{2,1,0:T(1,128)}, f32[2,1,768]{2,1,0:T(1,128)S(1)}, u32[]{:S(2)}, u32[]{:S(2)}) %collective-permute-start.15) | collective-permute-done | bytes 6176 | tf_op jit(solution)/shard_map/ppermute | solution.py:112
  86.0 3.0 %shard_map.91 = f32[2,1,768]{2,1,0:T(1,128)} custom-call(f32[2,1,768]{2,1,0:T(1,128)} %copy-done.13, bf16[2,48,768]{2,1,0:T(8,128)(2,1)} %bitcast.84, bf16[9,2,48,768]{3,2,1,0:T(8,128)(2,1)} %bitcast.74, f32[2,1,768]{2,1,0:T(1,128)} %shard_map.90.refs_3_, f32[2,1,768]{2,1,0:T(1,128)} %copy-done.21, f32[2,1,768]{2,1,0:T(1,128)} %copy-done.23, ...), custom_call_target="tpu_custom_call" | custom-call | tf_op jit(solution)/shard_map/pallas_call | solution.py:437
  92.4 1.9 %collective-permute-start.18 = (f32[24,4,128]{2,1,0:T(4,128)S(1)}, f32[24,4,128]{2,1,0:T(4,128)S(1)}, u32[]{:S(2)}, u32[]{:S(2)}) collective-permute-start(f32[24,4,128]{2,1,0:T(4,128)S(1)} %slice.48), channel_id=1, source_target_pairs={{4,0},{8,4},{12,8},{16,12},{20,16},{28,24},{0,28},{5,1},{9,5},{13,... | collective-permute-start | bytes 147464 | tf_op jit(solution)/shard_map/ppermute | solution.py:112
  94.3 3.9 %collective-permute-start.19 = (f32[24,4,128]{2,1,0:T(4,128)S(1)}, f32[24,4,128]{2,1,0:T(4,128)S(1)}, u32[]{:S(2)}, u32[]{:S(2)}) collective-permute-start(f32[24,4,128]{2,1,0:T(4,128)S(1)} %slice.49), channel_id=1, source_target_pairs={{28,0},{0,4},{4,8},{8,12},{12,16},{16,20},{24,28},{29,1},{1,5},{5,... | collective-permute-start | bytes 147464 | tf_op jit(solution)/shard_map/ppermute | solution.py:112
  98.3 4.6 %collective-permute-done.19.refs_10_ = f32[24,4,128]{2,1,0:T(4,128)S(1)} collective-permute-done((f32[24,4,128]{2,1,0:T(4,128)S(1)}, f32[24,4,128]{2,1,0:T(4,128)S(1)}, u32[]{:S(2)}, u32[]{:S(2)}) %collective-permute-start.19) | collective-permute-done | bytes 49184 | tf_op jit(solution)/shard_map/ppermute | solution.py:112
  104.3 5.2 %shard_map.92 = (f32[24,16,128]{2,1,0:T(8,128)}, f32[24,16,64]{2,1,0:T(8,128)}, f32[24,16,64]{2,1,0:T(8,128)}, f32[24,4,128]{2,1,0:T(4,128)}, f32[24,4,128]{2,1,0:T(4,128)}) custom-call(f32[24,16,128]{2,1,0:T(8,128)} %bitcast.78, bf16[4,18,16,128]{3,2,1,0:T(8,128)(2,1)} %bitcast.71, bf16[4,18,16,128]{3,2,1,0:T(8,128)(2,1)} %get-tuple-element.23.refs_2_, ...), custom_call_target="tpu_custom_call" | custom-call | tf_op jit(solution)/shard_map/pallas_call | solution.py:354
  112.0 3.9 %collective-permute-start.23 = (f32[24,4,128]{2,1,0:T(4,128)}, f32[24,4,128]{2,1,0:T(4,128)S(1)}, u32[]{:S(2)}, u32[]{:S(2)}) collective-permute-start(f32[24,4,128]{2,1,0:T(4,128)} %get-tuple-element.33), channel_id=1, source_target_pairs={{28,0},{0,4},{4,8},{8,12},{12,16},{16,20},{24,28},{29,1},{1,5},{5,... | collective-permute-start | bytes 147464 | tf_op jit(solution)/shard_map/ppermute | solution.py:112
  116.7 4.2 %collective-permute-done.23.refs_10_ = f32[24,4,128]{2,1,0:T(4,128)S(1)} collective-permute-done((f32[24,4,128]{2,1,0:T(4,128)}, f32[24,4,128]{2,1,0:T(4,128)S(1)}, u32[]{:S(2)}, u32[]{:S(2)}) %collective-permute-start.23) | collective-permute-done | bytes 49184 | tf_op jit(solution)/shard_map/ppermute | solution.py:112
  121.7 5.0 %shard_map.93 = f32[24,16,128]{2,1,0:T(8,128)} custom-call(f32[24,16,128]{2,1,0:T(8,128)} %bitcast.79, bf16[4,18,16,128]{3,2,1,0:T(8,128)(2,1)} %bitcast.72, bf16[4,18,16,128]{3,2,1,0:T(8,128)(2,1)} %get-tuple-element.23.refs_2_, f32[16,128]{1,0:T(8,128)} %add_convert_fusion.refs_2_.refs_3_, f32[16,16,128]{2,1,0:T(8,128)} %fusion.8.refs_3_.refs_4_, ...), custom_call_target="tpu_custom_call" | custom-call | tf_op jit(solution)/shard_map/pallas_call | solution.py:354
  (125 shorter events, 28.9 us)
Async XLA Ops:
  8.5 13.7 %collective-permute-start.1 = (f32[42,16,64]{2,1,0:T(8,128)}, f32[42,16,64]{2,1,0:T(8,128)S(1)}, u32[]{:S(2)}, u32[]{:S(2)}) collective-permute-start(f32[42,16,64]{2,1,0:T(8,128)} %get-tuple-element.20), channel_id=1, source_target_pairs={{3,0},{0,1},{1,2},{2,3},{7,4},{4,5},{5,6},{6,7},{11,8},{8,9},{9,10... | collective-permute-start | bytes 516104 | tf_op jit(solution)/shard_map/ppermute | solution.py:112
  8.9 13.2 %collective-permute-start = (f32[24,16,64]{2,1,0:T(8,128)}, f32[24,16,64]{2,1,0:T(8,128)S(1)}, u32[]{:S(2)}, u32[]{:S(2)}) collective-permute-start(f32[24,16,64]{2,1,0:T(8,128)} %get-tuple-element.19), channel_id=1, source_target_pairs={{1,0},{2,1},{3,2},{0,3},{5,4},{6,5},{7,6},{4,7},{9,8},{10,9},{11,1... | collective-permute-start | bytes 294920 | tf_op jit(solution)/shard_map/ppermute | solution.py:112
  10.9 11.3 %collective-permute-start.3 = (f32[42,4,128]{2,1,0:T(4,128)}, f32[42,4,128]{2,1,0:T(4,128)S(1)}, u32[]{:S(2)}, u32[]{:S(2)}) collective-permute-start(f32[42,4,128]{2,1,0:T(4,128)} %get-tuple-element.22), channel_id=1, source_target_pairs={{28,0},{0,4},{4,8},{8,12},{12,16},{16,20},{24,28},{29,1},{1,5},{5,... | collective-permute-start | bytes 258056 | tf_op jit(solution)/shard_map/ppermute | solution.py:112
  15.1 7.0 %collective-permute-start.2 = (f32[24,4,128]{2,1,0:T(4,128)}, f32[24,4,128]{2,1,0:T(4,128)S(1)}, u32[]{:S(2)}, u32[]{:S(2)}) collective-permute-start(f32[24,4,128]{2,1,0:T(4,128)} %get-tuple-element.21), channel_id=1, source_target_pairs={{4,0},{8,4},{12,8},{16,12},{20,16},{28,24},{0,28},{5,1},{9,5},{13,... | collective-permute-start | bytes 147464 | tf_op jit(solution)/shard_map/ppermute | solution.py:112
  28.3 16.7 %collective-permute-start.4 = (f32[24,16,64]{2,1,0:T(8,128)}, f32[24,16,64]{2,1,0:T(8,128)S(1)}, u32[]{:S(2)}, u32[]{:S(2)}) collective-permute-start(f32[24,16,64]{2,1,0:T(8,128)} %get-tuple-element.25), channel_id=1, source_target_pairs={{1,0},{2,1},{3,2},{0,3},{5,4},{6,5},{7,6},{4,7},{9,8},{10,9},{11,1... | collective-permute-start | bytes 294920 | tf_op jit(solution)/shard_map/ppermute | solution.py:112
  28.3 16.7 %collective-permute-start.5 = (f32[24,16,64]{2,1,0:T(8,128)}, f32[24,16,64]{2,1,0:T(8,128)S(1)}, u32[]{:S(2)}, u32[]{:S(2)}) collective-permute-start(f32[24,16,64]{2,1,0:T(8,128)} %get-tuple-element.26), channel_id=1, source_target_pairs={{3,0},{0,1},{1,2},{2,3},{7,4},{4,5},{5,6},{6,7},{11,8},{8,9},{9,10... | collective-permute-start | bytes 294920 | tf_op jit(solution)/shard_map/ppermute | solution.py:112
  28.9 15.5 %collective-permute-start.6 = (f32[24,4,128]{2,1,0:T(4,128)}, f32[24,4,128]{2,1,0:T(4,128)S(1)}, u32[]{:S(2)}, u32[]{:S(2)}) collective-permute-start(f32[24,4,128]{2,1,0:T(4,128)} %get-tuple-element.27), channel_id=1, source_target_pairs={{4,0},{8,4},{12,8},{16,12},{20,16},{28,24},{0,28},{5,1},{9,5},{13,... | collective-permute-start | bytes 147464 | tf_op jit(solution)/shard_map/ppermute | solution.py:112
  35.7 9.4 %collective-permute-start.7 = (f32[24,4,128]{2,1,0:T(4,128)}, f32[24,4,128]{2,1,0:T(4,128)S(1)}, u32[]{:S(2)}, u32[]{:S(2)}) collective-permute-start(f32[24,4,128]{2,1,0:T(4,128)} %get-tuple-element.28), channel_id=1, source_target_pairs={{28,0},{0,4},{4,8},{8,12},{12,16},{16,20},{24,28},{29,1},{1,5},{5,... | collective-permute-start | bytes 147464 | tf_op jit(solution)/shard_map/ppermute | solution.py:112
  55.9 8.6 %collective-permute-start.8 = (f32[2,1,768]{2,1,0:T(1,128)}, f32[2,1,768]{2,1,0:T(1,128)S(1)}, u32[]{:S(2)}, u32[]{:S(2)}) collective-permute-start(f32[2,1,768]{2,1,0:T(1,128)} %shard_map.89.refs_3_), channel_id=1, source_target_pairs={{1,0},{2,1},{3,2},{0,3},{5,4},{6,5},{7,6},{4,7},{9,8},{10,9},{11,1... | collective-permute-start | bytes 18440 | tf_op jit(solution)/shard_map/ppermute | solution.py:112
  56.2 8.3 %collective-permute-start.9 = (f32[2,1,768]{2,1,0:T(1,128)}, f32[2,1,768]{2,1,0:T(1,128)S(1)}, u32[]{:S(2)}, u32[]{:S(2)}) collective-permute-start(f32[2,1,768]{2,1,0:T(1,128)} %shard_map.89.refs_3_), channel_id=1, source_target_pairs={{3,0},{0,1},{1,2},{2,3},{7,4},{4,5},{5,6},{6,7},{11,8},{8,9},{9,10... | collective-permute-start | bytes 18440 | tf_op jit(solution)/shard_map/ppermute | solution.py:112
  56.4 8.2 %collective-permute-start.10 = (f32[2,1,768]{2,1,0:T(1,128)}, f32[2,1,768]{2,1,0:T(1,128)S(1)}, u32[]{:S(2)}, u32[]{:S(2)}) collective-permute-start(f32[2,1,768]{2,1,0:T(1,128)} %shard_map.89.refs_3_), channel_id=1, source_target_pairs={{4,0},{8,4},{12,8},{16,12},{20,16},{28,24},{0,28},{5,1},{9,5},{13,... | collective-permute-start | bytes 18440 | tf_op jit(solution)/shard_map/ppermute | solution.py:112
  62.5 8.4 %collective-permute-start.11 = (f32[2,1,768]{2,1,0:T(1,128)}, f32[2,1,768]{2,1,0:T(1,128)S(1)}, u32[]{:S(2)}, u32[]{:S(2)}) collective-permute-start(f32[2,1,768]{2,1,0:T(1,128)} %shard_map.89.refs_3_), channel_id=1, source_target_pairs={{28,0},{0,4},{4,8},{8,12},{12,16},{16,20},{24,28},{29,1},{1,5},{5,... | collective-permute-start | bytes 18440 | tf_op jit(solution)/shard_map/ppermute | solution.py:112
  74.5 6.5 %collective-permute-start.12 = (f32[2,1,768]{2,1,0:T(1,128)}, f32[2,1,768]{2,1,0:T(1,128)S(1)}, u32[]{:S(2)}, u32[]{:S(2)}) collective-permute-start(f32[2,1,768]{2,1,0:T(1,128)} %shard_map.90.refs_3_), channel_id=1, source_target_pairs={{1,0},{2,1},{3,2},{0,3},{5,4},{6,5},{7,6},{4,7},{9,8},{10,9},{11,1... | collective-permute-start | bytes 18440 | tf_op jit(solution)/shard_map/ppermute | solution.py:112
  74.9 6.3 %collective-permute-start.13 = (f32[2,1,768]{2,1,0:T(1,128)}, f32[2,1,768]{2,1,0:T(1,128)S(1)}, u32[]{:S(2)}, u32[]{:S(2)}) collective-permute-start(f32[2,1,768]{2,1,0:T(1,128)} %shard_map.90.refs_3_), channel_id=1, source_target_pairs={{3,0},{0,1},{1,2},{2,3},{7,4},{4,5},{5,6},{6,7},{11,8},{8,9},{9,10... | collective-permute-start | bytes 18440 | tf_op jit(solution)/shard_map/ppermute | solution.py:112
  75.1 6.1 %collective-permute-start.14 = (f32[2,1,768]{2,1,0:T(1,128)}, f32[2,1,768]{2,1,0:T(1,128)S(1)}, u32[]{:S(2)}, u32[]{:S(2)}) collective-permute-start(f32[2,1,768]{2,1,0:T(1,128)} %shard_map.90.refs_3_), channel_id=1, source_target_pairs={{4,0},{8,4},{12,8},{16,12},{20,16},{28,24},{0,28},{5,1},{9,5},{13,... | collective-permute-start | bytes 18440 | tf_op jit(solution)/shard_map/ppermute | solution.py:112
  77.0 8.4 %collective-permute-start.15 = (f32[2,1,768]{2,1,0:T(1,128)}, f32[2,1,768]{2,1,0:T(1,128)S(1)}, u32[]{:S(2)}, u32[]{:S(2)}) collective-permute-start(f32[2,1,768]{2,1,0:T(1,128)} %shard_map.90.refs_3_), channel_id=1, source_target_pairs={{28,0},{0,4},{4,8},{8,12},{12,16},{16,20},{24,28},{29,1},{1,5},{5,... | collective-permute-start | bytes 18440 | tf_op jit(solution)/shard_map/ppermute | solution.py:112
  91.7 11.3 %collective-permute-start.16 = (f32[24,16,64]{2,1,0:T(8,128)S(1)}, f32[24,16,64]{2,1,0:T(8,128)S(1)}, u32[]{:S(2)}, u32[]{:S(2)}) collective-permute-start(f32[24,16,64]{2,1,0:T(8,128)S(1)} %get-tuple-element.45), channel_id=1, source_target_pairs={{1,0},{2,1},{3,2},{0,3},{5,4},{6,5},{7,6},{4,7},{9,8},{10,9},{11,1... | collective-permute-start | bytes 294920 | tf_op jit(solution)/shard_map/ppermute | solution.py:112
  92.2 10.8 %collective-permute-start.17 = (f32[24,16,64]{2,1,0:T(8,128)S(1)}, f32[24,16,64]{2,1,0:T(8,128)S(1)}, u32[]{:S(2)}, u32[]{:S(2)}) collective-permute-start(f32[24,16,64]{2,1,0:T(8,128)S(1)} %get-tuple-element.44), channel_id=1, source_target_pairs={{3,0},{0,1},{1,2},{2,3},{7,4},{4,5},{5,6},{6,7},{11,8},{8,9},{9,10... | collective-permute-start | bytes 294920 | tf_op jit(solution)/shard_map/ppermute | solution.py:112
  92.4 6.0 %collective-permute-start.18 = (f32[24,4,128]{2,1,0:T(4,128)S(1)}, f32[24,4,128]{2,1,0:T(4,128)S(1)}, u32[]{:S(2)}, u32[]{:S(2)}) collective-permute-start(f32[24,4,128]{2,1,0:T(4,128)S(1)} %slice.48), channel_id=1, source_target_pairs={{4,0},{8,4},{12,8},{16,12},{20,16},{28,24},{0,28},{5,1},{9,5},{13,... | collective-permute-start | bytes 147464 | tf_op jit(solution)/shard_map/ppermute | solution.py:112
  94.3 8.7 %collective-permute-start.19 = (f32[24,4,128]{2,1,0:T(4,128)S(1)}, f32[24,4,128]{2,1,0:T(4,128)S(1)}, u32[]{:S(2)}, u32[]{:S(2)}) collective-permute-start(f32[24,4,128]{2,1,0:T(4,128)S(1)} %slice.49), channel_id=1, source_target_pairs={{28,0},{0,4},{4,8},{8,12},{12,16},{16,20},{24,28},{29,1},{1,5},{5,... | collective-permute-start | bytes 147464 | tf_op jit(solution)/shard_map/ppermute | solution.py:112
  109.5 11.4 %collective-permute-start.20 = (f32[24,16,64]{2,1,0:T(8,128)}, f32[24,16,64]{2,1,0:T(8,128)S(1)}, u32[]{:S(2)}, u32[]{:S(2)}) collective-permute-start(f32[24,16,64]{2,1,0:T(8,128)} %get-tuple-element.30), channel_id=1, source_target_pairs={{1,0},{2,1},{3,2},{0,3},{5,4},{6,5},{7,6},{4,7},{9,8},{10,9},{11,1... | collective-permute-start | bytes 294920 | tf_op jit(solution)/shard_map/ppermute | solution.py:112
  110.0 10.9 %collective-permute-start.21 = (f32[24,16,64]{2,1,0:T(8,128)}, f32[24,16,64]{2,1,0:T(8,128)S(1)}, u32[]{:S(2)}, u32[]{:S(2)}) collective-permute-start(f32[24,16,64]{2,1,0:T(8,128)} %get-tuple-element.31), channel_id=1, source_target_pairs={{3,0},{0,1},{1,2},{2,3},{7,4},{4,5},{5,6},{6,7},{11,8},{8,9},{9,10... | collective-permute-start | bytes 294920 | tf_op jit(solution)/shard_map/ppermute | solution.py:112
  110.1 6.6 %collective-permute-start.22 = (f32[24,4,128]{2,1,0:T(4,128)}, f32[24,4,128]{2,1,0:T(4,128)S(1)}, u32[]{:S(2)}, u32[]{:S(2)}) collective-permute-start(f32[24,4,128]{2,1,0:T(4,128)} %get-tuple-element.32), channel_id=1, source_target_pairs={{4,0},{8,4},{12,8},{16,12},{20,16},{28,24},{0,28},{5,1},{9,5},{13,... | collective-permute-start | bytes 147464 | tf_op jit(solution)/shard_map/ppermute | solution.py:112
  112.0 8.9 %collective-permute-start.23 = (f32[24,4,128]{2,1,0:T(4,128)}, f32[24,4,128]{2,1,0:T(4,128)S(1)}, u32[]{:S(2)}, u32[]{:S(2)}) collective-permute-start(f32[24,4,128]{2,1,0:T(4,128)} %get-tuple-element.33), channel_id=1, source_target_pairs={{28,0},{0,4},{4,8},{8,12},{12,16},{16,20},{24,28},{29,1},{1,5},{5,... | collective-permute-start | bytes 147464 | tf_op jit(solution)/shard_map/ppermute | solution.py:112
  (29 other events, 103.4 us)

commit v6 on v5

--- a/solution.py
+++ b/solution.py
@@ -186,7 +186,7 @@
     scratch[:, pl.ds(start, 4, stride=stride), :] = value
 
 
-def pass_kernel(*refs, first, residual_only, present, faces, link_mode, append_links, emit_back):
+def pass_kernel(*refs, first, residual_only, present, faces, link_mode, append_links, emit_back, colour_pass):
     refs = list(refs)
     width = 24
     ghost_dirs = [d for d in (1, 2, 3) if link_mode == "combined" and present["behind"][d]]
@@ -210,8 +210,7 @@
     links_ref = take()
     back_ref = take() if link_mode == "given" else None
     labels_ref = take()
-    member_ref = take()
-    cmask_ref = None if residual_only else take()
+    colouring_ref = None if residual_only else take()
     spinor_ref = None
     halo_refs = {}
     if not first:
@@ -263,13 +262,19 @@
         current = spinor_ref[...].reshape(shape)
         residue = source - wilson_global(current)
     if residual_only:
-        out_ref[...] = residue.reshape(out_ref.shape)
+        out_ref[...] = residue.reshape(out_ref.shape).astype(out_ref.dtype)
         return
 
-    labels = labels_ref[...]
+    label_index = labels_ref[...]
+    labels = (label_index + 1).astype(jnp.float32)
     ahead_masks = [(sh.ahead(d, labels, None) == labels).astype(jnp.float32) for d in range(4)]
     behind_masks = [(sh.behind(d, labels, None) == labels).astype(jnp.float32) for d in range(4)]
-    member = member_ref[...]
+    member_bool = label_index[None] == lax.broadcasted_iota(jnp.int32, (AGG, 1, 1), 0)
+    member = member_bool.astype(jnp.float32)
+    site_colour = jnp.zeros((rows, lanes), jnp.int32)
+    for block in range(AGG):
+        site_colour = jnp.where(label_index == block, colouring_ref[block], site_colour)
+    colour_mask = (site_colour == colour_pass).astype(jnp.float32)
 
     def wilson_block(spinor):
         ahead_list = [sh.ahead(d, spinor, None) * ahead_masks[d] for d in range(4)]
@@ -294,7 +299,7 @@
         step = complex_scale(factor_real, factor_imag, remainder)
         update = step if update is None else update + step
         remainder = remainder - complex_scale(factor_real, factor_imag, image)
-    update = update * cmask_ref[...]
+    update = update * colour_mask
     result = update if current is None else current + update
     out_ref[...] = result.reshape(out_ref.shape)
     if link_face_scratch is not None:
@@ -315,24 +320,27 @@
                 face_ref[width:] = link_all[3][:, start:start + 4, :]
 
 
-def run_pass(source, links, back, labels, member, cmask, spinor, halos, residual_only=False, faces=(),
+def run_pass(source, links, back, labels, colouring, colour_pass, spinor, halos, residual_only=False, faces=(),
              link_mode="given", append_links=False, emit_back=False):
     first = spinor is None
     present = {
         "ahead": [h is not None for h in halos["ahead"]] if not first else [False] * 4,
         "behind": [h is not None for h in halos["behind"]] if not first else [False] * 4,
     }
-    operands = [source, links] + ([back] if link_mode == "given" else []) + [labels, member]
+    operands = [source, links] + ([back] if link_mode == "given" else []) + [labels]
+    spaces = [pltpu.VMEM] * len(operands)
     if not residual_only:
-        operands.append(cmask)
+        operands.append(colouring)
+        spaces.append(pltpu.SMEM)
     if not first:
         operands.append(spinor)
         for key in HALO_KEYS:
             if present[key[0]][key[1]]:
                 operands.append(halos[key[0]][key[1]])
+    spaces += [pltpu.VMEM] * (len(operands) - len(spaces))
     kernel = functools.partial(
         pass_kernel, first=first, residual_only=residual_only, present=present, faces=faces,
-        link_mode=link_mode, append_links=append_links, emit_back=emit_back,
+        link_mode=link_mode, append_links=append_links, emit_back=emit_back, colour_pass=colour_pass,
     )
     width = source.shape[0]
 
@@ -342,7 +350,7 @@
             return (rows, source.shape[1], source.shape[2] // 2)
         return (rows, 4, source.shape[2])
 
-    out_shape = [jax.ShapeDtypeStruct(source.shape, jnp.float32)]
+    out_shape = [jax.ShapeDtypeStruct(source.shape, jnp.bfloat16 if residual_only else jnp.float32)]
     out_shape += [jax.ShapeDtypeStruct(face_shape(name), jnp.float32) for name in faces]
     if emit_back:
         out_shape.append(jax.ShapeDtypeStruct(links.shape, links.dtype))
@@ -351,7 +359,8 @@
         scratch += [pltpu.VMEM(links.shape[1:], jnp.float32) for d in (1, 2, 3) if present["behind"][d]]
     if append_links and "z_high" in faces:
         scratch.append(pltpu.VMEM(links.shape[1:], jnp.float32))
-    results = pl.pallas_call(kernel, out_shape=out_shape, scratch_shapes=scratch)(*operands)
+    in_specs = [pl.BlockSpec(memory_space=space) for space in spaces]
+    results = pl.pallas_call(kernel, out_shape=out_shape, scratch_shapes=scratch, in_specs=in_specs)(*operands)
     face_values = dict(zip(faces, results[1:1 + len(faces)]))
     return results[0], face_values, (results[-1] if emit_back else None)
 
@@ -458,10 +467,6 @@
     label_rows = aggregate_map.reshape(rows, line_extent)
     member = (label_rows[None] == jnp.arange(AGG, dtype=jnp.int32)[:, None, None]).astype(jnp.float32)
     colour_list = colouring.reshape(AGG)
-    colour_masks = [
-        jnp.sum(member * (colour_list == k).astype(jnp.float32)[:, None, None], axis=0) for k in range(2)
-    ]
-    labels = (label_rows + 1).astype(jnp.float32)
 
     def z_up_ok(i):
         return (i + 2) % PZ != PZ - 1
@@ -509,34 +514,35 @@
         }
 
     smoothed_first, first_faces, _ = run_pass(
-        source, link_rows, None, labels, member, colour_masks[0], None, None,
+        source, link_rows, None, label_rows, colour_list, 0, None, None,
         faces=tuple(needed), link_mode="none", append_links=True,
     )
+    vectors = test_vectors.reshape(NVEC, 2, 2, 6, site_count)
+    vectors, smoothed_first = lax.optimization_barrier((vectors, smoothed_first))
     smoothed, smoothed_faces, back_rows = run_pass(
-        source, link_rows, None, labels, member, colour_masks[1], smoothed_first,
+        source, link_rows, None, label_rows, colour_list, 1, smoothed_first,
         halos_of(smoothed_first, first_faces), faces=tuple(needed), link_mode="combined", emit_back=True,
     )
 
     def sweep(start, faces):
         current, current_faces, _ = run_pass(
-            source, link_rows, back_rows, labels, member, colour_masks[0], start, halos_of(start, faces),
+            source, link_rows, back_rows, label_rows, colour_list, 0, start, halos_of(start, faces),
             faces=tuple(needed),
         )
         result, _, _ = run_pass(
-            source, link_rows, back_rows, labels, member, colour_masks[1], current,
+            source, link_rows, back_rows, label_rows, colour_list, 1, current,
             halos_of(current, current_faces),
         )
         return result
 
     residue, _, _ = run_pass(
-        source, link_rows, back_rows, labels, member, None, smoothed, halos_of(smoothed, smoothed_faces),
+        source, link_rows, back_rows, label_rows, None, None, smoothed, halos_of(smoothed, smoothed_faces),
         residual_only=True,
     )
-    residual = residue.astype(jnp.bfloat16)
+    residual = residue
     membership = member.reshape(AGG, site_count).T
     member_weights = membership.astype(jnp.bfloat16)
     weighted = residual.reshape(2, 2, 6, site_count)[..., None] * member_weights
-    vectors = test_vectors.reshape(NVEC, 2, 2, 6, site_count)
 
     def contract(left, right):
         return jnp.einsum("kxqn,xqnj->xkj", left, right, preferred_element_type=jnp.float32)

time: 128 us -> 126 us (0.984)
  starting transfers between devices: 48.7 us -> 43.5 us
  waiting for transfers between devices: 21.6 us -> 25.3 us
  local copies, waits for them, and re-layouts: 15.7 us -> 19.3 us
  other arithmetic: 5.59 us -> 2.03 us
    ppermute x24, starting transfers between devices: 48.7 us -> 43.5 us  [permute_from(): return lax.ppermute(value, axis, pairs)]
    ppermute x24, waiting for transfers between devices: 21.6 us -> 25.3 us  [permute_from(): return lax.ppermute(value, axis, pairs)]
    convert_element_type x4 -> x0, other arithmetic: 2.88 us -> none  [the longest x1 0.94 us: body(): residual = residue.astype(jnp.bfloat16)]
    unnamed x61 -> x59, local copies, waits for them, and re-layouts: 9.03 us -> 11.2 us
  transfers between devices with their start and end apart: 24 -> 24, of which waited for: 7 -> 7; matrix products, arithmetic and copies ran while one was open for 7% -> 8% of each run, Pallas kernels for 0% -> 0%
where the time goes in v6:
time: 126 us; the launch traced here: 125 us
  starting transfers between devices  43.5 us (35%)
  Pallas kernels  30.2 us (24%)
  waiting for transfers between devices  25.3 us (20%)
  local copies, waits for them, and re-layouts  19.3 us (15%)
  matrix products  3.45 us (3%)
  other arithmetic  2.03 us (2%)
    ppermute x24, starting transfers between devices, permute_from(): return lax.ppermute(value, axis, pairs)  43.5 us
    ppermute x24, waiting for transfers between devices, permute_from(): return lax.ppermute(value, axis, pairs)  25.3 us
    pallas_call x5, Pallas kernels, run_pass(): pl.pallas_call(kernel, out_shape=out_shape, scratch_shapes=scratch, in_sp...  22.4 us
    unnamed x59, local copies, waits for them, and re-layouts  11.2 us
    pallas_call x3, Pallas kernels, run_coarse(): pl.pallas_call(kernel, out_shape=jax.ShapeDtypeStruct(source.shape, jnp.f...  7.76 us
    reshape x1, local copies, waits for them, and re-layouts, body(): vectors = test_vectors.reshape(NVEC, 2, 2, 6, site_count)  4.03 us
    dot_general x4, matrix products, contract(): jnp.einsum('kxqn,xqnj->xkj', left, right, preferred_element_type=jnp.floa...  3 us
  transfers between devices with their start and end apart: 24, of which 7 were waited for; matrix products, arithmetic and copies ran while one was open for 8% of the time, Pallas kernels for 0%

profile of v6, /device:TPU:0, one launch (start us, length us, event | category | flops | bytes accessed | tf_op | source)
XLA Modules:
  0.0 124.9 jit_solution(258486186977856622)
XLA Ops:
  2.0 4.2 %shard_map.86 = (f32[24,16,128]{2,1,0:T(8,128)}, f32[24,16,64]{2,1,0:T(8,128)}, f32[42,16,64]{2,1,0:T(8,128)}, f32[24,4,128]{2,1,0:T(4,128)}, f32[42,4,128]{2,1,0:T(4,128)}) custom-call(f32[24,16,128]{2,1,0:T(8,128)} %bitcast.74, bf16[4,18,16,128]{3,2,1,0:T(8,128)(2,1)} %bitcast.67, s32[16,128]{1,0:T(8,128)} %reshape.52.refs_2_.refs_3_, s32[16]{0:T(128)} %bitcast.87), custom_call_target="tpu_custom_call" | custom-call | tf_op jit(solution)/shard_map/pallas_call | solution.py:363
  6.7 1.9 %collective-permute-start = (f32[24,16,64]{2,1,0:T(8,128)}, f32[24,16,64]{2,1,0:T(8,128)S(1)}, u32[]{:S(2)}, u32[]{:S(2)}) collective-permute-start(f32[24,16,64]{2,1,0:T(8,128)} %get-tuple-element.22), channel_id=1, source_target_pairs={{1,0},{2,1},{3,2},{0,3},{5,4},{6,5},{7,6},{4,7},{9,8},{10,9},{11,1... | collective-permute-start | bytes 294920 | tf_op jit(solution)/shard_map/ppermute | solution.py:112
  8.6 4.2 %collective-permute-start.3 = (f32[42,4,128]{2,1,0:T(4,128)}, f32[42,4,128]{2,1,0:T(4,128)S(1)}, u32[]{:S(2)}, u32[]{:S(2)}) collective-permute-start(f32[42,4,128]{2,1,0:T(4,128)} %get-tuple-element.25), channel_id=1, source_target_pairs={{28,0},{0,4},{4,8},{8,12},{12,16},{16,20},{24,28},{29,1},{1,5},{5,... | collective-permute-start | bytes 258056 | tf_op jit(solution)/shard_map/ppermute | solution.py:112
  12.9 5.0 %collective-permute-start.2 = (f32[24,4,128]{2,1,0:T(4,128)}, f32[24,4,128]{2,1,0:T(4,128)S(1)}, u32[]{:S(2)}, u32[]{:S(2)}) collective-permute-start(f32[24,4,128]{2,1,0:T(4,128)} %get-tuple-element.24), channel_id=1, source_target_pairs={{4,0},{8,4},{12,8},{16,12},{20,16},{28,24},{0,28},{5,1},{9,5},{13,... | collective-permute-start | bytes 147464 | tf_op jit(solution)/shard_map/ppermute | solution.py:112
  18.6 4.3 %copy.13 = bf16[1,24,24,4,4,128]{5,4,3,1,2,0:T(4,128)(2,1)} copy(bf16[1,24,24,4,4,128]{5,4,3,2,1,0:T(4,128)(2,1)} %param.9) | data formatting | bytes 4718592 | tf_op args[2]
  22.9 4.0 %reshape.54 = bf16[24,2,2,6,2048]{4,0,3,2,1:T(8,128)(2,1)S(1)} reshape(bf16[1,24,24,4,4,128]{5,4,3,1,2,0:T(4,128)(2,1)} %copy.13) | data formatting | bytes 4718592 | tf_op jit(solution)/shard_map/reshape | solution.py:520
  28.4 5.3 %shard_map.87 = (f32[24,16,128]{2,1,0:T(8,128)}, f32[24,16,64]{2,1,0:T(8,128)}, f32[24,16,64]{2,1,0:T(8,128)}, f32[24,4,128]{2,1,0:T(4,128)}, f32[24,4,128]{2,1,0:T(4,128)}, /*index=5*/bf16[4,18,16,128]{3,2,1,0:T(8,128)(2,1)}) custom-call(f32[24,16,128]{2,1,0:T(8,128)} %bitcast.75, bf16[4,18,16,128]{3,2,1,0:T(8,128)(2,1)} %bitcast.68, ...), custom_call_target="tpu_custom_call" | custom-call | tf_op jit(solution)/shard_map/pallas_call | solution.py:363
  34.3 3.9 %collective-permute-start.6 = (f32[24,4,128]{2,1,0:T(4,128)}, f32[24,4,128]{2,1,0:T(4,128)S(1)}, u32[]{:S(2)}, u32[]{:S(2)}) collective-permute-start(f32[24,4,128]{2,1,0:T(4,128)} %get-tuple-element.31), channel_id=1, source_target_pairs={{4,0},{8,4},{12,8},{16,12},{20,16},{28,24},{0,28},{5,1},{9,5},{13,... | collective-permute-start | bytes 147464 | tf_op jit(solution)/shard_map/ppermute | solution.py:112
  38.2 1.9 %collective-permute-start.7 = (f32[24,4,128]{2,1,0:T(4,128)}, f32[24,4,128]{2,1,0:T(4,128)S(1)}, u32[]{:S(2)}, u32[]{:S(2)}) collective-permute-start(f32[24,4,128]{2,1,0:T(4,128)} %get-tuple-element.32), channel_id=1, source_target_pairs={{28,0},{0,4},{4,8},{8,12},{12,16},{16,20},{24,28},{29,1},{1,5},{5,... | collective-permute-start | bytes 147464 | tf_op jit(solution)/shard_map/ppermute | solution.py:112
  40.7 6.9 %collective-permute-done.7.refs_8_ = f32[24,4,128]{2,1,0:T(4,128)S(1)} collective-permute-done((f32[24,4,128]{2,1,0:T(4,128)}, f32[24,4,128]{2,1,0:T(4,128)S(1)}, u32[]{:S(2)}, u32[]{:S(2)}) %collective-permute-start.7) | collective-permute-done | bytes 49184 | tf_op jit(solution)/shard_map/ppermute | solution.py:112
  48.3 2.7 %shard_map.88 = bf16[24,16,128]{2,1,0:T(8,128)(2,1)} custom-call(f32[24,16,128]{2,1,0:T(8,128)} %bitcast.76, bf16[4,18,16,128]{3,2,1,0:T(8,128)(2,1)} %bitcast.69, bf16[4,18,16,128]{3,2,1,0:T(8,128)(2,1)} %get-tuple-element.26.refs_2_, s32[16,128]{1,0:T(8,128)} %reshape.52.refs_2_.refs_3_, f32[24,16,128]{2,1,0:T(8,128)} %get-tuple-element.27.refs_4_, ...), custom_call_target="tpu_custom_call" | custom-call | tf_op jit(solution)/shard_map/pallas_call | solution.py:363
  60.6 3.9 %collective-permute-start.11 = (f32[2,1,768]{2,1,0:T(1,128)}, f32[2,1,768]{2,1,0:T(1,128)S(1)}, u32[]{:S(2)}, u32[]{:S(2)}) collective-permute-start(f32[2,1,768]{2,1,0:T(1,128)} %shard_map.89.refs_3_), channel_id=1, source_target_pairs={{28,0},{0,4},{4,8},{8,12},{12,16},{16,20},{24,28},{29,1},{1,5},{5,... | collective-permute-start | bytes 18440 | tf_op jit(solution)/shard_map/ppermute | solution.py:112
  64.6 4.4 %collective-permute-done.11.refs_7_ = f32[2,1,768]{2,1,0:T(1,128)S(1)} collective-permute-done((f32[2,1,768]{2,1,0:T(1,128)}, f32[2,1,768]{2,1,0:T(1,128)S(1)}, u32[]{:S(2)}, u32[]{:S(2)}) %collective-permute-start.11) | collective-permute-done | bytes 6176 | tf_op jit(solution)/shard_map/ppermute | solution.py:112
  69.6 3.0 %shard_map.90.refs_3_ = f32[2,1,768]{2,1,0:T(1,128)} custom-call(f32[2,1,768]{2,1,0:T(1,128)} %copy-done.12, bf16[2,48,768]{2,1,0:T(8,128)(2,1)} %bitcast.82, bf16[9,2,48,768]{3,2,1,0:T(8,128)(2,1)} %bitcast.72, f32[2,1,768]{2,1,0:T(1,128)} %shard_map.89.refs_3_, f32[2,1,768]{2,1,0:T(1,128)} %copy-done.21, f32[2,1,768]{2,1,0:T(1,128)} %copy-done.23, ...), custom_call_target="tpu_custom_call" | custom-call | tf_op jit(solution)/shard_map/pallas_call | solution.py:446
  75.0 4.1 %collective-permute-start.15 = (f32[2,1,768]{2,1,0:T(1,128)}, f32[2,1,768]{2,1,0:T(1,128)S(1)}, u32[]{:S(2)}, u32[]{:S(2)}) collective-permute-start(f32[2,1,768]{2,1,0:T(1,128)} %shard_map.90.refs_3_), channel_id=1, source_target_pairs={{28,0},{0,4},{4,8},{8,12},{12,16},{16,20},{24,28},{29,1},{1,5},{5,... | collective-permute-start | bytes 18440 | tf_op jit(solution)/shard_map/ppermute | solution.py:112
  79.2 4.3 %collective-permute-done.15.refs_7_ = f32[2,1,768]{2,1,0:T(1,128)S(1)} collective-permute-done((f32[2,1,768]{2,1,0:T(1,128)}, f32[2,1,768]{2,1,0:T(1,128)S(1)}, u32[]{:S(2)}, u32[]{:S(2)}) %collective-permute-start.15) | collective-permute-done | bytes 6176 | tf_op jit(solution)/shard_map/ppermute | solution.py:112
  84.1 3.0 %shard_map.91 = f32[2,1,768]{2,1,0:T(1,128)} custom-call(f32[2,1,768]{2,1,0:T(1,128)} %copy-done.12, bf16[2,48,768]{2,1,0:T(8,128)(2,1)} %bitcast.83, bf16[9,2,48,768]{3,2,1,0:T(8,128)(2,1)} %bitcast.73, f32[2,1,768]{2,1,0:T(1,128)} %shard_map.90.refs_3_, f32[2,1,768]{2,1,0:T(1,128)} %copy-done.20, f32[2,1,768]{2,1,0:T(1,128)} %copy-done.22, ...), custom_call_target="tpu_custom_call" | custom-call | tf_op jit(solution)/shard_map/pallas_call | solution.py:446
  90.4 1.9 %collective-permute-start.18 = (f32[24,4,128]{2,1,0:T(4,128)S(1)}, f32[24,4,128]{2,1,0:T(4,128)S(1)}, u32[]{:S(2)}, u32[]{:S(2)}) collective-permute-start(f32[24,4,128]{2,1,0:T(4,128)S(1)} %slice.48), channel_id=1, source_target_pairs={{4,0},{8,4},{12,8},{16,12},{20,16},{28,24},{0,28},{5,1},{9,5},{13,... | collective-permute-start | bytes 147464 | tf_op jit(solution)/shard_map/ppermute | solution.py:112
  92.3 3.9 %collective-permute-start.19 = (f32[24,4,128]{2,1,0:T(4,128)S(1)}, f32[24,4,128]{2,1,0:T(4,128)S(1)}, u32[]{:S(2)}, u32[]{:S(2)}) collective-permute-start(f32[24,4,128]{2,1,0:T(4,128)S(1)} %slice.49), channel_id=1, source_target_pairs={{28,0},{0,4},{4,8},{8,12},{12,16},{16,20},{24,28},{29,1},{1,5},{5,... | collective-permute-start | bytes 147464 | tf_op jit(solution)/shard_map/ppermute | solution.py:112
  96.5 4.6 %collective-permute-done.19.refs_9_ = f32[24,4,128]{2,1,0:T(4,128)S(1)} collective-permute-done((f32[24,4,128]{2,1,0:T(4,128)S(1)}, f32[24,4,128]{2,1,0:T(4,128)S(1)}, u32[]{:S(2)}, u32[]{:S(2)}) %collective-permute-start.19) | collective-permute-done | bytes 49184 | tf_op jit(solution)/shard_map/ppermute | solution.py:112
  102.5 5.2 %shard_map.92 = (f32[24,16,128]{2,1,0:T(8,128)}, f32[24,16,64]{2,1,0:T(8,128)}, f32[24,16,64]{2,1,0:T(8,128)}, f32[24,4,128]{2,1,0:T(4,128)}, f32[24,4,128]{2,1,0:T(4,128)}) custom-call(f32[24,16,128]{2,1,0:T(8,128)} %bitcast.77, bf16[4,18,16,128]{3,2,1,0:T(8,128)(2,1)} %bitcast.70, bf16[4,18,16,128]{3,2,1,0:T(8,128)(2,1)} %get-tuple-element.26.refs_2_, ...), custom_call_target="tpu_custom_call" | custom-call | tf_op jit(solution)/shard_map/pallas_call | solution.py:363
  110.1 3.9 %collective-permute-start.23 = (f32[24,4,128]{2,1,0:T(4,128)}, f32[24,4,128]{2,1,0:T(4,128)S(1)}, u32[]{:S(2)}, u32[]{:S(2)}) collective-permute-start(f32[24,4,128]{2,1,0:T(4,128)} %get-tuple-element.37), channel_id=1, source_target_pairs={{28,0},{0,4},{4,8},{8,12},{12,16},{16,20},{24,28},{29,1},{1,5},{5,... | collective-permute-start | bytes 147464 | tf_op jit(solution)/shard_map/ppermute | solution.py:112
  114.8 4.3 %collective-permute-done.23.refs_9_ = f32[24,4,128]{2,1,0:T(4,128)S(1)} collective-permute-done((f32[24,4,128]{2,1,0:T(4,128)}, f32[24,4,128]{2,1,0:T(4,128)S(1)}, u32[]{:S(2)}, u32[]{:S(2)}) %collective-permute-start.23) | collective-permute-done | bytes 49184 | tf_op jit(solution)/shard_map/ppermute | solution.py:112
  119.9 5.0 %shard_map.93 = f32[24,16,128]{2,1,0:T(8,128)} custom-call(f32[24,16,128]{2,1,0:T(8,128)} %bitcast.78, bf16[4,18,16,128]{3,2,1,0:T(8,128)(2,1)} %bitcast.71, bf16[4,18,16,128]{3,2,1,0:T(8,128)(2,1)} %get-tuple-element.26.refs_2_, s32[16,128]{1,0:T(8,128)} %reshape.52.refs_2_.refs_3_, s32[16]{0:T(128)} %bitcast.90, f32[24,16,128]{2,1,0:T(8,128)} %get-tuple-element.33.refs_5_, ...), custom_call_target="tpu_custom_call" | custom-call | tf_op jit(solution)/shard_map/pallas_call | solution.py:363
  (118 shorter events, 27.8 us)
Async XLA Ops:
  6.2 20.8 %collective-permute-start.1 = (f32[42,16,64]{2,1,0:T(8,128)}, f32[42,16,64]{2,1,0:T(8,128)S(1)}, u32[]{:S(2)}, u32[]{:S(2)}) collective-permute-start(f32[42,16,64]{2,1,0:T(8,128)} %get-tuple-element.23), channel_id=1, source_target_pairs={{3,0},{0,1},{1,2},{2,3},{7,4},{4,5},{5,6},{6,7},{11,8},{8,9},{9,10... | collective-permute-start | bytes 516104 | tf_op jit(solution)/shard_map/ppermute | solution.py:112
  6.7 20.3 %collective-permute-start = (f32[24,16,64]{2,1,0:T(8,128)}, f32[24,16,64]{2,1,0:T(8,128)S(1)}, u32[]{:S(2)}, u32[]{:S(2)}) collective-permute-start(f32[24,16,64]{2,1,0:T(8,128)} %get-tuple-element.22), channel_id=1, source_target_pairs={{1,0},{2,1},{3,2},{0,3},{5,4},{6,5},{7,6},{4,7},{9,8},{10,9},{11,1... | collective-permute-start | bytes 294920 | tf_op jit(solution)/shard_map/ppermute | solution.py:112
  8.6 18.4 %collective-permute-start.3 = (f32[42,4,128]{2,1,0:T(4,128)}, f32[42,4,128]{2,1,0:T(4,128)S(1)}, u32[]{:S(2)}, u32[]{:S(2)}) collective-permute-start(f32[42,4,128]{2,1,0:T(4,128)} %get-tuple-element.25), channel_id=1, source_target_pairs={{28,0},{0,4},{4,8},{8,12},{12,16},{16,20},{24,28},{29,1},{1,5},{5,... | collective-permute-start | bytes 258056 | tf_op jit(solution)/shard_map/ppermute | solution.py:112
  12.9 14.1 %collective-permute-start.2 = (f32[24,4,128]{2,1,0:T(4,128)}, f32[24,4,128]{2,1,0:T(4,128)S(1)}, u32[]{:S(2)}, u32[]{:S(2)}) collective-permute-start(f32[24,4,128]{2,1,0:T(4,128)} %get-tuple-element.24), channel_id=1, source_target_pairs={{4,0},{8,4},{12,8},{16,12},{20,16},{28,24},{0,28},{5,1},{9,5},{13,... | collective-permute-start | bytes 147464 | tf_op jit(solution)/shard_map/ppermute | solution.py:112
  33.8 13.8 %collective-permute-start.4 = (f32[24,16,64]{2,1,0:T(8,128)}, f32[24,16,64]{2,1,0:T(8,128)S(1)}, u32[]{:S(2)}, u32[]{:S(2)}) collective-permute-start(f32[24,16,64]{2,1,0:T(8,128)} %get-tuple-element.29), channel_id=1, source_target_pairs={{1,0},{2,1},{3,2},{0,3},{5,4},{6,5},{7,6},{4,7},{9,8},{10,9},{11,1... | collective-permute-start | bytes 294920 | tf_op jit(solution)/shard_map/ppermute | solution.py:112
  33.8 13.8 %collective-permute-start.5 = (f32[24,16,64]{2,1,0:T(8,128)}, f32[24,16,64]{2,1,0:T(8,128)S(1)}, u32[]{:S(2)}, u32[]{:S(2)}) collective-permute-start(f32[24,16,64]{2,1,0:T(8,128)} %get-tuple-element.30), channel_id=1, source_target_pairs={{3,0},{0,1},{1,2},{2,3},{7,4},{4,5},{5,6},{6,7},{11,8},{8,9},{9,10... | collective-permute-start | bytes 294920 | tf_op jit(solution)/shard_map/ppermute | solution.py:112
  34.3 6.4 %collective-permute-start.6 = (f32[24,4,128]{2,1,0:T(4,128)}, f32[24,4,128]{2,1,0:T(4,128)S(1)}, u32[]{:S(2)}, u32[]{:S(2)}) collective-permute-start(f32[24,4,128]{2,1,0:T(4,128)} %get-tuple-element.31), channel_id=1, source_target_pairs={{4,0},{8,4},{12,8},{16,12},{20,16},{28,24},{0,28},{5,1},{9,5},{13,... | collective-permute-start | bytes 147464 | tf_op jit(solution)/shard_map/ppermute | solution.py:112
  38.2 9.3 %collective-permute-start.7 = (f32[24,4,128]{2,1,0:T(4,128)}, f32[24,4,128]{2,1,0:T(4,128)S(1)}, u32[]{:S(2)}, u32[]{:S(2)}) collective-permute-start(f32[24,4,128]{2,1,0:T(4,128)} %get-tuple-element.32), channel_id=1, source_target_pairs={{28,0},{0,4},{4,8},{8,12},{12,16},{16,20},{24,28},{29,1},{1,5},{5,... | collective-permute-start | bytes 147464 | tf_op jit(solution)/shard_map/ppermute | solution.py:112
  58.2 6.4 %collective-permute-start.8 = (f32[2,1,768]{2,1,0:T(1,128)}, f32[2,1,768]{2,1,0:T(1,128)S(1)}, u32[]{:S(2)}, u32[]{:S(2)}) collective-permute-start(f32[2,1,768]{2,1,0:T(1,128)} %shard_map.89.refs_3_), channel_id=1, source_target_pairs={{1,0},{2,1},{3,2},{0,3},{5,4},{6,5},{7,6},{4,7},{9,8},{10,9},{11,1... | collective-permute-start | bytes 18440 | tf_op jit(solution)/shard_map/ppermute | solution.py:112
  58.2 6.4 %collective-permute-start.9 = (f32[2,1,768]{2,1,0:T(1,128)}, f32[2,1,768]{2,1,0:T(1,128)S(1)}, u32[]{:S(2)}, u32[]{:S(2)}) collective-permute-start(f32[2,1,768]{2,1,0:T(1,128)} %shard_map.89.refs_3_), channel_id=1, source_target_pairs={{3,0},{0,1},{1,2},{2,3},{7,4},{4,5},{5,6},{6,7},{11,8},{8,9},{9,10... | collective-permute-start | bytes 18440 | tf_op jit(solution)/shard_map/ppermute | solution.py:112
  58.7 5.9 %collective-permute-start.10 = (f32[2,1,768]{2,1,0:T(1,128)}, f32[2,1,768]{2,1,0:T(1,128)S(1)}, u32[]{:S(2)}, u32[]{:S(2)}) collective-permute-start(f32[2,1,768]{2,1,0:T(1,128)} %shard_map.89.refs_3_), channel_id=1, source_target_pairs={{4,0},{8,4},{12,8},{16,12},{20,16},{28,24},{0,28},{5,1},{9,5},{13,... | collective-permute-start | bytes 18440 | tf_op jit(solution)/shard_map/ppermute | solution.py:112
  60.6 8.4 %collective-permute-start.11 = (f32[2,1,768]{2,1,0:T(1,128)}, f32[2,1,768]{2,1,0:T(1,128)S(1)}, u32[]{:S(2)}, u32[]{:S(2)}) collective-permute-start(f32[2,1,768]{2,1,0:T(1,128)} %shard_map.89.refs_3_), channel_id=1, source_target_pairs={{28,0},{0,4},{4,8},{8,12},{12,16},{16,20},{24,28},{29,1},{1,5},{5,... | collective-permute-start | bytes 18440 | tf_op jit(solution)/shard_map/ppermute | solution.py:112
  72.6 6.5 %collective-permute-start.12 = (f32[2,1,768]{2,1,0:T(1,128)}, f32[2,1,768]{2,1,0:T(1,128)S(1)}, u32[]{:S(2)}, u32[]{:S(2)}) collective-permute-start(f32[2,1,768]{2,1,0:T(1,128)} %shard_map.90.refs_3_), channel_id=1, source_target_pairs={{1,0},{2,1},{3,2},{0,3},{5,4},{6,5},{7,6},{4,7},{9,8},{10,9},{11,1... | collective-permute-start | bytes 18440 | tf_op jit(solution)/shard_map/ppermute | solution.py:112
  72.7 6.5 %collective-permute-start.13 = (f32[2,1,768]{2,1,0:T(1,128)}, f32[2,1,768]{2,1,0:T(1,128)S(1)}, u32[]{:S(2)}, u32[]{:S(2)}) collective-permute-start(f32[2,1,768]{2,1,0:T(1,128)} %shard_map.90.refs_3_), channel_id=1, source_target_pairs={{3,0},{0,1},{1,2},{2,3},{7,4},{4,5},{5,6},{6,7},{11,8},{8,9},{9,10... | collective-permute-start | bytes 18440 | tf_op jit(solution)/shard_map/ppermute | solution.py:112
  73.1 6.1 %collective-permute-start.14 = (f32[2,1,768]{2,1,0:T(1,128)}, f32[2,1,768]{2,1,0:T(1,128)S(1)}, u32[]{:S(2)}, u32[]{:S(2)}) collective-permute-start(f32[2,1,768]{2,1,0:T(1,128)} %shard_map.90.refs_3_), channel_id=1, source_target_pairs={{4,0},{8,4},{12,8},{16,12},{20,16},{28,24},{0,28},{5,1},{9,5},{13,... | collective-permute-start | bytes 18440 | tf_op jit(solution)/shard_map/ppermute | solution.py:112
  75.0 8.4 %collective-permute-start.15 = (f32[2,1,768]{2,1,0:T(1,128)}, f32[2,1,768]{2,1,0:T(1,128)S(1)}, u32[]{:S(2)}, u32[]{:S(2)}) collective-permute-start(f32[2,1,768]{2,1,0:T(1,128)} %shard_map.90.refs_3_), channel_id=1, source_target_pairs={{28,0},{0,4},{4,8},{8,12},{12,16},{16,20},{24,28},{29,1},{1,5},{5,... | collective-permute-start | bytes 18440 | tf_op jit(solution)/shard_map/ppermute | solution.py:112
  89.8 11.4 %collective-permute-start.16 = (f32[24,16,64]{2,1,0:T(8,128)S(1)}, f32[24,16,64]{2,1,0:T(8,128)S(1)}, u32[]{:S(2)}, u32[]{:S(2)}) collective-permute-start(f32[24,16,64]{2,1,0:T(8,128)S(1)} %get-tuple-element.47), channel_id=1, source_target_pairs={{1,0},{2,1},{3,2},{0,3},{5,4},{6,5},{7,6},{4,7},{9,8},{10,9},{11,1... | collective-permute-start | bytes 294920 | tf_op jit(solution)/shard_map/ppermute | solution.py:112
  90.0 11.2 %collective-permute-start.17 = (f32[24,16,64]{2,1,0:T(8,128)S(1)}, f32[24,16,64]{2,1,0:T(8,128)S(1)}, u32[]{:S(2)}, u32[]{:S(2)}) collective-permute-start(f32[24,16,64]{2,1,0:T(8,128)S(1)} %get-tuple-element.46), channel_id=1, source_target_pairs={{3,0},{0,1},{1,2},{2,3},{7,4},{4,5},{5,6},{6,7},{11,8},{8,9},{9,10... | collective-permute-start | bytes 294920 | tf_op jit(solution)/shard_map/ppermute | solution.py:112
  90.4 6.1 %collective-permute-start.18 = (f32[24,4,128]{2,1,0:T(4,128)S(1)}, f32[24,4,128]{2,1,0:T(4,128)S(1)}, u32[]{:S(2)}, u32[]{:S(2)}) collective-permute-start(f32[24,4,128]{2,1,0:T(4,128)S(1)} %slice.48), channel_id=1, source_target_pairs={{4,0},{8,4},{12,8},{16,12},{20,16},{28,24},{0,28},{5,1},{9,5},{13,... | collective-permute-start | bytes 147464 | tf_op jit(solution)/shard_map/ppermute | solution.py:112
  92.3 8.8 %collective-permute-start.19 = (f32[24,4,128]{2,1,0:T(4,128)S(1)}, f32[24,4,128]{2,1,0:T(4,128)S(1)}, u32[]{:S(2)}, u32[]{:S(2)}) collective-permute-start(f32[24,4,128]{2,1,0:T(4,128)S(1)} %slice.49), channel_id=1, source_target_pairs={{28,0},{0,4},{4,8},{8,12},{12,16},{16,20},{24,28},{29,1},{1,5},{5,... | collective-permute-start | bytes 147464 | tf_op jit(solution)/shard_map/ppermute | solution.py:112
  107.7 11.4 %collective-permute-start.20 = (f32[24,16,64]{2,1,0:T(8,128)}, f32[24,16,64]{2,1,0:T(8,128)S(1)}, u32[]{:S(2)}, u32[]{:S(2)}) collective-permute-start(f32[24,16,64]{2,1,0:T(8,128)} %get-tuple-element.34), channel_id=1, source_target_pairs={{1,0},{2,1},{3,2},{0,3},{5,4},{6,5},{7,6},{4,7},{9,8},{10,9},{11,1... | collective-permute-start | bytes 294920 | tf_op jit(solution)/shard_map/ppermute | solution.py:112
  108.2 10.9 %collective-permute-start.21 = (f32[24,16,64]{2,1,0:T(8,128)}, f32[24,16,64]{2,1,0:T(8,128)S(1)}, u32[]{:S(2)}, u32[]{:S(2)}) collective-permute-start(f32[24,16,64]{2,1,0:T(8,128)} %get-tuple-element.35), channel_id=1, source_target_pairs={{3,0},{0,1},{1,2},{2,3},{7,4},{4,5},{5,6},{6,7},{11,8},{8,9},{9,10... | collective-permute-start | bytes 294920 | tf_op jit(solution)/shard_map/ppermute | solution.py:112
  108.2 6.6 %collective-permute-start.22 = (f32[24,4,128]{2,1,0:T(4,128)}, f32[24,4,128]{2,1,0:T(4,128)S(1)}, u32[]{:S(2)}, u32[]{:S(2)}) collective-permute-start(f32[24,4,128]{2,1,0:T(4,128)} %get-tuple-element.36), channel_id=1, source_target_pairs={{4,0},{8,4},{12,8},{16,12},{20,16},{28,24},{0,28},{5,1},{9,5},{13,... | collective-permute-start | bytes 147464 | tf_op jit(solution)/shard_map/ppermute | solution.py:112
  110.1 9.0 %collective-permute-start.23 = (f32[24,4,128]{2,1,0:T(4,128)}, f32[24,4,128]{2,1,0:T(4,128)S(1)}, u32[]{:S(2)}, u32[]{:S(2)}) collective-permute-start(f32[24,4,128]{2,1,0:T(4,128)} %get-tuple-element.37), channel_id=1, source_target_pairs={{28,0},{0,4},{4,8},{8,12},{12,16},{16,20},{24,28},{29,1},{1,5},{5,... | collective-permute-start | bytes 147464 | tf_op jit(solution)/shard_map/ppermute | solution.py:112
  (28 other events, 66.7 us)

commit v7 on v6

--- a/solution.py
+++ b/solution.py
@@ -465,7 +465,6 @@
     source = fine_source.reshape(24, rows, line_extent)
     link_rows = links.reshape(4, 18, rows, line_extent)
     label_rows = aggregate_map.reshape(rows, line_extent)
-    member = (label_rows[None] == jnp.arange(AGG, dtype=jnp.int32)[:, None, None]).astype(jnp.float32)
     colour_list = colouring.reshape(AGG)
 
     def z_up_ok(i):
@@ -517,8 +516,6 @@
         source, link_rows, None, label_rows, colour_list, 0, None, None,
         faces=tuple(needed), link_mode="none", append_links=True,
     )
-    vectors = test_vectors.reshape(NVEC, 2, 2, 6, site_count)
-    vectors, smoothed_first = lax.optimization_barrier((vectors, smoothed_first))
     smoothed, smoothed_faces, back_rows = run_pass(
         source, link_rows, None, label_rows, colour_list, 1, smoothed_first,
         halos_of(smoothed_first, first_faces), faces=tuple(needed), link_mode="combined", emit_back=True,
@@ -539,13 +536,16 @@
         source, link_rows, back_rows, label_rows, None, None, smoothed, halos_of(smoothed, smoothed_faces),
         residual_only=True,
     )
-    residual = residue
-    membership = member.reshape(AGG, site_count).T
-    member_weights = membership.astype(jnp.bfloat16)
-    weighted = residual.reshape(2, 2, 6, site_count)[..., None] * member_weights
+    site_dims = (time_extent, plane_extent, line_extent)
+    vectors = test_vectors.reshape((NVEC, 2, 2, 6) + site_dims)
+    residual = residue.reshape((2, 2, 6) + site_dims)
+    member_sites = (
+        aggregate_map.reshape(site_dims)[None] == jnp.arange(AGG, dtype=jnp.int32)[:, None, None, None]
+    )
+    weighted = residual[:, :, None] * member_sites.astype(jnp.bfloat16)[None, None, :, None]
 
     def contract(left, right):
-        return jnp.einsum("kxqn,xqnj->xkj", left, right, preferred_element_type=jnp.float32)
+        return jnp.einsum("khqtzl,hjqtzl->hkj", left, right, preferred_element_type=jnp.float32)
 
     real_part = contract(vectors[:, 0], weighted[0]) + contract(vectors[:, 1], weighted[1])
     imag_part = contract(vectors[:, 0], weighted[1]) - contract(vectors[:, 1], weighted[0])
@@ -565,11 +565,14 @@
         ]
         correction = run_coarse(flat_source, inverse_blocks, operator_blocks, correction, nearby)
     correction = correction.reshape(2, CDOF, AGG)
-    expanded = jnp.dot(
-        correction.reshape(2 * CDOF, AGG), membership.T, precision=lax.Precision.HIGHEST
-    ).reshape(2, 2, NVEC, site_count)
-    spread_real = jnp.swapaxes(expanded[0], 0, 1)[:, :, None]
-    spread_imag = jnp.swapaxes(expanded[1], 0, 1)[:, :, None]
+    expanded = jnp.einsum(
+        "ahkj,jtzl->akhtzl",
+        correction.reshape(2, 2, NVEC, AGG),
+        member_sites.astype(jnp.float32),
+        precision=lax.Precision.HIGHEST,
+    )
+    spread_real = expanded[0][:, :, None]
+    spread_imag = expanded[1][:, :, None]
     real_part = jnp.sum(vectors[:, 0] * spread_real - vectors[:, 1] * spread_imag, axis=0)
     imag_part = jnp.sum(vectors[:, 0] * spread_imag + vectors[:, 1] * spread_real, axis=0)
     corrected = smoothed + jnp.stack([real_part, imag_part]).reshape(24, rows, line_extent)

time: 126 us -> 134 us (1.063)
  starting transfers between devices: 43.5 us -> 55.6 us
  waiting for transfers between devices: 25.3 us -> 21.7 us
  local copies, waits for them, and re-layouts: 19.3 us -> 16.7 us
  other arithmetic: 2.03 us -> 3.81 us
    ppermute x24, starting transfers between devices: 43.5 us -> 55.6 us  [permute_from(): return lax.ppermute(value, axis, pairs)]
    reshape x2 -> x0, local copies, waits for them, and re-layouts: 4.09 us -> none  [the longest x1 4.03 us: body(): vectors = test_vectors.reshape(NVEC, 2, 2, 6, site_count)]
    ppermute x24, waiting for transfers between devices: 25.3 us -> 21.7 us  [permute_from(): return lax.ppermute(value, axis, pairs)]
    squeeze x0 -> x2, local copies, waits for them, and re-layouts: none -> 2 us  [the longest x1 1.57 us: body(): vectors[:, 0] * spread_real - vectors[:, 1] * spread_imag]
    unnamed x59 -> x43, local copies, waits for them, and re-layouts: 11.2 us -> 10.3 us
  transfers between devices with their start and end apart: 24 -> 24, of which waited for: 7 -> 6; matrix products, arithmetic and copies ran while one was open for 8% -> 6% of each run, Pallas kernels for 0% -> 0%
where the time goes in v7:
time: 134 us; the launch traced here: 133 us
  starting transfers between devices  55.6 us (41%)
  Pallas kernels  30.2 us (23%)
  waiting for transfers between devices  21.7 us (16%)
  local copies, waits for them, and re-layouts  16.7 us (12%)
  other arithmetic  3.81 us (3%)
  matrix products  3.53 us (3%)
    ppermute x24, starting transfers between devices, permute_from(): return lax.ppermute(value, axis, pairs)  55.6 us
    pallas_call x5, Pallas kernels, run_pass(): pl.pallas_call(kernel, out_shape=out_shape, scratch_shapes=scratch, in_sp...  22.4 us
    ppermute x24, waiting for transfers between devices, permute_from(): return lax.ppermute(value, axis, pairs)  21.7 us
    unnamed x43, local copies, waits for them, and re-layouts  10.3 us
    pallas_call x3, Pallas kernels, run_coarse(): pl.pallas_call(kernel, out_shape=jax.ShapeDtypeStruct(source.shape, jnp.f...  7.77 us
    dot_general x4, matrix products, contract(): jnp.einsum('khqtzl,hjqtzl->hkj', left, right, preferred_element_type=jnp....  3.08 us
  transfers between devices with their start and end apart: 24, of which 6 were waited for; matrix products, arithmetic and copies ran while one was open for 6% of the time, Pallas kernels for 0%

profile of v7, /device:TPU:0, one launch (start us, length us, event | category | flops | bytes accessed | tf_op | source)
XLA Modules:
  0.0 132.6 jit_solution(13755641224405506927)
XLA Ops:
  2.0 4.2 %shard_map.86 = (f32[24,16,128]{2,1,0:T(8,128)}, f32[24,16,64]{2,1,0:T(8,128)}, f32[42,16,64]{2,1,0:T(8,128)}, f32[24,4,128]{2,1,0:T(4,128)}, f32[42,4,128]{2,1,0:T(4,128)}) custom-call(f32[24,16,128]{2,1,0:T(8,128)} %bitcast.78, bf16[4,18,16,128]{3,2,1,0:T(8,128)(2,1)} %bitcast.71, s32[16,128]{1,0:T(8,128)} %reshape.45.refs_2_.refs_3_, s32[16]{0:T(128)} %bitcast.91), custom_call_target="tpu_custom_call" | custom-call | tf_op jit(solution)/shard_map/pallas_call | solution.py:363
  6.2 7.9 %collective-permute-start.2 = (f32[24,4,128]{2,1,0:T(4,128)}, f32[24,4,128]{2,1,0:T(4,128)}, u32[]{:S(2)}, u32[]{:S(2)}) collective-permute-start(f32[24,4,128]{2,1,0:T(4,128)} %get-tuple-element.21), channel_id=1, source_target_pairs={{4,0},{8,4},{12,8},{16,12},{20,16},{28,24},{0,28},{5,1},{9,5},{13,... | collective-permute-start | bytes 147464 | tf_op jit(solution)/shard_map/ppermute | solution.py:112
  14.1 1.9 %collective-permute-start.3 = (f32[42,4,128]{2,1,0:T(4,128)}, f32[42,4,128]{2,1,0:T(4,128)}, u32[]{:S(2)}, u32[]{:S(2)}) collective-permute-start(f32[42,4,128]{2,1,0:T(4,128)} %get-tuple-element.22), channel_id=1, source_target_pairs={{28,0},{0,4},{4,8},{8,12},{12,16},{16,20},{24,28},{29,1},{1,5},{5,... | collective-permute-start | bytes 258056 | tf_op jit(solution)/shard_map/ppermute | solution.py:112
  16.8 4.4 %copy.16 = bf16[1,24,24,4,4,128]{5,1,4,3,2,0:T(8,128)(2,1)S(1)} copy(bf16[1,24,24,4,4,128]{5,4,3,2,1,0:T(4,128)(2,1)} %param.9) | data formatting | bytes 4718592 | tf_op args[2]
  25.3 5.4 %shard_map.87 = (f32[24,16,128]{2,1,0:T(8,128)}, f32[24,16,64]{2,1,0:T(8,128)}, f32[24,16,64]{2,1,0:T(8,128)}, f32[24,4,128]{2,1,0:T(4,128)}, f32[24,4,128]{2,1,0:T(4,128)}, /*index=5*/bf16[4,18,16,128]{3,2,1,0:T(8,128)(2,1)}) custom-call(f32[24,16,128]{2,1,0:T(8,128)} %bitcast.79, bf16[4,18,16,128]{3,2,1,0:T(8,128)(2,1)} %bitcast.72, ...), custom_call_target="tpu_custom_call" | custom-call | tf_op jit(solution)/shard_map/pallas_call | solution.py:363
  30.6 6.6 %collective-permute-start.6 = (f32[24,4,128]{2,1,0:T(4,128)}, f32[24,4,128]{2,1,0:T(4,128)}, u32[]{:S(2)}, u32[]{:S(2)}) collective-permute-start(f32[24,4,128]{2,1,0:T(4,128)} %get-tuple-element.27), channel_id=1, source_target_pairs={{4,0},{8,4},{12,8},{16,12},{20,16},{28,24},{0,28},{5,1},{9,5},{13,... | collective-permute-start | bytes 147464 | tf_op jit(solution)/shard_map/ppermute | solution.py:112
  37.2 1.9 %collective-permute-start.7 = (f32[24,4,128]{2,1,0:T(4,128)}, f32[24,4,128]{2,1,0:T(4,128)}, u32[]{:S(2)}, u32[]{:S(2)}) collective-permute-start(f32[24,4,128]{2,1,0:T(4,128)} %get-tuple-element.28), channel_id=1, source_target_pairs={{28,0},{0,4},{4,8},{8,12},{12,16},{16,20},{24,28},{29,1},{1,5},{5,... | collective-permute-start | bytes 147464 | tf_op jit(solution)/shard_map/ppermute | solution.py:112
  40.4 5.9 %collective-permute-done.7.refs_8_ = f32[24,4,128]{2,1,0:T(4,128)} collective-permute-done((f32[24,4,128]{2,1,0:T(4,128)}, f32[24,4,128]{2,1,0:T(4,128)}, u32[]{:S(2)}, u32[]{:S(2)}) %collective-permute-start.7) | collective-permute-done | bytes 49184 | tf_op jit(solution)/shard_map/ppermute | solution.py:112
  46.2 2.8 %shard_map.88 = bf16[24,16,128]{2,1,0:T(8,128)(2,1)} custom-call(f32[24,16,128]{2,1,0:T(8,128)} %bitcast.80, bf16[4,18,16,128]{3,2,1,0:T(8,128)(2,1)} %bitcast.73, bf16[4,18,16,128]{3,2,1,0:T(8,128)(2,1)} %get-tuple-element.23.refs_2_, s32[16,128]{1,0:T(8,128)} %reshape.45.refs_2_.refs_3_, f32[24,16,128]{2,1,0:T(8,128)} %get-tuple-element.24.refs_4_, ...), custom_call_target="tpu_custom_call" | custom-call | tf_op jit(solution)/shard_map/pallas_call | solution.py:363
  56.8 1.8 %shard_map.89.refs_3_ = f32[2,1,768]{2,1,0:T(1,128)} custom-call(f32[2,1,768]{2,1,0:T(1,128)} %copy-done.7, bf16[2,48,768]{2,1,0:T(8,128)(2,1)} %bitcast.83), custom_call_target="tpu_custom_call" | custom-call | tf_op jit(solution)/shard_map/pallas_call | solution.py:446
  58.6 1.9 %collective-permute-start.11 = (f32[2,1,768]{2,1,0:T(1,128)}, f32[2,1,768]{2,1,0:T(1,128)S(1)}, u32[]{:S(2)}, u32[]{:S(2)}) collective-permute-start(f32[2,1,768]{2,1,0:T(1,128)} %shard_map.89.refs_3_), channel_id=1, source_target_pairs={{28,0},{0,4},{4,8},{8,12},{12,16},{16,20},{24,28},{29,1},{1,5},{5,... | collective-permute-start | bytes 18440 | tf_op jit(solution)/shard_map/ppermute | solution.py:112
  60.5 6.6 %collective-permute-start.10 = (f32[2,1,768]{2,1,0:T(1,128)}, f32[2,1,768]{2,1,0:T(1,128)S(1)}, u32[]{:S(2)}, u32[]{:S(2)}) collective-permute-start(f32[2,1,768]{2,1,0:T(1,128)} %shard_map.89.refs_3_), channel_id=1, source_target_pairs={{4,0},{8,4},{12,8},{16,12},{20,16},{28,24},{0,28},{5,1},{9,5},{13,... | collective-permute-start | bytes 18440 | tf_op jit(solution)/shard_map/ppermute | solution.py:112
  71.1 3.0 %shard_map.90.refs_3_ = f32[2,1,768]{2,1,0:T(1,128)} custom-call(f32[2,1,768]{2,1,0:T(1,128)} %copy-done.7, bf16[2,48,768]{2,1,0:T(8,128)(2,1)} %bitcast.84, bf16[9,2,48,768]{3,2,1,0:T(8,128)(2,1)} %bitcast.76, f32[2,1,768]{2,1,0:T(1,128)} %shard_map.89.refs_3_, f32[2,1,768]{2,1,0:T(1,128)} %copy-done.19, f32[2,1,768]{2,1,0:T(1,128)} %copy-done.17, ...), custom_call_target="tpu_custom_call" | custom-call | tf_op jit(solution)/shard_map/pallas_call | solution.py:446
  74.1 1.9 %collective-permute-start.15 = (f32[2,1,768]{2,1,0:T(1,128)}, f32[2,1,768]{2,1,0:T(1,128)S(1)}, u32[]{:S(2)}, u32[]{:S(2)}) collective-permute-start(f32[2,1,768]{2,1,0:T(1,128)} %shard_map.90.refs_3_), channel_id=1, source_target_pairs={{28,0},{0,4},{4,8},{8,12},{12,16},{16,20},{24,28},{29,1},{1,5},{5,... | collective-permute-start | bytes 18440 | tf_op jit(solution)/shard_map/ppermute | solution.py:112
  76.0 6.6 %collective-permute-start.14 = (f32[2,1,768]{2,1,0:T(1,128)}, f32[2,1,768]{2,1,0:T(1,128)S(1)}, u32[]{:S(2)}, u32[]{:S(2)}) collective-permute-start(f32[2,1,768]{2,1,0:T(1,128)} %shard_map.90.refs_3_), channel_id=1, source_target_pairs={{4,0},{8,4},{12,8},{16,12},{20,16},{28,24},{0,28},{5,1},{9,5},{13,... | collective-permute-start | bytes 18440 | tf_op jit(solution)/shard_map/ppermute | solution.py:112
  87.1 3.0 %shard_map.91 = f32[2,1,768]{2,1,0:T(1,128)} custom-call(f32[2,1,768]{2,1,0:T(1,128)} %copy-done.7, bf16[2,48,768]{2,1,0:T(8,128)(2,1)} %bitcast.85, bf16[9,2,48,768]{3,2,1,0:T(8,128)(2,1)} %bitcast.77, f32[2,1,768]{2,1,0:T(1,128)} %shard_map.90.refs_3_, f32[2,1,768]{2,1,0:T(1,128)} %copy-done.18, f32[2,1,768]{2,1,0:T(1,128)} %copy-done.16, ...), custom_call_target="tpu_custom_call" | custom-call | tf_op jit(solution)/shard_map/pallas_call | solution.py:446
  94.9 5.1 %collective-permute-start.18 = (f32[24,4,128]{2,1,0:T(4,128)S(1)}, f32[24,4,128]{2,1,0:T(4,128)S(1)}, u32[]{:S(2)}, u32[]{:S(2)}) collective-permute-start(f32[24,4,128]{2,1,0:T(4,128)S(1)} %slice.46), channel_id=1, source_target_pairs={{4,0},{8,4},{12,8},{16,12},{20,16},{28,24},{0,28},{5,1},{9,5},{13,... | collective-permute-start | bytes 147464 | tf_op jit(solution)/shard_map/ppermute | solution.py:112
  100.0 1.9 %collective-permute-start.19 = (f32[24,4,128]{2,1,0:T(4,128)S(1)}, f32[24,4,128]{2,1,0:T(4,128)S(1)}, u32[]{:S(2)}, u32[]{:S(2)}) collective-permute-start(f32[24,4,128]{2,1,0:T(4,128)S(1)} %slice.47), channel_id=1, source_target_pairs={{28,0},{0,4},{4,8},{8,12},{12,16},{16,20},{24,28},{29,1},{1,5},{5,... | collective-permute-start | bytes 147464 | tf_op jit(solution)/shard_map/ppermute | solution.py:112
  101.9 6.7 %collective-permute-done.19.refs_9_ = f32[24,4,128]{2,1,0:T(4,128)S(1)} collective-permute-done((f32[24,4,128]{2,1,0:T(4,128)S(1)}, f32[24,4,128]{2,1,0:T(4,128)S(1)}, u32[]{:S(2)}, u32[]{:S(2)}) %collective-permute-start.19) | collective-permute-done | bytes 49184 | tf_op jit(solution)/shard_map/ppermute | solution.py:112
  110.0 5.2 %shard_map.92 = (f32[24,16,128]{2,1,0:T(8,128)}, f32[24,16,64]{2,1,0:T(8,128)}, f32[24,16,64]{2,1,0:T(8,128)}, f32[24,4,128]{2,1,0:T(4,128)}, f32[24,4,128]{2,1,0:T(4,128)}) custom-call(f32[24,16,128]{2,1,0:T(8,128)} %bitcast.81, bf16[4,18,16,128]{3,2,1,0:T(8,128)(2,1)} %bitcast.74, bf16[4,18,16,128]{3,2,1,0:T(8,128)(2,1)} %get-tuple-element.23.refs_2_, ...), custom_call_target="tpu_custom_call" | custom-call | tf_op jit(solution)/shard_map/pallas_call | solution.py:363
  115.7 1.9 %collective-permute-start.22 = (f32[24,4,128]{2,1,0:T(4,128)}, f32[24,4,128]{2,1,0:T(4,128)S(1)}, u32[]{:S(2)}, u32[]{:S(2)}) collective-permute-start(f32[24,4,128]{2,1,0:T(4,128)} %get-tuple-element.32), channel_id=1, source_target_pairs={{4,0},{8,4},{12,8},{16,12},{20,16},{28,24},{0,28},{5,1},{9,5},{13,... | collective-permute-start | bytes 147464 | tf_op jit(solution)/shard_map/ppermute | solution.py:112
  117.6 4.1 %collective-permute-start.23 = (f32[24,4,128]{2,1,0:T(4,128)}, f32[24,4,128]{2,1,0:T(4,128)S(1)}, u32[]{:S(2)}, u32[]{:S(2)}) collective-permute-start(f32[24,4,128]{2,1,0:T(4,128)} %get-tuple-element.33), channel_id=1, source_target_pairs={{28,0},{0,4},{4,8},{8,12},{12,16},{16,20},{24,28},{29,1},{1,5},{5,... | collective-permute-start | bytes 147464 | tf_op jit(solution)/shard_map/ppermute | solution.py:112
  122.6 4.3 %collective-permute-done.23.refs_9_ = f32[24,4,128]{2,1,0:T(4,128)S(1)} collective-permute-done((f32[24,4,128]{2,1,0:T(4,128)}, f32[24,4,128]{2,1,0:T(4,128)S(1)}, u32[]{:S(2)}, u32[]{:S(2)}) %collective-permute-start.23) | collective-permute-done | bytes 49184 | tf_op jit(solution)/shard_map/ppermute | solution.py:112
  127.6 5.0 %shard_map.93 = f32[24,16,128]{2,1,0:T(8,128)} custom-call(f32[24,16,128]{2,1,0:T(8,128)} %bitcast.82, bf16[4,18,16,128]{3,2,1,0:T(8,128)(2,1)} %bitcast.75, bf16[4,18,16,128]{3,2,1,0:T(8,128)(2,1)} %get-tuple-element.23.refs_2_, s32[16,128]{1,0:T(8,128)} %reshape.45.refs_2_.refs_3_, s32[16]{0:T(128)} %bitcast.94, f32[24,16,128]{2,1,0:T(8,128)} %get-tuple-element.29.refs_5_, ...), custom_call_target="tpu_custom_call" | custom-call | tf_op jit(solution)/shard_map/pallas_call | solution.py:363
  (101 shorter events, 31.6 us)
Async XLA Ops:
  6.2 17.3 %collective-permute-start.2 = (f32[24,4,128]{2,1,0:T(4,128)}, f32[24,4,128]{2,1,0:T(4,128)}, u32[]{:S(2)}, u32[]{:S(2)}) collective-permute-start(f32[24,4,128]{2,1,0:T(4,128)} %get-tuple-element.21), channel_id=1, source_target_pairs={{4,0},{8,4},{12,8},{16,12},{20,16},{28,24},{0,28},{5,1},{9,5},{13,... | collective-permute-start | bytes 147464 | tf_op jit(solution)/shard_map/ppermute | solution.py:112
  14.1 9.4 %collective-permute-start.3 = (f32[42,4,128]{2,1,0:T(4,128)}, f32[42,4,128]{2,1,0:T(4,128)}, u32[]{:S(2)}, u32[]{:S(2)}) collective-permute-start(f32[42,4,128]{2,1,0:T(4,128)} %get-tuple-element.22), channel_id=1, source_target_pairs={{28,0},{0,4},{4,8},{8,12},{12,16},{16,20},{24,28},{29,1},{1,5},{5,... | collective-permute-start | bytes 258056 | tf_op jit(solution)/shard_map/ppermute | solution.py:112
  16.1 7.5 %collective-permute-start = (f32[24,16,64]{2,1,0:T(8,128)}, f32[24,16,64]{2,1,0:T(8,128)}, u32[]{:S(2)}, u32[]{:S(2)}) collective-permute-start(f32[24,16,64]{2,1,0:T(8,128)} %get-tuple-element.19), channel_id=1, source_target_pairs={{1,0},{2,1},{3,2},{0,3},{5,4},{6,5},{7,6},{4,7},{9,8},{10,9},{11,1... | collective-permute-start | bytes 294920 | tf_op jit(solution)/shard_map/ppermute | solution.py:112
  16.8 8.5 %collective-permute-start.1 = (f32[42,16,64]{2,1,0:T(8,128)}, f32[42,16,64]{2,1,0:T(8,128)}, u32[]{:S(2)}, u32[]{:S(2)}) collective-permute-start(f32[42,16,64]{2,1,0:T(8,128)} %get-tuple-element.20), channel_id=1, source_target_pairs={{3,0},{0,1},{1,2},{2,3},{7,4},{4,5},{5,6},{6,7},{11,8},{8,9},{9,10... | collective-permute-start | bytes 516104 | tf_op jit(solution)/shard_map/ppermute | solution.py:112
  30.6 9.7 %collective-permute-start.6 = (f32[24,4,128]{2,1,0:T(4,128)}, f32[24,4,128]{2,1,0:T(4,128)}, u32[]{:S(2)}, u32[]{:S(2)}) collective-permute-start(f32[24,4,128]{2,1,0:T(4,128)} %get-tuple-element.27), channel_id=1, source_target_pairs={{4,0},{8,4},{12,8},{16,12},{20,16},{28,24},{0,28},{5,1},{9,5},{13,... | collective-permute-start | bytes 147464 | tf_op jit(solution)/shard_map/ppermute | solution.py:112
  37.2 9.0 %collective-permute-start.7 = (f32[24,4,128]{2,1,0:T(4,128)}, f32[24,4,128]{2,1,0:T(4,128)}, u32[]{:S(2)}, u32[]{:S(2)}) collective-permute-start(f32[24,4,128]{2,1,0:T(4,128)} %get-tuple-element.28), channel_id=1, source_target_pairs={{28,0},{0,4},{4,8},{8,12},{12,16},{16,20},{24,28},{29,1},{1,5},{5,... | collective-permute-start | bytes 147464 | tf_op jit(solution)/shard_map/ppermute | solution.py:112
  39.2 7.1 %collective-permute-start.4 = (f32[24,16,64]{2,1,0:T(8,128)}, f32[24,16,64]{2,1,0:T(8,128)}, u32[]{:S(2)}, u32[]{:S(2)}) collective-permute-start(f32[24,16,64]{2,1,0:T(8,128)} %get-tuple-element.25), channel_id=1, source_target_pairs={{1,0},{2,1},{3,2},{0,3},{5,4},{6,5},{7,6},{4,7},{9,8},{10,9},{11,1... | collective-permute-start | bytes 294920 | tf_op jit(solution)/shard_map/ppermute | solution.py:112
  39.2 7.0 %collective-permute-start.5 = (f32[24,16,64]{2,1,0:T(8,128)}, f32[24,16,64]{2,1,0:T(8,128)}, u32[]{:S(2)}, u32[]{:S(2)}) collective-permute-start(f32[24,16,64]{2,1,0:T(8,128)} %get-tuple-element.26), channel_id=1, source_target_pairs={{3,0},{0,1},{1,2},{2,3},{7,4},{4,5},{5,6},{6,7},{11,8},{8,9},{9,10... | collective-permute-start | bytes 294920 | tf_op jit(solution)/shard_map/ppermute | solution.py:112
  58.6 10.3 %collective-permute-start.11 = (f32[2,1,768]{2,1,0:T(1,128)}, f32[2,1,768]{2,1,0:T(1,128)S(1)}, u32[]{:S(2)}, u32[]{:S(2)}) collective-permute-start(f32[2,1,768]{2,1,0:T(1,128)} %shard_map.89.refs_3_), channel_id=1, source_target_pairs={{28,0},{0,4},{4,8},{8,12},{12,16},{16,20},{24,28},{29,1},{1,5},{5,... | collective-permute-start | bytes 18440 | tf_op jit(solution)/shard_map/ppermute | solution.py:112
  60.5 8.4 %collective-permute-start.10 = (f32[2,1,768]{2,1,0:T(1,128)}, f32[2,1,768]{2,1,0:T(1,128)S(1)}, u32[]{:S(2)}, u32[]{:S(2)}) collective-permute-start(f32[2,1,768]{2,1,0:T(1,128)} %shard_map.89.refs_3_), channel_id=1, source_target_pairs={{4,0},{8,4},{12,8},{16,12},{20,16},{28,24},{0,28},{5,1},{9,5},{13,... | collective-permute-start | bytes 18440 | tf_op jit(solution)/shard_map/ppermute | solution.py:112
  67.1 3.3 %collective-permute-start.9 = (f32[2,1,768]{2,1,0:T(1,128)}, f32[2,1,768]{2,1,0:T(1,128)S(1)}, u32[]{:S(2)}, u32[]{:S(2)}) collective-permute-start(f32[2,1,768]{2,1,0:T(1,128)} %shard_map.89.refs_3_), channel_id=1, source_target_pairs={{3,0},{0,1},{1,2},{2,3},{7,4},{4,5},{5,6},{6,7},{11,8},{8,9},{9,10... | collective-permute-start | bytes 18440 | tf_op jit(solution)/shard_map/ppermute | solution.py:112
  67.2 3.3 %collective-permute-start.8 = (f32[2,1,768]{2,1,0:T(1,128)}, f32[2,1,768]{2,1,0:T(1,128)S(1)}, u32[]{:S(2)}, u32[]{:S(2)}) collective-permute-start(f32[2,1,768]{2,1,0:T(1,128)} %shard_map.89.refs_3_), channel_id=1, source_target_pairs={{1,0},{2,1},{3,2},{0,3},{5,4},{6,5},{7,6},{4,7},{9,8},{10,9},{11,1... | collective-permute-start | bytes 18440 | tf_op jit(solution)/shard_map/ppermute | solution.py:112
  74.1 10.3 %collective-permute-start.15 = (f32[2,1,768]{2,1,0:T(1,128)}, f32[2,1,768]{2,1,0:T(1,128)S(1)}, u32[]{:S(2)}, u32[]{:S(2)}) collective-permute-start(f32[2,1,768]{2,1,0:T(1,128)} %shard_map.90.refs_3_), channel_id=1, source_target_pairs={{28,0},{0,4},{4,8},{8,12},{12,16},{16,20},{24,28},{29,1},{1,5},{5,... | collective-permute-start | bytes 18440 | tf_op jit(solution)/shard_map/ppermute | solution.py:112
  76.0 8.4 %collective-permute-start.14 = (f32[2,1,768]{2,1,0:T(1,128)}, f32[2,1,768]{2,1,0:T(1,128)S(1)}, u32[]{:S(2)}, u32[]{:S(2)}) collective-permute-start(f32[2,1,768]{2,1,0:T(1,128)} %shard_map.90.refs_3_), channel_id=1, source_target_pairs={{4,0},{8,4},{12,8},{16,12},{20,16},{28,24},{0,28},{5,1},{9,5},{13,... | collective-permute-start | bytes 18440 | tf_op jit(solution)/shard_map/ppermute | solution.py:112
  82.6 3.3 %collective-permute-start.13 = (f32[2,1,768]{2,1,0:T(1,128)}, f32[2,1,768]{2,1,0:T(1,128)S(1)}, u32[]{:S(2)}, u32[]{:S(2)}) collective-permute-start(f32[2,1,768]{2,1,0:T(1,128)} %shard_map.90.refs_3_), channel_id=1, source_target_pairs={{3,0},{0,1},{1,2},{2,3},{7,4},{4,5},{5,6},{6,7},{11,8},{8,9},{9,10... | collective-permute-start | bytes 18440 | tf_op jit(solution)/shard_map/ppermute | solution.py:112
  83.3 2.7 %collective-permute-start.12 = (f32[2,1,768]{2,1,0:T(1,128)}, f32[2,1,768]{2,1,0:T(1,128)S(1)}, u32[]{:S(2)}, u32[]{:S(2)}) collective-permute-start(f32[2,1,768]{2,1,0:T(1,128)} %shard_map.90.refs_3_), channel_id=1, source_target_pairs={{1,0},{2,1},{3,2},{0,3},{5,4},{6,5},{7,6},{4,7},{9,8},{10,9},{11,1... | collective-permute-start | bytes 18440 | tf_op jit(solution)/shard_map/ppermute | solution.py:112
  93.0 15.7 %collective-permute-start.17 = (f32[24,16,64]{2,1,0:T(8,128)S(1)}, f32[24,16,64]{2,1,0:T(8,128)S(1)}, u32[]{:S(2)}, u32[]{:S(2)}) collective-permute-start(f32[24,16,64]{2,1,0:T(8,128)S(1)} %get-tuple-element.46), channel_id=1, source_target_pairs={{3,0},{0,1},{1,2},{2,3},{7,4},{4,5},{5,6},{6,7},{11,8},{8,9},{9,10... | collective-permute-start | bytes 294920 | tf_op jit(solution)/shard_map/ppermute | solution.py:112
  93.7 15.0 %collective-permute-start.16 = (f32[24,16,64]{2,1,0:T(8,128)S(1)}, f32[24,16,64]{2,1,0:T(8,128)S(1)}, u32[]{:S(2)}, u32[]{:S(2)}) collective-permute-start(f32[24,16,64]{2,1,0:T(8,128)S(1)} %get-tuple-element.47), channel_id=1, source_target_pairs={{1,0},{2,1},{3,2},{0,3},{5,4},{6,5},{7,6},{4,7},{9,8},{10,9},{11,1... | collective-permute-start | bytes 294920 | tf_op jit(solution)/shard_map/ppermute | solution.py:112
  94.9 7.1 %collective-permute-start.18 = (f32[24,4,128]{2,1,0:T(4,128)S(1)}, f32[24,4,128]{2,1,0:T(4,128)S(1)}, u32[]{:S(2)}, u32[]{:S(2)}) collective-permute-start(f32[24,4,128]{2,1,0:T(4,128)S(1)} %slice.46), channel_id=1, source_target_pairs={{4,0},{8,4},{12,8},{16,12},{20,16},{28,24},{0,28},{5,1},{9,5},{13,... | collective-permute-start | bytes 147464 | tf_op jit(solution)/shard_map/ppermute | solution.py:112
  100.0 8.7 %collective-permute-start.19 = (f32[24,4,128]{2,1,0:T(4,128)S(1)}, f32[24,4,128]{2,1,0:T(4,128)S(1)}, u32[]{:S(2)}, u32[]{:S(2)}) collective-permute-start(f32[24,4,128]{2,1,0:T(4,128)S(1)} %slice.47), channel_id=1, source_target_pairs={{28,0},{0,4},{4,8},{8,12},{12,16},{16,20},{24,28},{29,1},{1,5},{5,... | collective-permute-start | bytes 147464 | tf_op jit(solution)/shard_map/ppermute | solution.py:112
  115.2 11.6 %collective-permute-start.20 = (f32[24,16,64]{2,1,0:T(8,128)}, f32[24,16,64]{2,1,0:T(8,128)S(1)}, u32[]{:S(2)}, u32[]{:S(2)}) collective-permute-start(f32[24,16,64]{2,1,0:T(8,128)} %get-tuple-element.30), channel_id=1, source_target_pairs={{1,0},{2,1},{3,2},{0,3},{5,4},{6,5},{7,6},{4,7},{9,8},{10,9},{11,1... | collective-permute-start | bytes 294920 | tf_op jit(solution)/shard_map/ppermute | solution.py:112
  115.2 11.6 %collective-permute-start.21 = (f32[24,16,64]{2,1,0:T(8,128)}, f32[24,16,64]{2,1,0:T(8,128)S(1)}, u32[]{:S(2)}, u32[]{:S(2)}) collective-permute-start(f32[24,16,64]{2,1,0:T(8,128)} %get-tuple-element.31), channel_id=1, source_target_pairs={{3,0},{0,1},{1,2},{2,3},{7,4},{4,5},{5,6},{6,7},{11,8},{8,9},{9,10... | collective-permute-start | bytes 294920 | tf_op jit(solution)/shard_map/ppermute | solution.py:112
  115.7 6.8 %collective-permute-start.22 = (f32[24,4,128]{2,1,0:T(4,128)}, f32[24,4,128]{2,1,0:T(4,128)S(1)}, u32[]{:S(2)}, u32[]{:S(2)}) collective-permute-start(f32[24,4,128]{2,1,0:T(4,128)} %get-tuple-element.32), channel_id=1, source_target_pairs={{4,0},{8,4},{12,8},{16,12},{20,16},{28,24},{0,28},{5,1},{9,5},{13,... | collective-permute-start | bytes 147464 | tf_op jit(solution)/shard_map/ppermute | solution.py:112
  117.6 9.2 %collective-permute-start.23 = (f32[24,4,128]{2,1,0:T(4,128)}, f32[24,4,128]{2,1,0:T(4,128)S(1)}, u32[]{:S(2)}, u32[]{:S(2)}) collective-permute-start(f32[24,4,128]{2,1,0:T(4,128)} %get-tuple-element.33), channel_id=1, source_target_pairs={{28,0},{0,4},{4,8},{8,12},{12,16},{16,20},{24,28},{29,1},{1,5},{5,... | collective-permute-start | bytes 147464 | tf_op jit(solution)/shard_map/ppermute | solution.py:112
  (20 other events, 42.7 us)

commit v8 on v6

--- a/solution.py
+++ b/solution.py
@@ -517,8 +517,6 @@
         source, link_rows, None, label_rows, colour_list, 0, None, None,
         faces=tuple(needed), link_mode="none", append_links=True,
     )
-    vectors = test_vectors.reshape(NVEC, 2, 2, 6, site_count)
-    vectors, smoothed_first = lax.optimization_barrier((vectors, smoothed_first))
     smoothed, smoothed_faces, back_rows = run_pass(
         source, link_rows, None, label_rows, colour_list, 1, smoothed_first,
         halos_of(smoothed_first, first_faces), faces=tuple(needed), link_mode="combined", emit_back=True,
@@ -543,6 +541,7 @@
     membership = member.reshape(AGG, site_count).T
     member_weights = membership.astype(jnp.bfloat16)
     weighted = residual.reshape(2, 2, 6, site_count)[..., None] * member_weights
+    vectors = test_vectors.reshape(NVEC, 2, 2, 6, site_count)
 
     def contract(left, right):
         return jnp.einsum("kxqn,xqnj->xkj", left, right, preferred_element_type=jnp.float32)

time: 126 us -> 127 us (level)
  starting transfers between devices: 43.5 us -> 49.4 us
  waiting for transfers between devices: 25.3 us -> 20.9 us
    ppermute x24, starting transfers between devices: 43.5 us -> 49.4 us  [permute_from(): return lax.ppermute(value, axis, pairs)]
    ppermute x24, waiting for transfers between devices: 25.3 us -> 20.9 us  [permute_from(): return lax.ppermute(value, axis, pairs)]
  transfers between devices with their start and end apart: 24 -> 24, of which waited for: 7 -> 6; matrix products, arithmetic and copies ran while one was open for 8% -> 8% of each run, Pallas kernels for 0% -> 0%
where the time goes in v8:
time: 127 us; the launch traced here: 126 us
  starting transfers between devices  49.4 us (39%)
  Pallas kernels  30.2 us (24%)
  waiting for transfers between devices  20.9 us (16%)
  local copies, waits for them, and re-layouts  18.7 us (15%)
  matrix products  3.42 us (3%)
  other arithmetic  2.01 us (2%)
    ppermute x24, starting transfers between devices, permute_from(): return lax.ppermute(value, axis, pairs)  49.4 us
    pallas_call x5, Pallas kernels, run_pass(): pl.pallas_call(kernel, out_shape=out_shape, scratch_shapes=scratch, in_sp...  22.4 us
    ppermute x24, waiting for transfers between devices, permute_from(): return lax.ppermute(value, axis, pairs)  20.9 us
    unnamed x59, local copies, waits for them, and re-layouts  10.7 us
    pallas_call x3, Pallas kernels, run_coarse(): pl.pallas_call(kernel, out_shape=jax.ShapeDtypeStruct(source.shape, jnp.f...  7.77 us
    reshape x1, local copies, waits for them, and re-layouts, body(): vectors = test_vectors.reshape(NVEC, 2, 2, 6, site_count)  4.03 us
    dot_general x4, matrix products, contract(): jnp.einsum('kxqn,xqnj->xkj', left, right, preferred_element_type=jnp.floa...  2.97 us
  transfers between devices with their start and end apart: 24, of which 6 were waited for; matrix products, arithmetic and copies ran while one was open for 8% of the time, Pallas kernels for 0%

profile of v8, /device:TPU:0, one launch (start us, length us, event | category | flops | bytes accessed | tf_op | source)
XLA Modules:
  0.0 125.8 jit_solution(25784056898015961)
XLA Ops:
  2.0 4.2 %shard_map.86 = (f32[24,16,128]{2,1,0:T(8,128)}, f32[24,16,64]{2,1,0:T(8,128)}, f32[42,16,64]{2,1,0:T(8,128)}, f32[24,4,128]{2,1,0:T(4,128)}, f32[42,4,128]{2,1,0:T(4,128)}) custom-call(f32[24,16,128]{2,1,0:T(8,128)} %bitcast.72, bf16[4,18,16,128]{3,2,1,0:T(8,128)(2,1)} %bitcast.65, s32[16,128]{1,0:T(8,128)} %reshape.52.refs_2_.refs_3_, s32[16]{0:T(128)} %bitcast.85), custom_call_target="tpu_custom_call" | custom-call | tf_op jit(solution)/shard_map/pallas_call | solution.py:363
  6.7 1.9 %collective-permute-start = (f32[24,16,64]{2,1,0:T(8,128)}, f32[24,16,64]{2,1,0:T(8,128)S(1)}, u32[]{:S(2)}, u32[]{:S(2)}) collective-permute-start(f32[24,16,64]{2,1,0:T(8,128)} %get-tuple-element.19), channel_id=1, source_target_pairs={{1,0},{2,1},{3,2},{0,3},{5,4},{6,5},{7,6},{4,7},{9,8},{10,9},{11,1... | collective-permute-start | bytes 294920 | tf_op jit(solution)/shard_map/ppermute | solution.py:112
  8.6 4.2 %collective-permute-start.3 = (f32[42,4,128]{2,1,0:T(4,128)}, f32[42,4,128]{2,1,0:T(4,128)S(1)}, u32[]{:S(2)}, u32[]{:S(2)}) collective-permute-start(f32[42,4,128]{2,1,0:T(4,128)} %get-tuple-element.22), channel_id=1, source_target_pairs={{28,0},{0,4},{4,8},{8,12},{12,16},{16,20},{24,28},{29,1},{1,5},{5,... | collective-permute-start | bytes 258056 | tf_op jit(solution)/shard_map/ppermute | solution.py:112
  12.9 5.0 %collective-permute-start.2 = (f32[24,4,128]{2,1,0:T(4,128)}, f32[24,4,128]{2,1,0:T(4,128)S(1)}, u32[]{:S(2)}, u32[]{:S(2)}) collective-permute-start(f32[24,4,128]{2,1,0:T(4,128)} %get-tuple-element.21), channel_id=1, source_target_pairs={{4,0},{8,4},{12,8},{16,12},{20,16},{28,24},{0,28},{5,1},{9,5},{13,... | collective-permute-start | bytes 147464 | tf_op jit(solution)/shard_map/ppermute | solution.py:112
  20.7 5.3 %shard_map.87 = (f32[24,16,128]{2,1,0:T(8,128)}, f32[24,16,64]{2,1,0:T(8,128)}, f32[24,16,64]{2,1,0:T(8,128)}, f32[24,4,128]{2,1,0:T(4,128)}, f32[24,4,128]{2,1,0:T(4,128)}, /*index=5*/bf16[4,18,16,128]{3,2,1,0:T(8,128)(2,1)}) custom-call(f32[24,16,128]{2,1,0:T(8,128)} %bitcast.73, bf16[4,18,16,128]{3,2,1,0:T(8,128)(2,1)} %bitcast.66, ...), custom_call_target="tpu_custom_call" | custom-call | tf_op jit(solution)/shard_map/pallas_call | solution.py:363
  26.6 6.8 %collective-permute-start.6 = (f32[24,4,128]{2,1,0:T(4,128)}, f32[24,4,128]{2,1,0:T(4,128)S(1)}, u32[]{:S(2)}, u32[]{:S(2)}) collective-permute-start(f32[24,4,128]{2,1,0:T(4,128)} %get-tuple-element.27), channel_id=1, source_target_pairs={{4,0},{8,4},{12,8},{16,12},{20,16},{28,24},{0,28},{5,1},{9,5},{13,... | collective-permute-start | bytes 147464 | tf_op jit(solution)/shard_map/ppermute | solution.py:112
  33.4 1.9 %collective-permute-start.7 = (f32[24,4,128]{2,1,0:T(4,128)}, f32[24,4,128]{2,1,0:T(4,128)S(1)}, u32[]{:S(2)}, u32[]{:S(2)}) collective-permute-start(f32[24,4,128]{2,1,0:T(4,128)} %get-tuple-element.28), channel_id=1, source_target_pairs={{28,0},{0,4},{4,8},{8,12},{12,16},{16,20},{24,28},{29,1},{1,5},{5,... | collective-permute-start | bytes 147464 | tf_op jit(solution)/shard_map/ppermute | solution.py:112
  35.4 4.3 %copy.13 = bf16[1,24,24,4,4,128]{5,4,3,1,2,0:T(4,128)(2,1)} copy(bf16[1,24,24,4,4,128]{5,4,3,2,1,0:T(4,128)(2,1)} %param.9) | data formatting | bytes 4718592 | tf_op args[2]
  39.7 4.0 %reshape.54 = bf16[24,2,2,6,2048]{4,0,3,2,1:T(8,128)(2,1)S(1)} reshape(bf16[1,24,24,4,4,128]{5,4,3,1,2,0:T(4,128)(2,1)} %copy.13) | data formatting | bytes 4718592 | tf_op jit(solution)/shard_map/reshape | solution.py:544
  44.5 2.7 %shard_map.88 = bf16[24,16,128]{2,1,0:T(8,128)(2,1)} custom-call(f32[24,16,128]{2,1,0:T(8,128)} %bitcast.74, bf16[4,18,16,128]{3,2,1,0:T(8,128)(2,1)} %bitcast.67, bf16[4,18,16,128]{3,2,1,0:T(8,128)(2,1)} %get-tuple-element.23.refs_2_, s32[16,128]{1,0:T(8,128)} %reshape.52.refs_2_.refs_3_, f32[24,16,128]{2,1,0:T(8,128)} %get-tuple-element.24.refs_4_, ...), custom_call_target="tpu_custom_call" | custom-call | tf_op jit(solution)/shard_map/pallas_call | solution.py:363
  55.4 6.3 %collective-permute-start.10 = (f32[2,1,768]{2,1,0:T(1,128)}, f32[2,1,768]{2,1,0:T(1,128)S(1)}, u32[]{:S(2)}, u32[]{:S(2)}) collective-permute-start(f32[2,1,768]{2,1,0:T(1,128)} %shard_map.89.refs_3_), channel_id=1, source_target_pairs={{4,0},{8,4},{12,8},{16,12},{20,16},{28,24},{0,28},{5,1},{9,5},{13,... | collective-permute-start | bytes 18440 | tf_op jit(solution)/shard_map/ppermute | solution.py:112
  61.7 1.9 %collective-permute-start.11 = (f32[2,1,768]{2,1,0:T(1,128)}, f32[2,1,768]{2,1,0:T(1,128)S(1)}, u32[]{:S(2)}, u32[]{:S(2)}) collective-permute-start(f32[2,1,768]{2,1,0:T(1,128)} %shard_map.89.refs_3_), channel_id=1, source_target_pairs={{28,0},{0,4},{4,8},{8,12},{12,16},{16,20},{24,28},{29,1},{1,5},{5,... | collective-permute-start | bytes 18440 | tf_op jit(solution)/shard_map/ppermute | solution.py:112
  63.7 6.4 %collective-permute-done.11.refs_7_ = f32[2,1,768]{2,1,0:T(1,128)S(1)} collective-permute-done((f32[2,1,768]{2,1,0:T(1,128)}, f32[2,1,768]{2,1,0:T(1,128)S(1)}, u32[]{:S(2)}, u32[]{:S(2)}) %collective-permute-start.11) | collective-permute-done | bytes 6176 | tf_op jit(solution)/shard_map/ppermute | solution.py:112
  70.8 3.0 %shard_map.90.refs_3_ = f32[2,1,768]{2,1,0:T(1,128)} custom-call(f32[2,1,768]{2,1,0:T(1,128)} %copy-done.12, bf16[2,48,768]{2,1,0:T(8,128)(2,1)} %bitcast.80, bf16[9,2,48,768]{3,2,1,0:T(8,128)(2,1)} %bitcast.70, f32[2,1,768]{2,1,0:T(1,128)} %shard_map.89.refs_3_, f32[2,1,768]{2,1,0:T(1,128)} %copy-done.21, f32[2,1,768]{2,1,0:T(1,128)} %copy-done.23, ...), custom_call_target="tpu_custom_call" | custom-call | tf_op jit(solution)/shard_map/pallas_call | solution.py:446
  76.2 4.1 %collective-permute-start.15 = (f32[2,1,768]{2,1,0:T(1,128)}, f32[2,1,768]{2,1,0:T(1,128)S(1)}, u32[]{:S(2)}, u32[]{:S(2)}) collective-permute-start(f32[2,1,768]{2,1,0:T(1,128)} %shard_map.90.refs_3_), channel_id=1, source_target_pairs={{28,0},{0,4},{4,8},{8,12},{12,16},{16,20},{24,28},{29,1},{1,5},{5,... | collective-permute-start | bytes 18440 | tf_op jit(solution)/shard_map/ppermute | solution.py:112
  80.4 4.3 %collective-permute-done.15.refs_7_ = f32[2,1,768]{2,1,0:T(1,128)S(1)} collective-permute-done((f32[2,1,768]{2,1,0:T(1,128)}, f32[2,1,768]{2,1,0:T(1,128)S(1)}, u32[]{:S(2)}, u32[]{:S(2)}) %collective-permute-start.15) | collective-permute-done | bytes 6176 | tf_op jit(solution)/shard_map/ppermute | solution.py:112
  85.2 3.0 %shard_map.91 = f32[2,1,768]{2,1,0:T(1,128)} custom-call(f32[2,1,768]{2,1,0:T(1,128)} %copy-done.12, bf16[2,48,768]{2,1,0:T(8,128)(2,1)} %bitcast.81, bf16[9,2,48,768]{3,2,1,0:T(8,128)(2,1)} %bitcast.71, f32[2,1,768]{2,1,0:T(1,128)} %shard_map.90.refs_3_, f32[2,1,768]{2,1,0:T(1,128)} %copy-done.20, f32[2,1,768]{2,1,0:T(1,128)} %copy-done.22, ...), custom_call_target="tpu_custom_call" | custom-call | tf_op jit(solution)/shard_map/pallas_call | solution.py:446
  91.6 1.9 %collective-permute-start.18 = (f32[24,4,128]{2,1,0:T(4,128)S(1)}, f32[24,4,128]{2,1,0:T(4,128)S(1)}, u32[]{:S(2)}, u32[]{:S(2)}) collective-permute-start(f32[24,4,128]{2,1,0:T(4,128)S(1)} %slice.48), channel_id=1, source_target_pairs={{4,0},{8,4},{12,8},{16,12},{20,16},{28,24},{0,28},{5,1},{9,5},{13,... | collective-permute-start | bytes 147464 | tf_op jit(solution)/shard_map/ppermute | solution.py:112
  93.5 3.9 %collective-permute-start.19 = (f32[24,4,128]{2,1,0:T(4,128)S(1)}, f32[24,4,128]{2,1,0:T(4,128)S(1)}, u32[]{:S(2)}, u32[]{:S(2)}) collective-permute-start(f32[24,4,128]{2,1,0:T(4,128)S(1)} %slice.49), channel_id=1, source_target_pairs={{28,0},{0,4},{4,8},{8,12},{12,16},{16,20},{24,28},{29,1},{1,5},{5,... | collective-permute-start | bytes 147464 | tf_op jit(solution)/shard_map/ppermute | solution.py:112
  97.6 4.6 %collective-permute-done.19.refs_9_ = f32[24,4,128]{2,1,0:T(4,128)S(1)} collective-permute-done((f32[24,4,128]{2,1,0:T(4,128)S(1)}, f32[24,4,128]{2,1,0:T(4,128)S(1)}, u32[]{:S(2)}, u32[]{:S(2)}) %collective-permute-start.19) | collective-permute-done | bytes 49184 | tf_op jit(solution)/shard_map/ppermute | solution.py:112
  103.6 5.2 %shard_map.92 = (f32[24,16,128]{2,1,0:T(8,128)}, f32[24,16,64]{2,1,0:T(8,128)}, f32[24,16,64]{2,1,0:T(8,128)}, f32[24,4,128]{2,1,0:T(4,128)}, f32[24,4,128]{2,1,0:T(4,128)}) custom-call(f32[24,16,128]{2,1,0:T(8,128)} %bitcast.75, bf16[4,18,16,128]{3,2,1,0:T(8,128)(2,1)} %bitcast.68, bf16[4,18,16,128]{3,2,1,0:T(8,128)(2,1)} %get-tuple-element.23.refs_2_, ...), custom_call_target="tpu_custom_call" | custom-call | tf_op jit(solution)/shard_map/pallas_call | solution.py:363
  111.2 3.9 %collective-permute-start.23 = (f32[24,4,128]{2,1,0:T(4,128)}, f32[24,4,128]{2,1,0:T(4,128)S(1)}, u32[]{:S(2)}, u32[]{:S(2)}) collective-permute-start(f32[24,4,128]{2,1,0:T(4,128)} %get-tuple-element.33), channel_id=1, source_target_pairs={{28,0},{0,4},{4,8},{8,12},{12,16},{16,20},{24,28},{29,1},{1,5},{5,... | collective-permute-start | bytes 147464 | tf_op jit(solution)/shard_map/ppermute | solution.py:112
  115.9 4.2 %collective-permute-done.23.refs_9_ = f32[24,4,128]{2,1,0:T(4,128)S(1)} collective-permute-done((f32[24,4,128]{2,1,0:T(4,128)}, f32[24,4,128]{2,1,0:T(4,128)S(1)}, u32[]{:S(2)}, u32[]{:S(2)}) %collective-permute-start.23) | collective-permute-done | bytes 49184 | tf_op jit(solution)/shard_map/ppermute | solution.py:112
  120.8 5.0 %shard_map.93 = f32[24,16,128]{2,1,0:T(8,128)} custom-call(f32[24,16,128]{2,1,0:T(8,128)} %bitcast.76, bf16[4,18,16,128]{3,2,1,0:T(8,128)(2,1)} %bitcast.69, bf16[4,18,16,128]{3,2,1,0:T(8,128)(2,1)} %get-tuple-element.23.refs_2_, s32[16,128]{1,0:T(8,128)} %reshape.52.refs_2_.refs_3_, s32[16]{0:T(128)} %bitcast.88, f32[24,16,128]{2,1,0:T(8,128)} %get-tuple-element.29.refs_5_, ...), custom_call_target="tpu_custom_call" | custom-call | tf_op jit(solution)/shard_map/pallas_call | solution.py:363
  (118 shorter events, 26.5 us)
Async XLA Ops:
  6.2 13.7 %collective-permute-start.1 = (f32[42,16,64]{2,1,0:T(8,128)}, f32[42,16,64]{2,1,0:T(8,128)S(1)}, u32[]{:S(2)}, u32[]{:S(2)}) collective-permute-start(f32[42,16,64]{2,1,0:T(8,128)} %get-tuple-element.20), channel_id=1, source_target_pairs={{3,0},{0,1},{1,2},{2,3},{7,4},{4,5},{5,6},{6,7},{11,8},{8,9},{9,10... | collective-permute-start | bytes 516104 | tf_op jit(solution)/shard_map/ppermute | solution.py:112
  6.7 13.2 %collective-permute-start = (f32[24,16,64]{2,1,0:T(8,128)}, f32[24,16,64]{2,1,0:T(8,128)S(1)}, u32[]{:S(2)}, u32[]{:S(2)}) collective-permute-start(f32[24,16,64]{2,1,0:T(8,128)} %get-tuple-element.19), channel_id=1, source_target_pairs={{1,0},{2,1},{3,2},{0,3},{5,4},{6,5},{7,6},{4,7},{9,8},{10,9},{11,1... | collective-permute-start | bytes 294920 | tf_op jit(solution)/shard_map/ppermute | solution.py:112
  8.6 11.3 %collective-permute-start.3 = (f32[42,4,128]{2,1,0:T(4,128)}, f32[42,4,128]{2,1,0:T(4,128)S(1)}, u32[]{:S(2)}, u32[]{:S(2)}) collective-permute-start(f32[42,4,128]{2,1,0:T(4,128)} %get-tuple-element.22), channel_id=1, source_target_pairs={{28,0},{0,4},{4,8},{8,12},{12,16},{16,20},{24,28},{29,1},{1,5},{5,... | collective-permute-start | bytes 258056 | tf_op jit(solution)/shard_map/ppermute | solution.py:112
  12.9 7.0 %collective-permute-start.2 = (f32[24,4,128]{2,1,0:T(4,128)}, f32[24,4,128]{2,1,0:T(4,128)S(1)}, u32[]{:S(2)}, u32[]{:S(2)}) collective-permute-start(f32[24,4,128]{2,1,0:T(4,128)} %get-tuple-element.21), channel_id=1, source_target_pairs={{4,0},{8,4},{12,8},{16,12},{20,16},{28,24},{0,28},{5,1},{9,5},{13,... | collective-permute-start | bytes 147464 | tf_op jit(solution)/shard_map/ppermute | solution.py:112
  26.1 17.7 %collective-permute-start.4 = (f32[24,16,64]{2,1,0:T(8,128)}, f32[24,16,64]{2,1,0:T(8,128)S(1)}, u32[]{:S(2)}, u32[]{:S(2)}) collective-permute-start(f32[24,16,64]{2,1,0:T(8,128)} %get-tuple-element.25), channel_id=1, source_target_pairs={{1,0},{2,1},{3,2},{0,3},{5,4},{6,5},{7,6},{4,7},{9,8},{10,9},{11,1... | collective-permute-start | bytes 294920 | tf_op jit(solution)/shard_map/ppermute | solution.py:112
  26.1 17.7 %collective-permute-start.5 = (f32[24,16,64]{2,1,0:T(8,128)}, f32[24,16,64]{2,1,0:T(8,128)S(1)}, u32[]{:S(2)}, u32[]{:S(2)}) collective-permute-start(f32[24,16,64]{2,1,0:T(8,128)} %get-tuple-element.26), channel_id=1, source_target_pairs={{3,0},{0,1},{1,2},{2,3},{7,4},{4,5},{5,6},{6,7},{11,8},{8,9},{9,10... | collective-permute-start | bytes 294920 | tf_op jit(solution)/shard_map/ppermute | solution.py:112
  26.6 17.1 %collective-permute-start.6 = (f32[24,4,128]{2,1,0:T(4,128)}, f32[24,4,128]{2,1,0:T(4,128)S(1)}, u32[]{:S(2)}, u32[]{:S(2)}) collective-permute-start(f32[24,4,128]{2,1,0:T(4,128)} %get-tuple-element.27), channel_id=1, source_target_pairs={{4,0},{8,4},{12,8},{16,12},{20,16},{28,24},{0,28},{5,1},{9,5},{13,... | collective-permute-start | bytes 147464 | tf_op jit(solution)/shard_map/ppermute | solution.py:112
  33.4 10.3 %collective-permute-start.7 = (f32[24,4,128]{2,1,0:T(4,128)}, f32[24,4,128]{2,1,0:T(4,128)S(1)}, u32[]{:S(2)}, u32[]{:S(2)}) collective-permute-start(f32[24,4,128]{2,1,0:T(4,128)} %get-tuple-element.28), channel_id=1, source_target_pairs={{28,0},{0,4},{4,8},{8,12},{12,16},{16,20},{24,28},{29,1},{1,5},{5,... | collective-permute-start | bytes 147464 | tf_op jit(solution)/shard_map/ppermute | solution.py:112
  54.4 9.3 %collective-permute-start.8 = (f32[2,1,768]{2,1,0:T(1,128)}, f32[2,1,768]{2,1,0:T(1,128)S(1)}, u32[]{:S(2)}, u32[]{:S(2)}) collective-permute-start(f32[2,1,768]{2,1,0:T(1,128)} %shard_map.89.refs_3_), channel_id=1, source_target_pairs={{1,0},{2,1},{3,2},{0,3},{5,4},{6,5},{7,6},{4,7},{9,8},{10,9},{11,1... | collective-permute-start | bytes 18440 | tf_op jit(solution)/shard_map/ppermute | solution.py:112
  55.4 8.3 %collective-permute-start.9 = (f32[2,1,768]{2,1,0:T(1,128)}, f32[2,1,768]{2,1,0:T(1,128)S(1)}, u32[]{:S(2)}, u32[]{:S(2)}) collective-permute-start(f32[2,1,768]{2,1,0:T(1,128)} %shard_map.89.refs_3_), channel_id=1, source_target_pairs={{3,0},{0,1},{1,2},{2,3},{7,4},{4,5},{5,6},{6,7},{11,8},{8,9},{9,10... | collective-permute-start | bytes 18440 | tf_op jit(solution)/shard_map/ppermute | solution.py:112
  55.4 8.3 %collective-permute-start.10 = (f32[2,1,768]{2,1,0:T(1,128)}, f32[2,1,768]{2,1,0:T(1,128)S(1)}, u32[]{:S(2)}, u32[]{:S(2)}) collective-permute-start(f32[2,1,768]{2,1,0:T(1,128)} %shard_map.89.refs_3_), channel_id=1, source_target_pairs={{4,0},{8,4},{12,8},{16,12},{20,16},{28,24},{0,28},{5,1},{9,5},{13,... | collective-permute-start | bytes 18440 | tf_op jit(solution)/shard_map/ppermute | solution.py:112
  61.7 8.4 %collective-permute-start.11 = (f32[2,1,768]{2,1,0:T(1,128)}, f32[2,1,768]{2,1,0:T(1,128)S(1)}, u32[]{:S(2)}, u32[]{:S(2)}) collective-permute-start(f32[2,1,768]{2,1,0:T(1,128)} %shard_map.89.refs_3_), channel_id=1, source_target_pairs={{28,0},{0,4},{4,8},{8,12},{12,16},{16,20},{24,28},{29,1},{1,5},{5,... | collective-permute-start | bytes 18440 | tf_op jit(solution)/shard_map/ppermute | solution.py:112
  73.8 6.5 %collective-permute-start.12 = (f32[2,1,768]{2,1,0:T(1,128)}, f32[2,1,768]{2,1,0:T(1,128)S(1)}, u32[]{:S(2)}, u32[]{:S(2)}) collective-permute-start(f32[2,1,768]{2,1,0:T(1,128)} %shard_map.90.refs_3_), channel_id=1, source_target_pairs={{1,0},{2,1},{3,2},{0,3},{5,4},{6,5},{7,6},{4,7},{9,8},{10,9},{11,1... | collective-permute-start | bytes 18440 | tf_op jit(solution)/shard_map/ppermute | solution.py:112
  74.1 6.3 %collective-permute-start.13 = (f32[2,1,768]{2,1,0:T(1,128)}, f32[2,1,768]{2,1,0:T(1,128)S(1)}, u32[]{:S(2)}, u32[]{:S(2)}) collective-permute-start(f32[2,1,768]{2,1,0:T(1,128)} %shard_map.90.refs_3_), channel_id=1, source_target_pairs={{3,0},{0,1},{1,2},{2,3},{7,4},{4,5},{5,6},{6,7},{11,8},{8,9},{9,10... | collective-permute-start | bytes 18440 | tf_op jit(solution)/shard_map/ppermute | solution.py:112
  74.3 6.1 %collective-permute-start.14 = (f32[2,1,768]{2,1,0:T(1,128)}, f32[2,1,768]{2,1,0:T(1,128)S(1)}, u32[]{:S(2)}, u32[]{:S(2)}) collective-permute-start(f32[2,1,768]{2,1,0:T(1,128)} %shard_map.90.refs_3_), channel_id=1, source_target_pairs={{4,0},{8,4},{12,8},{16,12},{20,16},{28,24},{0,28},{5,1},{9,5},{13,... | collective-permute-start | bytes 18440 | tf_op jit(solution)/shard_map/ppermute | solution.py:112
  76.2 8.4 %collective-permute-start.15 = (f32[2,1,768]{2,1,0:T(1,128)}, f32[2,1,768]{2,1,0:T(1,128)S(1)}, u32[]{:S(2)}, u32[]{:S(2)}) collective-permute-start(f32[2,1,768]{2,1,0:T(1,128)} %shard_map.90.refs_3_), channel_id=1, source_target_pairs={{28,0},{0,4},{4,8},{8,12},{12,16},{16,20},{24,28},{29,1},{1,5},{5,... | collective-permute-start | bytes 18440 | tf_op jit(solution)/shard_map/ppermute | solution.py:112
  90.9 11.3 %collective-permute-start.16 = (f32[24,16,64]{2,1,0:T(8,128)S(1)}, f32[24,16,64]{2,1,0:T(8,128)S(1)}, u32[]{:S(2)}, u32[]{:S(2)}) collective-permute-start(f32[24,16,64]{2,1,0:T(8,128)S(1)} %get-tuple-element.43), channel_id=1, source_target_pairs={{1,0},{2,1},{3,2},{0,3},{5,4},{6,5},{7,6},{4,7},{9,8},{10,9},{11,1... | collective-permute-start | bytes 294920 | tf_op jit(solution)/shard_map/ppermute | solution.py:112
  91.4 10.8 %collective-permute-start.17 = (f32[24,16,64]{2,1,0:T(8,128)S(1)}, f32[24,16,64]{2,1,0:T(8,128)S(1)}, u32[]{:S(2)}, u32[]{:S(2)}) collective-permute-start(f32[24,16,64]{2,1,0:T(8,128)S(1)} %get-tuple-element.42), channel_id=1, source_target_pairs={{3,0},{0,1},{1,2},{2,3},{7,4},{4,5},{5,6},{6,7},{11,8},{8,9},{9,10... | collective-permute-start | bytes 294920 | tf_op jit(solution)/shard_map/ppermute | solution.py:112
  91.6 6.0 %collective-permute-start.18 = (f32[24,4,128]{2,1,0:T(4,128)S(1)}, f32[24,4,128]{2,1,0:T(4,128)S(1)}, u32[]{:S(2)}, u32[]{:S(2)}) collective-permute-start(f32[24,4,128]{2,1,0:T(4,128)S(1)} %slice.48), channel_id=1, source_target_pairs={{4,0},{8,4},{12,8},{16,12},{20,16},{28,24},{0,28},{5,1},{9,5},{13,... | collective-permute-start | bytes 147464 | tf_op jit(solution)/shard_map/ppermute | solution.py:112
  93.5 8.7 %collective-permute-start.19 = (f32[24,4,128]{2,1,0:T(4,128)S(1)}, f32[24,4,128]{2,1,0:T(4,128)S(1)}, u32[]{:S(2)}, u32[]{:S(2)}) collective-permute-start(f32[24,4,128]{2,1,0:T(4,128)S(1)} %slice.49), channel_id=1, source_target_pairs={{28,0},{0,4},{4,8},{8,12},{12,16},{16,20},{24,28},{29,1},{1,5},{5,... | collective-permute-start | bytes 147464 | tf_op jit(solution)/shard_map/ppermute | solution.py:112
  108.7 11.4 %collective-permute-start.20 = (f32[24,16,64]{2,1,0:T(8,128)}, f32[24,16,64]{2,1,0:T(8,128)S(1)}, u32[]{:S(2)}, u32[]{:S(2)}) collective-permute-start(f32[24,16,64]{2,1,0:T(8,128)} %get-tuple-element.30), channel_id=1, source_target_pairs={{1,0},{2,1},{3,2},{0,3},{5,4},{6,5},{7,6},{4,7},{9,8},{10,9},{11,1... | collective-permute-start | bytes 294920 | tf_op jit(solution)/shard_map/ppermute | solution.py:112
  109.2 10.9 %collective-permute-start.21 = (f32[24,16,64]{2,1,0:T(8,128)}, f32[24,16,64]{2,1,0:T(8,128)S(1)}, u32[]{:S(2)}, u32[]{:S(2)}) collective-permute-start(f32[24,16,64]{2,1,0:T(8,128)} %get-tuple-element.31), channel_id=1, source_target_pairs={{3,0},{0,1},{1,2},{2,3},{7,4},{4,5},{5,6},{6,7},{11,8},{8,9},{9,10... | collective-permute-start | bytes 294920 | tf_op jit(solution)/shard_map/ppermute | solution.py:112
  109.3 6.6 %collective-permute-start.22 = (f32[24,4,128]{2,1,0:T(4,128)}, f32[24,4,128]{2,1,0:T(4,128)S(1)}, u32[]{:S(2)}, u32[]{:S(2)}) collective-permute-start(f32[24,4,128]{2,1,0:T(4,128)} %get-tuple-element.32), channel_id=1, source_target_pairs={{4,0},{8,4},{12,8},{16,12},{20,16},{28,24},{0,28},{5,1},{9,5},{13,... | collective-permute-start | bytes 147464 | tf_op jit(solution)/shard_map/ppermute | solution.py:112
  111.2 8.9 %collective-permute-start.23 = (f32[24,4,128]{2,1,0:T(4,128)}, f32[24,4,128]{2,1,0:T(4,128)S(1)}, u32[]{:S(2)}, u32[]{:S(2)}) collective-permute-start(f32[24,4,128]{2,1,0:T(4,128)} %get-tuple-element.33), channel_id=1, source_target_pairs={{28,0},{0,4},{4,8},{8,12},{12,16},{16,20},{24,28},{29,1},{1,5},{5,... | collective-permute-start | bytes 147464 | tf_op jit(solution)/shard_map/ppermute | solution.py:112
  (28 other events, 66.3 us)

commit v9 on v6

--- a/solution.py
+++ b/solution.py
@@ -544,11 +544,9 @@
     member_weights = membership.astype(jnp.bfloat16)
     weighted = residual.reshape(2, 2, 6, site_count)[..., None] * member_weights
 
-    def contract(left, right):
-        return jnp.einsum("kxqn,xqnj->xkj", left, right, preferred_element_type=jnp.float32)
-
-    real_part = contract(vectors[:, 0], weighted[0]) + contract(vectors[:, 1], weighted[1])
-    imag_part = contract(vectors[:, 0], weighted[1]) - contract(vectors[:, 1], weighted[0])
+    pairs = jnp.einsum("krxqn,sxqnj->rsxkj", vectors, weighted, preferred_element_type=jnp.float32)
+    real_part = pairs[0, 0] + pairs[1, 1]
+    imag_part = pairs[0, 1] - pairs[1, 0]
     coarse_source = jnp.stack([real_part, imag_part]).reshape(2, CDOF, AGG)
     flat_source = coarse_source.reshape(2, 1, CDOF * AGG)
     operator_blocks = coarse_operator.reshape(9, 2, CDOF, CDOF * AGG)

time: 126 us -> 125 us (level)
    dot_general x4 -> x1, matrix products: 3 us -> 2.5 us  [body(): jnp.einsum('krxqn,sxqnj->rsxkj', vectors, weighted, preferred_element_typ...]
    unnamed x59 -> x57, local copies, waits for them, and re-layouts: 11.2 us -> 11.1 us
where the time goes in v9:
time: 125 us; the launch traced here: 124 us
  starting transfers between devices  43.5 us (35%)
  Pallas kernels  30.2 us (24%)
  waiting for transfers between devices  25.3 us (20%)
  local copies, waits for them, and re-layouts  19.1 us (15%)
  matrix products  2.95 us (2%)
  other arithmetic  1.91 us (2%)
    ppermute x24, starting transfers between devices, permute_from(): return lax.ppermute(value, axis, pairs)  43.5 us
    ppermute x24, waiting for transfers between devices, permute_from(): return lax.ppermute(value, axis, pairs)  25.3 us
    pallas_call x5, Pallas kernels, run_pass(): pl.pallas_call(kernel, out_shape=out_shape, scratch_shapes=scratch, in_sp...  22.5 us
    unnamed x57, local copies, waits for them, and re-layouts  11.1 us
    pallas_call x3, Pallas kernels, run_coarse(): pl.pallas_call(kernel, out_shape=jax.ShapeDtypeStruct(source.shape, jnp.f...  7.77 us
    reshape x1, local copies, waits for them, and re-layouts, body(): vectors = test_vectors.reshape(NVEC, 2, 2, 6, site_count)  4.03 us
    dot_general x1, matrix products, body(): jnp.einsum('krxqn,sxqnj->rsxkj', vectors, weighted, preferred_element_typ...  2.5 us
  transfers between devices with their start and end apart: 24, of which 7 were waited for; matrix products, arithmetic and copies ran while one was open for 8% of the time, Pallas kernels for 0%

profile of v9, /device:TPU:0, one launch (start us, length us, event | category | flops | bytes accessed | tf_op | source)
XLA Modules:
  0.0 124.2 jit_solution(18389940087843639860)
XLA Ops:
  2.0 4.2 %shard_map.86 = (f32[24,16,128]{2,1,0:T(8,128)}, f32[24,16,64]{2,1,0:T(8,128)}, f32[42,16,64]{2,1,0:T(8,128)}, f32[24,4,128]{2,1,0:T(4,128)}, f32[42,4,128]{2,1,0:T(4,128)}) custom-call(f32[24,16,128]{2,1,0:T(8,128)} %bitcast.52, bf16[4,18,16,128]{3,2,1,0:T(8,128)(2,1)} %bitcast.45, s32[16,128]{1,0:T(8,128)} %reshape.94.refs_2_.refs_3_, s32[16]{0:T(128)} %bitcast.65), custom_call_target="tpu_custom_call" | custom-call | tf_op jit(solution)/shard_map/pallas_call | solution.py:363
  6.7 1.9 %collective-permute-start = (f32[24,16,64]{2,1,0:T(8,128)}, f32[24,16,64]{2,1,0:T(8,128)S(1)}, u32[]{:S(2)}, u32[]{:S(2)}) collective-permute-start(f32[24,16,64]{2,1,0:T(8,128)} %get-tuple-element.22), channel_id=1, source_target_pairs={{1,0},{2,1},{3,2},{0,3},{5,4},{6,5},{7,6},{4,7},{9,8},{10,9},{11,1... | collective-permute-start | bytes 294920 | tf_op jit(solution)/shard_map/ppermute | solution.py:112
  8.6 4.2 %collective-permute-start.3 = (f32[42,4,128]{2,1,0:T(4,128)}, f32[42,4,128]{2,1,0:T(4,128)S(1)}, u32[]{:S(2)}, u32[]{:S(2)}) collective-permute-start(f32[42,4,128]{2,1,0:T(4,128)} %get-tuple-element.25), channel_id=1, source_target_pairs={{28,0},{0,4},{4,8},{8,12},{12,16},{16,20},{24,28},{29,1},{1,5},{5,... | collective-permute-start | bytes 258056 | tf_op jit(solution)/shard_map/ppermute | solution.py:112
  12.9 5.0 %collective-permute-start.2 = (f32[24,4,128]{2,1,0:T(4,128)}, f32[24,4,128]{2,1,0:T(4,128)S(1)}, u32[]{:S(2)}, u32[]{:S(2)}) collective-permute-start(f32[24,4,128]{2,1,0:T(4,128)} %get-tuple-element.24), channel_id=1, source_target_pairs={{4,0},{8,4},{12,8},{16,12},{20,16},{28,24},{0,28},{5,1},{9,5},{13,... | collective-permute-start | bytes 147464 | tf_op jit(solution)/shard_map/ppermute | solution.py:112
  18.6 4.3 %copy.17 = bf16[1,24,24,4,4,128]{5,4,3,1,2,0:T(4,128)(2,1)} copy(bf16[1,24,24,4,4,128]{5,4,3,2,1,0:T(4,128)(2,1)} %param.9) | data formatting | bytes 4718592 | tf_op args[2]
  22.9 4.0 %reshape.96 = bf16[24,2,2,6,2048]{4,0,3,2,1:T(8,128)(2,1)S(1)} reshape(bf16[1,24,24,4,4,128]{5,4,3,1,2,0:T(4,128)(2,1)} %copy.17) | data formatting | bytes 4718592 | tf_op jit(solution)/shard_map/reshape | solution.py:520
  28.5 5.4 %shard_map.87 = (f32[24,16,128]{2,1,0:T(8,128)}, f32[24,16,64]{2,1,0:T(8,128)}, f32[24,16,64]{2,1,0:T(8,128)}, f32[24,4,128]{2,1,0:T(4,128)}, f32[24,4,128]{2,1,0:T(4,128)}, /*index=5*/bf16[4,18,16,128]{3,2,1,0:T(8,128)(2,1)}) custom-call(f32[24,16,128]{2,1,0:T(8,128)} %bitcast.53, bf16[4,18,16,128]{3,2,1,0:T(8,128)(2,1)} %bitcast.46, ...), custom_call_target="tpu_custom_call" | custom-call | tf_op jit(solution)/shard_map/pallas_call | solution.py:363
  34.3 3.9 %collective-permute-start.6 = (f32[24,4,128]{2,1,0:T(4,128)}, f32[24,4,128]{2,1,0:T(4,128)S(1)}, u32[]{:S(2)}, u32[]{:S(2)}) collective-permute-start(f32[24,4,128]{2,1,0:T(4,128)} %get-tuple-element.31), channel_id=1, source_target_pairs={{4,0},{8,4},{12,8},{16,12},{20,16},{28,24},{0,28},{5,1},{9,5},{13,... | collective-permute-start | bytes 147464 | tf_op jit(solution)/shard_map/ppermute | solution.py:112
  40.7 6.9 %collective-permute-done.7.refs_8_ = f32[24,4,128]{2,1,0:T(4,128)S(1)} collective-permute-done((f32[24,4,128]{2,1,0:T(4,128)}, f32[24,4,128]{2,1,0:T(4,128)S(1)}, u32[]{:S(2)}, u32[]{:S(2)}) %collective-permute-start.7) | collective-permute-done | bytes 49184 | tf_op jit(solution)/shard_map/ppermute | solution.py:112
  48.3 2.7 %shard_map.88 = bf16[24,16,128]{2,1,0:T(8,128)(2,1)} custom-call(f32[24,16,128]{2,1,0:T(8,128)} %bitcast.54, bf16[4,18,16,128]{3,2,1,0:T(8,128)(2,1)} %bitcast.47, bf16[4,18,16,128]{3,2,1,0:T(8,128)(2,1)} %get-tuple-element.26.refs_2_, s32[16,128]{1,0:T(8,128)} %reshape.94.refs_2_.refs_3_, f32[24,16,128]{2,1,0:T(8,128)} %get-tuple-element.27.refs_4_, ...), custom_call_target="tpu_custom_call" | custom-call | tf_op jit(solution)/shard_map/pallas_call | solution.py:363
  52.1 2.5 %fusion.8 = f32[2,2,2,24,16]{3,4,0,1,2:T(8,128)S(1)} fusion(bf16[2048,16]{0,1:T(8,128)(2,1)S(1)} %convert_convert_fusion, bf16[24,2,2,6,2048]{4,0,3,2,1:T(8,128)(2,1)S(1)} %reshape.96, bf16[2,2,6,2048]{3,2,1,0:T(8,128)(2,1)S(1)} %mul.20), kind=kOutput, calls=%fused_computation.12 | convolution fusion | flops 78643200 | bytes 2535424 | tf_op jit(solution)/shard_map/krxqn,sxqnj->rsxkj/dot_general | solution.py:547
  59.8 3.9 %collective-permute-start.11 = (f32[2,1,768]{2,1,0:T(1,128)}, f32[2,1,768]{2,1,0:T(1,128)S(1)}, u32[]{:S(2)}, u32[]{:S(2)}) collective-permute-start(f32[2,1,768]{2,1,0:T(1,128)} %shard_map.89.refs_3_), channel_id=1, source_target_pairs={{28,0},{0,4},{4,8},{8,12},{12,16},{16,20},{24,28},{29,1},{1,5},{5,... | collective-permute-start | bytes 18440 | tf_op jit(solution)/shard_map/ppermute | solution.py:112
  63.8 4.4 %collective-permute-done.11.refs_7_ = f32[2,1,768]{2,1,0:T(1,128)S(1)} collective-permute-done((f32[2,1,768]{2,1,0:T(1,128)}, f32[2,1,768]{2,1,0:T(1,128)S(1)}, u32[]{:S(2)}, u32[]{:S(2)}) %collective-permute-start.11) | collective-permute-done | bytes 6176 | tf_op jit(solution)/shard_map/ppermute | solution.py:112
  68.8 3.0 %shard_map.90.refs_3_ = f32[2,1,768]{2,1,0:T(1,128)} custom-call(f32[2,1,768]{2,1,0:T(1,128)} %copy-done.11, bf16[2,48,768]{2,1,0:T(8,128)(2,1)} %bitcast.60, bf16[9,2,48,768]{3,2,1,0:T(8,128)(2,1)} %bitcast.50, f32[2,1,768]{2,1,0:T(1,128)} %shard_map.89.refs_3_, f32[2,1,768]{2,1,0:T(1,128)} %copy-done.20, f32[2,1,768]{2,1,0:T(1,128)} %copy-done.22, ...), custom_call_target="tpu_custom_call" | custom-call | tf_op jit(solution)/shard_map/pallas_call | solution.py:446
  74.2 4.1 %collective-permute-start.15 = (f32[2,1,768]{2,1,0:T(1,128)}, f32[2,1,768]{2,1,0:T(1,128)S(1)}, u32[]{:S(2)}, u32[]{:S(2)}) collective-permute-start(f32[2,1,768]{2,1,0:T(1,128)} %shard_map.90.refs_3_), channel_id=1, source_target_pairs={{28,0},{0,4},{4,8},{8,12},{12,16},{16,20},{24,28},{29,1},{1,5},{5,... | collective-permute-start | bytes 18440 | tf_op jit(solution)/shard_map/ppermute | solution.py:112
  78.4 4.3 %collective-permute-done.15.refs_7_ = f32[2,1,768]{2,1,0:T(1,128)S(1)} collective-permute-done((f32[2,1,768]{2,1,0:T(1,128)}, f32[2,1,768]{2,1,0:T(1,128)S(1)}, u32[]{:S(2)}, u32[]{:S(2)}) %collective-permute-start.15) | collective-permute-done | bytes 6176 | tf_op jit(solution)/shard_map/ppermute | solution.py:112
  83.3 3.0 %shard_map.91 = f32[2,1,768]{2,1,0:T(1,128)} custom-call(f32[2,1,768]{2,1,0:T(1,128)} %copy-done.11, bf16[2,48,768]{2,1,0:T(8,128)(2,1)} %bitcast.61, bf16[9,2,48,768]{3,2,1,0:T(8,128)(2,1)} %bitcast.51, f32[2,1,768]{2,1,0:T(1,128)} %shard_map.90.refs_3_, f32[2,1,768]{2,1,0:T(1,128)} %copy-done.19, f32[2,1,768]{2,1,0:T(1,128)} %copy-done.21, ...), custom_call_target="tpu_custom_call" | custom-call | tf_op jit(solution)/shard_map/pallas_call | solution.py:446
  89.6 1.9 %collective-permute-start.18 = (f32[24,4,128]{2,1,0:T(4,128)S(1)}, f32[24,4,128]{2,1,0:T(4,128)S(1)}, u32[]{:S(2)}, u32[]{:S(2)}) collective-permute-start(f32[24,4,128]{2,1,0:T(4,128)S(1)} %slice.50), channel_id=1, source_target_pairs={{4,0},{8,4},{12,8},{16,12},{20,16},{28,24},{0,28},{5,1},{9,5},{13,... | collective-permute-start | bytes 147464 | tf_op jit(solution)/shard_map/ppermute | solution.py:112
  91.6 3.9 %collective-permute-start.19 = (f32[24,4,128]{2,1,0:T(4,128)S(1)}, f32[24,4,128]{2,1,0:T(4,128)S(1)}, u32[]{:S(2)}, u32[]{:S(2)}) collective-permute-start(f32[24,4,128]{2,1,0:T(4,128)S(1)} %slice.51), channel_id=1, source_target_pairs={{28,0},{0,4},{4,8},{8,12},{12,16},{16,20},{24,28},{29,1},{1,5},{5,... | collective-permute-start | bytes 147464 | tf_op jit(solution)/shard_map/ppermute | solution.py:112
  95.7 4.6 %collective-permute-done.19.refs_9_ = f32[24,4,128]{2,1,0:T(4,128)S(1)} collective-permute-done((f32[24,4,128]{2,1,0:T(4,128)S(1)}, f32[24,4,128]{2,1,0:T(4,128)S(1)}, u32[]{:S(2)}, u32[]{:S(2)}) %collective-permute-start.19) | collective-permute-done | bytes 49184 | tf_op jit(solution)/shard_map/ppermute | solution.py:112
  101.8 5.2 %shard_map.92 = (f32[24,16,128]{2,1,0:T(8,128)}, f32[24,16,64]{2,1,0:T(8,128)}, f32[24,16,64]{2,1,0:T(8,128)}, f32[24,4,128]{2,1,0:T(4,128)}, f32[24,4,128]{2,1,0:T(4,128)}) custom-call(f32[24,16,128]{2,1,0:T(8,128)} %bitcast.55, bf16[4,18,16,128]{3,2,1,0:T(8,128)(2,1)} %bitcast.48, bf16[4,18,16,128]{3,2,1,0:T(8,128)(2,1)} %get-tuple-element.26.refs_2_, ...), custom_call_target="tpu_custom_call" | custom-call | tf_op jit(solution)/shard_map/pallas_call | solution.py:363
  109.4 3.9 %collective-permute-start.23 = (f32[24,4,128]{2,1,0:T(4,128)}, f32[24,4,128]{2,1,0:T(4,128)S(1)}, u32[]{:S(2)}, u32[]{:S(2)}) collective-permute-start(f32[24,4,128]{2,1,0:T(4,128)} %get-tuple-element.37), channel_id=1, source_target_pairs={{28,0},{0,4},{4,8},{8,12},{12,16},{16,20},{24,28},{29,1},{1,5},{5,... | collective-permute-start | bytes 147464 | tf_op jit(solution)/shard_map/ppermute | solution.py:112
  114.1 4.3 %collective-permute-done.23.refs_9_ = f32[24,4,128]{2,1,0:T(4,128)S(1)} collective-permute-done((f32[24,4,128]{2,1,0:T(4,128)}, f32[24,4,128]{2,1,0:T(4,128)S(1)}, u32[]{:S(2)}, u32[]{:S(2)}) %collective-permute-start.23) | collective-permute-done | bytes 49184 | tf_op jit(solution)/shard_map/ppermute | solution.py:112
  119.2 5.0 %shard_map.93 = f32[24,16,128]{2,1,0:T(8,128)} custom-call(f32[24,16,128]{2,1,0:T(8,128)} %bitcast.56, bf16[4,18,16,128]{3,2,1,0:T(8,128)(2,1)} %bitcast.49, bf16[4,18,16,128]{3,2,1,0:T(8,128)(2,1)} %get-tuple-element.26.refs_2_, s32[16,128]{1,0:T(8,128)} %reshape.94.refs_2_.refs_3_, s32[16]{0:T(128)} %bitcast.68, f32[24,16,128]{2,1,0:T(8,128)} %get-tuple-element.33.refs_5_, ...), custom_call_target="tpu_custom_call" | custom-call | tf_op jit(solution)/shard_map/pallas_call | solution.py:363
  (113 shorter events, 26.5 us)
Async XLA Ops:
  6.2 20.8 %collective-permute-start.1 = (f32[42,16,64]{2,1,0:T(8,128)}, f32[42,16,64]{2,1,0:T(8,128)S(1)}, u32[]{:S(2)}, u32[]{:S(2)}) collective-permute-start(f32[42,16,64]{2,1,0:T(8,128)} %get-tuple-element.23), channel_id=1, source_target_pairs={{3,0},{0,1},{1,2},{2,3},{7,4},{4,5},{5,6},{6,7},{11,8},{8,9},{9,10... | collective-permute-start | bytes 516104 | tf_op jit(solution)/shard_map/ppermute | solution.py:112
  6.7 20.3 %collective-permute-start = (f32[24,16,64]{2,1,0:T(8,128)}, f32[24,16,64]{2,1,0:T(8,128)S(1)}, u32[]{:S(2)}, u32[]{:S(2)}) collective-permute-start(f32[24,16,64]{2,1,0:T(8,128)} %get-tuple-element.22), channel_id=1, source_target_pairs={{1,0},{2,1},{3,2},{0,3},{5,4},{6,5},{7,6},{4,7},{9,8},{10,9},{11,1... | collective-permute-start | bytes 294920 | tf_op jit(solution)/shard_map/ppermute | solution.py:112
  8.6 18.4 %collective-permute-start.3 = (f32[42,4,128]{2,1,0:T(4,128)}, f32[42,4,128]{2,1,0:T(4,128)S(1)}, u32[]{:S(2)}, u32[]{:S(2)}) collective-permute-start(f32[42,4,128]{2,1,0:T(4,128)} %get-tuple-element.25), channel_id=1, source_target_pairs={{28,0},{0,4},{4,8},{8,12},{12,16},{16,20},{24,28},{29,1},{1,5},{5,... | collective-permute-start | bytes 258056 | tf_op jit(solution)/shard_map/ppermute | solution.py:112
  12.9 14.1 %collective-permute-start.2 = (f32[24,4,128]{2,1,0:T(4,128)}, f32[24,4,128]{2,1,0:T(4,128)S(1)}, u32[]{:S(2)}, u32[]{:S(2)}) collective-permute-start(f32[24,4,128]{2,1,0:T(4,128)} %get-tuple-element.24), channel_id=1, source_target_pairs={{4,0},{8,4},{12,8},{16,12},{20,16},{28,24},{0,28},{5,1},{9,5},{13,... | collective-permute-start | bytes 147464 | tf_op jit(solution)/shard_map/ppermute | solution.py:112
  33.8 13.8 %collective-permute-start.4 = (f32[24,16,64]{2,1,0:T(8,128)}, f32[24,16,64]{2,1,0:T(8,128)S(1)}, u32[]{:S(2)}, u32[]{:S(2)}) collective-permute-start(f32[24,16,64]{2,1,0:T(8,128)} %get-tuple-element.29), channel_id=1, source_target_pairs={{1,0},{2,1},{3,2},{0,3},{5,4},{6,5},{7,6},{4,7},{9,8},{10,9},{11,1... | collective-permute-start | bytes 294920 | tf_op jit(solution)/shard_map/ppermute | solution.py:112
  33.8 13.8 %collective-permute-start.5 = (f32[24,16,64]{2,1,0:T(8,128)}, f32[24,16,64]{2,1,0:T(8,128)S(1)}, u32[]{:S(2)}, u32[]{:S(2)}) collective-permute-start(f32[24,16,64]{2,1,0:T(8,128)} %get-tuple-element.30), channel_id=1, source_target_pairs={{3,0},{0,1},{1,2},{2,3},{7,4},{4,5},{5,6},{6,7},{11,8},{8,9},{9,10... | collective-permute-start | bytes 294920 | tf_op jit(solution)/shard_map/ppermute | solution.py:112
  34.3 6.4 %collective-permute-start.6 = (f32[24,4,128]{2,1,0:T(4,128)}, f32[24,4,128]{2,1,0:T(4,128)S(1)}, u32[]{:S(2)}, u32[]{:S(2)}) collective-permute-start(f32[24,4,128]{2,1,0:T(4,128)} %get-tuple-element.31), channel_id=1, source_target_pairs={{4,0},{8,4},{12,8},{16,12},{20,16},{28,24},{0,28},{5,1},{9,5},{13,... | collective-permute-start | bytes 147464 | tf_op jit(solution)/shard_map/ppermute | solution.py:112
  38.2 9.3 %collective-permute-start.7 = (f32[24,4,128]{2,1,0:T(4,128)}, f32[24,4,128]{2,1,0:T(4,128)S(1)}, u32[]{:S(2)}, u32[]{:S(2)}) collective-permute-start(f32[24,4,128]{2,1,0:T(4,128)} %get-tuple-element.32), channel_id=1, source_target_pairs={{28,0},{0,4},{4,8},{8,12},{12,16},{16,20},{24,28},{29,1},{1,5},{5,... | collective-permute-start | bytes 147464 | tf_op jit(solution)/shard_map/ppermute | solution.py:112
  57.4 6.4 %collective-permute-start.8 = (f32[2,1,768]{2,1,0:T(1,128)}, f32[2,1,768]{2,1,0:T(1,128)S(1)}, u32[]{:S(2)}, u32[]{:S(2)}) collective-permute-start(f32[2,1,768]{2,1,0:T(1,128)} %shard_map.89.refs_3_), channel_id=1, source_target_pairs={{1,0},{2,1},{3,2},{0,3},{5,4},{6,5},{7,6},{4,7},{9,8},{10,9},{11,1... | collective-permute-start | bytes 18440 | tf_op jit(solution)/shard_map/ppermute | solution.py:112
  57.4 6.4 %collective-permute-start.9 = (f32[2,1,768]{2,1,0:T(1,128)}, f32[2,1,768]{2,1,0:T(1,128)S(1)}, u32[]{:S(2)}, u32[]{:S(2)}) collective-permute-start(f32[2,1,768]{2,1,0:T(1,128)} %shard_map.89.refs_3_), channel_id=1, source_target_pairs={{3,0},{0,1},{1,2},{2,3},{7,4},{4,5},{5,6},{6,7},{11,8},{8,9},{9,10... | collective-permute-start | bytes 18440 | tf_op jit(solution)/shard_map/ppermute | solution.py:112
  57.9 5.9 %collective-permute-start.10 = (f32[2,1,768]{2,1,0:T(1,128)}, f32[2,1,768]{2,1,0:T(1,128)S(1)}, u32[]{:S(2)}, u32[]{:S(2)}) collective-permute-start(f32[2,1,768]{2,1,0:T(1,128)} %shard_map.89.refs_3_), channel_id=1, source_target_pairs={{4,0},{8,4},{12,8},{16,12},{20,16},{28,24},{0,28},{5,1},{9,5},{13,... | collective-permute-start | bytes 18440 | tf_op jit(solution)/shard_map/ppermute | solution.py:112
  59.8 8.4 %collective-permute-start.11 = (f32[2,1,768]{2,1,0:T(1,128)}, f32[2,1,768]{2,1,0:T(1,128)S(1)}, u32[]{:S(2)}, u32[]{:S(2)}) collective-permute-start(f32[2,1,768]{2,1,0:T(1,128)} %shard_map.89.refs_3_), channel_id=1, source_target_pairs={{28,0},{0,4},{4,8},{8,12},{12,16},{16,20},{24,28},{29,1},{1,5},{5,... | collective-permute-start | bytes 18440 | tf_op jit(solution)/shard_map/ppermute | solution.py:112
  71.8 6.5 %collective-permute-start.12 = (f32[2,1,768]{2,1,0:T(1,128)}, f32[2,1,768]{2,1,0:T(1,128)S(1)}, u32[]{:S(2)}, u32[]{:S(2)}) collective-permute-start(f32[2,1,768]{2,1,0:T(1,128)} %shard_map.90.refs_3_), channel_id=1, source_target_pairs={{1,0},{2,1},{3,2},{0,3},{5,4},{6,5},{7,6},{4,7},{9,8},{10,9},{11,1... | collective-permute-start | bytes 18440 | tf_op jit(solution)/shard_map/ppermute | solution.py:112
  71.9 6.5 %collective-permute-start.13 = (f32[2,1,768]{2,1,0:T(1,128)}, f32[2,1,768]{2,1,0:T(1,128)S(1)}, u32[]{:S(2)}, u32[]{:S(2)}) collective-permute-start(f32[2,1,768]{2,1,0:T(1,128)} %shard_map.90.refs_3_), channel_id=1, source_target_pairs={{3,0},{0,1},{1,2},{2,3},{7,4},{4,5},{5,6},{6,7},{11,8},{8,9},{9,10... | collective-permute-start | bytes 18440 | tf_op jit(solution)/shard_map/ppermute | solution.py:112
  72.3 6.1 %collective-permute-start.14 = (f32[2,1,768]{2,1,0:T(1,128)}, f32[2,1,768]{2,1,0:T(1,128)S(1)}, u32[]{:S(2)}, u32[]{:S(2)}) collective-permute-start(f32[2,1,768]{2,1,0:T(1,128)} %shard_map.90.refs_3_), channel_id=1, source_target_pairs={{4,0},{8,4},{12,8},{16,12},{20,16},{28,24},{0,28},{5,1},{9,5},{13,... | collective-permute-start | bytes 18440 | tf_op jit(solution)/shard_map/ppermute | solution.py:112
  74.2 8.4 %collective-permute-start.15 = (f32[2,1,768]{2,1,0:T(1,128)}, f32[2,1,768]{2,1,0:T(1,128)S(1)}, u32[]{:S(2)}, u32[]{:S(2)}) collective-permute-start(f32[2,1,768]{2,1,0:T(1,128)} %shard_map.90.refs_3_), channel_id=1, source_target_pairs={{28,0},{0,4},{4,8},{8,12},{12,16},{16,20},{24,28},{29,1},{1,5},{5,... | collective-permute-start | bytes 18440 | tf_op jit(solution)/shard_map/ppermute | solution.py:112
  89.0 11.4 %collective-permute-start.16 = (f32[24,16,64]{2,1,0:T(8,128)S(1)}, f32[24,16,64]{2,1,0:T(8,128)S(1)}, u32[]{:S(2)}, u32[]{:S(2)}) collective-permute-start(f32[24,16,64]{2,1,0:T(8,128)S(1)} %get-tuple-element.47), channel_id=1, source_target_pairs={{1,0},{2,1},{3,2},{0,3},{5,4},{6,5},{7,6},{4,7},{9,8},{10,9},{11,1... | collective-permute-start | bytes 294920 | tf_op jit(solution)/shard_map/ppermute | solution.py:112
  89.2 11.2 %collective-permute-start.17 = (f32[24,16,64]{2,1,0:T(8,128)S(1)}, f32[24,16,64]{2,1,0:T(8,128)S(1)}, u32[]{:S(2)}, u32[]{:S(2)}) collective-permute-start(f32[24,16,64]{2,1,0:T(8,128)S(1)} %get-tuple-element.46), channel_id=1, source_target_pairs={{3,0},{0,1},{1,2},{2,3},{7,4},{4,5},{5,6},{6,7},{11,8},{8,9},{9,10... | collective-permute-start | bytes 294920 | tf_op jit(solution)/shard_map/ppermute | solution.py:112
  89.6 6.1 %collective-permute-start.18 = (f32[24,4,128]{2,1,0:T(4,128)S(1)}, f32[24,4,128]{2,1,0:T(4,128)S(1)}, u32[]{:S(2)}, u32[]{:S(2)}) collective-permute-start(f32[24,4,128]{2,1,0:T(4,128)S(1)} %slice.50), channel_id=1, source_target_pairs={{4,0},{8,4},{12,8},{16,12},{20,16},{28,24},{0,28},{5,1},{9,5},{13,... | collective-permute-start | bytes 147464 | tf_op jit(solution)/shard_map/ppermute | solution.py:112
  91.6 8.8 %collective-permute-start.19 = (f32[24,4,128]{2,1,0:T(4,128)S(1)}, f32[24,4,128]{2,1,0:T(4,128)S(1)}, u32[]{:S(2)}, u32[]{:S(2)}) collective-permute-start(f32[24,4,128]{2,1,0:T(4,128)S(1)} %slice.51), channel_id=1, source_target_pairs={{28,0},{0,4},{4,8},{8,12},{12,16},{16,20},{24,28},{29,1},{1,5},{5,... | collective-permute-start | bytes 147464 | tf_op jit(solution)/shard_map/ppermute | solution.py:112
  106.9 11.4 %collective-permute-start.20 = (f32[24,16,64]{2,1,0:T(8,128)}, f32[24,16,64]{2,1,0:T(8,128)S(1)}, u32[]{:S(2)}, u32[]{:S(2)}) collective-permute-start(f32[24,16,64]{2,1,0:T(8,128)} %get-tuple-element.34), channel_id=1, source_target_pairs={{1,0},{2,1},{3,2},{0,3},{5,4},{6,5},{7,6},{4,7},{9,8},{10,9},{11,1... | collective-permute-start | bytes 294920 | tf_op jit(solution)/shard_map/ppermute | solution.py:112
  107.5 10.9 %collective-permute-start.21 = (f32[24,16,64]{2,1,0:T(8,128)}, f32[24,16,64]{2,1,0:T(8,128)S(1)}, u32[]{:S(2)}, u32[]{:S(2)}) collective-permute-start(f32[24,16,64]{2,1,0:T(8,128)} %get-tuple-element.35), channel_id=1, source_target_pairs={{3,0},{0,1},{1,2},{2,3},{7,4},{4,5},{5,6},{6,7},{11,8},{8,9},{9,10... | collective-permute-start | bytes 294920 | tf_op jit(solution)/shard_map/ppermute | solution.py:112
  107.5 6.6 %collective-permute-start.22 = (f32[24,4,128]{2,1,0:T(4,128)}, f32[24,4,128]{2,1,0:T(4,128)S(1)}, u32[]{:S(2)}, u32[]{:S(2)}) collective-permute-start(f32[24,4,128]{2,1,0:T(4,128)} %get-tuple-element.36), channel_id=1, source_target_pairs={{4,0},{8,4},{12,8},{16,12},{20,16},{28,24},{0,28},{5,1},{9,5},{13,... | collective-permute-start | bytes 147464 | tf_op jit(solution)/shard_map/ppermute | solution.py:112
  109.4 9.0 %collective-permute-start.23 = (f32[24,4,128]{2,1,0:T(4,128)}, f32[24,4,128]{2,1,0:T(4,128)S(1)}, u32[]{:S(2)}, u32[]{:S(2)}) collective-permute-start(f32[24,4,128]{2,1,0:T(4,128)} %get-tuple-element.37), channel_id=1, source_target_pairs={{28,0},{0,4},{4,8},{8,12},{12,16},{16,20},{24,28},{29,1},{1,5},{5,... | collective-permute-start | bytes 147464 | tf_op jit(solution)/shard_map/ppermute | solution.py:112
  (27 other events, 65.6 us)

commit v10 on v9

--- a/solution.py
+++ b/solution.py
@@ -367,6 +367,7 @@
 
 def coarse_kernel(*refs, present):
     refs = list(refs)
+    natural_ref = refs.pop()
     out_ref = refs.pop()
     source_ref, inverse_ref = refs[0], refs[1]
     first = len(refs) == 2
@@ -378,7 +379,7 @@
         lax.broadcasted_iota(jnp.int32, (8, 128), 1) // AGG == lax.broadcasted_iota(jnp.int32, (8, 128), 0)
     ).astype(jnp.float32)
 
-    def reduce_flat(product):
+    def reduce_both(product):
         partial = product[:, 0:128]
         for q in range(1, chunks):
             partial = partial + product[:, q * 128:(q + 1) * 128]
@@ -387,7 +388,10 @@
         pieces = [
             jnp.sum(partial[8 * q:8 * q + 8] * selector, axis=0, keepdims=True) for q in range(chunks)
         ]
-        return jnp.concatenate(pieces, axis=1)
+        return jnp.concatenate(pieces, axis=1), partial[:, :AGG]
+
+    def reduce_flat(product):
+        return reduce_both(product)[0]
 
     def roll_within(vector, shift):
         pieces = [pltpu.roll(vector[:, q * 128:(q + 1) * 128], shift % 128, 1) for q in range(chunks)]
@@ -404,14 +408,16 @@
 
     def precondition(vector):
         acc = accumulate(None, inverse_ref, (), vector)
-        return [reduce_flat(acc[0]), reduce_flat(acc[1])]
+        return [reduce_both(acc[0]), reduce_both(acc[1])]
 
     source = [source_ref[0], source_ref[1]]
     if first:
-        result = precondition(source)
+        step = precondition(source)
+        result = [step[0][0], step[1][0]]
+        natural = [step[0][1], step[1][1]]
     else:
-        operator_ref, current_ref = refs[2], refs[3]
-        nearby_refs = refs[4:]
+        operator_ref, current_ref, current_natural_ref = refs[2], refs[3], refs[4]
+        nearby_refs = refs[5:]
         current = [current_ref[0], current_ref[1]]
         ahead = [
             jnp.where(position == AGG - 1, roll_within(c, AGG - 1), roll_within(c, -1)) for c in current
@@ -431,9 +437,12 @@
                 acc = accumulate(acc, operator_ref, (direction,), vector)
         residue = [source[0] - reduce_flat(acc[0]), source[1] - reduce_flat(acc[1])]
         step = precondition(residue)
-        result = [current[0] + step[0], current[1] + step[1]]
+        result = [current[0] + step[0][0], current[1] + step[1][0]]
+        natural = [current_natural_ref[0] + step[0][1], current_natural_ref[1] + step[1][1]]
     out_ref[0] = result[0]
     out_ref[1] = result[1]
+    natural_ref[0] = natural[0]
+    natural_ref[1] = natural[1]
 
 
 def run_coarse(source, inverse_blocks, operator_blocks, current, nearby):
@@ -441,9 +450,14 @@
     present = ()
     if current is not None:
         present = tuple(v is not None for v in nearby)
-        operands += [operator_blocks, current] + [v for v in nearby if v is not None]
+        operands += [operator_blocks, current[0], current[1]] + [v for v in nearby if v is not None]
     kernel = functools.partial(coarse_kernel, present=present)
-    return pl.pallas_call(kernel, out_shape=jax.ShapeDtypeStruct(source.shape, jnp.float32))(*operands)
+    natural_shape = (2, inverse_blocks.shape[1], AGG)
+    out_shape = [
+        jax.ShapeDtypeStruct(source.shape, jnp.float32),
+        jax.ShapeDtypeStruct(natural_shape, jnp.float32),
+    ]
+    return pl.pallas_call(kernel, out_shape=out_shape)(*operands)
 
 
 def body(
@@ -551,18 +565,19 @@
     flat_source = coarse_source.reshape(2, 1, CDOF * AGG)
     operator_blocks = coarse_operator.reshape(9, 2, CDOF, CDOF * AGG)
     inverse_blocks = block_inverse.reshape(2, CDOF, CDOF * AGG)
-    correction = run_coarse(flat_source, inverse_blocks, operator_blocks, None, None)
+    state = run_coarse(flat_source, inverse_blocks, operator_blocks, None, None)
     for repeat in range(2):
+        flat = state[0]
         nearby = [
-            permute_from(correction, "grp", 1, lambda i: True),
-            permute_from(correction, "grp", -1, lambda i: True),
-            permute_from(correction, "lat", 1, z_up_ok),
-            permute_from(correction, "lat", -1, z_down_ok),
-            permute_from(correction, "lat", PZ, t_up_ok),
-            permute_from(correction, "lat", -PZ, t_down_ok),
+            permute_from(flat, "grp", 1, lambda i: True),
+            permute_from(flat, "grp", -1, lambda i: True),
+            permute_from(flat, "lat", 1, z_up_ok),
+            permute_from(flat, "lat", -1, z_down_ok),
+            permute_from(flat, "lat", PZ, t_up_ok),
+            permute_from(flat, "lat", -PZ, t_down_ok),
         ]
-        correction = run_coarse(flat_source, inverse_blocks, operator_blocks, correction, nearby)
-    correction = correction.reshape(2, CDOF, AGG)
+        state = run_coarse(flat_source, inverse_blocks, operator_blocks, state, nearby)
+    correction = state[1]
     expanded = jnp.dot(
         correction.reshape(2 * CDOF, AGG), membership.T, precision=lax.Precision.HIGHEST
     ).reshape(2, 2, NVEC, site_count)

time: 125 us -> 125 us (level)
    unnamed x57 -> x59, local copies, waits for them, and re-layouts: 11.1 us -> 11 us
where the time goes in v10:
time: 125 us; the launch traced here: 124 us
  starting transfers between devices  43.5 us (35%)
  Pallas kernels  30.3 us (24%)
  waiting for transfers between devices  25.4 us (20%)
  local copies, waits for them, and re-layouts  18.9 us (15%)
  matrix products  3.75 us (3%)
    ppermute x24, starting transfers between devices, permute_from(): return lax.ppermute(value, axis, pairs)  43.5 us
    ppermute x24, waiting for transfers between devices, permute_from(): return lax.ppermute(value, axis, pairs)  25.4 us
    pallas_call x5, Pallas kernels, run_pass(): pl.pallas_call(kernel, out_shape=out_shape, scratch_shapes=scratch, in_sp...  22.4 us
    unnamed x59, local copies, waits for them, and re-layouts  11 us
    pallas_call x3, Pallas kernels, run_coarse(): return pl.pallas_call(kernel, out_shape=out_shape)(*operands)  7.85 us
    reshape x1, local copies, waits for them, and re-layouts, body(): vectors = test_vectors.reshape(NVEC, 2, 2, 6, site_count)  4.03 us
    dot_general x1, matrix products, body(): jnp.einsum('krxqn,sxqnj->rsxkj', vectors, weighted, preferred_element_typ...  2.5 us
  transfers between devices with their start and end apart: 24, of which 7 were waited for; matrix products, arithmetic and copies ran while one was open for 8% of the time, Pallas kernels for 0%

profile of v10, /device:TPU:0, one launch (start us, length us, event | category | flops | bytes accessed | tf_op | source)
XLA Modules:
  0.0 124.1 jit_solution(5561335492861752188)
XLA Ops:
  2.0 4.2 %shard_map.86 = (f32[24,16,128]{2,1,0:T(8,128)}, f32[24,16,64]{2,1,0:T(8,128)}, f32[42,16,64]{2,1,0:T(8,128)}, f32[24,4,128]{2,1,0:T(4,128)}, f32[42,4,128]{2,1,0:T(4,128)}) custom-call(f32[24,16,128]{2,1,0:T(8,128)} %bitcast.54, bf16[4,18,16,128]{3,2,1,0:T(8,128)(2,1)} %bitcast.47, s32[16,128]{1,0:T(8,128)} %reshape.100.refs_2_.refs_3_, s32[16]{0:T(128)} %bitcast.69), custom_call_target="tpu_custom_call" | custom-call | tf_op jit(solution)/shard_map/pallas_call | solution.py:363
  6.7 1.9 %collective-permute-start = (f32[24,16,64]{2,1,0:T(8,128)}, f32[24,16,64]{2,1,0:T(8,128)S(1)}, u32[]{:S(2)}, u32[]{:S(2)}) collective-permute-start(f32[24,16,64]{2,1,0:T(8,128)} %get-tuple-element.27), channel_id=1, source_target_pairs={{1,0},{2,1},{3,2},{0,3},{5,4},{6,5},{7,6},{4,7},{9,8},{10,9},{11,1... | collective-permute-start | bytes 294920 | tf_op jit(solution)/shard_map/ppermute | solution.py:112
  8.6 4.2 %collective-permute-start.3 = (f32[42,4,128]{2,1,0:T(4,128)}, f32[42,4,128]{2,1,0:T(4,128)S(1)}, u32[]{:S(2)}, u32[]{:S(2)}) collective-permute-start(f32[42,4,128]{2,1,0:T(4,128)} %get-tuple-element.30), channel_id=1, source_target_pairs={{28,0},{0,4},{4,8},{8,12},{12,16},{16,20},{24,28},{29,1},{1,5},{5,... | collective-permute-start | bytes 258056 | tf_op jit(solution)/shard_map/ppermute | solution.py:112
  12.8 5.0 %collective-permute-start.2 = (f32[24,4,128]{2,1,0:T(4,128)}, f32[24,4,128]{2,1,0:T(4,128)S(1)}, u32[]{:S(2)}, u32[]{:S(2)}) collective-permute-start(f32[24,4,128]{2,1,0:T(4,128)} %get-tuple-element.29), channel_id=1, source_target_pairs={{4,0},{8,4},{12,8},{16,12},{20,16},{28,24},{0,28},{5,1},{9,5},{13,... | collective-permute-start | bytes 147464 | tf_op jit(solution)/shard_map/ppermute | solution.py:112
  18.6 4.3 %copy.17 = bf16[1,24,24,4,4,128]{5,4,3,1,2,0:T(4,128)(2,1)} copy(bf16[1,24,24,4,4,128]{5,4,3,2,1,0:T(4,128)(2,1)} %param.9) | data formatting | bytes 4718592 | tf_op args[2]
  22.9 4.0 %reshape.102 = bf16[24,2,2,6,2048]{4,0,3,2,1:T(8,128)(2,1)S(1)} reshape(bf16[1,24,24,4,4,128]{5,4,3,1,2,0:T(4,128)(2,1)} %copy.17) | data formatting | bytes 4718592 | tf_op jit(solution)/shard_map/reshape | solution.py:534
  28.4 5.4 %shard_map.87 = (f32[24,16,128]{2,1,0:T(8,128)}, f32[24,16,64]{2,1,0:T(8,128)}, f32[24,16,64]{2,1,0:T(8,128)}, f32[24,4,128]{2,1,0:T(4,128)}, f32[24,4,128]{2,1,0:T(4,128)}, /*index=5*/bf16[4,18,16,128]{3,2,1,0:T(8,128)(2,1)}) custom-call(f32[24,16,128]{2,1,0:T(8,128)} %bitcast.55, bf16[4,18,16,128]{3,2,1,0:T(8,128)(2,1)} %bitcast.48, ...), custom_call_target="tpu_custom_call" | custom-call | tf_op jit(solution)/shard_map/pallas_call | solution.py:363
  34.3 3.9 %collective-permute-start.6 = (f32[24,4,128]{2,1,0:T(4,128)}, f32[24,4,128]{2,1,0:T(4,128)S(1)}, u32[]{:S(2)}, u32[]{:S(2)}) collective-permute-start(f32[24,4,128]{2,1,0:T(4,128)} %get-tuple-element.36), channel_id=1, source_target_pairs={{4,0},{8,4},{12,8},{16,12},{20,16},{28,24},{0,28},{5,1},{9,5},{13,... | collective-permute-start | bytes 147464 | tf_op jit(solution)/shard_map/ppermute | solution.py:112
  40.7 6.9 %collective-permute-done.7.refs_8_ = f32[24,4,128]{2,1,0:T(4,128)S(1)} collective-permute-done((f32[24,4,128]{2,1,0:T(4,128)}, f32[24,4,128]{2,1,0:T(4,128)S(1)}, u32[]{:S(2)}, u32[]{:S(2)}) %collective-permute-start.7) | collective-permute-done | bytes 49184 | tf_op jit(solution)/shard_map/ppermute | solution.py:112
  48.3 2.7 %shard_map.88 = bf16[24,16,128]{2,1,0:T(8,128)(2,1)} custom-call(f32[24,16,128]{2,1,0:T(8,128)} %bitcast.56, bf16[4,18,16,128]{3,2,1,0:T(8,128)(2,1)} %bitcast.49, bf16[4,18,16,128]{3,2,1,0:T(8,128)(2,1)} %get-tuple-element.31.refs_2_, s32[16,128]{1,0:T(8,128)} %reshape.100.refs_2_.refs_3_, f32[24,16,128]{2,1,0:T(8,128)} %get-tuple-element.32.refs_4_, ...), custom_call_target="tpu_custom_call" | custom-call | tf_op jit(solution)/shard_map/pallas_call | solution.py:363
  52.1 2.5 %fusion.8 = f32[2,2,2,24,16]{3,4,0,1,2:T(8,128)S(1)} fusion(bf16[2048,16]{0,1:T(8,128)(2,1)S(1)} %convert_convert_fusion, bf16[24,2,2,6,2048]{4,0,3,2,1:T(8,128)(2,1)S(1)} %reshape.102, bf16[2,2,6,2048]{3,2,1,0:T(8,128)(2,1)S(1)} %mul.20), kind=kOutput, calls=%fused_computation.12 | convolution fusion | flops 78643200 | bytes 2535424 | tf_op jit(solution)/shard_map/krxqn,sxqnj->rsxkj/dot_general | solution.py:561
  59.8 3.9 %collective-permute-start.11 = (f32[2,1,768]{2,1,0:T(1,128)}, f32[2,1,768]{2,1,0:T(1,128)S(1)}, u32[]{:S(2)}, u32[]{:S(2)}) collective-permute-start(f32[2,1,768]{2,1,0:T(1,128)} %get-tuple-element.38.refs_3_), channel_id=1, source_target_pairs={{28,0},{0,4},{4,8},{8,12},{12,16},{16,20},{24,28},{29,1},{1,5},{5,... | collective-permute-start | bytes 18440 | tf_op jit(solution)/shard_map/ppermute | solution.py:112
  63.8 4.4 %collective-permute-done.11.refs_8_ = f32[2,1,768]{2,1,0:T(1,128)S(1)} collective-permute-done((f32[2,1,768]{2,1,0:T(1,128)}, f32[2,1,768]{2,1,0:T(1,128)S(1)}, u32[]{:S(2)}, u32[]{:S(2)}) %collective-permute-start.11) | collective-permute-done | bytes 6176 | tf_op jit(solution)/shard_map/ppermute | solution.py:112
  68.8 3.0 %shard_map.90 = (f32[2,1,768]{2,1,0:T(1,128)}, f32[2,48,16]{2,1,0:T(8,128)}) custom-call(f32[2,1,768]{2,1,0:T(1,128)} %copy-done.12, bf16[2,48,768]{2,1,0:T(8,128)(2,1)} %bitcast.62, bf16[9,2,48,768]{3,2,1,0:T(8,128)(2,1)} %bitcast.52, f32[2,1,768]{2,1,0:T(1,128)} %get-tuple-element.38.refs_3_, f32[2,48,16]{2,1,0:T(8,128)} %get-tuple-element.39.refs_4_, ...), custom_call_target="tpu_custom_call" | custom-call | tf_op jit(solution)/shard_map/pallas_call | solution.py:460
  74.2 4.1 %collective-permute-start.15 = (f32[2,1,768]{2,1,0:T(1,128)}, f32[2,1,768]{2,1,0:T(1,128)S(1)}, u32[]{:S(2)}, u32[]{:S(2)}) collective-permute-start(f32[2,1,768]{2,1,0:T(1,128)} %get-tuple-element.40.refs_3_), channel_id=1, source_target_pairs={{28,0},{0,4},{4,8},{8,12},{12,16},{16,20},{24,28},{29,1},{1,5},{5,... | collective-permute-start | bytes 18440 | tf_op jit(solution)/shard_map/ppermute | solution.py:112
  78.4 4.3 %collective-permute-done.15.refs_8_ = f32[2,1,768]{2,1,0:T(1,128)S(1)} collective-permute-done((f32[2,1,768]{2,1,0:T(1,128)}, f32[2,1,768]{2,1,0:T(1,128)S(1)}, u32[]{:S(2)}, u32[]{:S(2)}) %collective-permute-start.15) | collective-permute-done | bytes 6176 | tf_op jit(solution)/shard_map/ppermute | solution.py:112
  83.3 3.0 %shard_map.91 = (f32[2,1,768]{2,1,0:T(1,128)}, f32[2,48,16]{2,1,0:T(8,128)}) custom-call(f32[2,1,768]{2,1,0:T(1,128)} %copy-done.12, bf16[2,48,768]{2,1,0:T(8,128)(2,1)} %bitcast.63, bf16[9,2,48,768]{3,2,1,0:T(8,128)(2,1)} %bitcast.53, f32[2,1,768]{2,1,0:T(1,128)} %get-tuple-element.40.refs_3_, f32[2,48,16]{2,1,0:T(8,128)} %get-tuple-element.41.refs_4_, ...), custom_call_target="tpu_custom_call" | custom-call | tf_op jit(solution)/shard_map/pallas_call | solution.py:460
  89.6 1.9 %collective-permute-start.18 = (f32[24,4,128]{2,1,0:T(4,128)S(1)}, f32[24,4,128]{2,1,0:T(4,128)S(1)}, u32[]{:S(2)}, u32[]{:S(2)}) collective-permute-start(f32[24,4,128]{2,1,0:T(4,128)S(1)} %slice.50), channel_id=1, source_target_pairs={{4,0},{8,4},{12,8},{16,12},{20,16},{28,24},{0,28},{5,1},{9,5},{13,... | collective-permute-start | bytes 147464 | tf_op jit(solution)/shard_map/ppermute | solution.py:112
  91.6 3.9 %collective-permute-start.19 = (f32[24,4,128]{2,1,0:T(4,128)S(1)}, f32[24,4,128]{2,1,0:T(4,128)S(1)}, u32[]{:S(2)}, u32[]{:S(2)}) collective-permute-start(f32[24,4,128]{2,1,0:T(4,128)S(1)} %slice.51), channel_id=1, source_target_pairs={{28,0},{0,4},{4,8},{8,12},{12,16},{16,20},{24,28},{29,1},{1,5},{5,... | collective-permute-start | bytes 147464 | tf_op jit(solution)/shard_map/ppermute | solution.py:112
  95.8 4.6 %collective-permute-done.19.refs_9_ = f32[24,4,128]{2,1,0:T(4,128)S(1)} collective-permute-done((f32[24,4,128]{2,1,0:T(4,128)S(1)}, f32[24,4,128]{2,1,0:T(4,128)S(1)}, u32[]{:S(2)}, u32[]{:S(2)}) %collective-permute-start.19) | collective-permute-done | bytes 49184 | tf_op jit(solution)/shard_map/ppermute | solution.py:112
  101.8 5.1 %shard_map.92 = (f32[24,16,128]{2,1,0:T(8,128)}, f32[24,16,64]{2,1,0:T(8,128)}, f32[24,16,64]{2,1,0:T(8,128)}, f32[24,4,128]{2,1,0:T(4,128)}, f32[24,4,128]{2,1,0:T(4,128)}) custom-call(f32[24,16,128]{2,1,0:T(8,128)} %bitcast.57, bf16[4,18,16,128]{3,2,1,0:T(8,128)(2,1)} %bitcast.50, bf16[4,18,16,128]{3,2,1,0:T(8,128)(2,1)} %get-tuple-element.31.refs_2_, ...), custom_call_target="tpu_custom_call" | custom-call | tf_op jit(solution)/shard_map/pallas_call | solution.py:363
  109.4 3.9 %collective-permute-start.23 = (f32[24,4,128]{2,1,0:T(4,128)}, f32[24,4,128]{2,1,0:T(4,128)S(1)}, u32[]{:S(2)}, u32[]{:S(2)}) collective-permute-start(f32[24,4,128]{2,1,0:T(4,128)} %get-tuple-element.47), channel_id=1, source_target_pairs={{28,0},{0,4},{4,8},{8,12},{12,16},{16,20},{24,28},{29,1},{1,5},{5,... | collective-permute-start | bytes 147464 | tf_op jit(solution)/shard_map/ppermute | solution.py:112
  114.0 4.4 %collective-permute-done.23.refs_9_ = f32[24,4,128]{2,1,0:T(4,128)S(1)} collective-permute-done((f32[24,4,128]{2,1,0:T(4,128)}, f32[24,4,128]{2,1,0:T(4,128)S(1)}, u32[]{:S(2)}, u32[]{:S(2)}) %collective-permute-start.23) | collective-permute-done | bytes 49184 | tf_op jit(solution)/shard_map/ppermute | solution.py:112
  119.1 5.0 %shard_map.93 = f32[24,16,128]{2,1,0:T(8,128)} custom-call(f32[24,16,128]{2,1,0:T(8,128)} %bitcast.58, bf16[4,18,16,128]{3,2,1,0:T(8,128)(2,1)} %bitcast.51, bf16[4,18,16,128]{3,2,1,0:T(8,128)(2,1)} %get-tuple-element.31.refs_2_, s32[16,128]{1,0:T(8,128)} %reshape.100.refs_2_.refs_3_, s32[16]{0:T(128)} %bitcast.72, ...), custom_call_target="tpu_custom_call" | custom-call | tf_op jit(solution)/shard_map/pallas_call | solution.py:363
  (112 shorter events, 26.3 us)
Async XLA Ops:
  6.2 20.8 %collective-permute-start.1 = (f32[42,16,64]{2,1,0:T(8,128)}, f32[42,16,64]{2,1,0:T(8,128)S(1)}, u32[]{:S(2)}, u32[]{:S(2)}) collective-permute-start(f32[42,16,64]{2,1,0:T(8,128)} %get-tuple-element.28), channel_id=1, source_target_pairs={{3,0},{0,1},{1,2},{2,3},{7,4},{4,5},{5,6},{6,7},{11,8},{8,9},{9,10... | collective-permute-start | bytes 516104 | tf_op jit(solution)/shard_map/ppermute | solution.py:112
  6.7 20.3 %collective-permute-start = (f32[24,16,64]{2,1,0:T(8,128)}, f32[24,16,64]{2,1,0:T(8,128)S(1)}, u32[]{:S(2)}, u32[]{:S(2)}) collective-permute-start(f32[24,16,64]{2,1,0:T(8,128)} %get-tuple-element.27), channel_id=1, source_target_pairs={{1,0},{2,1},{3,2},{0,3},{5,4},{6,5},{7,6},{4,7},{9,8},{10,9},{11,1... | collective-permute-start | bytes 294920 | tf_op jit(solution)/shard_map/ppermute | solution.py:112
  8.6 18.3 %collective-permute-start.3 = (f32[42,4,128]{2,1,0:T(4,128)}, f32[42,4,128]{2,1,0:T(4,128)S(1)}, u32[]{:S(2)}, u32[]{:S(2)}) collective-permute-start(f32[42,4,128]{2,1,0:T(4,128)} %get-tuple-element.30), channel_id=1, source_target_pairs={{28,0},{0,4},{4,8},{8,12},{12,16},{16,20},{24,28},{29,1},{1,5},{5,... | collective-permute-start | bytes 258056 | tf_op jit(solution)/shard_map/ppermute | solution.py:112
  12.8 14.1 %collective-permute-start.2 = (f32[24,4,128]{2,1,0:T(4,128)}, f32[24,4,128]{2,1,0:T(4,128)S(1)}, u32[]{:S(2)}, u32[]{:S(2)}) collective-permute-start(f32[24,4,128]{2,1,0:T(4,128)} %get-tuple-element.29), channel_id=1, source_target_pairs={{4,0},{8,4},{12,8},{16,12},{20,16},{28,24},{0,28},{5,1},{9,5},{13,... | collective-permute-start | bytes 147464 | tf_op jit(solution)/shard_map/ppermute | solution.py:112
  33.8 13.8 %collective-permute-start.4 = (f32[24,16,64]{2,1,0:T(8,128)}, f32[24,16,64]{2,1,0:T(8,128)S(1)}, u32[]{:S(2)}, u32[]{:S(2)}) collective-permute-start(f32[24,16,64]{2,1,0:T(8,128)} %get-tuple-element.34), channel_id=1, source_target_pairs={{1,0},{2,1},{3,2},{0,3},{5,4},{6,5},{7,6},{4,7},{9,8},{10,9},{11,1... | collective-permute-start | bytes 294920 | tf_op jit(solution)/shard_map/ppermute | solution.py:112
  33.8 13.8 %collective-permute-start.5 = (f32[24,16,64]{2,1,0:T(8,128)}, f32[24,16,64]{2,1,0:T(8,128)S(1)}, u32[]{:S(2)}, u32[]{:S(2)}) collective-permute-start(f32[24,16,64]{2,1,0:T(8,128)} %get-tuple-element.35), channel_id=1, source_target_pairs={{3,0},{0,1},{1,2},{2,3},{7,4},{4,5},{5,6},{6,7},{11,8},{8,9},{9,10... | collective-permute-start | bytes 294920 | tf_op jit(solution)/shard_map/ppermute | solution.py:112
  34.3 6.4 %collective-permute-start.6 = (f32[24,4,128]{2,1,0:T(4,128)}, f32[24,4,128]{2,1,0:T(4,128)S(1)}, u32[]{:S(2)}, u32[]{:S(2)}) collective-permute-start(f32[24,4,128]{2,1,0:T(4,128)} %get-tuple-element.36), channel_id=1, source_target_pairs={{4,0},{8,4},{12,8},{16,12},{20,16},{28,24},{0,28},{5,1},{9,5},{13,... | collective-permute-start | bytes 147464 | tf_op jit(solution)/shard_map/ppermute | solution.py:112
  38.2 9.3 %collective-permute-start.7 = (f32[24,4,128]{2,1,0:T(4,128)}, f32[24,4,128]{2,1,0:T(4,128)S(1)}, u32[]{:S(2)}, u32[]{:S(2)}) collective-permute-start(f32[24,4,128]{2,1,0:T(4,128)} %get-tuple-element.37), channel_id=1, source_target_pairs={{28,0},{0,4},{4,8},{8,12},{12,16},{16,20},{24,28},{29,1},{1,5},{5,... | collective-permute-start | bytes 147464 | tf_op jit(solution)/shard_map/ppermute | solution.py:112
  57.3 6.4 %collective-permute-start.8 = (f32[2,1,768]{2,1,0:T(1,128)}, f32[2,1,768]{2,1,0:T(1,128)S(1)}, u32[]{:S(2)}, u32[]{:S(2)}) collective-permute-start(f32[2,1,768]{2,1,0:T(1,128)} %get-tuple-element.38.refs_3_), channel_id=1, source_target_pairs={{1,0},{2,1},{3,2},{0,3},{5,4},{6,5},{7,6},{4,7},{9,8},{10,9},{11,1... | collective-permute-start | bytes 18440 | tf_op jit(solution)/shard_map/ppermute | solution.py:112
  57.3 6.4 %collective-permute-start.9 = (f32[2,1,768]{2,1,0:T(1,128)}, f32[2,1,768]{2,1,0:T(1,128)S(1)}, u32[]{:S(2)}, u32[]{:S(2)}) collective-permute-start(f32[2,1,768]{2,1,0:T(1,128)} %get-tuple-element.38.refs_3_), channel_id=1, source_target_pairs={{3,0},{0,1},{1,2},{2,3},{7,4},{4,5},{5,6},{6,7},{11,8},{8,9},{9,10... | collective-permute-start | bytes 18440 | tf_op jit(solution)/shard_map/ppermute | solution.py:112
  57.9 5.9 %collective-permute-start.10 = (f32[2,1,768]{2,1,0:T(1,128)}, f32[2,1,768]{2,1,0:T(1,128)S(1)}, u32[]{:S(2)}, u32[]{:S(2)}) collective-permute-start(f32[2,1,768]{2,1,0:T(1,128)} %get-tuple-element.38.refs_3_), channel_id=1, source_target_pairs={{4,0},{8,4},{12,8},{16,12},{20,16},{28,24},{0,28},{5,1},{9,5},{13,... | collective-permute-start | bytes 18440 | tf_op jit(solution)/shard_map/ppermute | solution.py:112
  59.8 8.4 %collective-permute-start.11 = (f32[2,1,768]{2,1,0:T(1,128)}, f32[2,1,768]{2,1,0:T(1,128)S(1)}, u32[]{:S(2)}, u32[]{:S(2)}) collective-permute-start(f32[2,1,768]{2,1,0:T(1,128)} %get-tuple-element.38.refs_3_), channel_id=1, source_target_pairs={{28,0},{0,4},{4,8},{8,12},{12,16},{16,20},{24,28},{29,1},{1,5},{5,... | collective-permute-start | bytes 18440 | tf_op jit(solution)/shard_map/ppermute | solution.py:112
  71.8 6.5 %collective-permute-start.12 = (f32[2,1,768]{2,1,0:T(1,128)}, f32[2,1,768]{2,1,0:T(1,128)S(1)}, u32[]{:S(2)}, u32[]{:S(2)}) collective-permute-start(f32[2,1,768]{2,1,0:T(1,128)} %get-tuple-element.40.refs_3_), channel_id=1, source_target_pairs={{1,0},{2,1},{3,2},{0,3},{5,4},{6,5},{7,6},{4,7},{9,8},{10,9},{11,1... | collective-permute-start | bytes 18440 | tf_op jit(solution)/shard_map/ppermute | solution.py:112
  71.9 6.5 %collective-permute-start.13 = (f32[2,1,768]{2,1,0:T(1,128)}, f32[2,1,768]{2,1,0:T(1,128)S(1)}, u32[]{:S(2)}, u32[]{:S(2)}) collective-permute-start(f32[2,1,768]{2,1,0:T(1,128)} %get-tuple-element.40.refs_3_), channel_id=1, source_target_pairs={{3,0},{0,1},{1,2},{2,3},{7,4},{4,5},{5,6},{6,7},{11,8},{8,9},{9,10... | collective-permute-start | bytes 18440 | tf_op jit(solution)/shard_map/ppermute | solution.py:112
  72.3 6.1 %collective-permute-start.14 = (f32[2,1,768]{2,1,0:T(1,128)}, f32[2,1,768]{2,1,0:T(1,128)S(1)}, u32[]{:S(2)}, u32[]{:S(2)}) collective-permute-start(f32[2,1,768]{2,1,0:T(1,128)} %get-tuple-element.40.refs_3_), channel_id=1, source_target_pairs={{4,0},{8,4},{12,8},{16,12},{20,16},{28,24},{0,28},{5,1},{9,5},{13,... | collective-permute-start | bytes 18440 | tf_op jit(solution)/shard_map/ppermute | solution.py:112
  74.2 8.4 %collective-permute-start.15 = (f32[2,1,768]{2,1,0:T(1,128)}, f32[2,1,768]{2,1,0:T(1,128)S(1)}, u32[]{:S(2)}, u32[]{:S(2)}) collective-permute-start(f32[2,1,768]{2,1,0:T(1,128)} %get-tuple-element.40.refs_3_), channel_id=1, source_target_pairs={{28,0},{0,4},{4,8},{8,12},{12,16},{16,20},{24,28},{29,1},{1,5},{5,... | collective-permute-start | bytes 18440 | tf_op jit(solution)/shard_map/ppermute | solution.py:112
  89.0 11.4 %collective-permute-start.16 = (f32[24,16,64]{2,1,0:T(8,128)S(1)}, f32[24,16,64]{2,1,0:T(8,128)S(1)}, u32[]{:S(2)}, u32[]{:S(2)}) collective-permute-start(f32[24,16,64]{2,1,0:T(8,128)S(1)} %get-tuple-element.57), channel_id=1, source_target_pairs={{1,0},{2,1},{3,2},{0,3},{5,4},{6,5},{7,6},{4,7},{9,8},{10,9},{11,1... | collective-permute-start | bytes 294920 | tf_op jit(solution)/shard_map/ppermute | solution.py:112
  89.2 11.2 %collective-permute-start.17 = (f32[24,16,64]{2,1,0:T(8,128)S(1)}, f32[24,16,64]{2,1,0:T(8,128)S(1)}, u32[]{:S(2)}, u32[]{:S(2)}) collective-permute-start(f32[24,16,64]{2,1,0:T(8,128)S(1)} %get-tuple-element.56), channel_id=1, source_target_pairs={{3,0},{0,1},{1,2},{2,3},{7,4},{4,5},{5,6},{6,7},{11,8},{8,9},{9,10... | collective-permute-start | bytes 294920 | tf_op jit(solution)/shard_map/ppermute | solution.py:112
  89.6 6.1 %collective-permute-start.18 = (f32[24,4,128]{2,1,0:T(4,128)S(1)}, f32[24,4,128]{2,1,0:T(4,128)S(1)}, u32[]{:S(2)}, u32[]{:S(2)}) collective-permute-start(f32[24,4,128]{2,1,0:T(4,128)S(1)} %slice.50), channel_id=1, source_target_pairs={{4,0},{8,4},{12,8},{16,12},{20,16},{28,24},{0,28},{5,1},{9,5},{13,... | collective-permute-start | bytes 147464 | tf_op jit(solution)/shard_map/ppermute | solution.py:112
  91.6 8.8 %collective-permute-start.19 = (f32[24,4,128]{2,1,0:T(4,128)S(1)}, f32[24,4,128]{2,1,0:T(4,128)S(1)}, u32[]{:S(2)}, u32[]{:S(2)}) collective-permute-start(f32[24,4,128]{2,1,0:T(4,128)S(1)} %slice.51), channel_id=1, source_target_pairs={{28,0},{0,4},{4,8},{8,12},{12,16},{16,20},{24,28},{29,1},{1,5},{5,... | collective-permute-start | bytes 147464 | tf_op jit(solution)/shard_map/ppermute | solution.py:112
  106.9 11.4 %collective-permute-start.20 = (f32[24,16,64]{2,1,0:T(8,128)}, f32[24,16,64]{2,1,0:T(8,128)S(1)}, u32[]{:S(2)}, u32[]{:S(2)}) collective-permute-start(f32[24,16,64]{2,1,0:T(8,128)} %get-tuple-element.44), channel_id=1, source_target_pairs={{1,0},{2,1},{3,2},{0,3},{5,4},{6,5},{7,6},{4,7},{9,8},{10,9},{11,1... | collective-permute-start | bytes 294920 | tf_op jit(solution)/shard_map/ppermute | solution.py:112
  107.4 10.9 %collective-permute-start.21 = (f32[24,16,64]{2,1,0:T(8,128)}, f32[24,16,64]{2,1,0:T(8,128)S(1)}, u32[]{:S(2)}, u32[]{:S(2)}) collective-permute-start(f32[24,16,64]{2,1,0:T(8,128)} %get-tuple-element.45), channel_id=1, source_target_pairs={{3,0},{0,1},{1,2},{2,3},{7,4},{4,5},{5,6},{6,7},{11,8},{8,9},{9,10... | collective-permute-start | bytes 294920 | tf_op jit(solution)/shard_map/ppermute | solution.py:112
  107.4 6.5 %collective-permute-start.22 = (f32[24,4,128]{2,1,0:T(4,128)}, f32[24,4,128]{2,1,0:T(4,128)S(1)}, u32[]{:S(2)}, u32[]{:S(2)}) collective-permute-start(f32[24,4,128]{2,1,0:T(4,128)} %get-tuple-element.46), channel_id=1, source_target_pairs={{4,0},{8,4},{12,8},{16,12},{20,16},{28,24},{0,28},{5,1},{9,5},{13,... | collective-permute-start | bytes 147464 | tf_op jit(solution)/shard_map/ppermute | solution.py:112
  109.4 9.0 %collective-permute-start.23 = (f32[24,4,128]{2,1,0:T(4,128)}, f32[24,4,128]{2,1,0:T(4,128)S(1)}, u32[]{:S(2)}, u32[]{:S(2)}) collective-permute-start(f32[24,4,128]{2,1,0:T(4,128)} %get-tuple-element.47), channel_id=1, source_target_pairs={{28,0},{0,4},{4,8},{8,12},{12,16},{16,20},{24,28},{29,1},{1,5},{5,... | collective-permute-start | bytes 147464 | tf_op jit(solution)/shard_map/ppermute | solution.py:112
  (28 other events, 90.2 us)

commit v11 on v9

--- a/solution.py
+++ b/solution.py
@@ -436,14 +436,101 @@
     out_ref[1] = result[1]
 
 
+def coarse_step_kernel(*refs, count):
+    refs = list(refs)
+    acc_ref = refs.pop()
+    out_ref = refs.pop()
+    source_ref, inverse_ref, operator_ref, current_ref = refs[:4]
+    nearby_refs = refs[4:]
+    step_index = pl.program_id(0)
+    width = source_ref.shape[-1]
+    chunks = width // 128
+    lane = lax.broadcasted_iota(jnp.int32, (1, width), 1)
+    position = lane % AGG
+    selector = (
+        lax.broadcasted_iota(jnp.int32, (8, 128), 1) // AGG == lax.broadcasted_iota(jnp.int32, (8, 128), 0)
+    ).astype(jnp.float32)
+
+    def reduce_flat(product):
+        partial = product[:, 0:128]
+        for q in range(1, chunks):
+            partial = partial + product[:, q * 128:(q + 1) * 128]
+        for shift in (64, 32, 16):
+            partial = partial + pltpu.roll(partial, shift, 1)
+        pieces = [
+            jnp.sum(partial[8 * q:8 * q + 8] * selector, axis=0, keepdims=True) for q in range(chunks)
+        ]
+        return jnp.concatenate(pieces, axis=1)
+
+    def roll_within(vector, shift):
+        pieces = [pltpu.roll(vector[:, q * 128:(q + 1) * 128], shift % 128, 1) for q in range(chunks)]
+        return jnp.concatenate(pieces, axis=1)
+
+    def product(blocks_ref, index, vector):
+        block_real = blocks_ref[index + (0,)].astype(jnp.float32)
+        block_imag = blocks_ref[index + (1,)].astype(jnp.float32)
+        return [
+            block_real * vector[0] - block_imag * vector[1],
+            block_real * vector[1] + block_imag * vector[0],
+        ]
+
+    def vector_of(direction):
+        current = [current_ref[0], current_ref[1]]
+        if direction == 0:
+            return current
+        if direction == 1:
+            return [jnp.where(position == AGG - 1, roll_within(c, AGG - 1), roll_within(c, -1)) for c in current]
+        if direction == 2:
+            return [jnp.where(position == 0, roll_within(c, 1 - AGG), roll_within(c, 1)) for c in current]
+        ref = nearby_refs[direction - 3]
+        return [ref[0], ref[1]]
+
+    for direction in range(count):
+        @pl.when(step_index == direction)
+        def _():
+            part = product(operator_ref, (0,), vector_of(direction))
+            if direction == 0:
+                acc_ref[0] = part[0]
+                acc_ref[1] = part[1]
+            else:
+                acc_ref[0] = acc_ref[0] + part[0]
+                acc_ref[1] = acc_ref[1] + part[1]
+
+    @pl.when(step_index == count - 1)
+    def _():
+        residue = [source_ref[0] - reduce_flat(acc_ref[0]), source_ref[1] - reduce_flat(acc_ref[1])]
+        acc = product(inverse_ref, (), residue)
+        out_ref[0] = current_ref[0] + reduce_flat(acc[0])
+        out_ref[1] = current_ref[1] + reduce_flat(acc[1])
+
+
 def run_coarse(source, inverse_blocks, operator_blocks, current, nearby):
-    operands = [source, inverse_blocks]
-    present = ()
-    if current is not None:
-        present = tuple(v is not None for v in nearby)
-        operands += [operator_blocks, current] + [v for v in nearby if v is not None]
-    kernel = functools.partial(coarse_kernel, present=present)
-    return pl.pallas_call(kernel, out_shape=jax.ShapeDtypeStruct(source.shape, jnp.float32))(*operands)
+    if current is None:
+        kernel = functools.partial(coarse_kernel, present=())
+        return pl.pallas_call(kernel, out_shape=jax.ShapeDtypeStruct(source.shape, jnp.float32))(
+            source, inverse_blocks
+        )
+    present = [v is not None for v in nearby]
+    count = 3 + sum(present)
+    if present[:count - 3] != [True] * (count - 3):
+        raise ValueError("not a prefix")
+    arrays = [v for v in nearby if v is not None]
+
+    def whole(array):
+        return pl.BlockSpec(array.shape, lambda i, n=array.ndim: (0,) * n)
+
+    in_specs = [whole(source), whole(inverse_blocks)]
+    in_specs.append(pl.BlockSpec((1,) + operator_blocks.shape[1:], lambda i: (i, 0, 0, 0)))
+    in_specs += [whole(current)] + [whole(v) for v in arrays]
+    kernel = functools.partial(coarse_step_kernel, count=count)
+    return pl.pallas_call(
+        kernel,
+        out_shape=jax.ShapeDtypeStruct(source.shape, jnp.float32),
+        grid=(count,),
+        in_specs=in_specs,
+        out_specs=whole(source),
+        scratch_shapes=[pltpu.VMEM((2,) + operator_blocks.shape[2:], jnp.float32)],
+    )(source, inverse_blocks, operator_blocks, current, *arrays)
 
 
 def body(

time: 125 us -> 130 us (1.040)
  Pallas kernels: 30.2 us -> 34.9 us
    pallas_call x3, Pallas kernels: 7.77 us -> 12.4 us  [run_coarse(): pl.pallas_call(kernel, out_shape=jax.ShapeDtypeStruct(source.shape, jnp.f...]
where the time goes in v11:
time: 130 us; the launch traced here: 129 us
  starting transfers between devices  43.5 us (33%)
  Pallas kernels  34.9 us (27%)
  waiting for transfers between devices  25.3 us (19%)
  local copies, waits for them, and re-layouts  19.1 us (15%)
  matrix products  2.95 us (2%)
  other arithmetic  1.91 us (1%)
    ppermute x24, starting transfers between devices, permute_from(): return lax.ppermute(value, axis, pairs)  43.5 us
    ppermute x24, waiting for transfers between devices, permute_from(): return lax.ppermute(value, axis, pairs)  25.3 us
    pallas_call x5, Pallas kernels, run_pass(): pl.pallas_call(kernel, out_shape=out_shape, scratch_shapes=scratch, in_sp...  22.5 us
    pallas_call x3, Pallas kernels, run_coarse(): pl.pallas_call(kernel, out_shape=jax.ShapeDtypeStruct(source.shape, jnp.f...  12.4 us
    unnamed x57, local copies, waits for them, and re-layouts  11.1 us
    reshape x1, local copies, waits for them, and re-layouts, body(): vectors = test_vectors.reshape(NVEC, 2, 2, 6, site_count)  4.03 us
  transfers between devices with their start and end apart: 24, of which 7 were waited for; matrix products, arithmetic and copies ran while one was open for 8% of the time, Pallas kernels for 0%

profile of v11, /device:TPU:0, one launch (start us, length us, event | category | flops | bytes accessed | tf_op | source)
XLA Modules:
  0.0 128.8 jit_solution(2458525769180623465)
XLA Ops:
  2.0 4.2 %shard_map.86 = (f32[24,16,128]{2,1,0:T(8,128)}, f32[24,16,64]{2,1,0:T(8,128)}, f32[42,16,64]{2,1,0:T(8,128)}, f32[24,4,128]{2,1,0:T(4,128)}, f32[42,4,128]{2,1,0:T(4,128)}) custom-call(f32[24,16,128]{2,1,0:T(8,128)} %bitcast.52, bf16[4,18,16,128]{3,2,1,0:T(8,128)(2,1)} %bitcast.45, s32[16,128]{1,0:T(8,128)} %reshape.94.refs_2_.refs_3_, s32[16]{0:T(128)} %bitcast.65), custom_call_target="tpu_custom_call" | custom-call | tf_op jit(solution)/shard_map/pallas_call | solution.py:363
  6.7 1.9 %collective-permute-start = (f32[24,16,64]{2,1,0:T(8,128)}, f32[24,16,64]{2,1,0:T(8,128)S(1)}, u32[]{:S(2)}, u32[]{:S(2)}) collective-permute-start(f32[24,16,64]{2,1,0:T(8,128)} %get-tuple-element.22), channel_id=1, source_target_pairs={{1,0},{2,1},{3,2},{0,3},{5,4},{6,5},{7,6},{4,7},{9,8},{10,9},{11,1... | collective-permute-start | bytes 294920 | tf_op jit(solution)/shard_map/ppermute | solution.py:112
  8.6 4.2 %collective-permute-start.3 = (f32[42,4,128]{2,1,0:T(4,128)}, f32[42,4,128]{2,1,0:T(4,128)S(1)}, u32[]{:S(2)}, u32[]{:S(2)}) collective-permute-start(f32[42,4,128]{2,1,0:T(4,128)} %get-tuple-element.25), channel_id=1, source_target_pairs={{28,0},{0,4},{4,8},{8,12},{12,16},{16,20},{24,28},{29,1},{1,5},{5,... | collective-permute-start | bytes 258056 | tf_op jit(solution)/shard_map/ppermute | solution.py:112
  12.9 5.0 %collective-permute-start.2 = (f32[24,4,128]{2,1,0:T(4,128)}, f32[24,4,128]{2,1,0:T(4,128)S(1)}, u32[]{:S(2)}, u32[]{:S(2)}) collective-permute-start(f32[24,4,128]{2,1,0:T(4,128)} %get-tuple-element.24), channel_id=1, source_target_pairs={{4,0},{8,4},{12,8},{16,12},{20,16},{28,24},{0,28},{5,1},{9,5},{13,... | collective-permute-start | bytes 147464 | tf_op jit(solution)/shard_map/ppermute | solution.py:112
  18.6 4.3 %copy.17 = bf16[1,24,24,4,4,128]{5,4,3,1,2,0:T(4,128)(2,1)} copy(bf16[1,24,24,4,4,128]{5,4,3,2,1,0:T(4,128)(2,1)} %param.9) | data formatting | bytes 4718592 | tf_op args[2]
  22.9 4.0 %reshape.96 = bf16[24,2,2,6,2048]{4,0,3,2,1:T(8,128)(2,1)S(1)} reshape(bf16[1,24,24,4,4,128]{5,4,3,1,2,0:T(4,128)(2,1)} %copy.17) | data formatting | bytes 4718592 | tf_op jit(solution)/shard_map/reshape | solution.py:607
  28.5 5.4 %shard_map.87 = (f32[24,16,128]{2,1,0:T(8,128)}, f32[24,16,64]{2,1,0:T(8,128)}, f32[24,16,64]{2,1,0:T(8,128)}, f32[24,4,128]{2,1,0:T(4,128)}, f32[24,4,128]{2,1,0:T(4,128)}, /*index=5*/bf16[4,18,16,128]{3,2,1,0:T(8,128)(2,1)}) custom-call(f32[24,16,128]{2,1,0:T(8,128)} %bitcast.53, bf16[4,18,16,128]{3,2,1,0:T(8,128)(2,1)} %bitcast.46, ...), custom_call_target="tpu_custom_call" | custom-call | tf_op jit(solution)/shard_map/pallas_call | solution.py:363
  34.3 3.9 %collective-permute-start.6 = (f32[24,4,128]{2,1,0:T(4,128)}, f32[24,4,128]{2,1,0:T(4,128)S(1)}, u32[]{:S(2)}, u32[]{:S(2)}) collective-permute-start(f32[24,4,128]{2,1,0:T(4,128)} %get-tuple-element.31), channel_id=1, source_target_pairs={{4,0},{8,4},{12,8},{16,12},{20,16},{28,24},{0,28},{5,1},{9,5},{13,... | collective-permute-start | bytes 147464 | tf_op jit(solution)/shard_map/ppermute | solution.py:112
  40.7 6.9 %collective-permute-done.7.refs_8_ = f32[24,4,128]{2,1,0:T(4,128)S(1)} collective-permute-done((f32[24,4,128]{2,1,0:T(4,128)}, f32[24,4,128]{2,1,0:T(4,128)S(1)}, u32[]{:S(2)}, u32[]{:S(2)}) %collective-permute-start.7) | collective-permute-done | bytes 49184 | tf_op jit(solution)/shard_map/ppermute | solution.py:112
  48.3 2.7 %shard_map.88 = bf16[24,16,128]{2,1,0:T(8,128)(2,1)} custom-call(f32[24,16,128]{2,1,0:T(8,128)} %bitcast.54, bf16[4,18,16,128]{3,2,1,0:T(8,128)(2,1)} %bitcast.47, bf16[4,18,16,128]{3,2,1,0:T(8,128)(2,1)} %get-tuple-element.26.refs_2_, s32[16,128]{1,0:T(8,128)} %reshape.94.refs_2_.refs_3_, f32[24,16,128]{2,1,0:T(8,128)} %get-tuple-element.27.refs_4_, ...), custom_call_target="tpu_custom_call" | custom-call | tf_op jit(solution)/shard_map/pallas_call | solution.py:363
  52.1 2.5 %fusion.8 = f32[2,2,2,24,16]{3,4,0,1,2:T(8,128)S(1)} fusion(bf16[2048,16]{0,1:T(8,128)(2,1)S(1)} %convert_convert_fusion, bf16[24,2,2,6,2048]{4,0,3,2,1:T(8,128)(2,1)S(1)} %reshape.96, bf16[2,2,6,2048]{3,2,1,0:T(8,128)(2,1)S(1)} %mul.20), kind=kOutput, calls=%fused_computation.12 | convolution fusion | flops 78643200 | bytes 2535424 | tf_op jit(solution)/shard_map/krxqn,sxqnj->rsxkj/dot_general | solution.py:634
  59.8 3.9 %collective-permute-start.11 = (f32[2,1,768]{2,1,0:T(1,128)}, f32[2,1,768]{2,1,0:T(1,128)S(1)}, u32[]{:S(2)}, u32[]{:S(2)}) collective-permute-start(f32[2,1,768]{2,1,0:T(1,128)} %shard_map.89.refs_3_), channel_id=1, source_target_pairs={{28,0},{0,4},{4,8},{8,12},{12,16},{16,20},{24,28},{29,1},{1,5},{5,... | collective-permute-start | bytes 18440 | tf_op jit(solution)/shard_map/ppermute | solution.py:112
  63.8 4.4 %collective-permute-done.11.refs_7_ = f32[2,1,768]{2,1,0:T(1,128)S(1)} collective-permute-done((f32[2,1,768]{2,1,0:T(1,128)}, f32[2,1,768]{2,1,0:T(1,128)S(1)}, u32[]{:S(2)}, u32[]{:S(2)}) %collective-permute-start.11) | collective-permute-done | bytes 6176 | tf_op jit(solution)/shard_map/ppermute | solution.py:112
  68.8 5.3 %shard_map.90.refs_3_ = f32[2,1,768]{2,1,0:T(1,128)} custom-call(f32[2,1,768]{2,1,0:T(1,128)} %copy-done.11, bf16[2,48,768]{2,1,0:T(8,128)(2,1)} %bitcast.60, bf16[9,2,48,768]{3,2,1,0:T(8,128)(2,1)} %bitcast.50, f32[2,1,768]{2,1,0:T(1,128)} %shard_map.89.refs_3_, f32[2,1,768]{2,1,0:T(1,128)} %copy-done.20, f32[2,1,768]{2,1,0:T(1,128)} %copy-done.22, ...), custom_call_target="tpu_custom_call" | custom-call | tf_op jit(solution)/shard_map/pallas_call | solution.py:526
  76.5 4.1 %collective-permute-start.15 = (f32[2,1,768]{2,1,0:T(1,128)}, f32[2,1,768]{2,1,0:T(1,128)S(1)}, u32[]{:S(2)}, u32[]{:S(2)}) collective-permute-start(f32[2,1,768]{2,1,0:T(1,128)} %shard_map.90.refs_3_), channel_id=1, source_target_pairs={{28,0},{0,4},{4,8},{8,12},{12,16},{16,20},{24,28},{29,1},{1,5},{5,... | collective-permute-start | bytes 18440 | tf_op jit(solution)/shard_map/ppermute | solution.py:112
  80.7 4.3 %collective-permute-done.15.refs_7_ = f32[2,1,768]{2,1,0:T(1,128)S(1)} collective-permute-done((f32[2,1,768]{2,1,0:T(1,128)}, f32[2,1,768]{2,1,0:T(1,128)S(1)}, u32[]{:S(2)}, u32[]{:S(2)}) %collective-permute-start.15) | collective-permute-done | bytes 6176 | tf_op jit(solution)/shard_map/ppermute | solution.py:112
  85.6 5.3 %shard_map.91 = f32[2,1,768]{2,1,0:T(1,128)} custom-call(f32[2,1,768]{2,1,0:T(1,128)} %copy-done.11, bf16[2,48,768]{2,1,0:T(8,128)(2,1)} %bitcast.61, bf16[9,2,48,768]{3,2,1,0:T(8,128)(2,1)} %bitcast.51, f32[2,1,768]{2,1,0:T(1,128)} %shard_map.90.refs_3_, f32[2,1,768]{2,1,0:T(1,128)} %copy-done.19, f32[2,1,768]{2,1,0:T(1,128)} %copy-done.21, ...), custom_call_target="tpu_custom_call" | custom-call | tf_op jit(solution)/shard_map/pallas_call | solution.py:526
  94.3 1.9 %collective-permute-start.18 = (f32[24,4,128]{2,1,0:T(4,128)S(1)}, f32[24,4,128]{2,1,0:T(4,128)S(1)}, u32[]{:S(2)}, u32[]{:S(2)}) collective-permute-start(f32[24,4,128]{2,1,0:T(4,128)S(1)} %slice.50), channel_id=1, source_target_pairs={{4,0},{8,4},{12,8},{16,12},{20,16},{28,24},{0,28},{5,1},{9,5},{13,... | collective-permute-start | bytes 147464 | tf_op jit(solution)/shard_map/ppermute | solution.py:112
  96.2 3.9 %collective-permute-start.19 = (f32[24,4,128]{2,1,0:T(4,128)S(1)}, f32[24,4,128]{2,1,0:T(4,128)S(1)}, u32[]{:S(2)}, u32[]{:S(2)}) collective-permute-start(f32[24,4,128]{2,1,0:T(4,128)S(1)} %slice.51), channel_id=1, source_target_pairs={{28,0},{0,4},{4,8},{8,12},{12,16},{16,20},{24,28},{29,1},{1,5},{5,... | collective-permute-start | bytes 147464 | tf_op jit(solution)/shard_map/ppermute | solution.py:112
  100.4 4.6 %collective-permute-done.19.refs_9_ = f32[24,4,128]{2,1,0:T(4,128)S(1)} collective-permute-done((f32[24,4,128]{2,1,0:T(4,128)S(1)}, f32[24,4,128]{2,1,0:T(4,128)S(1)}, u32[]{:S(2)}, u32[]{:S(2)}) %collective-permute-start.19) | collective-permute-done | bytes 49184 | tf_op jit(solution)/shard_map/ppermute | solution.py:112
  106.4 5.2 %shard_map.92 = (f32[24,16,128]{2,1,0:T(8,128)}, f32[24,16,64]{2,1,0:T(8,128)}, f32[24,16,64]{2,1,0:T(8,128)}, f32[24,4,128]{2,1,0:T(4,128)}, f32[24,4,128]{2,1,0:T(4,128)}) custom-call(f32[24,16,128]{2,1,0:T(8,128)} %bitcast.55, bf16[4,18,16,128]{3,2,1,0:T(8,128)(2,1)} %bitcast.48, bf16[4,18,16,128]{3,2,1,0:T(8,128)(2,1)} %get-tuple-element.26.refs_2_, ...), custom_call_target="tpu_custom_call" | custom-call | tf_op jit(solution)/shard_map/pallas_call | solution.py:363
  114.0 3.9 %collective-permute-start.23 = (f32[24,4,128]{2,1,0:T(4,128)}, f32[24,4,128]{2,1,0:T(4,128)S(1)}, u32[]{:S(2)}, u32[]{:S(2)}) collective-permute-start(f32[24,4,128]{2,1,0:T(4,128)} %get-tuple-element.37), channel_id=1, source_target_pairs={{28,0},{0,4},{4,8},{8,12},{12,16},{16,20},{24,28},{29,1},{1,5},{5,... | collective-permute-start | bytes 147464 | tf_op jit(solution)/shard_map/ppermute | solution.py:112
  118.7 4.3 %collective-permute-done.23.refs_9_ = f32[24,4,128]{2,1,0:T(4,128)S(1)} collective-permute-done((f32[24,4,128]{2,1,0:T(4,128)}, f32[24,4,128]{2,1,0:T(4,128)S(1)}, u32[]{:S(2)}, u32[]{:S(2)}) %collective-permute-start.23) | collective-permute-done | bytes 49184 | tf_op jit(solution)/shard_map/ppermute | solution.py:112
  123.8 5.0 %shard_map.93 = f32[24,16,128]{2,1,0:T(8,128)} custom-call(f32[24,16,128]{2,1,0:T(8,128)} %bitcast.56, bf16[4,18,16,128]{3,2,1,0:T(8,128)(2,1)} %bitcast.49, bf16[4,18,16,128]{3,2,1,0:T(8,128)(2,1)} %get-tuple-element.26.refs_2_, s32[16,128]{1,0:T(8,128)} %reshape.94.refs_2_.refs_3_, s32[16]{0:T(128)} %bitcast.68, f32[24,16,128]{2,1,0:T(8,128)} %get-tuple-element.33.refs_5_, ...), custom_call_target="tpu_custom_call" | custom-call | tf_op jit(solution)/shard_map/pallas_call | solution.py:363
  (113 shorter events, 26.5 us)
Async XLA Ops:
  6.2 20.8 %collective-permute-start.1 = (f32[42,16,64]{2,1,0:T(8,128)}, f32[42,16,64]{2,1,0:T(8,128)S(1)}, u32[]{:S(2)}, u32[]{:S(2)}) collective-permute-start(f32[42,16,64]{2,1,0:T(8,128)} %get-tuple-element.23), channel_id=1, source_target_pairs={{3,0},{0,1},{1,2},{2,3},{7,4},{4,5},{5,6},{6,7},{11,8},{8,9},{9,10... | collective-permute-start | bytes 516104 | tf_op jit(solution)/shard_map/ppermute | solution.py:112
  6.7 20.3 %collective-permute-start = (f32[24,16,64]{2,1,0:T(8,128)}, f32[24,16,64]{2,1,0:T(8,128)S(1)}, u32[]{:S(2)}, u32[]{:S(2)}) collective-permute-start(f32[24,16,64]{2,1,0:T(8,128)} %get-tuple-element.22), channel_id=1, source_target_pairs={{1,0},{2,1},{3,2},{0,3},{5,4},{6,5},{7,6},{4,7},{9,8},{10,9},{11,1... | collective-permute-start | bytes 294920 | tf_op jit(solution)/shard_map/ppermute | solution.py:112
  8.6 18.4 %collective-permute-start.3 = (f32[42,4,128]{2,1,0:T(4,128)}, f32[42,4,128]{2,1,0:T(4,128)S(1)}, u32[]{:S(2)}, u32[]{:S(2)}) collective-permute-start(f32[42,4,128]{2,1,0:T(4,128)} %get-tuple-element.25), channel_id=1, source_target_pairs={{28,0},{0,4},{4,8},{8,12},{12,16},{16,20},{24,28},{29,1},{1,5},{5,... | collective-permute-start | bytes 258056 | tf_op jit(solution)/shard_map/ppermute | solution.py:112
  12.9 14.1 %collective-permute-start.2 = (f32[24,4,128]{2,1,0:T(4,128)}, f32[24,4,128]{2,1,0:T(4,128)S(1)}, u32[]{:S(2)}, u32[]{:S(2)}) collective-permute-start(f32[24,4,128]{2,1,0:T(4,128)} %get-tuple-element.24), channel_id=1, source_target_pairs={{4,0},{8,4},{12,8},{16,12},{20,16},{28,24},{0,28},{5,1},{9,5},{13,... | collective-permute-start | bytes 147464 | tf_op jit(solution)/shard_map/ppermute | solution.py:112
  33.8 13.8 %collective-permute-start.4 = (f32[24,16,64]{2,1,0:T(8,128)}, f32[24,16,64]{2,1,0:T(8,128)S(1)}, u32[]{:S(2)}, u32[]{:S(2)}) collective-permute-start(f32[24,16,64]{2,1,0:T(8,128)} %get-tuple-element.29), channel_id=1, source_target_pairs={{1,0},{2,1},{3,2},{0,3},{5,4},{6,5},{7,6},{4,7},{9,8},{10,9},{11,1... | collective-permute-start | bytes 294920 | tf_op jit(solution)/shard_map/ppermute | solution.py:112
  33.8 13.8 %collective-permute-start.5 = (f32[24,16,64]{2,1,0:T(8,128)}, f32[24,16,64]{2,1,0:T(8,128)S(1)}, u32[]{:S(2)}, u32[]{:S(2)}) collective-permute-start(f32[24,16,64]{2,1,0:T(8,128)} %get-tuple-element.30), channel_id=1, source_target_pairs={{3,0},{0,1},{1,2},{2,3},{7,4},{4,5},{5,6},{6,7},{11,8},{8,9},{9,10... | collective-permute-start | bytes 294920 | tf_op jit(solution)/shard_map/ppermute | solution.py:112
  34.3 6.4 %collective-permute-start.6 = (f32[24,4,128]{2,1,0:T(4,128)}, f32[24,4,128]{2,1,0:T(4,128)S(1)}, u32[]{:S(2)}, u32[]{:S(2)}) collective-permute-start(f32[24,4,128]{2,1,0:T(4,128)} %get-tuple-element.31), channel_id=1, source_target_pairs={{4,0},{8,4},{12,8},{16,12},{20,16},{28,24},{0,28},{5,1},{9,5},{13,... | collective-permute-start | bytes 147464 | tf_op jit(solution)/shard_map/ppermute | solution.py:112
  38.2 9.3 %collective-permute-start.7 = (f32[24,4,128]{2,1,0:T(4,128)}, f32[24,4,128]{2,1,0:T(4,128)S(1)}, u32[]{:S(2)}, u32[]{:S(2)}) collective-permute-start(f32[24,4,128]{2,1,0:T(4,128)} %get-tuple-element.32), channel_id=1, source_target_pairs={{28,0},{0,4},{4,8},{8,12},{12,16},{16,20},{24,28},{29,1},{1,5},{5,... | collective-permute-start | bytes 147464 | tf_op jit(solution)/shard_map/ppermute | solution.py:112
  57.4 6.4 %collective-permute-start.8 = (f32[2,1,768]{2,1,0:T(1,128)}, f32[2,1,768]{2,1,0:T(1,128)S(1)}, u32[]{:S(2)}, u32[]{:S(2)}) collective-permute-start(f32[2,1,768]{2,1,0:T(1,128)} %shard_map.89.refs_3_), channel_id=1, source_target_pairs={{1,0},{2,1},{3,2},{0,3},{5,4},{6,5},{7,6},{4,7},{9,8},{10,9},{11,1... | collective-permute-start | bytes 18440 | tf_op jit(solution)/shard_map/ppermute | solution.py:112
  57.4 6.4 %collective-permute-start.9 = (f32[2,1,768]{2,1,0:T(1,128)}, f32[2,1,768]{2,1,0:T(1,128)S(1)}, u32[]{:S(2)}, u32[]{:S(2)}) collective-permute-start(f32[2,1,768]{2,1,0:T(1,128)} %shard_map.89.refs_3_), channel_id=1, source_target_pairs={{3,0},{0,1},{1,2},{2,3},{7,4},{4,5},{5,6},{6,7},{11,8},{8,9},{9,10... | collective-permute-start | bytes 18440 | tf_op jit(solution)/shard_map/ppermute | solution.py:112
  57.9 5.9 %collective-permute-start.10 = (f32[2,1,768]{2,1,0:T(1,128)}, f32[2,1,768]{2,1,0:T(1,128)S(1)}, u32[]{:S(2)}, u32[]{:S(2)}) collective-permute-start(f32[2,1,768]{2,1,0:T(1,128)} %shard_map.89.refs_3_), channel_id=1, source_target_pairs={{4,0},{8,4},{12,8},{16,12},{20,16},{28,24},{0,28},{5,1},{9,5},{13,... | collective-permute-start | bytes 18440 | tf_op jit(solution)/shard_map/ppermute | solution.py:112
  59.8 8.4 %collective-permute-start.11 = (f32[2,1,768]{2,1,0:T(1,128)}, f32[2,1,768]{2,1,0:T(1,128)S(1)}, u32[]{:S(2)}, u32[]{:S(2)}) collective-permute-start(f32[2,1,768]{2,1,0:T(1,128)} %shard_map.89.refs_3_), channel_id=1, source_target_pairs={{28,0},{0,4},{4,8},{8,12},{12,16},{16,20},{24,28},{29,1},{1,5},{5,... | collective-permute-start | bytes 18440 | tf_op jit(solution)/shard_map/ppermute | solution.py:112
  74.1 6.5 %collective-permute-start.12 = (f32[2,1,768]{2,1,0:T(1,128)}, f32[2,1,768]{2,1,0:T(1,128)S(1)}, u32[]{:S(2)}, u32[]{:S(2)}) collective-permute-start(f32[2,1,768]{2,1,0:T(1,128)} %shard_map.90.refs_3_), channel_id=1, source_target_pairs={{1,0},{2,1},{3,2},{0,3},{5,4},{6,5},{7,6},{4,7},{9,8},{10,9},{11,1... | collective-permute-start | bytes 18440 | tf_op jit(solution)/shard_map/ppermute | solution.py:112
  74.2 6.5 %collective-permute-start.13 = (f32[2,1,768]{2,1,0:T(1,128)}, f32[2,1,768]{2,1,0:T(1,128)S(1)}, u32[]{:S(2)}, u32[]{:S(2)}) collective-permute-start(f32[2,1,768]{2,1,0:T(1,128)} %shard_map.90.refs_3_), channel_id=1, source_target_pairs={{3,0},{0,1},{1,2},{2,3},{7,4},{4,5},{5,6},{6,7},{11,8},{8,9},{9,10... | collective-permute-start | bytes 18440 | tf_op jit(solution)/shard_map/ppermute | solution.py:112
  74.6 6.1 %collective-permute-start.14 = (f32[2,1,768]{2,1,0:T(1,128)}, f32[2,1,768]{2,1,0:T(1,128)S(1)}, u32[]{:S(2)}, u32[]{:S(2)}) collective-permute-start(f32[2,1,768]{2,1,0:T(1,128)} %shard_map.90.refs_3_), channel_id=1, source_target_pairs={{4,0},{8,4},{12,8},{16,12},{20,16},{28,24},{0,28},{5,1},{9,5},{13,... | collective-permute-start | bytes 18440 | tf_op jit(solution)/shard_map/ppermute | solution.py:112
  76.5 8.4 %collective-permute-start.15 = (f32[2,1,768]{2,1,0:T(1,128)}, f32[2,1,768]{2,1,0:T(1,128)S(1)}, u32[]{:S(2)}, u32[]{:S(2)}) collective-permute-start(f32[2,1,768]{2,1,0:T(1,128)} %shard_map.90.refs_3_), channel_id=1, source_target_pairs={{28,0},{0,4},{4,8},{8,12},{12,16},{16,20},{24,28},{29,1},{1,5},{5,... | collective-permute-start | bytes 18440 | tf_op jit(solution)/shard_map/ppermute | solution.py:112
  93.6 11.4 %collective-permute-start.16 = (f32[24,16,64]{2,1,0:T(8,128)S(1)}, f32[24,16,64]{2,1,0:T(8,128)S(1)}, u32[]{:S(2)}, u32[]{:S(2)}) collective-permute-start(f32[24,16,64]{2,1,0:T(8,128)S(1)} %get-tuple-element.47), channel_id=1, source_target_pairs={{1,0},{2,1},{3,2},{0,3},{5,4},{6,5},{7,6},{4,7},{9,8},{10,9},{11,1... | collective-permute-start | bytes 294920 | tf_op jit(solution)/shard_map/ppermute | solution.py:112
  93.9 11.2 %collective-permute-start.17 = (f32[24,16,64]{2,1,0:T(8,128)S(1)}, f32[24,16,64]{2,1,0:T(8,128)S(1)}, u32[]{:S(2)}, u32[]{:S(2)}) collective-permute-start(f32[24,16,64]{2,1,0:T(8,128)S(1)} %get-tuple-element.46), channel_id=1, source_target_pairs={{3,0},{0,1},{1,2},{2,3},{7,4},{4,5},{5,6},{6,7},{11,8},{8,9},{9,10... | collective-permute-start | bytes 294920 | tf_op jit(solution)/shard_map/ppermute | solution.py:112
  94.3 6.1 %collective-permute-start.18 = (f32[24,4,128]{2,1,0:T(4,128)S(1)}, f32[24,4,128]{2,1,0:T(4,128)S(1)}, u32[]{:S(2)}, u32[]{:S(2)}) collective-permute-start(f32[24,4,128]{2,1,0:T(4,128)S(1)} %slice.50), channel_id=1, source_target_pairs={{4,0},{8,4},{12,8},{16,12},{20,16},{28,24},{0,28},{5,1},{9,5},{13,... | collective-permute-start | bytes 147464 | tf_op jit(solution)/shard_map/ppermute | solution.py:112
  96.2 8.8 %collective-permute-start.19 = (f32[24,4,128]{2,1,0:T(4,128)S(1)}, f32[24,4,128]{2,1,0:T(4,128)S(1)}, u32[]{:S(2)}, u32[]{:S(2)}) collective-permute-start(f32[24,4,128]{2,1,0:T(4,128)S(1)} %slice.51), channel_id=1, source_target_pairs={{28,0},{0,4},{4,8},{8,12},{12,16},{16,20},{24,28},{29,1},{1,5},{5,... | collective-permute-start | bytes 147464 | tf_op jit(solution)/shard_map/ppermute | solution.py:112
  111.6 11.4 %collective-permute-start.20 = (f32[24,16,64]{2,1,0:T(8,128)}, f32[24,16,64]{2,1,0:T(8,128)S(1)}, u32[]{:S(2)}, u32[]{:S(2)}) collective-permute-start(f32[24,16,64]{2,1,0:T(8,128)} %get-tuple-element.34), channel_id=1, source_target_pairs={{1,0},{2,1},{3,2},{0,3},{5,4},{6,5},{7,6},{4,7},{9,8},{10,9},{11,1... | collective-permute-start | bytes 294920 | tf_op jit(solution)/shard_map/ppermute | solution.py:112
  112.1 10.9 %collective-permute-start.21 = (f32[24,16,64]{2,1,0:T(8,128)}, f32[24,16,64]{2,1,0:T(8,128)S(1)}, u32[]{:S(2)}, u32[]{:S(2)}) collective-permute-start(f32[24,16,64]{2,1,0:T(8,128)} %get-tuple-element.35), channel_id=1, source_target_pairs={{3,0},{0,1},{1,2},{2,3},{7,4},{4,5},{5,6},{6,7},{11,8},{8,9},{9,10... | collective-permute-start | bytes 294920 | tf_op jit(solution)/shard_map/ppermute | solution.py:112
  112.1 6.6 %collective-permute-start.22 = (f32[24,4,128]{2,1,0:T(4,128)}, f32[24,4,128]{2,1,0:T(4,128)S(1)}, u32[]{:S(2)}, u32[]{:S(2)}) collective-permute-start(f32[24,4,128]{2,1,0:T(4,128)} %get-tuple-element.36), channel_id=1, source_target_pairs={{4,0},{8,4},{12,8},{16,12},{20,16},{28,24},{0,28},{5,1},{9,5},{13,... | collective-permute-start | bytes 147464 | tf_op jit(solution)/shard_map/ppermute | solution.py:112
  114.0 9.0 %collective-permute-start.23 = (f32[24,4,128]{2,1,0:T(4,128)}, f32[24,4,128]{2,1,0:T(4,128)S(1)}, u32[]{:S(2)}, u32[]{:S(2)}) collective-permute-start(f32[24,4,128]{2,1,0:T(4,128)} %get-tuple-element.37), channel_id=1, source_target_pairs={{28,0},{0,4},{4,8},{8,12},{12,16},{16,20},{24,28},{29,1},{1,5},{5,... | collective-permute-start | bytes 147464 | tf_op jit(solution)/shard_map/ppermute | solution.py:112
  (27 other events, 65.6 us)

commit v12 on v9

--- a/solution.py
+++ b/solution.py
@@ -564,7 +564,7 @@
         correction = run_coarse(flat_source, inverse_blocks, operator_blocks, correction, nearby)
     correction = correction.reshape(2, CDOF, AGG)
     expanded = jnp.dot(
-        correction.reshape(2 * CDOF, AGG), membership.T, precision=lax.Precision.HIGHEST
+        correction.reshape(2 * CDOF, AGG), membership.T, precision=lax.Precision.HIGH
     ).reshape(2, 2, NVEC, site_count)
     spread_real = jnp.swapaxes(expanded[0], 0, 1)[:, :, None]
     spread_imag = jnp.swapaxes(expanded[1], 0, 1)[:, :, None]

time: 125 us -> 125 us (level)
  no operation moved by 1% of the time
where the time goes in v12:
time: 125 us; the launch traced here: 124 us
  starting transfers between devices  43.5 us (35%)
  Pallas kernels  30.2 us (24%)
  waiting for transfers between devices  25.3 us (20%)
  local copies, waits for them, and re-layouts  19.1 us (15%)
  matrix products  2.85 us (2%)
  other arithmetic  1.91 us (2%)
    ppermute x24, starting transfers between devices, permute_from(): return lax.ppermute(value, axis, pairs)  43.5 us
    ppermute x24, waiting for transfers between devices, permute_from(): return lax.ppermute(value, axis, pairs)  25.3 us
    pallas_call x5, Pallas kernels, run_pass(): pl.pallas_call(kernel, out_shape=out_shape, scratch_shapes=scratch, in_sp...  22.5 us
    unnamed x57, local copies, waits for them, and re-layouts  11.1 us
    pallas_call x3, Pallas kernels, run_coarse(): pl.pallas_call(kernel, out_shape=jax.ShapeDtypeStruct(source.shape, jnp.f...  7.77 us
    reshape x1, local copies, waits for them, and re-layouts, body(): vectors = test_vectors.reshape(NVEC, 2, 2, 6, site_count)  4.03 us
    dot_general x1, matrix products, body(): jnp.einsum('krxqn,sxqnj->rsxkj', vectors, weighted, preferred_element_typ...  2.5 us
  transfers between devices with their start and end apart: 24, of which 7 were waited for; matrix products, arithmetic and copies ran while one was open for 8% of the time, Pallas kernels for 0%

profile of v12, /device:TPU:0, one launch (start us, length us, event | category | flops | bytes accessed | tf_op | source)
XLA Modules:
  0.0 124.1 jit_solution(4282364157159341828)
XLA Ops:
  2.0 4.2 %shard_map.86 = (f32[24,16,128]{2,1,0:T(8,128)}, f32[24,16,64]{2,1,0:T(8,128)}, f32[42,16,64]{2,1,0:T(8,128)}, f32[24,4,128]{2,1,0:T(4,128)}, f32[42,4,128]{2,1,0:T(4,128)}) custom-call(f32[24,16,128]{2,1,0:T(8,128)} %bitcast.52, bf16[4,18,16,128]{3,2,1,0:T(8,128)(2,1)} %bitcast.45, s32[16,128]{1,0:T(8,128)} %reshape.94.refs_2_.refs_3_, s32[16]{0:T(128)} %bitcast.65), custom_call_target="tpu_custom_call" | custom-call | tf_op jit(solution)/shard_map/pallas_call | solution.py:363
  6.7 1.9 %collective-permute-start = (f32[24,16,64]{2,1,0:T(8,128)}, f32[24,16,64]{2,1,0:T(8,128)S(1)}, u32[]{:S(2)}, u32[]{:S(2)}) collective-permute-start(f32[24,16,64]{2,1,0:T(8,128)} %get-tuple-element.22), channel_id=1, source_target_pairs={{1,0},{2,1},{3,2},{0,3},{5,4},{6,5},{7,6},{4,7},{9,8},{10,9},{11,1... | collective-permute-start | bytes 294920 | tf_op jit(solution)/shard_map/ppermute | solution.py:112
  8.6 4.2 %collective-permute-start.3 = (f32[42,4,128]{2,1,0:T(4,128)}, f32[42,4,128]{2,1,0:T(4,128)S(1)}, u32[]{:S(2)}, u32[]{:S(2)}) collective-permute-start(f32[42,4,128]{2,1,0:T(4,128)} %get-tuple-element.25), channel_id=1, source_target_pairs={{28,0},{0,4},{4,8},{8,12},{12,16},{16,20},{24,28},{29,1},{1,5},{5,... | collective-permute-start | bytes 258056 | tf_op jit(solution)/shard_map/ppermute | solution.py:112
  12.9 5.0 %collective-permute-start.2 = (f32[24,4,128]{2,1,0:T(4,128)}, f32[24,4,128]{2,1,0:T(4,128)S(1)}, u32[]{:S(2)}, u32[]{:S(2)}) collective-permute-start(f32[24,4,128]{2,1,0:T(4,128)} %get-tuple-element.24), channel_id=1, source_target_pairs={{4,0},{8,4},{12,8},{16,12},{20,16},{28,24},{0,28},{5,1},{9,5},{13,... | collective-permute-start | bytes 147464 | tf_op jit(solution)/shard_map/ppermute | solution.py:112
  18.6 4.3 %copy.17 = bf16[1,24,24,4,4,128]{5,4,3,1,2,0:T(4,128)(2,1)} copy(bf16[1,24,24,4,4,128]{5,4,3,2,1,0:T(4,128)(2,1)} %param.9) | data formatting | bytes 4718592 | tf_op args[2]
  22.9 4.0 %reshape.96 = bf16[24,2,2,6,2048]{4,0,3,2,1:T(8,128)(2,1)S(1)} reshape(bf16[1,24,24,4,4,128]{5,4,3,1,2,0:T(4,128)(2,1)} %copy.17) | data formatting | bytes 4718592 | tf_op jit(solution)/shard_map/reshape | solution.py:520
  28.5 5.4 %shard_map.87 = (f32[24,16,128]{2,1,0:T(8,128)}, f32[24,16,64]{2,1,0:T(8,128)}, f32[24,16,64]{2,1,0:T(8,128)}, f32[24,4,128]{2,1,0:T(4,128)}, f32[24,4,128]{2,1,0:T(4,128)}, /*index=5*/bf16[4,18,16,128]{3,2,1,0:T(8,128)(2,1)}) custom-call(f32[24,16,128]{2,1,0:T(8,128)} %bitcast.53, bf16[4,18,16,128]{3,2,1,0:T(8,128)(2,1)} %bitcast.46, ...), custom_call_target="tpu_custom_call" | custom-call | tf_op jit(solution)/shard_map/pallas_call | solution.py:363
  34.3 3.9 %collective-permute-start.6 = (f32[24,4,128]{2,1,0:T(4,128)}, f32[24,4,128]{2,1,0:T(4,128)S(1)}, u32[]{:S(2)}, u32[]{:S(2)}) collective-permute-start(f32[24,4,128]{2,1,0:T(4,128)} %get-tuple-element.31), channel_id=1, source_target_pairs={{4,0},{8,4},{12,8},{16,12},{20,16},{28,24},{0,28},{5,1},{9,5},{13,... | collective-permute-start | bytes 147464 | tf_op jit(solution)/shard_map/ppermute | solution.py:112
  40.7 6.9 %collective-permute-done.7.refs_8_ = f32[24,4,128]{2,1,0:T(4,128)S(1)} collective-permute-done((f32[24,4,128]{2,1,0:T(4,128)}, f32[24,4,128]{2,1,0:T(4,128)S(1)}, u32[]{:S(2)}, u32[]{:S(2)}) %collective-permute-start.7) | collective-permute-done | bytes 49184 | tf_op jit(solution)/shard_map/ppermute | solution.py:112
  48.3 2.7 %shard_map.88 = bf16[24,16,128]{2,1,0:T(8,128)(2,1)} custom-call(f32[24,16,128]{2,1,0:T(8,128)} %bitcast.54, bf16[4,18,16,128]{3,2,1,0:T(8,128)(2,1)} %bitcast.47, bf16[4,18,16,128]{3,2,1,0:T(8,128)(2,1)} %get-tuple-element.26.refs_2_, s32[16,128]{1,0:T(8,128)} %reshape.94.refs_2_.refs_3_, f32[24,16,128]{2,1,0:T(8,128)} %get-tuple-element.27.refs_4_, ...), custom_call_target="tpu_custom_call" | custom-call | tf_op jit(solution)/shard_map/pallas_call | solution.py:363
  52.1 2.5 %fusion.8 = f32[2,2,2,24,16]{3,4,0,1,2:T(8,128)S(1)} fusion(bf16[2048,16]{0,1:T(8,128)(2,1)S(1)} %convert_convert_fusion, bf16[24,2,2,6,2048]{4,0,3,2,1:T(8,128)(2,1)S(1)} %reshape.96, bf16[2,2,6,2048]{3,2,1,0:T(8,128)(2,1)S(1)} %mul.20), kind=kOutput, calls=%fused_computation.12 | convolution fusion | flops 78643200 | bytes 2535424 | tf_op jit(solution)/shard_map/krxqn,sxqnj->rsxkj/dot_general | solution.py:547
  59.8 3.9 %collective-permute-start.11 = (f32[2,1,768]{2,1,0:T(1,128)}, f32[2,1,768]{2,1,0:T(1,128)S(1)}, u32[]{:S(2)}, u32[]{:S(2)}) collective-permute-start(f32[2,1,768]{2,1,0:T(1,128)} %shard_map.89.refs_3_), channel_id=1, source_target_pairs={{28,0},{0,4},{4,8},{8,12},{12,16},{16,20},{24,28},{29,1},{1,5},{5,... | collective-permute-start | bytes 18440 | tf_op jit(solution)/shard_map/ppermute | solution.py:112
  63.8 4.4 %collective-permute-done.11.refs_7_ = f32[2,1,768]{2,1,0:T(1,128)S(1)} collective-permute-done((f32[2,1,768]{2,1,0:T(1,128)}, f32[2,1,768]{2,1,0:T(1,128)S(1)}, u32[]{:S(2)}, u32[]{:S(2)}) %collective-permute-start.11) | collective-permute-done | bytes 6176 | tf_op jit(solution)/shard_map/ppermute | solution.py:112
  68.8 3.0 %shard_map.90.refs_3_ = f32[2,1,768]{2,1,0:T(1,128)} custom-call(f32[2,1,768]{2,1,0:T(1,128)} %copy-done.11, bf16[2,48,768]{2,1,0:T(8,128)(2,1)} %bitcast.60, bf16[9,2,48,768]{3,2,1,0:T(8,128)(2,1)} %bitcast.50, f32[2,1,768]{2,1,0:T(1,128)} %shard_map.89.refs_3_, f32[2,1,768]{2,1,0:T(1,128)} %copy-done.20, f32[2,1,768]{2,1,0:T(1,128)} %copy-done.22, ...), custom_call_target="tpu_custom_call" | custom-call | tf_op jit(solution)/shard_map/pallas_call | solution.py:446
  74.2 4.1 %collective-permute-start.15 = (f32[2,1,768]{2,1,0:T(1,128)}, f32[2,1,768]{2,1,0:T(1,128)S(1)}, u32[]{:S(2)}, u32[]{:S(2)}) collective-permute-start(f32[2,1,768]{2,1,0:T(1,128)} %shard_map.90.refs_3_), channel_id=1, source_target_pairs={{28,0},{0,4},{4,8},{8,12},{12,16},{16,20},{24,28},{29,1},{1,5},{5,... | collective-permute-start | bytes 18440 | tf_op jit(solution)/shard_map/ppermute | solution.py:112
  78.4 4.3 %collective-permute-done.15.refs_7_ = f32[2,1,768]{2,1,0:T(1,128)S(1)} collective-permute-done((f32[2,1,768]{2,1,0:T(1,128)}, f32[2,1,768]{2,1,0:T(1,128)S(1)}, u32[]{:S(2)}, u32[]{:S(2)}) %collective-permute-start.15) | collective-permute-done | bytes 6176 | tf_op jit(solution)/shard_map/ppermute | solution.py:112
  83.3 3.0 %shard_map.91 = f32[2,1,768]{2,1,0:T(1,128)} custom-call(f32[2,1,768]{2,1,0:T(1,128)} %copy-done.11, bf16[2,48,768]{2,1,0:T(8,128)(2,1)} %bitcast.61, bf16[9,2,48,768]{3,2,1,0:T(8,128)(2,1)} %bitcast.51, f32[2,1,768]{2,1,0:T(1,128)} %shard_map.90.refs_3_, f32[2,1,768]{2,1,0:T(1,128)} %copy-done.19, f32[2,1,768]{2,1,0:T(1,128)} %copy-done.21, ...), custom_call_target="tpu_custom_call" | custom-call | tf_op jit(solution)/shard_map/pallas_call | solution.py:446
  89.5 1.9 %collective-permute-start.18 = (f32[24,4,128]{2,1,0:T(4,128)S(1)}, f32[24,4,128]{2,1,0:T(4,128)S(1)}, u32[]{:S(2)}, u32[]{:S(2)}) collective-permute-start(f32[24,4,128]{2,1,0:T(4,128)S(1)} %slice.50), channel_id=1, source_target_pairs={{4,0},{8,4},{12,8},{16,12},{20,16},{28,24},{0,28},{5,1},{9,5},{13,... | collective-permute-start | bytes 147464 | tf_op jit(solution)/shard_map/ppermute | solution.py:112
  91.5 3.9 %collective-permute-start.19 = (f32[24,4,128]{2,1,0:T(4,128)S(1)}, f32[24,4,128]{2,1,0:T(4,128)S(1)}, u32[]{:S(2)}, u32[]{:S(2)}) collective-permute-start(f32[24,4,128]{2,1,0:T(4,128)S(1)} %slice.51), channel_id=1, source_target_pairs={{28,0},{0,4},{4,8},{8,12},{12,16},{16,20},{24,28},{29,1},{1,5},{5,... | collective-permute-start | bytes 147464 | tf_op jit(solution)/shard_map/ppermute | solution.py:112
  95.7 4.6 %collective-permute-done.19.refs_9_ = f32[24,4,128]{2,1,0:T(4,128)S(1)} collective-permute-done((f32[24,4,128]{2,1,0:T(4,128)S(1)}, f32[24,4,128]{2,1,0:T(4,128)S(1)}, u32[]{:S(2)}, u32[]{:S(2)}) %collective-permute-start.19) | collective-permute-done | bytes 49184 | tf_op jit(solution)/shard_map/ppermute | solution.py:112
  101.7 5.2 %shard_map.92 = (f32[24,16,128]{2,1,0:T(8,128)}, f32[24,16,64]{2,1,0:T(8,128)}, f32[24,16,64]{2,1,0:T(8,128)}, f32[24,4,128]{2,1,0:T(4,128)}, f32[24,4,128]{2,1,0:T(4,128)}) custom-call(f32[24,16,128]{2,1,0:T(8,128)} %bitcast.55, bf16[4,18,16,128]{3,2,1,0:T(8,128)(2,1)} %bitcast.48, bf16[4,18,16,128]{3,2,1,0:T(8,128)(2,1)} %get-tuple-element.26.refs_2_, ...), custom_call_target="tpu_custom_call" | custom-call | tf_op jit(solution)/shard_map/pallas_call | solution.py:363
  109.3 3.9 %collective-permute-start.23 = (f32[24,4,128]{2,1,0:T(4,128)}, f32[24,4,128]{2,1,0:T(4,128)S(1)}, u32[]{:S(2)}, u32[]{:S(2)}) collective-permute-start(f32[24,4,128]{2,1,0:T(4,128)} %get-tuple-element.37), channel_id=1, source_target_pairs={{28,0},{0,4},{4,8},{8,12},{12,16},{16,20},{24,28},{29,1},{1,5},{5,... | collective-permute-start | bytes 147464 | tf_op jit(solution)/shard_map/ppermute | solution.py:112
  114.0 4.3 %collective-permute-done.23.refs_9_ = f32[24,4,128]{2,1,0:T(4,128)S(1)} collective-permute-done((f32[24,4,128]{2,1,0:T(4,128)}, f32[24,4,128]{2,1,0:T(4,128)S(1)}, u32[]{:S(2)}, u32[]{:S(2)}) %collective-permute-start.23) | collective-permute-done | bytes 49184 | tf_op jit(solution)/shard_map/ppermute | solution.py:112
  119.1 5.0 %shard_map.93 = f32[24,16,128]{2,1,0:T(8,128)} custom-call(f32[24,16,128]{2,1,0:T(8,128)} %bitcast.56, bf16[4,18,16,128]{3,2,1,0:T(8,128)(2,1)} %bitcast.49, bf16[4,18,16,128]{3,2,1,0:T(8,128)(2,1)} %get-tuple-element.26.refs_2_, s32[16,128]{1,0:T(8,128)} %reshape.94.refs_2_.refs_3_, s32[16]{0:T(128)} %bitcast.68, f32[24,16,128]{2,1,0:T(8,128)} %get-tuple-element.33.refs_5_, ...), custom_call_target="tpu_custom_call" | custom-call | tf_op jit(solution)/shard_map/pallas_call | solution.py:363
  (113 shorter events, 26.4 us)
Async XLA Ops:
  6.2 20.8 %collective-permute-start.1 = (f32[42,16,64]{2,1,0:T(8,128)}, f32[42,16,64]{2,1,0:T(8,128)S(1)}, u32[]{:S(2)}, u32[]{:S(2)}) collective-permute-start(f32[42,16,64]{2,1,0:T(8,128)} %get-tuple-element.23), channel_id=1, source_target_pairs={{3,0},{0,1},{1,2},{2,3},{7,4},{4,5},{5,6},{6,7},{11,8},{8,9},{9,10... | collective-permute-start | bytes 516104 | tf_op jit(solution)/shard_map/ppermute | solution.py:112
  6.7 20.3 %collective-permute-start = (f32[24,16,64]{2,1,0:T(8,128)}, f32[24,16,64]{2,1,0:T(8,128)S(1)}, u32[]{:S(2)}, u32[]{:S(2)}) collective-permute-start(f32[24,16,64]{2,1,0:T(8,128)} %get-tuple-element.22), channel_id=1, source_target_pairs={{1,0},{2,1},{3,2},{0,3},{5,4},{6,5},{7,6},{4,7},{9,8},{10,9},{11,1... | collective-permute-start | bytes 294920 | tf_op jit(solution)/shard_map/ppermute | solution.py:112
  8.6 18.4 %collective-permute-start.3 = (f32[42,4,128]{2,1,0:T(4,128)}, f32[42,4,128]{2,1,0:T(4,128)S(1)}, u32[]{:S(2)}, u32[]{:S(2)}) collective-permute-start(f32[42,4,128]{2,1,0:T(4,128)} %get-tuple-element.25), channel_id=1, source_target_pairs={{28,0},{0,4},{4,8},{8,12},{12,16},{16,20},{24,28},{29,1},{1,5},{5,... | collective-permute-start | bytes 258056 | tf_op jit(solution)/shard_map/ppermute | solution.py:112
  12.9 14.1 %collective-permute-start.2 = (f32[24,4,128]{2,1,0:T(4,128)}, f32[24,4,128]{2,1,0:T(4,128)S(1)}, u32[]{:S(2)}, u32[]{:S(2)}) collective-permute-start(f32[24,4,128]{2,1,0:T(4,128)} %get-tuple-element.24), channel_id=1, source_target_pairs={{4,0},{8,4},{12,8},{16,12},{20,16},{28,24},{0,28},{5,1},{9,5},{13,... | collective-permute-start | bytes 147464 | tf_op jit(solution)/shard_map/ppermute | solution.py:112
  33.8 13.8 %collective-permute-start.4 = (f32[24,16,64]{2,1,0:T(8,128)}, f32[24,16,64]{2,1,0:T(8,128)S(1)}, u32[]{:S(2)}, u32[]{:S(2)}) collective-permute-start(f32[24,16,64]{2,1,0:T(8,128)} %get-tuple-element.29), channel_id=1, source_target_pairs={{1,0},{2,1},{3,2},{0,3},{5,4},{6,5},{7,6},{4,7},{9,8},{10,9},{11,1... | collective-permute-start | bytes 294920 | tf_op jit(solution)/shard_map/ppermute | solution.py:112
  33.8 13.8 %collective-permute-start.5 = (f32[24,16,64]{2,1,0:T(8,128)}, f32[24,16,64]{2,1,0:T(8,128)S(1)}, u32[]{:S(2)}, u32[]{:S(2)}) collective-permute-start(f32[24,16,64]{2,1,0:T(8,128)} %get-tuple-element.30), channel_id=1, source_target_pairs={{3,0},{0,1},{1,2},{2,3},{7,4},{4,5},{5,6},{6,7},{11,8},{8,9},{9,10... | collective-permute-start | bytes 294920 | tf_op jit(solution)/shard_map/ppermute | solution.py:112
  34.3 6.4 %collective-permute-start.6 = (f32[24,4,128]{2,1,0:T(4,128)}, f32[24,4,128]{2,1,0:T(4,128)S(1)}, u32[]{:S(2)}, u32[]{:S(2)}) collective-permute-start(f32[24,4,128]{2,1,0:T(4,128)} %get-tuple-element.31), channel_id=1, source_target_pairs={{4,0},{8,4},{12,8},{16,12},{20,16},{28,24},{0,28},{5,1},{9,5},{13,... | collective-permute-start | bytes 147464 | tf_op jit(solution)/shard_map/ppermute | solution.py:112
  38.2 9.3 %collective-permute-start.7 = (f32[24,4,128]{2,1,0:T(4,128)}, f32[24,4,128]{2,1,0:T(4,128)S(1)}, u32[]{:S(2)}, u32[]{:S(2)}) collective-permute-start(f32[24,4,128]{2,1,0:T(4,128)} %get-tuple-element.32), channel_id=1, source_target_pairs={{28,0},{0,4},{4,8},{8,12},{12,16},{16,20},{24,28},{29,1},{1,5},{5,... | collective-permute-start | bytes 147464 | tf_op jit(solution)/shard_map/ppermute | solution.py:112
  57.4 6.4 %collective-permute-start.8 = (f32[2,1,768]{2,1,0:T(1,128)}, f32[2,1,768]{2,1,0:T(1,128)S(1)}, u32[]{:S(2)}, u32[]{:S(2)}) collective-permute-start(f32[2,1,768]{2,1,0:T(1,128)} %shard_map.89.refs_3_), channel_id=1, source_target_pairs={{1,0},{2,1},{3,2},{0,3},{5,4},{6,5},{7,6},{4,7},{9,8},{10,9},{11,1... | collective-permute-start | bytes 18440 | tf_op jit(solution)/shard_map/ppermute | solution.py:112
  57.4 6.4 %collective-permute-start.9 = (f32[2,1,768]{2,1,0:T(1,128)}, f32[2,1,768]{2,1,0:T(1,128)S(1)}, u32[]{:S(2)}, u32[]{:S(2)}) collective-permute-start(f32[2,1,768]{2,1,0:T(1,128)} %shard_map.89.refs_3_), channel_id=1, source_target_pairs={{3,0},{0,1},{1,2},{2,3},{7,4},{4,5},{5,6},{6,7},{11,8},{8,9},{9,10... | collective-permute-start | bytes 18440 | tf_op jit(solution)/shard_map/ppermute | solution.py:112
  57.9 5.9 %collective-permute-start.10 = (f32[2,1,768]{2,1,0:T(1,128)}, f32[2,1,768]{2,1,0:T(1,128)S(1)}, u32[]{:S(2)}, u32[]{:S(2)}) collective-permute-start(f32[2,1,768]{2,1,0:T(1,128)} %shard_map.89.refs_3_), channel_id=1, source_target_pairs={{4,0},{8,4},{12,8},{16,12},{20,16},{28,24},{0,28},{5,1},{9,5},{13,... | collective-permute-start | bytes 18440 | tf_op jit(solution)/shard_map/ppermute | solution.py:112
  59.8 8.4 %collective-permute-start.11 = (f32[2,1,768]{2,1,0:T(1,128)}, f32[2,1,768]{2,1,0:T(1,128)S(1)}, u32[]{:S(2)}, u32[]{:S(2)}) collective-permute-start(f32[2,1,768]{2,1,0:T(1,128)} %shard_map.89.refs_3_), channel_id=1, source_target_pairs={{28,0},{0,4},{4,8},{8,12},{12,16},{16,20},{24,28},{29,1},{1,5},{5,... | collective-permute-start | bytes 18440 | tf_op jit(solution)/shard_map/ppermute | solution.py:112
  71.8 6.5 %collective-permute-start.12 = (f32[2,1,768]{2,1,0:T(1,128)}, f32[2,1,768]{2,1,0:T(1,128)S(1)}, u32[]{:S(2)}, u32[]{:S(2)}) collective-permute-start(f32[2,1,768]{2,1,0:T(1,128)} %shard_map.90.refs_3_), channel_id=1, source_target_pairs={{1,0},{2,1},{3,2},{0,3},{5,4},{6,5},{7,6},{4,7},{9,8},{10,9},{11,1... | collective-permute-start | bytes 18440 | tf_op jit(solution)/shard_map/ppermute | solution.py:112
  71.9 6.5 %collective-permute-start.13 = (f32[2,1,768]{2,1,0:T(1,128)}, f32[2,1,768]{2,1,0:T(1,128)S(1)}, u32[]{:S(2)}, u32[]{:S(2)}) collective-permute-start(f32[2,1,768]{2,1,0:T(1,128)} %shard_map.90.refs_3_), channel_id=1, source_target_pairs={{3,0},{0,1},{1,2},{2,3},{7,4},{4,5},{5,6},{6,7},{11,8},{8,9},{9,10... | collective-permute-start | bytes 18440 | tf_op jit(solution)/shard_map/ppermute | solution.py:112
  72.3 6.1 %collective-permute-start.14 = (f32[2,1,768]{2,1,0:T(1,128)}, f32[2,1,768]{2,1,0:T(1,128)S(1)}, u32[]{:S(2)}, u32[]{:S(2)}) collective-permute-start(f32[2,1,768]{2,1,0:T(1,128)} %shard_map.90.refs_3_), channel_id=1, source_target_pairs={{4,0},{8,4},{12,8},{16,12},{20,16},{28,24},{0,28},{5,1},{9,5},{13,... | collective-permute-start | bytes 18440 | tf_op jit(solution)/shard_map/ppermute | solution.py:112
  74.2 8.4 %collective-permute-start.15 = (f32[2,1,768]{2,1,0:T(1,128)}, f32[2,1,768]{2,1,0:T(1,128)S(1)}, u32[]{:S(2)}, u32[]{:S(2)}) collective-permute-start(f32[2,1,768]{2,1,0:T(1,128)} %shard_map.90.refs_3_), channel_id=1, source_target_pairs={{28,0},{0,4},{4,8},{8,12},{12,16},{16,20},{24,28},{29,1},{1,5},{5,... | collective-permute-start | bytes 18440 | tf_op jit(solution)/shard_map/ppermute | solution.py:112
  88.9 11.4 %collective-permute-start.16 = (f32[24,16,64]{2,1,0:T(8,128)S(1)}, f32[24,16,64]{2,1,0:T(8,128)S(1)}, u32[]{:S(2)}, u32[]{:S(2)}) collective-permute-start(f32[24,16,64]{2,1,0:T(8,128)S(1)} %get-tuple-element.47), channel_id=1, source_target_pairs={{1,0},{2,1},{3,2},{0,3},{5,4},{6,5},{7,6},{4,7},{9,8},{10,9},{11,1... | collective-permute-start | bytes 294920 | tf_op jit(solution)/shard_map/ppermute | solution.py:112
  89.1 11.2 %collective-permute-start.17 = (f32[24,16,64]{2,1,0:T(8,128)S(1)}, f32[24,16,64]{2,1,0:T(8,128)S(1)}, u32[]{:S(2)}, u32[]{:S(2)}) collective-permute-start(f32[24,16,64]{2,1,0:T(8,128)S(1)} %get-tuple-element.46), channel_id=1, source_target_pairs={{3,0},{0,1},{1,2},{2,3},{7,4},{4,5},{5,6},{6,7},{11,8},{8,9},{9,10... | collective-permute-start | bytes 294920 | tf_op jit(solution)/shard_map/ppermute | solution.py:112
  89.5 6.1 %collective-permute-start.18 = (f32[24,4,128]{2,1,0:T(4,128)S(1)}, f32[24,4,128]{2,1,0:T(4,128)S(1)}, u32[]{:S(2)}, u32[]{:S(2)}) collective-permute-start(f32[24,4,128]{2,1,0:T(4,128)S(1)} %slice.50), channel_id=1, source_target_pairs={{4,0},{8,4},{12,8},{16,12},{20,16},{28,24},{0,28},{5,1},{9,5},{13,... | collective-permute-start | bytes 147464 | tf_op jit(solution)/shard_map/ppermute | solution.py:112
  91.5 8.8 %collective-permute-start.19 = (f32[24,4,128]{2,1,0:T(4,128)S(1)}, f32[24,4,128]{2,1,0:T(4,128)S(1)}, u32[]{:S(2)}, u32[]{:S(2)}) collective-permute-start(f32[24,4,128]{2,1,0:T(4,128)S(1)} %slice.51), channel_id=1, source_target_pairs={{28,0},{0,4},{4,8},{8,12},{12,16},{16,20},{24,28},{29,1},{1,5},{5,... | collective-permute-start | bytes 147464 | tf_op jit(solution)/shard_map/ppermute | solution.py:112
  106.9 11.4 %collective-permute-start.20 = (f32[24,16,64]{2,1,0:T(8,128)}, f32[24,16,64]{2,1,0:T(8,128)S(1)}, u32[]{:S(2)}, u32[]{:S(2)}) collective-permute-start(f32[24,16,64]{2,1,0:T(8,128)} %get-tuple-element.34), channel_id=1, source_target_pairs={{1,0},{2,1},{3,2},{0,3},{5,4},{6,5},{7,6},{4,7},{9,8},{10,9},{11,1... | collective-permute-start | bytes 294920 | tf_op jit(solution)/shard_map/ppermute | solution.py:112
  107.3 11.0 %collective-permute-start.21 = (f32[24,16,64]{2,1,0:T(8,128)}, f32[24,16,64]{2,1,0:T(8,128)S(1)}, u32[]{:S(2)}, u32[]{:S(2)}) collective-permute-start(f32[24,16,64]{2,1,0:T(8,128)} %get-tuple-element.35), channel_id=1, source_target_pairs={{3,0},{0,1},{1,2},{2,3},{7,4},{4,5},{5,6},{6,7},{11,8},{8,9},{9,10... | collective-permute-start | bytes 294920 | tf_op jit(solution)/shard_map/ppermute | solution.py:112
  107.4 6.6 %collective-permute-start.22 = (f32[24,4,128]{2,1,0:T(4,128)}, f32[24,4,128]{2,1,0:T(4,128)S(1)}, u32[]{:S(2)}, u32[]{:S(2)}) collective-permute-start(f32[24,4,128]{2,1,0:T(4,128)} %get-tuple-element.36), channel_id=1, source_target_pairs={{4,0},{8,4},{12,8},{16,12},{20,16},{28,24},{0,28},{5,1},{9,5},{13,... | collective-permute-start | bytes 147464 | tf_op jit(solution)/shard_map/ppermute | solution.py:112
  109.3 9.0 %collective-permute-start.23 = (f32[24,4,128]{2,1,0:T(4,128)}, f32[24,4,128]{2,1,0:T(4,128)S(1)}, u32[]{:S(2)}, u32[]{:S(2)}) collective-permute-start(f32[24,4,128]{2,1,0:T(4,128)} %get-tuple-element.37), channel_id=1, source_target_pairs={{28,0},{0,4},{4,8},{8,12},{12,16},{16,20},{24,28},{29,1},{1,5},{5,... | collective-permute-start | bytes 147464 | tf_op jit(solution)/shard_map/ppermute | solution.py:112
  (27 other events, 65.6 us)

commit v13 on v9

--- a/solution.py
+++ b/solution.py
@@ -282,7 +282,7 @@
         return hopping(spinor, links, back_links, ahead_list, behind_list)
 
     def block_total(values):
-        return jnp.sum(jnp.sum(member * values[None], axis=2, keepdims=True), axis=1, keepdims=True)
+        return jnp.sum(member * values[None], axis=(1, 2), keepdims=True)
 
     update = None
     remainder = residue

time: 125 us -> 125 us (level)
  no operation moved by 1% of the time
where the time goes in v13:
time: 125 us; the launch traced here: 124 us
  starting transfers between devices  43.5 us (35%)
  Pallas kernels  29.9 us (24%)
  waiting for transfers between devices  25.3 us (20%)
  local copies, waits for them, and re-layouts  19.1 us (15%)
  matrix products  2.96 us (2%)
  other arithmetic  1.91 us (2%)
    ppermute x24, starting transfers between devices, permute_from(): return lax.ppermute(value, axis, pairs)  43.5 us
    ppermute x24, waiting for transfers between devices, permute_from(): return lax.ppermute(value, axis, pairs)  25.3 us
    pallas_call x5, Pallas kernels, run_pass(): pl.pallas_call(kernel, out_shape=out_shape, scratch_shapes=scratch, in_sp...  22.1 us
    unnamed x57, local copies, waits for them, and re-layouts  11.1 us
    pallas_call x3, Pallas kernels, run_coarse(): pl.pallas_call(kernel, out_shape=jax.ShapeDtypeStruct(source.shape, jnp.f...  7.77 us
    reshape x1, local copies, waits for them, and re-layouts, body(): vectors = test_vectors.reshape(NVEC, 2, 2, 6, site_count)  4.03 us
    dot_general x1, matrix products, body(): jnp.einsum('krxqn,sxqnj->rsxkj', vectors, weighted, preferred_element_typ...  2.51 us
  transfers between devices with their start and end apart: 24, of which 7 were waited for; matrix products, arithmetic and copies ran while one was open for 8% of the time, Pallas kernels for 0%

profile of v13, /device:TPU:0, one launch (start us, length us, event | category | flops | bytes accessed | tf_op | source)
XLA Modules:
  0.0 123.8 jit_solution(8324926519108661484)
XLA Ops:
  2.0 4.1 %shard_map.86 = (f32[24,16,128]{2,1,0:T(8,128)}, f32[24,16,64]{2,1,0:T(8,128)}, f32[42,16,64]{2,1,0:T(8,128)}, f32[24,4,128]{2,1,0:T(4,128)}, f32[42,4,128]{2,1,0:T(4,128)}) custom-call(f32[24,16,128]{2,1,0:T(8,128)} %bitcast.52, bf16[4,18,16,128]{3,2,1,0:T(8,128)(2,1)} %bitcast.45, s32[16,128]{1,0:T(8,128)} %reshape.94.refs_2_.refs_3_, s32[16]{0:T(128)} %bitcast.65), custom_call_target="tpu_custom_call" | custom-call | tf_op jit(solution)/shard_map/pallas_call | solution.py:363
  6.6 1.9 %collective-permute-start = (f32[24,16,64]{2,1,0:T(8,128)}, f32[24,16,64]{2,1,0:T(8,128)S(1)}, u32[]{:S(2)}, u32[]{:S(2)}) collective-permute-start(f32[24,16,64]{2,1,0:T(8,128)} %get-tuple-element.22), channel_id=1, source_target_pairs={{1,0},{2,1},{3,2},{0,3},{5,4},{6,5},{7,6},{4,7},{9,8},{10,9},{11,1... | collective-permute-start | bytes 294920 | tf_op jit(solution)/shard_map/ppermute | solution.py:112
  8.5 4.2 %collective-permute-start.3 = (f32[42,4,128]{2,1,0:T(4,128)}, f32[42,4,128]{2,1,0:T(4,128)S(1)}, u32[]{:S(2)}, u32[]{:S(2)}) collective-permute-start(f32[42,4,128]{2,1,0:T(4,128)} %get-tuple-element.25), channel_id=1, source_target_pairs={{28,0},{0,4},{4,8},{8,12},{12,16},{16,20},{24,28},{29,1},{1,5},{5,... | collective-permute-start | bytes 258056 | tf_op jit(solution)/shard_map/ppermute | solution.py:112
  12.8 5.0 %collective-permute-start.2 = (f32[24,4,128]{2,1,0:T(4,128)}, f32[24,4,128]{2,1,0:T(4,128)S(1)}, u32[]{:S(2)}, u32[]{:S(2)}) collective-permute-start(f32[24,4,128]{2,1,0:T(4,128)} %get-tuple-element.24), channel_id=1, source_target_pairs={{4,0},{8,4},{12,8},{16,12},{20,16},{28,24},{0,28},{5,1},{9,5},{13,... | collective-permute-start | bytes 147464 | tf_op jit(solution)/shard_map/ppermute | solution.py:112
  18.5 4.3 %copy.17 = bf16[1,24,24,4,4,128]{5,4,3,1,2,0:T(4,128)(2,1)} copy(bf16[1,24,24,4,4,128]{5,4,3,2,1,0:T(4,128)(2,1)} %param.9) | data formatting | bytes 4718592 | tf_op args[2]
  22.8 4.0 %reshape.96 = bf16[24,2,2,6,2048]{4,0,3,2,1:T(8,128)(2,1)S(1)} reshape(bf16[1,24,24,4,4,128]{5,4,3,1,2,0:T(4,128)(2,1)} %copy.17) | data formatting | bytes 4718592 | tf_op jit(solution)/shard_map/reshape | solution.py:520
  28.4 5.2 %shard_map.87 = (f32[24,16,128]{2,1,0:T(8,128)}, f32[24,16,64]{2,1,0:T(8,128)}, f32[24,16,64]{2,1,0:T(8,128)}, f32[24,4,128]{2,1,0:T(4,128)}, f32[24,4,128]{2,1,0:T(4,128)}, /*index=5*/bf16[4,18,16,128]{3,2,1,0:T(8,128)(2,1)}) custom-call(f32[24,16,128]{2,1,0:T(8,128)} %bitcast.53, bf16[4,18,16,128]{3,2,1,0:T(8,128)(2,1)} %bitcast.46, ...), custom_call_target="tpu_custom_call" | custom-call | tf_op jit(solution)/shard_map/pallas_call | solution.py:363
  34.1 3.9 %collective-permute-start.6 = (f32[24,4,128]{2,1,0:T(4,128)}, f32[24,4,128]{2,1,0:T(4,128)S(1)}, u32[]{:S(2)}, u32[]{:S(2)}) collective-permute-start(f32[24,4,128]{2,1,0:T(4,128)} %get-tuple-element.31), channel_id=1, source_target_pairs={{4,0},{8,4},{12,8},{16,12},{20,16},{28,24},{0,28},{5,1},{9,5},{13,... | collective-permute-start | bytes 147464 | tf_op jit(solution)/shard_map/ppermute | solution.py:112
  40.5 6.9 %collective-permute-done.7.refs_8_ = f32[24,4,128]{2,1,0:T(4,128)S(1)} collective-permute-done((f32[24,4,128]{2,1,0:T(4,128)}, f32[24,4,128]{2,1,0:T(4,128)S(1)}, u32[]{:S(2)}, u32[]{:S(2)}) %collective-permute-start.7) | collective-permute-done | bytes 49184 | tf_op jit(solution)/shard_map/ppermute | solution.py:112
  48.1 2.7 %shard_map.88 = bf16[24,16,128]{2,1,0:T(8,128)(2,1)} custom-call(f32[24,16,128]{2,1,0:T(8,128)} %bitcast.54, bf16[4,18,16,128]{3,2,1,0:T(8,128)(2,1)} %bitcast.47, bf16[4,18,16,128]{3,2,1,0:T(8,128)(2,1)} %get-tuple-element.26.refs_2_, s32[16,128]{1,0:T(8,128)} %reshape.94.refs_2_.refs_3_, f32[24,16,128]{2,1,0:T(8,128)} %get-tuple-element.27.refs_4_, ...), custom_call_target="tpu_custom_call" | custom-call | tf_op jit(solution)/shard_map/pallas_call | solution.py:363
  51.9 2.5 %fusion.8 = f32[2,2,2,24,16]{3,4,0,1,2:T(8,128)S(1)} fusion(bf16[2048,16]{0,1:T(8,128)(2,1)S(1)} %convert_convert_fusion, bf16[24,2,2,6,2048]{4,0,3,2,1:T(8,128)(2,1)S(1)} %reshape.96, bf16[2,2,6,2048]{3,2,1,0:T(8,128)(2,1)S(1)} %mul.20), kind=kOutput, calls=%fused_computation.12 | convolution fusion | flops 78643200 | bytes 2535424 | tf_op jit(solution)/shard_map/krxqn,sxqnj->rsxkj/dot_general | solution.py:547
  59.6 3.9 %collective-permute-start.11 = (f32[2,1,768]{2,1,0:T(1,128)}, f32[2,1,768]{2,1,0:T(1,128)S(1)}, u32[]{:S(2)}, u32[]{:S(2)}) collective-permute-start(f32[2,1,768]{2,1,0:T(1,128)} %shard_map.89.refs_3_), channel_id=1, source_target_pairs={{28,0},{0,4},{4,8},{8,12},{12,16},{16,20},{24,28},{29,1},{1,5},{5,... | collective-permute-start | bytes 18440 | tf_op jit(solution)/shard_map/ppermute | solution.py:112
  63.6 4.4 %collective-permute-done.11.refs_7_ = f32[2,1,768]{2,1,0:T(1,128)S(1)} collective-permute-done((f32[2,1,768]{2,1,0:T(1,128)}, f32[2,1,768]{2,1,0:T(1,128)S(1)}, u32[]{:S(2)}, u32[]{:S(2)}) %collective-permute-start.11) | collective-permute-done | bytes 6176 | tf_op jit(solution)/shard_map/ppermute | solution.py:112
  68.6 3.0 %shard_map.90.refs_3_ = f32[2,1,768]{2,1,0:T(1,128)} custom-call(f32[2,1,768]{2,1,0:T(1,128)} %copy-done.11, bf16[2,48,768]{2,1,0:T(8,128)(2,1)} %bitcast.60, bf16[9,2,48,768]{3,2,1,0:T(8,128)(2,1)} %bitcast.50, f32[2,1,768]{2,1,0:T(1,128)} %shard_map.89.refs_3_, f32[2,1,768]{2,1,0:T(1,128)} %copy-done.20, f32[2,1,768]{2,1,0:T(1,128)} %copy-done.22, ...), custom_call_target="tpu_custom_call" | custom-call | tf_op jit(solution)/shard_map/pallas_call | solution.py:446
  74.0 4.1 %collective-permute-start.15 = (f32[2,1,768]{2,1,0:T(1,128)}, f32[2,1,768]{2,1,0:T(1,128)S(1)}, u32[]{:S(2)}, u32[]{:S(2)}) collective-permute-start(f32[2,1,768]{2,1,0:T(1,128)} %shard_map.90.refs_3_), channel_id=1, source_target_pairs={{28,0},{0,4},{4,8},{8,12},{12,16},{16,20},{24,28},{29,1},{1,5},{5,... | collective-permute-start | bytes 18440 | tf_op jit(solution)/shard_map/ppermute | solution.py:112
  78.2 4.3 %collective-permute-done.15.refs_7_ = f32[2,1,768]{2,1,0:T(1,128)S(1)} collective-permute-done((f32[2,1,768]{2,1,0:T(1,128)}, f32[2,1,768]{2,1,0:T(1,128)S(1)}, u32[]{:S(2)}, u32[]{:S(2)}) %collective-permute-start.15) | collective-permute-done | bytes 6176 | tf_op jit(solution)/shard_map/ppermute | solution.py:112
  83.1 3.0 %shard_map.91 = f32[2,1,768]{2,1,0:T(1,128)} custom-call(f32[2,1,768]{2,1,0:T(1,128)} %copy-done.11, bf16[2,48,768]{2,1,0:T(8,128)(2,1)} %bitcast.61, bf16[9,2,48,768]{3,2,1,0:T(8,128)(2,1)} %bitcast.51, f32[2,1,768]{2,1,0:T(1,128)} %shard_map.90.refs_3_, f32[2,1,768]{2,1,0:T(1,128)} %copy-done.19, f32[2,1,768]{2,1,0:T(1,128)} %copy-done.21, ...), custom_call_target="tpu_custom_call" | custom-call | tf_op jit(solution)/shard_map/pallas_call | solution.py:446
  89.4 1.9 %collective-permute-start.18 = (f32[24,4,128]{2,1,0:T(4,128)S(1)}, f32[24,4,128]{2,1,0:T(4,128)S(1)}, u32[]{:S(2)}, u32[]{:S(2)}) collective-permute-start(f32[24,4,128]{2,1,0:T(4,128)S(1)} %slice.50), channel_id=1, source_target_pairs={{4,0},{8,4},{12,8},{16,12},{20,16},{28,24},{0,28},{5,1},{9,5},{13,... | collective-permute-start | bytes 147464 | tf_op jit(solution)/shard_map/ppermute | solution.py:112
  91.4 3.9 %collective-permute-start.19 = (f32[24,4,128]{2,1,0:T(4,128)S(1)}, f32[24,4,128]{2,1,0:T(4,128)S(1)}, u32[]{:S(2)}, u32[]{:S(2)}) collective-permute-start(f32[24,4,128]{2,1,0:T(4,128)S(1)} %slice.51), channel_id=1, source_target_pairs={{28,0},{0,4},{4,8},{8,12},{12,16},{16,20},{24,28},{29,1},{1,5},{5,... | collective-permute-start | bytes 147464 | tf_op jit(solution)/shard_map/ppermute | solution.py:112
  95.6 4.6 %collective-permute-done.19.refs_9_ = f32[24,4,128]{2,1,0:T(4,128)S(1)} collective-permute-done((f32[24,4,128]{2,1,0:T(4,128)S(1)}, f32[24,4,128]{2,1,0:T(4,128)S(1)}, u32[]{:S(2)}, u32[]{:S(2)}) %collective-permute-start.19) | collective-permute-done | bytes 49184 | tf_op jit(solution)/shard_map/ppermute | solution.py:112
  101.6 5.1 %shard_map.92 = (f32[24,16,128]{2,1,0:T(8,128)}, f32[24,16,64]{2,1,0:T(8,128)}, f32[24,16,64]{2,1,0:T(8,128)}, f32[24,4,128]{2,1,0:T(4,128)}, f32[24,4,128]{2,1,0:T(4,128)}) custom-call(f32[24,16,128]{2,1,0:T(8,128)} %bitcast.55, bf16[4,18,16,128]{3,2,1,0:T(8,128)(2,1)} %bitcast.48, bf16[4,18,16,128]{3,2,1,0:T(8,128)(2,1)} %get-tuple-element.26.refs_2_, ...), custom_call_target="tpu_custom_call" | custom-call | tf_op jit(solution)/shard_map/pallas_call | solution.py:363
  109.1 3.9 %collective-permute-start.23 = (f32[24,4,128]{2,1,0:T(4,128)}, f32[24,4,128]{2,1,0:T(4,128)S(1)}, u32[]{:S(2)}, u32[]{:S(2)}) collective-permute-start(f32[24,4,128]{2,1,0:T(4,128)} %get-tuple-element.37), channel_id=1, source_target_pairs={{28,0},{0,4},{4,8},{8,12},{12,16},{16,20},{24,28},{29,1},{1,5},{5,... | collective-permute-start | bytes 147464 | tf_op jit(solution)/shard_map/ppermute | solution.py:112
  113.8 4.3 %collective-permute-done.23.refs_9_ = f32[24,4,128]{2,1,0:T(4,128)S(1)} collective-permute-done((f32[24,4,128]{2,1,0:T(4,128)}, f32[24,4,128]{2,1,0:T(4,128)S(1)}, u32[]{:S(2)}, u32[]{:S(2)}) %collective-permute-start.23) | collective-permute-done | bytes 49184 | tf_op jit(solution)/shard_map/ppermute | solution.py:112
  118.9 4.9 %shard_map.93 = f32[24,16,128]{2,1,0:T(8,128)} custom-call(f32[24,16,128]{2,1,0:T(8,128)} %bitcast.56, bf16[4,18,16,128]{3,2,1,0:T(8,128)(2,1)} %bitcast.49, bf16[4,18,16,128]{3,2,1,0:T(8,128)(2,1)} %get-tuple-element.26.refs_2_, s32[16,128]{1,0:T(8,128)} %reshape.94.refs_2_.refs_3_, s32[16]{0:T(128)} %bitcast.68, f32[24,16,128]{2,1,0:T(8,128)} %get-tuple-element.33.refs_5_, ...), custom_call_target="tpu_custom_call" | custom-call | tf_op jit(solution)/shard_map/pallas_call | solution.py:363
  (113 shorter events, 26.5 us)
Async XLA Ops:
  6.1 20.8 %collective-permute-start.1 = (f32[42,16,64]{2,1,0:T(8,128)}, f32[42,16,64]{2,1,0:T(8,128)S(1)}, u32[]{:S(2)}, u32[]{:S(2)}) collective-permute-start(f32[42,16,64]{2,1,0:T(8,128)} %get-tuple-element.23), channel_id=1, source_target_pairs={{3,0},{0,1},{1,2},{2,3},{7,4},{4,5},{5,6},{6,7},{11,8},{8,9},{9,10... | collective-permute-start | bytes 516104 | tf_op jit(solution)/shard_map/ppermute | solution.py:112
  6.6 20.3 %collective-permute-start = (f32[24,16,64]{2,1,0:T(8,128)}, f32[24,16,64]{2,1,0:T(8,128)S(1)}, u32[]{:S(2)}, u32[]{:S(2)}) collective-permute-start(f32[24,16,64]{2,1,0:T(8,128)} %get-tuple-element.22), channel_id=1, source_target_pairs={{1,0},{2,1},{3,2},{0,3},{5,4},{6,5},{7,6},{4,7},{9,8},{10,9},{11,1... | collective-permute-start | bytes 294920 | tf_op jit(solution)/shard_map/ppermute | solution.py:112
  8.5 18.4 %collective-permute-start.3 = (f32[42,4,128]{2,1,0:T(4,128)}, f32[42,4,128]{2,1,0:T(4,128)S(1)}, u32[]{:S(2)}, u32[]{:S(2)}) collective-permute-start(f32[42,4,128]{2,1,0:T(4,128)} %get-tuple-element.25), channel_id=1, source_target_pairs={{28,0},{0,4},{4,8},{8,12},{12,16},{16,20},{24,28},{29,1},{1,5},{5,... | collective-permute-start | bytes 258056 | tf_op jit(solution)/shard_map/ppermute | solution.py:112
  12.8 14.1 %collective-permute-start.2 = (f32[24,4,128]{2,1,0:T(4,128)}, f32[24,4,128]{2,1,0:T(4,128)S(1)}, u32[]{:S(2)}, u32[]{:S(2)}) collective-permute-start(f32[24,4,128]{2,1,0:T(4,128)} %get-tuple-element.24), channel_id=1, source_target_pairs={{4,0},{8,4},{12,8},{16,12},{20,16},{28,24},{0,28},{5,1},{9,5},{13,... | collective-permute-start | bytes 147464 | tf_op jit(solution)/shard_map/ppermute | solution.py:112
  33.6 13.8 %collective-permute-start.4 = (f32[24,16,64]{2,1,0:T(8,128)}, f32[24,16,64]{2,1,0:T(8,128)S(1)}, u32[]{:S(2)}, u32[]{:S(2)}) collective-permute-start(f32[24,16,64]{2,1,0:T(8,128)} %get-tuple-element.29), channel_id=1, source_target_pairs={{1,0},{2,1},{3,2},{0,3},{5,4},{6,5},{7,6},{4,7},{9,8},{10,9},{11,1... | collective-permute-start | bytes 294920 | tf_op jit(solution)/shard_map/ppermute | solution.py:112
  33.6 13.8 %collective-permute-start.5 = (f32[24,16,64]{2,1,0:T(8,128)}, f32[24,16,64]{2,1,0:T(8,128)S(1)}, u32[]{:S(2)}, u32[]{:S(2)}) collective-permute-start(f32[24,16,64]{2,1,0:T(8,128)} %get-tuple-element.30), channel_id=1, source_target_pairs={{3,0},{0,1},{1,2},{2,3},{7,4},{4,5},{5,6},{6,7},{11,8},{8,9},{9,10... | collective-permute-start | bytes 294920 | tf_op jit(solution)/shard_map/ppermute | solution.py:112
  34.1 6.4 %collective-permute-start.6 = (f32[24,4,128]{2,1,0:T(4,128)}, f32[24,4,128]{2,1,0:T(4,128)S(1)}, u32[]{:S(2)}, u32[]{:S(2)}) collective-permute-start(f32[24,4,128]{2,1,0:T(4,128)} %get-tuple-element.31), channel_id=1, source_target_pairs={{4,0},{8,4},{12,8},{16,12},{20,16},{28,24},{0,28},{5,1},{9,5},{13,... | collective-permute-start | bytes 147464 | tf_op jit(solution)/shard_map/ppermute | solution.py:112
  38.0 9.3 %collective-permute-start.7 = (f32[24,4,128]{2,1,0:T(4,128)}, f32[24,4,128]{2,1,0:T(4,128)S(1)}, u32[]{:S(2)}, u32[]{:S(2)}) collective-permute-start(f32[24,4,128]{2,1,0:T(4,128)} %get-tuple-element.32), channel_id=1, source_target_pairs={{28,0},{0,4},{4,8},{8,12},{12,16},{16,20},{24,28},{29,1},{1,5},{5,... | collective-permute-start | bytes 147464 | tf_op jit(solution)/shard_map/ppermute | solution.py:112
  57.2 6.4 %collective-permute-start.8 = (f32[2,1,768]{2,1,0:T(1,128)}, f32[2,1,768]{2,1,0:T(1,128)S(1)}, u32[]{:S(2)}, u32[]{:S(2)}) collective-permute-start(f32[2,1,768]{2,1,0:T(1,128)} %shard_map.89.refs_3_), channel_id=1, source_target_pairs={{1,0},{2,1},{3,2},{0,3},{5,4},{6,5},{7,6},{4,7},{9,8},{10,9},{11,1... | collective-permute-start | bytes 18440 | tf_op jit(solution)/shard_map/ppermute | solution.py:112
  57.2 6.4 %collective-permute-start.9 = (f32[2,1,768]{2,1,0:T(1,128)}, f32[2,1,768]{2,1,0:T(1,128)S(1)}, u32[]{:S(2)}, u32[]{:S(2)}) collective-permute-start(f32[2,1,768]{2,1,0:T(1,128)} %shard_map.89.refs_3_), channel_id=1, source_target_pairs={{3,0},{0,1},{1,2},{2,3},{7,4},{4,5},{5,6},{6,7},{11,8},{8,9},{9,10... | collective-permute-start | bytes 18440 | tf_op jit(solution)/shard_map/ppermute | solution.py:112
  57.7 5.9 %collective-permute-start.10 = (f32[2,1,768]{2,1,0:T(1,128)}, f32[2,1,768]{2,1,0:T(1,128)S(1)}, u32[]{:S(2)}, u32[]{:S(2)}) collective-permute-start(f32[2,1,768]{2,1,0:T(1,128)} %shard_map.89.refs_3_), channel_id=1, source_target_pairs={{4,0},{8,4},{12,8},{16,12},{20,16},{28,24},{0,28},{5,1},{9,5},{13,... | collective-permute-start | bytes 18440 | tf_op jit(solution)/shard_map/ppermute | solution.py:112
  59.6 8.4 %collective-permute-start.11 = (f32[2,1,768]{2,1,0:T(1,128)}, f32[2,1,768]{2,1,0:T(1,128)S(1)}, u32[]{:S(2)}, u32[]{:S(2)}) collective-permute-start(f32[2,1,768]{2,1,0:T(1,128)} %shard_map.89.refs_3_), channel_id=1, source_target_pairs={{28,0},{0,4},{4,8},{8,12},{12,16},{16,20},{24,28},{29,1},{1,5},{5,... | collective-permute-start | bytes 18440 | tf_op jit(solution)/shard_map/ppermute | solution.py:112
  71.6 6.5 %collective-permute-start.12 = (f32[2,1,768]{2,1,0:T(1,128)}, f32[2,1,768]{2,1,0:T(1,128)S(1)}, u32[]{:S(2)}, u32[]{:S(2)}) collective-permute-start(f32[2,1,768]{2,1,0:T(1,128)} %shard_map.90.refs_3_), channel_id=1, source_target_pairs={{1,0},{2,1},{3,2},{0,3},{5,4},{6,5},{7,6},{4,7},{9,8},{10,9},{11,1... | collective-permute-start | bytes 18440 | tf_op jit(solution)/shard_map/ppermute | solution.py:112
  71.7 6.5 %collective-permute-start.13 = (f32[2,1,768]{2,1,0:T(1,128)}, f32[2,1,768]{2,1,0:T(1,128)S(1)}, u32[]{:S(2)}, u32[]{:S(2)}) collective-permute-start(f32[2,1,768]{2,1,0:T(1,128)} %shard_map.90.refs_3_), channel_id=1, source_target_pairs={{3,0},{0,1},{1,2},{2,3},{7,4},{4,5},{5,6},{6,7},{11,8},{8,9},{9,10... | collective-permute-start | bytes 18440 | tf_op jit(solution)/shard_map/ppermute | solution.py:112
  72.1 6.1 %collective-permute-start.14 = (f32[2,1,768]{2,1,0:T(1,128)}, f32[2,1,768]{2,1,0:T(1,128)S(1)}, u32[]{:S(2)}, u32[]{:S(2)}) collective-permute-start(f32[2,1,768]{2,1,0:T(1,128)} %shard_map.90.refs_3_), channel_id=1, source_target_pairs={{4,0},{8,4},{12,8},{16,12},{20,16},{28,24},{0,28},{5,1},{9,5},{13,... | collective-permute-start | bytes 18440 | tf_op jit(solution)/shard_map/ppermute | solution.py:112
  74.0 8.4 %collective-permute-start.15 = (f32[2,1,768]{2,1,0:T(1,128)}, f32[2,1,768]{2,1,0:T(1,128)S(1)}, u32[]{:S(2)}, u32[]{:S(2)}) collective-permute-start(f32[2,1,768]{2,1,0:T(1,128)} %shard_map.90.refs_3_), channel_id=1, source_target_pairs={{28,0},{0,4},{4,8},{8,12},{12,16},{16,20},{24,28},{29,1},{1,5},{5,... | collective-permute-start | bytes 18440 | tf_op jit(solution)/shard_map/ppermute | solution.py:112
  88.8 11.4 %collective-permute-start.16 = (f32[24,16,64]{2,1,0:T(8,128)S(1)}, f32[24,16,64]{2,1,0:T(8,128)S(1)}, u32[]{:S(2)}, u32[]{:S(2)}) collective-permute-start(f32[24,16,64]{2,1,0:T(8,128)S(1)} %get-tuple-element.47), channel_id=1, source_target_pairs={{1,0},{2,1},{3,2},{0,3},{5,4},{6,5},{7,6},{4,7},{9,8},{10,9},{11,1... | collective-permute-start | bytes 294920 | tf_op jit(solution)/shard_map/ppermute | solution.py:112
  89.0 11.2 %collective-permute-start.17 = (f32[24,16,64]{2,1,0:T(8,128)S(1)}, f32[24,16,64]{2,1,0:T(8,128)S(1)}, u32[]{:S(2)}, u32[]{:S(2)}) collective-permute-start(f32[24,16,64]{2,1,0:T(8,128)S(1)} %get-tuple-element.46), channel_id=1, source_target_pairs={{3,0},{0,1},{1,2},{2,3},{7,4},{4,5},{5,6},{6,7},{11,8},{8,9},{9,10... | collective-permute-start | bytes 294920 | tf_op jit(solution)/shard_map/ppermute | solution.py:112
  89.4 6.1 %collective-permute-start.18 = (f32[24,4,128]{2,1,0:T(4,128)S(1)}, f32[24,4,128]{2,1,0:T(4,128)S(1)}, u32[]{:S(2)}, u32[]{:S(2)}) collective-permute-start(f32[24,4,128]{2,1,0:T(4,128)S(1)} %slice.50), channel_id=1, source_target_pairs={{4,0},{8,4},{12,8},{16,12},{20,16},{28,24},{0,28},{5,1},{9,5},{13,... | collective-permute-start | bytes 147464 | tf_op jit(solution)/shard_map/ppermute | solution.py:112
  91.4 8.8 %collective-permute-start.19 = (f32[24,4,128]{2,1,0:T(4,128)S(1)}, f32[24,4,128]{2,1,0:T(4,128)S(1)}, u32[]{:S(2)}, u32[]{:S(2)}) collective-permute-start(f32[24,4,128]{2,1,0:T(4,128)S(1)} %slice.51), channel_id=1, source_target_pairs={{28,0},{0,4},{4,8},{8,12},{12,16},{16,20},{24,28},{29,1},{1,5},{5,... | collective-permute-start | bytes 147464 | tf_op jit(solution)/shard_map/ppermute | solution.py:112
  106.7 11.4 %collective-permute-start.20 = (f32[24,16,64]{2,1,0:T(8,128)}, f32[24,16,64]{2,1,0:T(8,128)S(1)}, u32[]{:S(2)}, u32[]{:S(2)}) collective-permute-start(f32[24,16,64]{2,1,0:T(8,128)} %get-tuple-element.34), channel_id=1, source_target_pairs={{1,0},{2,1},{3,2},{0,3},{5,4},{6,5},{7,6},{4,7},{9,8},{10,9},{11,1... | collective-permute-start | bytes 294920 | tf_op jit(solution)/shard_map/ppermute | solution.py:112
  107.2 11.0 %collective-permute-start.21 = (f32[24,16,64]{2,1,0:T(8,128)}, f32[24,16,64]{2,1,0:T(8,128)S(1)}, u32[]{:S(2)}, u32[]{:S(2)}) collective-permute-start(f32[24,16,64]{2,1,0:T(8,128)} %get-tuple-element.35), channel_id=1, source_target_pairs={{3,0},{0,1},{1,2},{2,3},{7,4},{4,5},{5,6},{6,7},{11,8},{8,9},{9,10... | collective-permute-start | bytes 294920 | tf_op jit(solution)/shard_map/ppermute | solution.py:112
  107.2 6.6 %collective-permute-start.22 = (f32[24,4,128]{2,1,0:T(4,128)}, f32[24,4,128]{2,1,0:T(4,128)S(1)}, u32[]{:S(2)}, u32[]{:S(2)}) collective-permute-start(f32[24,4,128]{2,1,0:T(4,128)} %get-tuple-element.36), channel_id=1, source_target_pairs={{4,0},{8,4},{12,8},{16,12},{20,16},{28,24},{0,28},{5,1},{9,5},{13,... | collective-permute-start | bytes 147464 | tf_op jit(solution)/shard_map/ppermute | solution.py:112
  109.1 9.0 %collective-permute-start.23 = (f32[24,4,128]{2,1,0:T(4,128)}, f32[24,4,128]{2,1,0:T(4,128)S(1)}, u32[]{:S(2)}, u32[]{:S(2)}) collective-permute-start(f32[24,4,128]{2,1,0:T(4,128)} %get-tuple-element.37), channel_id=1, source_target_pairs={{28,0},{0,4},{4,8},{8,12},{12,16},{16,20},{24,28},{29,1},{1,5},{5,... | collective-permute-start | bytes 147464 | tf_op jit(solution)/shard_map/ppermute | solution.py:112
  (27 other events, 65.6 us)
